TPU v7x, 512 devices: a whole 4x4x16 slice. The times are simulated.
512 devices in a mesh: row: 64 (over z, y_lo, core), col: 8 (over y_hi, x).
Axes of the slice: x: 4, y: 4 (y_hi: 2, y_lo: 2; y = y_hi * 2 + y_lo), z: 16, core: 2. Of those that a mesh axis runs over, the one named last changes fastest.
Arguments:
- p_band: bfloat16 [640, 16, 128, 128], P('row', 'col'), may hold values from -6 to 6
- blocks: bfloat16 [640, 3, 128, 128], P('row'), may hold values from -0.375 to 0.375
- block_offsets: int32 [640, 3], P('row'), may hold values from -1 to 1
- block_live: int32 [640], P('row'), may hold values from 1 to 3, as said below
- q_var: float32 [640, 128], P('row'), may hold values from 0.1 to 1
Outputs:
- propagated: bfloat16 [640, 16, 128, 128], P('row', 'col')
Inputs may be any that keep to these rules, and one draw needn't show every extreme that they name: `block_live`: tile rows with all 3 blocks live come in runs.
All inputs are finite; a program needn't handle non-finite values.
Results may differ from a plain program's by a relative error of at most 0.0058.
Values may be sent and summed in bfloat16 or wider, within the bound.
No kernel may reach another device: no remote copies, remote signals or barrier semaphores. Data moves between devices by JAX's collectives and lax.ppermute only.
A program may use at most 64 MiB of HBM per device.

v0:
```python
import jax
import jax.numpy as jnp
from jax import lax
from jax.sharding import PartitionSpec as P


def padded_2(cells, sides, width):
    for axis, dim in sides:
        count = lax.axis_size(axis)
        ends = count - 1
        head = lax.slice_in_dim(cells, 0, width, axis=dim)
        tail = lax.slice_in_dim(cells, cells.shape[dim] - width, cells.shape[dim], axis=dim)
        cells = jnp.concatenate(
            [
                lax.ppermute(tail, axis, [(i, (i + 1) % count) for i in range(ends)]),
                cells,
                lax.ppermute(head, axis, [((i + 1) % count, i) for i in range(ends)]),
            ],
            axis=dim,
        )
    return cells


def assemble(blocks, block_offsets, block_live):
    slot_ids = jnp.arange(blocks.shape[1], dtype=jnp.int32)
    alive = slot_ids[None, :] < block_live[:, None]
    targets = jnp.arange(3, dtype=jnp.int32) - 1
    choose = (block_offsets[:, :, None] == targets[None, None, :]) & alive[:, :, None]
    summed_total = jnp.einsum(
        "tmf,tmab->tfab", choose.astype(jnp.bfloat16), blocks, preferred_element_type=jnp.float32
    )
    return summed_total.astype(jnp.bfloat16)


def tile_product(form, operand_one, operand_two):
    batched = "t" + form.replace(",", ",t").replace(">", ">t")
    return jnp.einsum(batched, operand_one, operand_two, preferred_element_type=jnp.float32)


def shards(p_band, blocks, block_offsets, block_live, q_var):
    tile_rows = p_band.shape[0]
    band_local = p_band.shape[1]
    tile_size = p_band.shape[2]
    col_count = lax.axis_size("col")
    half_band = band_local * col_count // 2
    grid_tiles = tile_rows * lax.axis_size("row")
    col_id = lax.axis_index("col")
    first_row = lax.axis_index("row") * tile_rows
    low_offset = col_id * band_local - half_band
    row_ids = first_row + jnp.arange(tile_rows, dtype=jnp.int32)[:, None]
    columns = row_ids + low_offset + jnp.arange(band_local, dtype=jnp.int32)[None, :]
    inside = (columns >= 0) & (columns < grid_tiles)
    prior = jnp.where(inside[:, :, None, None], p_band, jnp.zeros_like(p_band))
    jacobian = assemble(blocks, block_offsets, block_live)
    widened = padded_2(prior, (("row", 0), ("col", 1)), 2)
    padded = widened[1:-1]
    extended = band_local + 2
    spread_shape = (tile_rows, extended, tile_size, tile_size)
    spread_sum = jnp.zeros(spread_shape, jnp.float32)
    for shift_f in range(3):
        source = padded[shift_f : shift_f + tile_rows, 2 - shift_f : 2 - shift_f + extended]
        spread_sum = spread_sum + tile_product("ab,ubc->uac", jacobian[:, shift_f], source)
    spread_out_block = spread_sum.astype(jnp.bfloat16)
    beside_all = padded_2(jacobian, (("row", 0),), half_band)
    window_slice = lax.dynamic_slice_in_dim(
        beside_all, col_id * band_local, tile_rows + band_local - 1, 0
    )
    eye_tile = jnp.eye(tile_size, dtype=jnp.float32)
    noise = q_var[:, :, None] * eye_tile[None]
    tile_shape = (tile_rows, tile_size, tile_size)
    results = []
    for offset_position in range(band_local):
        summed_total = jnp.zeros(tile_shape, jnp.float32)
        for shift_amount_second in range(3):
            summed_total = summed_total + tile_product(
                "ab,cb->ac",
                spread_out_block[:, offset_position + shift_amount_second],
                window_slice[offset_position : offset_position + tile_rows, shift_amount_second],
            )
        on_diagonal = low_offset + offset_position == 0
        summed_total = summed_total + jnp.where(on_diagonal, noise, jnp.zeros_like(noise))
        results.append(summed_total)
    stacked = jnp.stack(results, axis=1)
    return jnp.where(inside[:, :, None, None], stacked, jnp.zeros_like(stacked)).astype(
        jnp.bfloat16
    )


def solution(mesh):
    placed = (
        P("row", "col", None, None),
        P("row", None, None, None),
        P("row", None),
        P("row"),
        P("row", None),
    )
    return jax.shard_map(
        shards, mesh=mesh, in_specs=placed, out_specs=P("row", "col", None, None), check_vma=False
    )
```

profile of v0, /device:TPU:501, one launch (start us, length us, event | category | flops | bytes accessed | tf_op | source)
XLA Modules:
  0.0 70.6 jit_solution(10119421956551068363)
XLA Ops:
  0.0 0.9 %copy.41 = s32[10,3]{1,0:T(8,128)S(1)} copy(s32[10,3]{0,1:T(4,128)} %param.7) | data formatting | bytes 240 | tf_op args[2]
  0.9 0.7 %iota_compare_fusion.1 = pred[10,3]{1,0:T(8,128)(4,1)S(1)} fusion(s32[10]{0:T(128)} %param.8), kind=kLoop, calls=%fused_computation.81 | loop fusion | flops 30 | bytes 70 | tf_op jit(solution)/shard_map/lt | solution.py:26
  1.6 1.0 %convolution_convert_fusion = bf16[10,3,128,128]{3,1,2,0:T(4,128)(2,1)S(1)} fusion(bf16[10,3,128,128]{3,2,1,0:T(8,128)(2,1)S(1)} %copy-done, s32[10,3]{1,0:T(8,128)S(1)} %copy.41, s32[3]{0:T(128)S(1)} %iota_add_fusion.1, pred[10,3]{1,0:T(8,128)(4,1)S(1)} %iota_compare_fusion.1), kind=kOutput, calls=%fused_computation.30 | convolution fusion | flops 3440820 | bytes 1966242 | tf_op jit(solution)/shard_map/tmf,tmab->tfab/dot_general | solution.py:29
  2.6 0.9 %fusion.74 = (bf16[8,3,128,128]{3,1,2,0:T(4,128)(2,1)S(1)}, bf16[8,3,128,128]{3,1,2,0:T(4,128)(2,1)S(1)}) fusion(bf16[10,3,128,128]{3,1,2,0:T(4,128)(2,1)S(1)} %convolution_convert_fusion), kind=kLoop, calls=%fused_computation.93 | loop fusion | bytes 3145728 | tf_op jit(solution)/shard_map/slice | solution.py:11
  3.5 1.1 %copy.43 = bf16[8,3,128,128]{3,2,1,0:T(8,128)(2,1)} copy(bf16[8,3,128,128]{3,1,2,0:T(4,128)(2,1)S(1)} %get-tuple-element.15) | data formatting | bytes 1572864 | tf_op jit(solution)/shard_map/slice | solution.py:12
  4.6 3.5 %collective-permute-start.4 = (bf16[8,3,128,128]{3,2,1,0:T(8,128)(2,1)}, bf16[8,3,128,128]{3,2,1,0:T(8,128)(2,1)}, u32[]{:S(2)}, u32[]{:S(2)}) collective-permute-start(bf16[8,3,128,128]{3,2,1,0:T(8,128)(2,1)} %copy.43), channel_id=1, source_target_pairs={{0,8},{8,16},{16,24},{24,32},{32,40},{40,48},{48,56},{56,64},{64,7... | collective-permute-start | bytes 2359304 | tf_op jit(solution)/shard_map/ppermute | solution.py:15
  8.1 1.1 %copy.44 = bf16[8,3,128,128]{3,2,1,0:T(8,128)(2,1)} copy(bf16[8,3,128,128]{3,1,2,0:T(4,128)(2,1)S(1)} %get-tuple-element.14) | data formatting | bytes 1572864 | tf_op jit(solution)/shard_map/slice | solution.py:11
  9.2 1.9 %collective-permute-start.5 = (bf16[8,3,128,128]{3,2,1,0:T(8,128)(2,1)}, bf16[8,3,128,128]{3,2,1,0:T(8,128)(2,1)}, u32[]{:S(2)}, u32[]{:S(2)}) collective-permute-start(bf16[8,3,128,128]{3,2,1,0:T(8,128)(2,1)} %copy.44), channel_id=1, source_target_pairs={{8,0},{16,8},{24,16},{32,24},{40,32},{48,40},{56,48},{64,56},{72,6... | collective-permute-start | bytes 2359304 | tf_op jit(solution)/shard_map/ppermute | solution.py:17
  11.2 1.1 %copy.40 = bf16[10,2,128,128]{2,3,1,0:T(8,128)(2,1)} copy(bf16[10,2,128,128]{3,2,1,0:T(8,128)(2,1)S(1)} %copy-done.1) | data formatting | bytes 1310720 | tf_op args[0]
  12.3 1.2 %broadcast_select_fusion = bf16[10,2,128,128]{2,3,1,0:T(8,128)(2,1)S(1)} fusion(bf16[10,2,128,128]{2,3,1,0:T(8,128)(2,1)} %copy.40, pred[10,2]{1,0:T(8,128)(4,1)S(1)} %fusion.68), kind=kLoop, calls=%fused_computation.48 | loop fusion | flops 327680 | bytes 1310740 | tf_op jit(solution)/shard_map/jit(_where)/select_n | solution.py:53
  13.5 3.6 %collective-permute-start = (bf16[2,2,128,128]{2,3,1,0:T(8,128)(2,1)S(1)}, bf16[2,2,128,128]{2,3,1,0:T(8,128)(2,1)S(1)}, u32[]{:S(2)}, u32[]{:S(2)}) collective-permute-start(bf16[2,2,128,128]{2,3,1,0:T(8,128)(2,1)S(1)} %get-tuple-element.16), channel_id=1, source_target_pairs={{0,8},{8,16},{16,24},{24,32},{32,40},{40,48},{48,56},{56,64},{64,7... | collective-permute-start | bytes 393224 | tf_op jit(solution)/shard_map/ppermute | solution.py:15
  17.2 1.9 %collective-permute-start.1 = (bf16[2,2,128,128]{2,3,1,0:T(8,128)(2,1)S(1)}, bf16[2,2,128,128]{2,3,1,0:T(8,128)(2,1)S(1)}, u32[]{:S(2)}, u32[]{:S(2)}) collective-permute-start(bf16[2,2,128,128]{2,3,1,0:T(8,128)(2,1)S(1)} %get-tuple-element.17), channel_id=1, source_target_pairs={{8,0},{16,8},{24,16},{32,24},{40,32},{48,40},{56,48},{64,56},{72,6... | collective-permute-start | bytes 393224 | tf_op jit(solution)/shard_map/ppermute | solution.py:17
  19.1 2.6 %fusion.73 = (bf16[10,1,128,128]{3,1,2,0:T(2,128)(2,1)}, bf16[10,1,128,128]{3,1,2,0:T(2,128)(2,1)}, bf16[10,1,128,128]{3,1,2,0:T(2,128)(2,1)}) fusion(bf16[10,3,128,128]{3,1,2,0:T(4,128)(2,1)S(1)} %convolution_convert_fusion), kind=kLoop, calls=%fused_computation.92 | loop fusion | bytes 1966080 | tf_op jit(solution)/shard_map/slice | solution.py:62
  21.7 8.8 %collective-permute-done.1 = bf16[2,2,128,128]{2,3,1,0:T(8,128)(2,1)S(1)} collective-permute-done((bf16[2,2,128,128]{2,3,1,0:T(8,128)(2,1)S(1)}, bf16[2,2,128,128]{2,3,1,0:T(8,128)(2,1)S(1)}, u32[]{:S(2)}, u32[]{:S(2)}) %collective-permute-start.1) | collective-permute-done | bytes 131104 | tf_op jit(solution)/shard_map/ppermute | solution.py:17
  30.7 2.2 %collective-permute-start.2 = (bf16[14,2,128,128]{2,3,1,0:T(8,128)(2,1)S(1)}, bf16[14,2,128,128]{2,3,1,0:T(8,128)(2,1)S(1)}, u32[]{:S(2)}, u32[]{:S(2)}) collective-permute-start(bf16[14,2,128,128]{2,3,1,0:T(8,128)(2,1)S(1)} %pad_maximum_fusion), channel_id=1, source_target_pairs={{1,0},{2,1},{3,2},{4,3},{5,4},{6,5},{7,6},{9,8},{10,9},{11,10},{12... | collective-permute-start | bytes 2752520 | tf_op jit(solution)/shard_map/ppermute | solution.py:17
  32.8 21.6 %collective-permute-start.3 = (bf16[14,2,128,128]{2,3,1,0:T(8,128)(2,1)S(1)}, bf16[14,2,128,128]{2,3,1,0:T(8,128)(2,1)S(1)}, u32[]{:S(2)}, u32[]{:S(2)}) collective-permute-start(bf16[14,2,128,128]{2,3,1,0:T(8,128)(2,1)S(1)} %pad_maximum_fusion), channel_id=1, source_target_pairs={{0,1},{1,2},{2,3},{3,4},{4,5},{5,6},{6,7},{8,9},{9,10},{10,11},{11... | collective-permute-start | bytes 2752520 | tf_op jit(solution)/shard_map/ppermute | solution.py:15
  54.4 1.8 %copy.45 = bf16[8,3,128,128]{3,1,2,0:T(4,128)(2,1)S(1)} copy(bf16[8,3,128,128]{3,2,1,0:T(8,128)(2,1)} %collective-permute-done.4) | data formatting | bytes 1572864 | tf_op jit(solution)/shard_map/ppermute | solution.py:15
  56.3 1.8 %copy.46 = bf16[8,3,128,128]{3,1,2,0:T(4,128)(2,1)S(1)} copy(bf16[8,3,128,128]{3,2,1,0:T(8,128)(2,1)} %collective-permute-done.5) | data formatting | bytes 1572864 | tf_op jit(solution)/shard_map/ppermute | solution.py:17
  58.1 2.4 %fusion.27 = bf16[11,3,128,128]{3,1,2,0:T(4,128)(2,1)S(1)} fusion(s32[]{:T(128)S(6)} %select_n.26, bf16[8,3,128,128]{3,1,2,0:T(4,128)(2,1)S(1)} %copy.45, bf16[10,3,128,128]{3,1,2,0:T(4,128)(2,1)S(1)} %convolution_convert_fusion, bf16[8,3,128,128]{3,1,2,0:T(4,128)(2,1)S(1)} %copy.46), kind=kLoop, calls=%fused_computation.32 | loop fusion | flops 1081344 | bytes 3637252 | tf_op jit(solution)/shard_map/concatenate | solution.py:13
  60.4 4.4 %fusion.72 = (bf16[10,1,128,128]{3,1,2,0:T(2,128)(2,1)S(1)}, bf16[10,1,128,128]{3,1,2,0:T(2,128)(2,1)S(1)}, bf16[10,1,128,128]{3,1,2,0:T(2,128)(2,1)S(1)}, bf16[...) fusion(bf16[11,3,128,128]{3,1,2,0:T(4,128)(2,1)S(1)} %fusion.27), kind=kLoop, calls=%fused_computation.91 | loop fusion | bytes 3932160 | tf_op jit(solution)/shard_map/slice | solution.py:78
  65.4 0.6 copy-done.3
  66.5 0.6 copy-done.2
  67.0 0.5 fusion.30
  69.5 1.1 %copy.60 = bf16[10,2,128,128]{3,2,1,0:T(8,128)(2,1)} copy(bf16[10,2,128,128]{2,3,1,0:T(8,128)(2,1)S(1)} %fusion.33) | data formatting | bytes 1310720 | tf_op jit(solution)/shard_map/convert_element_type | solution.py:84
  (30 shorter events, 3.1 us)
Async XLA Ops:
  0.0 1.6 %copy-start = (bf16[10,3,128,128]{3,2,1,0:T(8,128)(2,1)S(1)}, bf16[10,3,128,128]{3,2,1,0:T(8,128)(2,1)}, u32[]{:S(2)}) copy-start(bf16[10,3,128,128]{3,2,1,0:T(8,128)(2,1)} %param.6) | copy-start | bytes 2949124
  3.5 7.7 %copy-start.1 = (bf16[10,2,128,128]{3,2,1,0:T(8,128)(2,1)S(1)}, bf16[10,2,128,128]{3,2,1,0:T(8,128)(2,1)}, u32[]{:S(2)}) copy-start(bf16[10,2,128,128]{3,2,1,0:T(8,128)(2,1)} %param.5) | copy-start | bytes 1966084
  4.6 49.8 %collective-permute-start.4 = (bf16[8,3,128,128]{3,2,1,0:T(8,128)(2,1)}, bf16[8,3,128,128]{3,2,1,0:T(8,128)(2,1)}, u32[]{:S(2)}, u32[]{:S(2)}) collective-permute-start(bf16[8,3,128,128]{3,2,1,0:T(8,128)(2,1)} %copy.43), channel_id=1, source_target_pairs={{0,8},{8,16},{16,24},{24,32},{32,40},{40,48},{48,56},{56,64},{64,7... | collective-permute-start | bytes 2359304 | tf_op jit(solution)/shard_map/ppermute | solution.py:15
  9.2 47.0 %collective-permute-start.5 = (bf16[8,3,128,128]{3,2,1,0:T(8,128)(2,1)}, bf16[8,3,128,128]{3,2,1,0:T(8,128)(2,1)}, u32[]{:S(2)}, u32[]{:S(2)}) collective-permute-start(bf16[8,3,128,128]{3,2,1,0:T(8,128)(2,1)} %copy.44), channel_id=1, source_target_pairs={{8,0},{16,8},{24,16},{32,24},{40,32},{48,40},{56,48},{64,56},{72,6... | collective-permute-start | bytes 2359304 | tf_op jit(solution)/shard_map/ppermute | solution.py:17
  13.5 8.2 %collective-permute-start = (bf16[2,2,128,128]{2,3,1,0:T(8,128)(2,1)S(1)}, bf16[2,2,128,128]{2,3,1,0:T(8,128)(2,1)S(1)}, u32[]{:S(2)}, u32[]{:S(2)}) collective-permute-start(bf16[2,2,128,128]{2,3,1,0:T(8,128)(2,1)S(1)} %get-tuple-element.16), channel_id=1, source_target_pairs={{0,8},{8,16},{16,24},{24,32},{32,40},{40,48},{48,56},{56,64},{64,7... | collective-permute-start | bytes 393224 | tf_op jit(solution)/shard_map/ppermute | solution.py:15
  17.2 13.4 %collective-permute-start.1 = (bf16[2,2,128,128]{2,3,1,0:T(8,128)(2,1)S(1)}, bf16[2,2,128,128]{2,3,1,0:T(8,128)(2,1)S(1)}, u32[]{:S(2)}, u32[]{:S(2)}) collective-permute-start(bf16[2,2,128,128]{2,3,1,0:T(8,128)(2,1)S(1)} %get-tuple-element.17), channel_id=1, source_target_pairs={{8,0},{16,8},{24,16},{32,24},{40,32},{48,40},{56,48},{64,56},{72,6... | collective-permute-start | bytes 393224 | tf_op jit(solution)/shard_map/ppermute | solution.py:17
  30.7 34.2 %collective-permute-start.2 = (bf16[14,2,128,128]{2,3,1,0:T(8,128)(2,1)S(1)}, bf16[14,2,128,128]{2,3,1,0:T(8,128)(2,1)S(1)}, u32[]{:S(2)}, u32[]{:S(2)}) collective-permute-start(bf16[14,2,128,128]{2,3,1,0:T(8,128)(2,1)S(1)} %pad_maximum_fusion), channel_id=1, source_target_pairs={{1,0},{2,1},{3,2},{4,3},{5,4},{6,5},{7,6},{9,8},{10,9},{11,10},{12... | collective-permute-start | bytes 2752520 | tf_op jit(solution)/shard_map/ppermute | solution.py:17
  32.8 32.6 %collective-permute-start.3 = (bf16[14,2,128,128]{2,3,1,0:T(8,128)(2,1)S(1)}, bf16[14,2,128,128]{2,3,1,0:T(8,128)(2,1)S(1)}, u32[]{:S(2)}, u32[]{:S(2)}) collective-permute-start(bf16[14,2,128,128]{2,3,1,0:T(8,128)(2,1)S(1)} %pad_maximum_fusion), channel_id=1, source_target_pairs={{0,1},{1,2},{2,3},{3,4},{4,5},{5,6},{6,7},{8,9},{9,10},{10,11},{11... | collective-permute-start | bytes 2752520 | tf_op jit(solution)/shard_map/ppermute | solution.py:15
  60.4 4.4 %copy-start.4 = (bf16[10,1,128,128]{3,1,2,0:T(2,128)(2,1)S(1)}, bf16[10,1,128,128]{3,1,2,0:T(2,128)(2,1)}, u32[]{:S(2)}) copy-start(bf16[10,1,128,128]{3,1,2,0:T(2,128)(2,1)} %get-tuple-element.13) | copy-start | bytes 983044
  64.9 1.1 %copy-start.3 = (bf16[10,1,128,128]{3,1,2,0:T(2,128)(2,1)S(1)}, bf16[10,1,128,128]{3,1,2,0:T(2,128)(2,1)}, u32[]{:S(2)}) copy-start(bf16[10,1,128,128]{3,1,2,0:T(2,128)(2,1)} %get-tuple-element.12) | copy-start | bytes 983044
  66.0 1.1 %copy-start.2 = (bf16[10,1,128,128]{3,1,2,0:T(2,128)(2,1)S(1)}, bf16[10,1,128,128]{3,1,2,0:T(2,128)(2,1)}, u32[]{:S(2)}) copy-start(bf16[10,1,128,128]{3,1,2,0:T(2,128)(2,1)} %get-tuple-element.11) | copy-start | bytes 983044
  68.1 0.7 copy-start.5
where the time goes:
time: 71.1 us; the launch traced here: 70.6 us
  starting transfers between devices  34.7 us (49%)
  local copies, waits for them, and re-layouts  18.1 us (25%)
  waiting for transfers between devices  8.85 us (12%)
  other arithmetic  4.69 us (7%)
  matrix products  4 us (6%)
    ppermute x3, starting transfers between devices, padded_2(): lax.ppermute(tail, axis, [(i, (i + 1) % count) for i in range(ends)])  28.7 us
    ppermute x3, waiting for transfers between devices, padded_2(): lax.ppermute(head, axis, [((i + 1) % count, i) for i in range(ends)])  8.85 us
    ppermute x3, starting transfers between devices, padded_2(): lax.ppermute(head, axis, [((i + 1) % count, i) for i in range(ends)])  6 us
    slice x1, local copies, waits for them, and re-layouts, shards(): window_slice[offset_position:offset_position + tile_rows, shift_amount_se...  4.4 us
    unnamed x14, local copies, waits for them, and re-layouts  3.28 us
    dot_general x9, matrix products, tile_product(): jnp.einsum(batched, operand_one, operand_two, preferred_element_type=jnp....  2.98 us
    slice x1, local copies, waits for them, and re-layouts, shards(): jacobian[:, shift_f]  2.58 us
    concatenate x2, other arithmetic, padded_2(): jnp.concatenate([lax.ppermute(tail, axis, [(i, (i + 1) % count) for i in...  2.47 us
  transfers between devices with their start and end apart: 6, of which 1 were waited for; matrix products, arithmetic and copies ran while one was open for 24% of the time, Pallas kernels for 0%

commit v1 on v0

--- a/solution.py
+++ b/solution.py
@@ -2,23 +2,6 @@
 import jax.numpy as jnp
 from jax import lax
 from jax.sharding import PartitionSpec as P
-
-
-def padded_2(cells, sides, width):
-    for axis, dim in sides:
-        count = lax.axis_size(axis)
-        ends = count - 1
-        head = lax.slice_in_dim(cells, 0, width, axis=dim)
-        tail = lax.slice_in_dim(cells, cells.shape[dim] - width, cells.shape[dim], axis=dim)
-        cells = jnp.concatenate(
-            [
-                lax.ppermute(tail, axis, [(i, (i + 1) % count) for i in range(ends)]),
-                cells,
-                lax.ppermute(head, axis, [((i + 1) % count, i) for i in range(ends)]),
-            ],
-            axis=dim,
-        )
-    return cells
 
 
 def assemble(blocks, block_offsets, block_live):
@@ -38,33 +21,67 @@
 
 
 def shards(p_band, blocks, block_offsets, block_live, q_var):
-    tile_rows = p_band.shape[0]
-    band_local = p_band.shape[1]
-    tile_size = p_band.shape[2]
+    tile_rows, band_local, tile_size = p_band.shape[0], p_band.shape[1], p_band.shape[2]
+    row_count = lax.axis_size("row")
     col_count = lax.axis_size("col")
     half_band = band_local * col_count // 2
-    grid_tiles = tile_rows * lax.axis_size("row")
+    grid_tiles = tile_rows * row_count
+    row_id = lax.axis_index("row")
     col_id = lax.axis_index("col")
-    first_row = lax.axis_index("row") * tile_rows
+    first_row = row_id * tile_rows
     low_offset = col_id * band_local - half_band
     row_ids = first_row + jnp.arange(tile_rows, dtype=jnp.int32)[:, None]
     columns = row_ids + low_offset + jnp.arange(band_local, dtype=jnp.int32)[None, :]
     inside = (columns >= 0) & (columns < grid_tiles)
     prior = jnp.where(inside[:, :, None, None], p_band, jnp.zeros_like(p_band))
     jacobian = assemble(blocks, block_offsets, block_live)
-    widened = padded_2(prior, (("row", 0), ("col", 1)), 2)
-    padded = widened[1:-1]
+
+    def flat(a, b):
+        return a * col_count + b
+
+    left = lax.ppermute(prior, "col", [(b, b + 1) for b in range(col_count - 1)])
+    right = lax.ppermute(prior, "col", [(b + 1, b) for b in range(col_count - 1)])
+    up = lax.ppermute(prior[-1], "row", [(a, a + 1) for a in range(row_count - 1)])
+    down = lax.ppermute(prior[0], "row", [(a + 1, a) for a in range(row_count - 1)])
+    up_right = lax.ppermute(
+        prior[-1],
+        ("row", "col"),
+        [(flat(a, b), flat(a + 1, b - 1)) for a in range(row_count - 1) for b in range(1, col_count)],
+    )
+    down_left = lax.ppermute(
+        prior[0],
+        ("row", "col"),
+        [(flat(a, b), flat(a - 1, b + 1)) for a in range(1, row_count) for b in range(col_count - 1)],
+    )
+
+    window = tile_rows + band_local - 1
+    sent_rows = half_band
+    lower_half = col_id < col_count // 2
+    send_start = jnp.where(lower_half, tile_rows - sent_rows, 0)
+    sent = lax.dynamic_slice_in_dim(jacobian, send_start, sent_rows, 0)
+    pairs = []
+    for b in range(col_count):
+        if b * band_local - half_band < 0:
+            pairs += [(flat(a, b), flat(a + 1, b)) for a in range(row_count - 1)]
+        else:
+            pairs += [(flat(a, b), flat(a - 1, b)) for a in range(1, row_count)]
+    received = lax.ppermute(sent, ("row", "col"), pairs)
+    extended_rows = jnp.concatenate([received, jacobian, received], axis=0)
+    window_slice = lax.dynamic_slice_in_dim(extended_rows, sent_rows + low_offset, window, 0)
+
+    zero_pair = jnp.zeros((2, tile_size, tile_size), prior.dtype)
+    middle = jnp.concatenate([left[:, band_local - 2 :], prior, right[:, :2]], axis=1)
+    top = jnp.concatenate([zero_pair, up, up_right[:2]], axis=0)
+    bottom = jnp.concatenate([down_left[band_local - 2 :], down, zero_pair], axis=0)
+    padded = jnp.concatenate([top[None], middle, bottom[None]], axis=0)
+
     extended = band_local + 2
-    spread_shape = (tile_rows, extended, tile_size, tile_size)
-    spread_sum = jnp.zeros(spread_shape, jnp.float32)
+    spread_sum = jnp.zeros((tile_rows, extended, tile_size, tile_size), jnp.float32)
     for shift_f in range(3):
         source = padded[shift_f : shift_f + tile_rows, 2 - shift_f : 2 - shift_f + extended]
         spread_sum = spread_sum + tile_product("ab,ubc->uac", jacobian[:, shift_f], source)
     spread_out_block = spread_sum.astype(jnp.bfloat16)
-    beside_all = padded_2(jacobian, (("row", 0),), half_band)
-    window_slice = lax.dynamic_slice_in_dim(
-        beside_all, col_id * band_local, tile_rows + band_local - 1, 0
-    )
+
     eye_tile = jnp.eye(tile_size, dtype=jnp.float32)
     noise = q_var[:, :, None] * eye_tile[None]
     tile_shape = (tile_rows, tile_size, tile_size)

time: 71.1 us -> 61.4 us (0.86)
  the two profiles are of different devices: /device:TPU:501 before, /device:TPU:225 now
where the time goes in v1:
time: 61.4 us; the launch traced here: 60.9 us
  starting transfers between devices  22.2 us (36%)
  waiting for transfers between devices  14 us (23%)
  local copies, waits for them, and re-layouts  11.7 us (19%)
  matrix products  8.15 us (13%)
  other arithmetic  4.59 us (7%)
    ppermute x1, waiting for transfers between devices, shards(): lax.ppermute(prior[0], 'row', [(a + 1, a) for a in range(row_count - 1)])  14 us
    dot_general x9, matrix products, tile_product(): jnp.einsum(batched, operand_one, operand_two, preferred_element_type=jnp....  7.13 us
    ppermute x1, starting transfers between devices, shards(): lax.ppermute(prior[0], ('row', 'col'), [(flat(a, b), flat(a - 1, b + 1))...  5.69 us
    ppermute x1, starting transfers between devices, shards(): lax.ppermute(prior, 'col', [(b, b + 1) for b in range(col_count - 1)])  4.62 us
    ppermute x1, starting transfers between devices, shards(): lax.ppermute(prior[-1], 'row', [(a, a + 1) for a in range(row_count - 1)])  3.77 us
    ppermute x1, starting transfers between devices, shards(): received = lax.ppermute(sent, ('row', 'col'), pairs)  3.56 us
    slice x1, local copies, waits for them, and re-layouts, shards(): window_slice[offset_position:offset_position + tile_rows, shift_amount_se...  3.15 us
    slice x1, local copies, waits for them, and re-layouts, shards(): jacobian[:, shift_f]  2.59 us
  transfers between devices with their start and end apart: 7, of which 1 were waited for; matrix products, arithmetic and copies ran while one was open for 19% of the time, Pallas kernels for 0%

profile of v1, /device:TPU:225, one launch (start us, length us, event | category | flops | bytes accessed | tf_op | source)
XLA Modules:
  0.0 60.9 jit_solution(3144833375196629944)
XLA Ops:
  0.1 1.5 %copy.40 = bf16[10,2,128,128]{2,3,1,0:T(8,128)(2,1)S(1)} copy(bf16[10,2,128,128]{3,2,1,0:T(8,128)(2,1)} %param.5) | data formatting | bytes 1310720 | tf_op args[0]
  1.6 1.0 %broadcast_select_fusion = bf16[10,2,128,128]{2,3,1,0:T(8,128)(2,1)} fusion(bf16[10,2,128,128]{2,3,1,0:T(8,128)(2,1)S(1)} %copy.40, pred[10,2]{1,0:T(8,128)(4,1)S(1)} %fusion.64), kind=kLoop, calls=%fused_computation.43 | loop fusion | flops 327680 | bytes 1310740 | tf_op jit(solution)/shard_map/jit(_where)/select_n | solution.py:36
  2.5 0.9 %slice_bitcast_fusion.11 = (bf16[2,128,128]{1,2,0:T(8,128)(2,1)S(1)}, bf16[2,128,128]{1,2,0:T(8,128)(2,1)S(1)}) fusion(bf16[10,2,128,128]{2,3,1,0:T(8,128)(2,1)} %broadcast_select_fusion), kind=kLoop, calls=%fused_computation.71 | loop fusion | bytes 262144 | tf_op jit(solution)/shard_map/squeeze | solution.py:44
  3.4 3.8 %collective-permute-start = (bf16[2,128,128]{1,2,0:T(8,128)(2,1)S(1)}, bf16[2,128,128]{1,2,0:T(8,128)(2,1)S(1)}, u32[]{:S(2)}, u32[]{:S(2)}) collective-permute-start(bf16[2,128,128]{1,2,0:T(8,128)(2,1)S(1)} %get-tuple-element.14), channel_id=1, source_target_pairs={{0,8},{8,16},{16,24},{24,32},{32,40},{40,48},{48,56},{56,64},{64,7... | collective-permute-start | bytes 196616 | tf_op jit(solution)/shard_map/ppermute | solution.py:44
  7.2 1.3 %collective-permute-start.1 = (bf16[2,128,128]{1,2,0:T(8,128)(2,1)S(1)}, bf16[2,128,128]{1,2,0:T(8,128)(2,1)}, u32[]{:S(2)}, u32[]{:S(2)}) collective-permute-start(bf16[2,128,128]{1,2,0:T(8,128)(2,1)S(1)} %get-tuple-element.14), channel_id=1, source_target_pairs={{1,8},{2,9},{3,10},{4,11},{5,12},{6,13},{7,14},{9,16},{10,17},{11,... | collective-permute-start | bytes 196616 | tf_op jit(solution)/shard_map/ppermute | solution.py:46
  8.5 4.6 %collective-permute-start.2 = (bf16[10,2,128,128]{2,3,1,0:T(8,128)(2,1)}, bf16[10,2,128,128]{2,3,1,0:T(8,128)(2,1)}, u32[]{:S(2)}, u32[]{:S(2)}) collective-permute-start(bf16[10,2,128,128]{2,3,1,0:T(8,128)(2,1)} %broadcast_select_fusion), channel_id=1, source_target_pairs={{0,1},{1,2},{2,3},{3,4},{4,5},{5,6},{6,7},{8,9},{9,10},{10,11},{11... | collective-permute-start | bytes 1966088 | tf_op jit(solution)/shard_map/ppermute | solution.py:42
  13.1 1.3 %collective-permute-start.3 = (bf16[10,2,128,128]{2,3,1,0:T(8,128)(2,1)}, bf16[10,2,128,128]{2,3,1,0:T(8,128)(2,1)}, u32[]{:S(2)}, u32[]{:S(2)}) collective-permute-start(bf16[10,2,128,128]{2,3,1,0:T(8,128)(2,1)} %broadcast_select_fusion), channel_id=1, source_target_pairs={{1,0},{2,1},{3,2},{4,3},{5,4},{6,5},{7,6},{9,8},{10,9},{11,10},{12... | collective-permute-start | bytes 1966088 | tf_op jit(solution)/shard_map/ppermute | solution.py:43
  14.4 5.7 %collective-permute-start.4 = (bf16[2,128,128]{1,2,0:T(8,128)(2,1)S(1)}, bf16[2,128,128]{1,2,0:T(8,128)(2,1)}, u32[]{:S(2)}, u32[]{:S(2)}) collective-permute-start(bf16[2,128,128]{1,2,0:T(8,128)(2,1)S(1)} %get-tuple-element.15), channel_id=1, source_target_pairs={{8,1},{9,2},{10,3},{11,4},{12,5},{13,6},{14,7},{16,9},{17,10},{18,... | collective-permute-start | bytes 196616 | tf_op jit(solution)/shard_map/ppermute | solution.py:51
  20.3 1.0 %convolution_convert_fusion = bf16[10,3,128,128]{3,1,2,0:T(4,128)(2,1)S(1)} fusion(bf16[10,3,128,128]{3,2,1,0:T(8,128)(2,1)S(1)} %copy-done, s32[10,3]{1,0:T(8,128)S(1)} %copy.41, s32[3]{0:T(128)S(1)} %iota_add_fusion.1, pred[10,3]{1,0:T(8,128)(4,1)S(1)} %iota_compare_fusion.1), kind=kOutput, calls=%fused_computation.26 | convolution fusion | flops 3440820 | bytes 1966242 | tf_op jit(solution)/shard_map/tmf,tmab->tfab/dot_general | solution.py:12
  21.3 2.6 %fusion.69 = (bf16[10,1,128,128]{3,1,2,0:T(2,128)(2,1)}, bf16[10,1,128,128]{3,1,2,0:T(2,128)(2,1)}, bf16[10,1,128,128]{3,1,2,0:T(2,128)(2,1)}) fusion(bf16[10,3,128,128]{3,1,2,0:T(4,128)(2,1)S(1)} %convolution_convert_fusion), kind=kLoop, calls=%fused_computation.92 | loop fusion | bytes 1966080 | tf_op jit(solution)/shard_map/slice | solution.py:82
  23.9 0.4 constant_dynamic-slice_fusion
  24.3 1.1 %copy.43 = bf16[8,3,128,128]{3,2,1,0:T(8,128)(2,1)} copy(bf16[8,3,128,128]{3,1,2,0:T(4,128)(2,1)S(1)} %constant_dynamic-slice_fusion) | data formatting | bytes 1572864 | tf_op jit(solution)/shard_map/dynamic_slice | solution.py:61
  25.4 2.0 %collective-permute-start.5 = (bf16[2,128,128]{1,2,0:T(8,128)(2,1)S(1)}, bf16[2,128,128]{1,2,0:T(8,128)(2,1)S(1)}, u32[]{:S(2)}, u32[]{:S(2)}) collective-permute-start(bf16[2,128,128]{1,2,0:T(8,128)(2,1)S(1)} %get-tuple-element.15), channel_id=1, source_target_pairs={{8,0},{16,8},{24,16},{32,24},{40,32},{48,40},{56,48},{64,56},{72,6... | collective-permute-start | bytes 196616 | tf_op jit(solution)/shard_map/ppermute | solution.py:45
  27.4 3.6 %collective-permute-start.6 = (bf16[8,3,128,128]{3,2,1,0:T(8,128)(2,1)}, bf16[8,3,128,128]{3,2,1,0:T(8,128)(2,1)S(1)}, u32[]{:S(2)}, u32[]{:S(2)}) collective-permute-start(bf16[8,3,128,128]{3,2,1,0:T(8,128)(2,1)} %copy.43), channel_id=1, source_target_pairs={{0,8},{8,16},{16,24},{24,32},{32,40},{40,48},{48,56},{56,64},{64,7... | collective-permute-start | bytes 2359304 | tf_op jit(solution)/shard_map/ppermute | solution.py:68
  31.0 14.0 %collective-permute-done.5 = bf16[2,128,128]{1,2,0:T(8,128)(2,1)S(1)} collective-permute-done((bf16[2,128,128]{1,2,0:T(8,128)(2,1)S(1)}, bf16[2,128,128]{1,2,0:T(8,128)(2,1)S(1)}, u32[]{:S(2)}, u32[]{:S(2)}) %collective-permute-start.5) | collective-permute-done | bytes 65568 | tf_op jit(solution)/shard_map/ppermute | solution.py:45
  45.0 0.9 %maximum_bitcast_fusion = (bf16[1,6,128,128]{2,3,1,0:T(8,128)(2,1)S(1)}, bf16[1,6,128,128]{2,3,1,0:T(8,128)(2,1)S(1)}) fusion(bf16[2,128,128]{1,2,0:T(8,128)(2,1)} %collective-permute-done.1, bf16[2,128,128]{1,2,0:T(8,128)(2,1)S(1)} %collective-permute-done, bf16[2,128,128]{1,2,0:T(8,128)(2,1)S(1)} %broadcast_in_dim.22, ...), kind=kLoop, calls=%fused_computation.68 | loop fusion | flops 393216 | bytes 720896 | tf_op jit(solution)/shard_map/broadcast_in_dim | solution.py:76
  45.9 2.1 %fusion.16 = f32[10,4,128,128]{3,2,1,0:T(8,128)S(1)} fusion(bf16[10,2,128,128]{2,3,1,0:T(8,128)(2,1)} %collective-permute-done.3, bf16[10,2,128,128]{2,3,1,0:T(8,128)(2,1)} %broadcast_select_fusion, bf16[10,2,128,128]{2,3,1,0:T(8,128)(2,1)} %collective-permute-done.2, bf16[10,1,128,128]{3,1,2,0:T(2,128)(2,1)} %get-tuple-element.12), kind=kOutput, calls=%fused_computation.20 | convolution fusion | flops 173670400 | bytes 4915200 | tf_op jit(solution)/shard_map/tab,tubc->tuac/dot_general | solution.py:20
  48.0 1.8 %fusion = f32[10,4,128,128]{3,2,1,0:T(8,128)S(1)} fusion(bf16[10,2,128,128]{2,3,1,0:T(8,128)(2,1)} %collective-permute-done.3, bf16[10,2,128,128]{2,3,1,0:T(8,128)(2,1)} %broadcast_select_fusion, bf16[10,2,128,128]{2,3,1,0:T(8,128)(2,1)} %collective-permute-done.2, bf16[1,6,128,128]{2,3,1,0:T(8,128)(2,1)S(1)} %get-tuple-element.16, ...), kind=kOutput, calls=%fused_computation.4 | convolution fusion | flops 176422912 | bytes 5111808 | tf_op jit(solution)/shard_map/tab,tubc->tuac/dot_general | solution.py:20
  49.8 1.8 %fusion.26 = bf16[10,4,128,128]{2,3,1,0:T(8,128)(2,1)S(1)} fusion(bf16[1,6,128,128]{2,3,1,0:T(8,128)(2,1)S(1)} %get-tuple-element.17, bf16[10,2,128,128]{2,3,1,0:T(8,128)(2,1)} %collective-permute-done.3, bf16[10,2,128,128]{2,3,1,0:T(8,128)(2,1)} %broadcast_select_fusion, bf16[10,2,128,128]{2,3,1,0:T(8,128)(2,1)} %collective-permute-done.2, ...), kind=kOutput, calls=%fused_computation.29 | convolution fusion | flops 178388992 | bytes 9043968 | tf_op jit(solution)/shard_map/tab,tubc->tuac/dot_general | solution.py:20
  51.7 0.7 %copy.44 = bf16[8,3,128,128]{3,1,2,0:T(4,128)(2,1)S(1)} copy(bf16[8,3,128,128]{3,2,1,0:T(8,128)(2,1)S(1)} %collective-permute-done.6) | data formatting | bytes 1572864 | tf_op jit(solution)/shard_map/ppermute | solution.py:68
  52.3 2.4 %fusion.25 = bf16[11,3,128,128]{3,1,2,0:T(4,128)(2,1)S(1)} fusion(s32[]{:T(128)S(6)} %select_n.32, bf16[8,3,128,128]{3,1,2,0:T(4,128)(2,1)S(1)} %copy.44, bf16[10,3,128,128]{3,1,2,0:T(4,128)(2,1)S(1)} %convolution_convert_fusion), kind=kLoop, calls=%fused_computation.28 | loop fusion | flops 1081344 | bytes 2850820 | tf_op jit(solution)/shard_map/concatenate | solution.py:69
  54.7 3.1 %fusion.68 = (bf16[10,1,128,128]{3,1,2,0:T(2,128)(2,1)S(1)}, bf16[10,1,128,128]{3,1,2,0:T(2,128)(2,1)S(1)}, bf16[10,1,128,128]{3,1,2,0:T(2,128)(2,1)S(1)}, bf16[...) fusion(bf16[11,3,128,128]{3,1,2,0:T(4,128)(2,1)S(1)} %fusion.25), kind=kLoop, calls=%fused_computation.91 | loop fusion | bytes 3932160 | tf_op jit(solution)/shard_map/slice | solution.py:95
  59.3 0.3 fusion.34
  59.8 1.1 %copy.59 = bf16[10,2,128,128]{3,2,1,0:T(8,128)(2,1)} copy(bf16[10,2,128,128]{2,3,1,0:T(8,128)(2,1)S(1)} %fusion.29) | data formatting | bytes 1310720 | tf_op jit(solution)/shard_map/convert_element_type | solution.py:101
  (31 shorter events, 1.9 us)
Async XLA Ops:
  0.0 20.3 %copy-start = (bf16[10,3,128,128]{3,2,1,0:T(8,128)(2,1)S(1)}, bf16[10,3,128,128]{3,2,1,0:T(8,128)(2,1)}, u32[]{:S(2)}) copy-start(bf16[10,3,128,128]{3,2,1,0:T(8,128)(2,1)} %param.6) | copy-start | bytes 2949124
  0.0 20.1 %copy-start.4 = (s32[10,3]{0,1:T(4,128)S(1)}, s32[10,3]{0,1:T(4,128)}, u32[]{:S(2)}) copy-start(s32[10,3]{0,1:T(4,128)} %param.7) | copy-start | bytes 364
  0.0 20.2 %copy-start.5 = (s32[10]{0:T(128)S(1)}, s32[10]{0:T(128)}, u32[]{:S(2)}) copy-start(s32[10]{0:T(128)} %param.8) | copy-start | bytes 124
  3.4 22.0 %collective-permute-start = (bf16[2,128,128]{1,2,0:T(8,128)(2,1)S(1)}, bf16[2,128,128]{1,2,0:T(8,128)(2,1)S(1)}, u32[]{:S(2)}, u32[]{:S(2)}) collective-permute-start(bf16[2,128,128]{1,2,0:T(8,128)(2,1)S(1)} %get-tuple-element.14), channel_id=1, source_target_pairs={{0,8},{8,16},{16,24},{24,32},{32,40},{40,48},{48,56},{56,64},{64,7... | collective-permute-start | bytes 196616 | tf_op jit(solution)/shard_map/ppermute | solution.py:44
  7.2 20.2 %collective-permute-start.1 = (bf16[2,128,128]{1,2,0:T(8,128)(2,1)S(1)}, bf16[2,128,128]{1,2,0:T(8,128)(2,1)}, u32[]{:S(2)}, u32[]{:S(2)}) collective-permute-start(bf16[2,128,128]{1,2,0:T(8,128)(2,1)S(1)} %get-tuple-element.14), channel_id=1, source_target_pairs={{1,8},{2,9},{3,10},{4,11},{5,12},{6,13},{7,14},{9,16},{10,17},{11,... | collective-permute-start | bytes 196616 | tf_op jit(solution)/shard_map/ppermute | solution.py:46
  8.5 37.4 %collective-permute-start.2 = (bf16[10,2,128,128]{2,3,1,0:T(8,128)(2,1)}, bf16[10,2,128,128]{2,3,1,0:T(8,128)(2,1)}, u32[]{:S(2)}, u32[]{:S(2)}) collective-permute-start(bf16[10,2,128,128]{2,3,1,0:T(8,128)(2,1)} %broadcast_select_fusion), channel_id=1, source_target_pairs={{0,1},{1,2},{2,3},{3,4},{4,5},{5,6},{6,7},{8,9},{9,10},{10,11},{11... | collective-permute-start | bytes 1966088 | tf_op jit(solution)/shard_map/ppermute | solution.py:42
  13.1 32.8 %collective-permute-start.3 = (bf16[10,2,128,128]{2,3,1,0:T(8,128)(2,1)}, bf16[10,2,128,128]{2,3,1,0:T(8,128)(2,1)}, u32[]{:S(2)}, u32[]{:S(2)}) collective-permute-start(bf16[10,2,128,128]{2,3,1,0:T(8,128)(2,1)} %broadcast_select_fusion), channel_id=1, source_target_pairs={{1,0},{2,1},{3,2},{4,3},{5,4},{6,5},{7,6},{9,8},{10,9},{11,10},{12... | collective-permute-start | bytes 1966088 | tf_op jit(solution)/shard_map/ppermute | solution.py:43
  14.4 16.6 %collective-permute-start.4 = (bf16[2,128,128]{1,2,0:T(8,128)(2,1)S(1)}, bf16[2,128,128]{1,2,0:T(8,128)(2,1)}, u32[]{:S(2)}, u32[]{:S(2)}) collective-permute-start(bf16[2,128,128]{1,2,0:T(8,128)(2,1)S(1)} %get-tuple-element.15), channel_id=1, source_target_pairs={{8,1},{9,2},{10,3},{11,4},{12,5},{13,6},{14,7},{16,9},{17,10},{18,... | collective-permute-start | bytes 196616 | tf_op jit(solution)/shard_map/ppermute | solution.py:51
  25.4 19.6 %collective-permute-start.5 = (bf16[2,128,128]{1,2,0:T(8,128)(2,1)S(1)}, bf16[2,128,128]{1,2,0:T(8,128)(2,1)S(1)}, u32[]{:S(2)}, u32[]{:S(2)}) collective-permute-start(bf16[2,128,128]{1,2,0:T(8,128)(2,1)S(1)} %get-tuple-element.15), channel_id=1, source_target_pairs={{8,0},{16,8},{24,16},{32,24},{40,32},{48,40},{56,48},{64,56},{72,6... | collective-permute-start | bytes 196616 | tf_op jit(solution)/shard_map/ppermute | solution.py:45
  27.4 24.2 %collective-permute-start.6 = (bf16[8,3,128,128]{3,2,1,0:T(8,128)(2,1)}, bf16[8,3,128,128]{3,2,1,0:T(8,128)(2,1)S(1)}, u32[]{:S(2)}, u32[]{:S(2)}) collective-permute-start(bf16[8,3,128,128]{3,2,1,0:T(8,128)(2,1)} %copy.43), channel_id=1, source_target_pairs={{0,8},{8,16},{16,24},{24,32},{32,40},{40,48},{48,56},{56,64},{64,7... | collective-permute-start | bytes 2359304 | tf_op jit(solution)/shard_map/ppermute | solution.py:68
  45.9 2.1 %copy-start.2 = (bf16[10,1,128,128]{3,1,2,0:T(2,128)(2,1)S(1)}, bf16[10,1,128,128]{3,1,2,0:T(2,128)(2,1)}, u32[]{:S(2)}) copy-start(bf16[10,1,128,128]{3,1,2,0:T(2,128)(2,1)} %get-tuple-element.13) | copy-start | bytes 983044
  48.0 1.8 %copy-start.1 = (bf16[10,1,128,128]{3,1,2,0:T(2,128)(2,1)S(1)}, bf16[10,1,128,128]{3,1,2,0:T(2,128)(2,1)}, u32[]{:S(2)}) copy-start(bf16[10,1,128,128]{3,1,2,0:T(2,128)(2,1)} %get-tuple-element.11) | copy-start | bytes 983044
  58.3 0.7 %copy-start.3 = (f32[10,128]{1,0:T(8,128)S(1)}, f32[10,128]{1,0:T(8,128)}, u32[]{:S(2)}) copy-start(f32[10,128]{1,0:T(8,128)} %param.9) | copy-start | bytes 15364

commit v2 on v1

v2 whole, which is shorter than its diff:
```python
import jax
import jax.numpy as jnp
from jax import lax
from jax.experimental import pallas as pl
from jax.experimental.pallas import tpu as pltpu
from jax.sharding import PartitionSpec as P


def assemble(blocks, block_offsets, block_live):
    slot_ids = jnp.arange(blocks.shape[1], dtype=jnp.int32)
    alive = slot_ids[None, :] < block_live[:, None]
    pieces = []
    for target in (-1, 0, 1):
        choose = (block_offsets == target) & alive
        total = jnp.zeros(blocks.shape[:1] + blocks.shape[2:], jnp.float32)
        for m in range(blocks.shape[1]):
            total = total + jnp.where(choose[:, m, None, None], blocks[:, m].astype(jnp.float32), 0.0)
        pieces.append(total.astype(jnp.bfloat16))
    return jnp.stack(pieces, axis=1)


def band_kernel(tile_rows, band_local, half_band, grid_tiles):
    extended = band_local + 2

    def kernel(ids, q_ref, jac_ref, win_ref, mid_ref, left_ref, right_ref, top_ref, bot_ref, out_ref):
        row_id = ids[0]
        col_id = ids[1]
        first_row = row_id * tile_rows
        low_slot = col_id * band_local - 2
        size = jac_ref.shape[-1]

        def prior_tile(ext_row, ext_slot):
            if ext_row == 0:
                tile = top_ref[ext_slot]
            elif ext_row == tile_rows + 1:
                tile = bot_ref[ext_slot]
            elif ext_slot < 2:
                tile = left_ref[ext_row - 1, band_local - 2 + ext_slot]
            elif ext_slot < 2 + band_local:
                tile = mid_ref[ext_row - 1, ext_slot - 2]
            else:
                tile = right_ref[ext_row - 1, ext_slot - 2 - band_local]
            column = first_row + ext_row - 1 + low_slot + ext_slot - half_band
            keep = (column >= 0) & (column < grid_tiles)
            return jnp.where(keep, tile, jnp.zeros_like(tile))

        eye = lax.broadcasted_iota(jnp.int32, (size, size), 0) == lax.broadcasted_iota(
            jnp.int32, (size, size), 1
        )
        for row in range(tile_rows):
            lhs = jnp.concatenate([jac_ref[row, f] for f in range(3)], axis=1)
            rhs = jnp.concatenate(
                [
                    jnp.concatenate(
                        [prior_tile(row + f, u - f + 2) for u in range(extended)], axis=1
                    )
                    for f in range(3)
                ],
                axis=0,
            )
            spread = jnp.dot(lhs, rhs, preferred_element_type=jnp.float32).astype(jnp.bfloat16)
            for k in range(band_local):
                left_side = spread[:, k * size : (k + 3) * size]
                right_side = jnp.concatenate([win_ref[row + k, g] for g in range(3)], axis=1)
                total = lax.dot_general(
                    left_side,
                    right_side,
                    (((1,), (1,)), ((), ())),
                    preferred_element_type=jnp.float32,
                )
                on_diagonal = col_id * band_local + k == half_band
                noise = jnp.where(eye & on_diagonal, q_ref[pl.ds(row, 1), :], 0.0)
                total = total + noise
                column = first_row + row + col_id * band_local + k - half_band
                keep = (column >= 0) & (column < grid_tiles)
                total = jnp.where(keep, total, jnp.zeros_like(total))
                out_ref[row, k] = total.astype(out_ref.dtype)

    return kernel


def shards(p_band, blocks, block_offsets, block_live, q_var):
    tile_rows, band_local, tile_size = p_band.shape[0], p_band.shape[1], p_band.shape[2]
    row_count = lax.axis_size("row")
    col_count = lax.axis_size("col")
    half_band = band_local * col_count // 2
    grid_tiles = tile_rows * row_count
    row_id = lax.axis_index("row")
    col_id = lax.axis_index("col")
    low_offset = col_id * band_local - half_band

    def flat(a, b):
        return a * col_count + b

    left = lax.ppermute(p_band, "col", [(b, b + 1) for b in range(col_count - 1)])
    right = lax.ppermute(p_band, "col", [(b + 1, b) for b in range(col_count - 1)])
    up = lax.ppermute(p_band[-1], "row", [(a, a + 1) for a in range(row_count - 1)])
    down = lax.ppermute(p_band[0], "row", [(a + 1, a) for a in range(row_count - 1)])
    up_right = lax.ppermute(
        p_band[-1],
        ("row", "col"),
        [(flat(a, b), flat(a + 1, b - 1)) for a in range(row_count - 1) for b in range(1, col_count)],
    )
    down_left = lax.ppermute(
        p_band[0],
        ("row", "col"),
        [(flat(a, b), flat(a - 1, b + 1)) for a in range(1, row_count) for b in range(col_count - 1)],
    )

    jacobian = assemble(blocks, block_offsets, block_live)

    window = tile_rows + band_local - 1
    sent_rows = half_band
    lower_half = col_id < col_count // 2
    send_start = jnp.where(lower_half, tile_rows - sent_rows, 0)
    sent = lax.dynamic_slice_in_dim(jacobian, send_start, sent_rows, 0)
    pairs = []
    for b in range(col_count):
        if b * band_local - half_band < 0:
            pairs += [(flat(a, b), flat(a + 1, b)) for a in range(row_count - 1)]
        else:
            pairs += [(flat(a, b), flat(a - 1, b)) for a in range(1, row_count)]
    received = lax.ppermute(sent, ("row", "col"), pairs)
    extended_rows = jnp.concatenate([received, jacobian, received], axis=0)
    window_slice = lax.dynamic_slice_in_dim(extended_rows, sent_rows + low_offset, window, 0)

    zero_pair = jnp.zeros((2, tile_size, tile_size), p_band.dtype)
    top = jnp.concatenate([zero_pair, up, up_right[:2]], axis=0)
    bottom = jnp.concatenate([down_left[band_local - 2 :], down, zero_pair], axis=0)

    ids = jnp.stack([row_id, col_id]).astype(jnp.int32)
    vmem = pl.BlockSpec(memory_space=pltpu.MemorySpace.VMEM)
    smem = pl.BlockSpec(memory_space=pltpu.MemorySpace.SMEM)
    return pl.pallas_call(
        band_kernel(tile_rows, band_local, half_band, grid_tiles),
        out_shape=jax.ShapeDtypeStruct(p_band.shape, p_band.dtype),
        in_specs=[smem] + [vmem] * 8,
        out_specs=vmem,
    )(ids, q_var, jacobian, window_slice, p_band, left, right, top, bottom)


def solution(mesh):
    placed = (
        P("row", "col", None, None),
        P("row", None, None, None),
        P("row", None),
        P("row"),
        P("row", None),
    )
    return jax.shard_map(
        shards, mesh=mesh, in_specs=placed, out_specs=P("row", "col", None, None), check_vma=False
    )
```

time: 61.4 us -> 54.3 us (0.88)
  the two profiles are of different devices: /device:TPU:225 before, /device:TPU:285 now
where the time goes in v2:
time: 54.3 us; the launch traced here: 53.8 us
  starting transfers between devices  36.5 us (67%)
  other arithmetic  7.5 us (14%)
  Pallas kernels  5.55 us (10%)
  waiting for transfers between devices  3.97 us (7%)
    ppermute x1, starting transfers between devices, shards(): lax.ppermute(p_band[0], ('row', 'col'), [(flat(a, b), flat(a - 1, b + 1))...  20.2 us
    pallas_call x1, Pallas kernels, shards(): pl.pallas_call(band_kernel(tile_rows, band_local, half_band, grid_tiles),...  5.55 us
    ppermute x1, starting transfers between devices, shards(): lax.ppermute(p_band[-1], 'row', [(a, a + 1) for a in range(row_count - 1)])  4.44 us
    ppermute x1, waiting for transfers between devices, shards(): lax.ppermute(p_band[0], 'row', [(a + 1, a) for a in range(row_count - 1)])  3.96 us
    ppermute x1, starting transfers between devices, shards(): lax.ppermute(p_band, 'col', [(b, b + 1) for b in range(col_count - 1)])  2.83 us
    ppermute x1, starting transfers between devices, shards(): received = lax.ppermute(sent, ('row', 'col'), pairs)  2.72 us
    concatenate x1, other arithmetic, shards(): extended_rows = jnp.concatenate([received, jacobian, received], axis=0)  2.69 us
    ppermute x1, starting transfers between devices, shards(): lax.ppermute(p_band, 'col', [(b + 1, b) for b in range(col_count - 1)])  2.46 us
  transfers between devices with their start and end apart: 7, of which 1 were waited for; matrix products, arithmetic and copies ran while one was open for 9% of the time, Pallas kernels for 0%

profile of v2, /device:TPU:285, one launch (start us, length us, event | category | flops | bytes accessed | tf_op | source)
XLA Modules:
  0.0 53.8 jit_solution(9435944964670778236)
XLA Ops:
  0.0 0.7 %fusion.15 = (pred[10,3]{0,1:T(4,128)(4,1)S(1)}, pred[10,3]{0,1:T(4,128)(4,1)S(1)}, pred[10,3]{0,1:T(4,128)(4,1)S(1)}) fusion(s32[10,3]{0,1:T(4,128)} %param.7, s32[10]{0:T(128)} %param.8), kind=kLoop, calls=%fused_computation.35 | loop fusion | flops 210 | bytes 250 | tf_op jit(solution)/shard_map/and | solution.py:14
  0.7 1.7 %fusion.6 = (bf16[10,1,128,128]{3,2,1,0:T(8,128)(2,1)S(1)}, bf16[10,1,128,128]{3,2,1,0:T(8,128)(2,1)S(1)}, bf16[10,1,128,128]{3,2,1,0:T(8,128)(2,1)S(1)}) fusion(pred[10]{0:T(512)(128)(4,1)S(1)} %get-tuple-element.16, pred[10]{0:T(512)(128)(4,1)S(1)} %get-tuple-element.17, pred[10]{0:T(512)(128)(4,1)S(1)} %get-tuple-element.15, ...), kind=kLoop, calls=%fused_computation.21 | loop fusion | flops 3440640 | bytes 1966170 | tf_op jit(solution)/shard_map/convert_element_type | solution.py:18
  2.5 0.1 pad_maximum_fusion.jac_ref
  2.6 0.0 copy-start.1
  2.6 0.1 constant_dynamic-slice_fusion
  2.7 2.7 %collective-permute-start = (bf16[8,3,128,128]{3,2,1,0:T(8,128)(2,1)S(1)}, bf16[8,3,128,128]{3,2,1,0:T(8,128)(2,1)}, u32[]{:S(2)}, u32[]{:S(2)}) collective-permute-start(bf16[8,3,128,128]{3,2,1,0:T(8,128)(2,1)S(1)} %constant_dynamic-slice_fusion), channel_id=1, source_target_pairs={{0,8},{8,16},{16,24},{24,32},{32,40},{40,48},{48,56},{56,64},{64,7... | collective-permute-start | bytes 2359304 | tf_op jit(solution)/shard_map/ppermute | solution.py:123
  5.4 0.0 copy-done.1
  5.4 2.8 %collective-permute-start.1 = (bf16[10,2,128,128]{3,2,1,0:T(8,128)(2,1)S(1)}, bf16[10,2,128,128]{3,2,1,0:T(8,128)(2,1)}, u32[]{:S(2)}, u32[]{:S(2)}) collective-permute-start(bf16[10,2,128,128]{3,2,1,0:T(8,128)(2,1)S(1)} %copy-done.1), channel_id=1, source_target_pairs={{0,1},{1,2},{2,3},{3,4},{4,5},{5,6},{6,7},{8,9},{9,10},{10,11},{11... | collective-permute-start | bytes 1966088 | tf_op jit(solution)/shard_map/ppermute | solution.py:95
  8.3 2.5 %collective-permute-start.2 = (bf16[10,2,128,128]{3,2,1,0:T(8,128)(2,1)S(1)}, bf16[10,2,128,128]{3,2,1,0:T(8,128)(2,1)}, u32[]{:S(2)}, u32[]{:S(2)}) collective-permute-start(bf16[10,2,128,128]{3,2,1,0:T(8,128)(2,1)S(1)} %copy-done.1), channel_id=1, source_target_pairs={{1,0},{2,1},{3,2},{4,3},{5,4},{6,5},{7,6},{9,8},{10,9},{11,10},{12... | collective-permute-start | bytes 1966088 | tf_op jit(solution)/shard_map/ppermute | solution.py:96
  10.7 4.4 %collective-permute-start.3 = (bf16[2,128,128]{2,1,0:T(8,128)(2,1)S(1)}, bf16[2,128,128]{2,1,0:T(8,128)(2,1)}, u32[]{:S(2)}, u32[]{:S(2)}) collective-permute-start(bf16[2,128,128]{2,1,0:T(8,128)(2,1)S(1)} %get-tuple-element.9), channel_id=1, source_target_pairs={{0,8},{8,16},{16,24},{24,32},{32,40},{40,48},{48,56},{56,64},{64,7... | collective-permute-start | bytes 196616 | tf_op jit(solution)/shard_map/ppermute | solution.py:97
  15.2 1.9 %collective-permute-start.4 = (bf16[2,128,128]{2,1,0:T(8,128)(2,1)S(1)}, bf16[2,128,128]{2,1,0:T(8,128)(2,1)}, u32[]{:S(2)}, u32[]{:S(2)}) collective-permute-start(bf16[2,128,128]{2,1,0:T(8,128)(2,1)S(1)} %get-tuple-element.9), channel_id=1, source_target_pairs={{1,8},{2,9},{3,10},{4,11},{5,12},{6,13},{7,14},{9,16},{10,17},{11,... | collective-permute-start | bytes 196616 | tf_op jit(solution)/shard_map/ppermute | solution.py:99
  17.1 0.0 collective-permute-done.3
  17.1 20.2 %collective-permute-start.5 = (bf16[2,128,128]{2,1,0:T(8,128)(2,1)S(1)}, bf16[2,128,128]{2,1,0:T(8,128)(2,1)S(1)}, u32[]{:S(2)}, u32[]{:S(2)}) collective-permute-start(bf16[2,128,128]{2,1,0:T(8,128)(2,1)S(1)} %get-tuple-element.8), channel_id=1, source_target_pairs={{8,1},{9,2},{10,3},{11,4},{12,5},{13,6},{14,7},{16,9},{17,10},{18,... | collective-permute-start | bytes 196616 | tf_op jit(solution)/shard_map/ppermute | solution.py:104
  37.4 0.0 collective-permute-done.4
  37.4 1.9 %collective-permute-start.6 = (bf16[2,128,128]{2,1,0:T(8,128)(2,1)S(1)}, bf16[2,128,128]{2,1,0:T(8,128)(2,1)S(1)}, u32[]{:S(2)}, u32[]{:S(2)}) collective-permute-start(bf16[2,128,128]{2,1,0:T(8,128)(2,1)S(1)} %get-tuple-element.8), channel_id=1, source_target_pairs={{8,0},{16,8},{24,16},{32,24},{40,32},{48,40},{56,48},{64,56},{72,6... | collective-permute-start | bytes 196616 | tf_op jit(solution)/shard_map/ppermute | solution.py:98
  39.3 0.6 %pad_add_fusion.ids = s32[2]{0:T(128)} fusion(s32[1]{0:T(128)} %bitcast.1, s32[1]{0:T(128)} %bitcast), kind=kLoop, calls=%fused_computation.46 | loop fusion | flops 2 | bytes 16 | tf_op jit(solution)/shard_map/stack | solution.py:131
  39.9 0.0 collective-permute-done.5
  39.9 4.0 %collective-permute-done.6 = bf16[2,128,128]{2,1,0:T(8,128)(2,1)S(1)} collective-permute-done((bf16[2,128,128]{2,1,0:T(8,128)(2,1)S(1)}, bf16[2,128,128]{2,1,0:T(8,128)(2,1)S(1)}, u32[]{:S(2)}, u32[]{:S(2)}) %collective-permute-start.6) | collective-permute-done | bytes 65568 | tf_op jit(solution)/shard_map/ppermute | solution.py:98
  43.9 1.7 %pad_maximum_fusion.2 = (bf16[6,128,128]{2,1,0:T(8,128)(2,1)}, bf16[6,128,128]{2,1,0:T(8,128)(2,1)}) fusion(bf16[2,128,128]{2,1,0:T(8,128)(2,1)S(1)} %broadcast_in_dim.102, bf16[2,128,128]{2,1,0:T(8,128)(2,1)S(1)} %collective-permute-done.6, bf16[2,128,128]{2,1,0:T(8,128)(2,1)S(1)} %collective-permute-done.5, ...), kind=kLoop, calls=%fused_computation.29 | loop fusion | flops 393216 | bytes 720896 | tf_op jit(solution)/shard_map/concatenate | solution.py:129
  45.6 0.0 collective-permute-done
  45.6 2.7 %fusion.1.win_ref = bf16[11,3,128,128]{3,2,1,0:T(8,128)(2,1)} fusion(s32[]{:T(128)S(6)} %select_n.55, bf16[8,3,128,128]{3,2,1,0:T(8,128)(2,1)} %collective-permute-done, bf16[10,1,128,128]{3,2,1,0:T(8,128)(2,1)S(1)} %get-tuple-element.5, bf16[10,1,128,128]{3,2,1,0:T(8,128)(2,1)S(1)} %get-tuple-element.6, bf16[10,1,128,128]{3,2,1,0:T(8,128)(2,1)S(1)} %get-tuple-element.7), kind=kLoop, calls=%fused_computation.6 | loop fusion | flops 2162688 | bytes 2850820 | tf_op jit(solution)/shard_map/concatenate | solution.py:124
  48.3 0.0 collective-permute-done.1.left_ref
  48.3 0.0 collective-permute-done.2.right_ref
  48.3 5.6 %shard_map.55 = bf16[10,2,128,128]{3,2,1,0:T(8,128)(2,1)} custom-call(s32[2]{0:T(128)} %pad_add_fusion.ids, f32[10,128]{1,0:T(8,128)} %q_ref.1, bf16[10,3,128,128]{3,2,1,0:T(8,128)(2,1)} %copy-done, bf16[11,3,128,128]{3,2,1,0:T(8,128)(2,1)} %fusion.1.win_ref, bf16[10,2,128,128]{3,2,1,0:T(8,128)(2,1)} %mid_ref.1, ...), custom_call_target="tpu_custom_call" | custom-call | tf_op jit(solution)/shard_map/pallas_call | solution.py:134
  (6 shorter events, 0.0 us)
Async XLA Ops:
  2.6 43.0 %copy-start = (bf16[10,3,128,128]{3,2,1,0:T(8,128)(2,1)}, bf16[10,3,128,128]{3,2,1,0:T(8,128)(2,1)S(1)}, u32[]{:S(2)}) copy-start(bf16[10,3,128,128]{3,2,1,0:T(8,128)(2,1)S(1)} %pad_maximum_fusion.jac_ref) | copy-start | bytes 2949124
  2.6 2.8 %copy-start.1 = (bf16[10,2,128,128]{3,2,1,0:T(8,128)(2,1)S(1)}, bf16[10,2,128,128]{3,2,1,0:T(8,128)(2,1)}, u32[]{:S(2)}) copy-start(bf16[10,2,128,128]{3,2,1,0:T(8,128)(2,1)} %mid_ref.1) | copy-start | bytes 1966084
  2.7 42.9 %collective-permute-start = (bf16[8,3,128,128]{3,2,1,0:T(8,128)(2,1)S(1)}, bf16[8,3,128,128]{3,2,1,0:T(8,128)(2,1)}, u32[]{:S(2)}, u32[]{:S(2)}) collective-permute-start(bf16[8,3,128,128]{3,2,1,0:T(8,128)(2,1)S(1)} %constant_dynamic-slice_fusion), channel_id=1, source_target_pairs={{0,8},{8,16},{16,24},{24,32},{32,40},{40,48},{48,56},{56,64},{64,7... | collective-permute-start | bytes 2359304 | tf_op jit(solution)/shard_map/ppermute | solution.py:123
  5.4 42.9 %collective-permute-start.1 = (bf16[10,2,128,128]{3,2,1,0:T(8,128)(2,1)S(1)}, bf16[10,2,128,128]{3,2,1,0:T(8,128)(2,1)}, u32[]{:S(2)}, u32[]{:S(2)}) collective-permute-start(bf16[10,2,128,128]{3,2,1,0:T(8,128)(2,1)S(1)} %copy-done.1), channel_id=1, source_target_pairs={{0,1},{1,2},{2,3},{3,4},{4,5},{5,6},{6,7},{8,9},{9,10},{10,11},{11... | collective-permute-start | bytes 1966088 | tf_op jit(solution)/shard_map/ppermute | solution.py:95
  8.3 40.0 %collective-permute-start.2 = (bf16[10,2,128,128]{3,2,1,0:T(8,128)(2,1)S(1)}, bf16[10,2,128,128]{3,2,1,0:T(8,128)(2,1)}, u32[]{:S(2)}, u32[]{:S(2)}) collective-permute-start(bf16[10,2,128,128]{3,2,1,0:T(8,128)(2,1)S(1)} %copy-done.1), channel_id=1, source_target_pairs={{1,0},{2,1},{3,2},{4,3},{5,4},{6,5},{7,6},{9,8},{10,9},{11,10},{12... | collective-permute-start | bytes 1966088 | tf_op jit(solution)/shard_map/ppermute | solution.py:96
  10.7 6.4 %collective-permute-start.3 = (bf16[2,128,128]{2,1,0:T(8,128)(2,1)S(1)}, bf16[2,128,128]{2,1,0:T(8,128)(2,1)}, u32[]{:S(2)}, u32[]{:S(2)}) collective-permute-start(bf16[2,128,128]{2,1,0:T(8,128)(2,1)S(1)} %get-tuple-element.9), channel_id=1, source_target_pairs={{0,8},{8,16},{16,24},{24,32},{32,40},{40,48},{48,56},{56,64},{64,7... | collective-permute-start | bytes 196616 | tf_op jit(solution)/shard_map/ppermute | solution.py:97
  15.2 22.2 %collective-permute-start.4 = (bf16[2,128,128]{2,1,0:T(8,128)(2,1)S(1)}, bf16[2,128,128]{2,1,0:T(8,128)(2,1)}, u32[]{:S(2)}, u32[]{:S(2)}) collective-permute-start(bf16[2,128,128]{2,1,0:T(8,128)(2,1)S(1)} %get-tuple-element.9), channel_id=1, source_target_pairs={{1,8},{2,9},{3,10},{4,11},{5,12},{6,13},{7,14},{9,16},{10,17},{11,... | collective-permute-start | bytes 196616 | tf_op jit(solution)/shard_map/ppermute | solution.py:99
  17.1 22.8 %collective-permute-start.5 = (bf16[2,128,128]{2,1,0:T(8,128)(2,1)S(1)}, bf16[2,128,128]{2,1,0:T(8,128)(2,1)S(1)}, u32[]{:S(2)}, u32[]{:S(2)}) collective-permute-start(bf16[2,128,128]{2,1,0:T(8,128)(2,1)S(1)} %get-tuple-element.8), channel_id=1, source_target_pairs={{8,1},{9,2},{10,3},{11,4},{12,5},{13,6},{14,7},{16,9},{17,10},{18,... | collective-permute-start | bytes 196616 | tf_op jit(solution)/shard_map/ppermute | solution.py:104
  37.4 6.5 %collective-permute-start.6 = (bf16[2,128,128]{2,1,0:T(8,128)(2,1)S(1)}, bf16[2,128,128]{2,1,0:T(8,128)(2,1)S(1)}, u32[]{:S(2)}, u32[]{:S(2)}) collective-permute-start(bf16[2,128,128]{2,1,0:T(8,128)(2,1)S(1)} %get-tuple-element.8), channel_id=1, source_target_pairs={{8,0},{16,8},{24,16},{32,24},{40,32},{48,40},{56,48},{64,56},{72,6... | collective-permute-start | bytes 196616 | tf_op jit(solution)/shard_map/ppermute | solution.py:98

commit v3 on v2

--- a/solution.py
+++ b/solution.py
@@ -19,21 +19,29 @@
     return jnp.stack(pieces, axis=1)
 
 
-def band_kernel(tile_rows, band_local, half_band, grid_tiles):
+def band_kernel(tile_rows, band_local, half_band, grid_tiles, sent_rows):
     extended = band_local + 2
 
-    def kernel(ids, q_ref, jac_ref, win_ref, mid_ref, left_ref, right_ref, top_ref, bot_ref, out_ref):
+    def kernel(ids, q_ref, jac_ref, recv_ref, mid_ref, left_ref, right_ref, up_ref, up_right_ref,
+               down_ref, down_left_ref, out_ref):
         row_id = ids[0]
         col_id = ids[1]
         first_row = row_id * tile_rows
         low_slot = col_id * band_local - 2
+        low_offset = col_id * band_local - half_band
         size = jac_ref.shape[-1]
 
         def prior_tile(ext_row, ext_slot):
             if ext_row == 0:
-                tile = top_ref[ext_slot]
+                if ext_slot < 2 + band_local:
+                    tile = up_ref[ext_slot - 2]
+                else:
+                    tile = up_right_ref[ext_slot - 2 - band_local]
             elif ext_row == tile_rows + 1:
-                tile = bot_ref[ext_slot]
+                if ext_slot < 2:
+                    tile = down_left_ref[band_local - 2 + ext_slot]
+                else:
+                    tile = down_ref[ext_slot - 2]
             elif ext_slot < 2:
                 tile = left_ref[ext_row - 1, band_local - 2 + ext_slot]
             elif ext_slot < 2 + band_local:
@@ -43,6 +51,13 @@
             column = first_row + ext_row - 1 + low_slot + ext_slot - half_band
             keep = (column >= 0) & (column < grid_tiles)
             return jnp.where(keep, tile, jnp.zeros_like(tile))
+
+        def window_tile(position, g):
+            at = sent_rows + low_offset + position
+            before = recv_ref[jnp.clip(at, 0, sent_rows - 1), g]
+            own = jac_ref[jnp.clip(at - sent_rows, 0, tile_rows - 1), g]
+            after = recv_ref[jnp.clip(at - sent_rows - tile_rows, 0, sent_rows - 1), g]
+            return jnp.where(at < sent_rows, before, jnp.where(at < sent_rows + tile_rows, own, after))
 
         eye = lax.broadcasted_iota(jnp.int32, (size, size), 0) == lax.broadcasted_iota(
             jnp.int32, (size, size), 1
@@ -61,17 +76,17 @@
             spread = jnp.dot(lhs, rhs, preferred_element_type=jnp.float32).astype(jnp.bfloat16)
             for k in range(band_local):
                 left_side = spread[:, k * size : (k + 3) * size]
-                right_side = jnp.concatenate([win_ref[row + k, g] for g in range(3)], axis=1)
+                right_side = jnp.concatenate([window_tile(row + k, g) for g in range(3)], axis=1)
                 total = lax.dot_general(
                     left_side,
                     right_side,
                     (((1,), (1,)), ((), ())),
                     preferred_element_type=jnp.float32,
                 )
-                on_diagonal = col_id * band_local + k == half_band
+                on_diagonal = low_offset + k == 0
                 noise = jnp.where(eye & on_diagonal, q_ref[pl.ds(row, 1), :], 0.0)
                 total = total + noise
-                column = first_row + row + col_id * band_local + k - half_band
+                column = first_row + row + low_offset + k
                 keep = (column >= 0) & (column < grid_tiles)
                 total = jnp.where(keep, total, jnp.zeros_like(total))
                 out_ref[row, k] = total.astype(out_ref.dtype)
@@ -109,7 +124,6 @@
 
     jacobian = assemble(blocks, block_offsets, block_live)
 
-    window = tile_rows + band_local - 1
     sent_rows = half_band
     lower_half = col_id < col_count // 2
     send_start = jnp.where(lower_half, tile_rows - sent_rows, 0)
@@ -121,22 +135,16 @@
         else:
             pairs += [(flat(a, b), flat(a - 1, b)) for a in range(1, row_count)]
     received = lax.ppermute(sent, ("row", "col"), pairs)
-    extended_rows = jnp.concatenate([received, jacobian, received], axis=0)
-    window_slice = lax.dynamic_slice_in_dim(extended_rows, sent_rows + low_offset, window, 0)
-
-    zero_pair = jnp.zeros((2, tile_size, tile_size), p_band.dtype)
-    top = jnp.concatenate([zero_pair, up, up_right[:2]], axis=0)
-    bottom = jnp.concatenate([down_left[band_local - 2 :], down, zero_pair], axis=0)
 
     ids = jnp.stack([row_id, col_id]).astype(jnp.int32)
     vmem = pl.BlockSpec(memory_space=pltpu.MemorySpace.VMEM)
     smem = pl.BlockSpec(memory_space=pltpu.MemorySpace.SMEM)
     return pl.pallas_call(
-        band_kernel(tile_rows, band_local, half_band, grid_tiles),
+        band_kernel(tile_rows, band_local, half_band, grid_tiles, sent_rows),
         out_shape=jax.ShapeDtypeStruct(p_band.shape, p_band.dtype),
-        in_specs=[smem] + [vmem] * 8,
+        in_specs=[smem] + [vmem] * 10,
         out_specs=vmem,
-    )(ids, q_var, jacobian, window_slice, p_band, left, right, top, bottom)
+    )(ids, q_var, jacobian, received, p_band, left, right, up, up_right, down, down_left)
 
 
 def solution(mesh):

time: 54.3 us -> 52.5 us (0.967)
  the two profiles are of different devices: /device:TPU:285 before, /device:TPU:103 now
where the time goes in v3:
time: 52.5 us; the launch traced here: 52.1 us
  waiting for transfers between devices  21 us (40%)
  starting transfers between devices  20.2 us (38%)
  Pallas kernels  5.39 us (10%)
  other arithmetic  3.11 us (6%)
  local copies, waits for them, and re-layouts  2.28 us (4%)
    ppermute x1, waiting for transfers between devices, shards(): lax.ppermute(p_band[-1], ('row', 'col'), [(flat(a, b), flat(a + 1, b - 1)...  17 us
    pallas_call x1, Pallas kernels, shards(): pl.pallas_call(band_kernel(tile_rows, band_local, half_band, grid_tiles,...  5.39 us
    ppermute x1, starting transfers between devices, shards(): lax.ppermute(p_band[-1], ('row', 'col'), [(flat(a, b), flat(a + 1, b - 1)...  4.36 us
    ppermute x1, waiting for transfers between devices, shards(): lax.ppermute(p_band[0], ('row', 'col'), [(flat(a, b), flat(a - 1, b + 1))...  3.96 us
    ppermute x1, starting transfers between devices, shards(): received = lax.ppermute(sent, ('row', 'col'), pairs)  3.9 us
    ppermute x1, starting transfers between devices, shards(): lax.ppermute(p_band, 'col', [(b, b + 1) for b in range(col_count - 1)])  3.56 us
    ppermute x1, starting transfers between devices, shards(): lax.ppermute(p_band[-1], 'row', [(a, a + 1) for a in range(row_count - 1)])  2.65 us
    unnamed x16, local copies, waits for them, and re-layouts  2.17 us
  transfers between devices with their start and end apart: 7, of which 2 were waited for; matrix products, arithmetic and copies ran while one was open for 1% of the time, Pallas kernels for 0%

profile of v3, /device:TPU:103, one launch (start us, length us, event | category | flops | bytes accessed | tf_op | source)
XLA Modules:
  0.0 52.1 jit_solution(12366968261098769676)
XLA Ops:
  0.0 0.7 %copy-done.7 = s32[10]{0:T(128)S(1)} copy-done((s32[10]{0:T(128)S(1)}, s32[10]{0:T(128)}, u32[]{:S(2)}) %copy-start.7) | copy-done | bytes 64
  0.7 0.7 %fusion.11 = (pred[10,3]{0,1:T(4,128)(4,1)S(1)}, pred[10,3]{0,1:T(4,128)(4,1)S(1)}, pred[10,3]{0,1:T(4,128)(4,1)S(1)}) fusion(s32[10,3]{0,1:T(4,128)} %param.7, s32[10]{0:T(128)S(1)} %copy-done.7), kind=kLoop, calls=%fused_computation.24 | loop fusion | flops 210 | bytes 250 | tf_op jit(solution)/shard_map/and | solution.py:14
  1.4 1.7 %fusion.2 = (bf16[10,1,128,128]{3,2,1,0:T(8,128)(2,1)S(1)}, bf16[10,1,128,128]{3,2,1,0:T(8,128)(2,1)S(1)}, bf16[10,1,128,128]{3,2,1,0:T(8,128)(2,1)S(1)}) fusion(pred[10]{0:T(512)(128)(4,1)S(1)} %get-tuple-element.14, pred[10]{0:T(512)(128)(4,1)S(1)} %get-tuple-element.15, pred[10]{0:T(512)(128)(4,1)S(1)} %get-tuple-element.13, ...), kind=kLoop, calls=%fused_computation.12 | loop fusion | flops 3440640 | bytes 1966170 | tf_op jit(solution)/shard_map/convert_element_type | solution.py:18
  3.1 0.1 pad_maximum_fusion.jac_ref
  3.2 0.0 copy-start.1
  3.3 0.1 constant_dynamic-slice_fusion
  3.3 3.9 %collective-permute-start = (bf16[8,3,128,128]{3,2,1,0:T(8,128)(2,1)S(1)}, bf16[8,3,128,128]{3,2,1,0:T(8,128)(2,1)S(1)}, u32[]{:S(2)}, u32[]{:S(2)}) collective-permute-start(bf16[8,3,128,128]{3,2,1,0:T(8,128)(2,1)S(1)} %constant_dynamic-slice_fusion), channel_id=1, source_target_pairs={{0,8},{8,16},{16,24},{24,32},{32,40},{40,48},{48,56},{56,64},{64,7... | collective-permute-start | bytes 2359304 | tf_op jit(solution)/shard_map/ppermute | solution.py:137
  7.3 3.6 %collective-permute-start.1 = (bf16[10,2,128,128]{3,2,1,0:T(8,128)(2,1)S(1)}, bf16[10,2,128,128]{3,2,1,0:T(8,128)(2,1)}, u32[]{:S(2)}, u32[]{:S(2)}) collective-permute-start(bf16[10,2,128,128]{3,2,1,0:T(8,128)(2,1)S(1)} %copy-done.1), channel_id=1, source_target_pairs={{0,1},{1,2},{2,3},{3,4},{4,5},{5,6},{6,7},{8,9},{9,10},{10,11},{11... | collective-permute-start | bytes 1966088 | tf_op jit(solution)/shard_map/ppermute | solution.py:110
  10.8 1.9 %collective-permute-start.2 = (bf16[10,2,128,128]{3,2,1,0:T(8,128)(2,1)S(1)}, bf16[10,2,128,128]{3,2,1,0:T(8,128)(2,1)}, u32[]{:S(2)}, u32[]{:S(2)}) collective-permute-start(bf16[10,2,128,128]{3,2,1,0:T(8,128)(2,1)S(1)} %copy-done.1), channel_id=1, source_target_pairs={{1,0},{2,1},{3,2},{4,3},{5,4},{6,5},{7,6},{9,8},{10,9},{11,10},{12... | collective-permute-start | bytes 1966088 | tf_op jit(solution)/shard_map/ppermute | solution.py:111
  12.8 2.7 %collective-permute-start.3 = (bf16[2,128,128]{2,1,0:T(8,128)(2,1)S(1)}, bf16[2,128,128]{2,1,0:T(8,128)(2,1)S(1)}, u32[]{:S(2)}, u32[]{:S(2)}) collective-permute-start(bf16[2,128,128]{2,1,0:T(8,128)(2,1)S(1)} %get-tuple-element.9), channel_id=1, source_target_pairs={{0,8},{8,16},{16,24},{24,32},{32,40},{40,48},{48,56},{56,64},{64,7... | collective-permute-start | bytes 196616 | tf_op jit(solution)/shard_map/ppermute | solution.py:112
  15.4 4.4 %collective-permute-start.4 = (bf16[2,128,128]{2,1,0:T(8,128)(2,1)S(1)}, bf16[2,128,128]{2,1,0:T(8,128)(2,1)S(1)}, u32[]{:S(2)}, u32[]{:S(2)}) collective-permute-start(bf16[2,128,128]{2,1,0:T(8,128)(2,1)S(1)} %get-tuple-element.9), channel_id=1, source_target_pairs={{1,8},{2,9},{3,10},{4,11},{5,12},{6,13},{7,14},{9,16},{10,17},{11,... | collective-permute-start | bytes 196616 | tf_op jit(solution)/shard_map/ppermute | solution.py:114
  19.8 0.0 collective-permute-done.3.up_ref
  19.8 1.9 %collective-permute-start.5 = (bf16[2,128,128]{2,1,0:T(8,128)(2,1)S(1)}, bf16[2,128,128]{2,1,0:T(8,128)(2,1)S(1)}, u32[]{:S(2)}, u32[]{:S(2)}) collective-permute-start(bf16[2,128,128]{2,1,0:T(8,128)(2,1)S(1)} %get-tuple-element.8), channel_id=1, source_target_pairs={{8,0},{16,8},{24,16},{32,24},{40,32},{48,40},{56,48},{64,56},{72,6... | collective-permute-start | bytes 196616 | tf_op jit(solution)/shard_map/ppermute | solution.py:113
  21.8 17.0 %collective-permute-done.4.up_right_ref = bf16[2,128,128]{2,1,0:T(8,128)(2,1)S(1)} collective-permute-done((bf16[2,128,128]{2,1,0:T(8,128)(2,1)S(1)}, bf16[2,128,128]{2,1,0:T(8,128)(2,1)S(1)}, u32[]{:S(2)}, u32[]{:S(2)}) %collective-permute-start.4) | collective-permute-done | bytes 65568 | tf_op jit(solution)/shard_map/ppermute | solution.py:114
  38.7 1.9 %collective-permute-start.6 = (bf16[2,128,128]{2,1,0:T(8,128)(2,1)S(1)}, bf16[2,128,128]{2,1,0:T(8,128)(2,1)S(1)}, u32[]{:S(2)}, u32[]{:S(2)}) collective-permute-start(bf16[2,128,128]{2,1,0:T(8,128)(2,1)S(1)} %get-tuple-element.8), channel_id=1, source_target_pairs={{8,1},{9,2},{10,3},{11,4},{12,5},{13,6},{14,7},{16,9},{17,10},{18,... | collective-permute-start | bytes 196616 | tf_op jit(solution)/shard_map/ppermute | solution.py:119
  40.7 0.6 %pad_add_fusion.ids = s32[2]{0:T(128)} fusion(s32[1]{0:T(128)} %bitcast.1, s32[1]{0:T(128)} %bitcast), kind=kLoop, calls=%fused_computation.34 | loop fusion | flops 2 | bytes 16 | tf_op jit(solution)/shard_map/stack | solution.py:139
  41.2 0.0 collective-permute-done.5.down_ref
  41.2 4.0 %collective-permute-done.6.down_left_ref = bf16[2,128,128]{2,1,0:T(8,128)(2,1)S(1)} collective-permute-done((bf16[2,128,128]{2,1,0:T(8,128)(2,1)S(1)}, bf16[2,128,128]{2,1,0:T(8,128)(2,1)S(1)}, u32[]{:S(2)}, u32[]{:S(2)}) %collective-permute-start.6) | collective-permute-done | bytes 65568 | tf_op jit(solution)/shard_map/ppermute | solution.py:119
  45.2 0.0 collective-permute-done.1.left_ref
  45.2 0.0 collective-permute-done.2.right_ref
  45.2 0.0 collective-permute-done.recv_ref
  45.3 0.6 %copy-done.6 = bf16[2,128,128]{2,1,0:T(8,128)(2,1)} copy-done((bf16[2,128,128]{2,1,0:T(8,128)(2,1)}, bf16[2,128,128]{2,1,0:T(8,128)(2,1)S(1)}, u32[]{:S(2)}) %copy-start.6) | copy-done | bytes 65560
  45.8 0.9 %copy-done.2 = bf16[8,3,128,128]{3,2,1,0:T(8,128)(2,1)} copy-done((bf16[8,3,128,128]{3,2,1,0:T(8,128)(2,1)}, bf16[8,3,128,128]{3,2,1,0:T(8,128)(2,1)S(1)}, u32[]{:S(2)}) %copy-start.2) | copy-done | bytes 786456
  46.8 5.4 %shard_map.55 = bf16[10,2,128,128]{3,2,1,0:T(8,128)(2,1)} custom-call(s32[2]{0:T(128)} %pad_add_fusion.ids, f32[10,128]{1,0:T(8,128)} %q_ref.1, bf16[10,3,128,128]{3,2,1,0:T(8,128)(2,1)} %copy-done, bf16[8,3,128,128]{3,2,1,0:T(8,128)(2,1)} %copy-done.2, bf16[10,2,128,128]{3,2,1,0:T(8,128)(2,1)} %mid_ref.1, ...), custom_call_target="tpu_custom_call" | custom-call | tf_op jit(solution)/shard_map/pallas_call | solution.py:142
  (15 shorter events, 0.1 us)
Async XLA Ops:
  0.0 0.7 %copy-start.7 = (s32[10]{0:T(128)S(1)}, s32[10]{0:T(128)}, u32[]{:S(2)}) copy-start(s32[10]{0:T(128)} %param.8) | copy-start | bytes 124
  3.2 42.0 %copy-start = (bf16[10,3,128,128]{3,2,1,0:T(8,128)(2,1)}, bf16[10,3,128,128]{3,2,1,0:T(8,128)(2,1)S(1)}, u32[]{:S(2)}) copy-start(bf16[10,3,128,128]{3,2,1,0:T(8,128)(2,1)S(1)} %pad_maximum_fusion.jac_ref) | copy-start | bytes 2949124
  3.2 4.0 %copy-start.1 = (bf16[10,2,128,128]{3,2,1,0:T(8,128)(2,1)S(1)}, bf16[10,2,128,128]{3,2,1,0:T(8,128)(2,1)}, u32[]{:S(2)}) copy-start(bf16[10,2,128,128]{3,2,1,0:T(8,128)(2,1)} %mid_ref.1) | copy-start | bytes 1966084
  3.3 41.9 %collective-permute-start = (bf16[8,3,128,128]{3,2,1,0:T(8,128)(2,1)S(1)}, bf16[8,3,128,128]{3,2,1,0:T(8,128)(2,1)S(1)}, u32[]{:S(2)}, u32[]{:S(2)}) collective-permute-start(bf16[8,3,128,128]{3,2,1,0:T(8,128)(2,1)S(1)} %constant_dynamic-slice_fusion), channel_id=1, source_target_pairs={{0,8},{8,16},{16,24},{24,32},{32,40},{40,48},{48,56},{56,64},{64,7... | collective-permute-start | bytes 2359304 | tf_op jit(solution)/shard_map/ppermute | solution.py:137
  7.3 38.0 %collective-permute-start.1 = (bf16[10,2,128,128]{3,2,1,0:T(8,128)(2,1)S(1)}, bf16[10,2,128,128]{3,2,1,0:T(8,128)(2,1)}, u32[]{:S(2)}, u32[]{:S(2)}) collective-permute-start(bf16[10,2,128,128]{3,2,1,0:T(8,128)(2,1)S(1)} %copy-done.1), channel_id=1, source_target_pairs={{0,1},{1,2},{2,3},{3,4},{4,5},{5,6},{6,7},{8,9},{9,10},{10,11},{11... | collective-permute-start | bytes 1966088 | tf_op jit(solution)/shard_map/ppermute | solution.py:110
  10.8 34.4 %collective-permute-start.2 = (bf16[10,2,128,128]{3,2,1,0:T(8,128)(2,1)S(1)}, bf16[10,2,128,128]{3,2,1,0:T(8,128)(2,1)}, u32[]{:S(2)}, u32[]{:S(2)}) collective-permute-start(bf16[10,2,128,128]{3,2,1,0:T(8,128)(2,1)S(1)} %copy-done.1), channel_id=1, source_target_pairs={{1,0},{2,1},{3,2},{4,3},{5,4},{6,5},{7,6},{9,8},{10,9},{11,10},{12... | collective-permute-start | bytes 1966088 | tf_op jit(solution)/shard_map/ppermute | solution.py:111
  12.8 7.0 %collective-permute-start.3 = (bf16[2,128,128]{2,1,0:T(8,128)(2,1)S(1)}, bf16[2,128,128]{2,1,0:T(8,128)(2,1)S(1)}, u32[]{:S(2)}, u32[]{:S(2)}) collective-permute-start(bf16[2,128,128]{2,1,0:T(8,128)(2,1)S(1)} %get-tuple-element.9), channel_id=1, source_target_pairs={{0,8},{8,16},{16,24},{24,32},{32,40},{40,48},{48,56},{56,64},{64,7... | collective-permute-start | bytes 196616 | tf_op jit(solution)/shard_map/ppermute | solution.py:112
  15.4 23.3 %collective-permute-start.4 = (bf16[2,128,128]{2,1,0:T(8,128)(2,1)S(1)}, bf16[2,128,128]{2,1,0:T(8,128)(2,1)S(1)}, u32[]{:S(2)}, u32[]{:S(2)}) collective-permute-start(bf16[2,128,128]{2,1,0:T(8,128)(2,1)S(1)} %get-tuple-element.9), channel_id=1, source_target_pairs={{1,8},{2,9},{3,10},{4,11},{5,12},{6,13},{7,14},{9,16},{10,17},{11,... | collective-permute-start | bytes 196616 | tf_op jit(solution)/shard_map/ppermute | solution.py:114
  19.8 25.4 %copy-start.3 = (bf16[2,128,128]{2,1,0:T(8,128)(2,1)}, bf16[2,128,128]{2,1,0:T(8,128)(2,1)S(1)}, u32[]{:S(2)}) copy-start(bf16[2,128,128]{2,1,0:T(8,128)(2,1)S(1)} %collective-permute-done.3.up_ref) | copy-start | bytes 196612
  19.8 21.4 %collective-permute-start.5 = (bf16[2,128,128]{2,1,0:T(8,128)(2,1)S(1)}, bf16[2,128,128]{2,1,0:T(8,128)(2,1)S(1)}, u32[]{:S(2)}, u32[]{:S(2)}) collective-permute-start(bf16[2,128,128]{2,1,0:T(8,128)(2,1)S(1)} %get-tuple-element.8), channel_id=1, source_target_pairs={{8,0},{16,8},{24,16},{32,24},{40,32},{48,40},{56,48},{64,56},{72,6... | collective-permute-start | bytes 196616 | tf_op jit(solution)/shard_map/ppermute | solution.py:113
  38.7 6.5 %copy-start.4 = (bf16[2,128,128]{2,1,0:T(8,128)(2,1)}, bf16[2,128,128]{2,1,0:T(8,128)(2,1)S(1)}, u32[]{:S(2)}) copy-start(bf16[2,128,128]{2,1,0:T(8,128)(2,1)S(1)} %collective-permute-done.4.up_right_ref) | copy-start | bytes 196612
  38.7 6.5 %collective-permute-start.6 = (bf16[2,128,128]{2,1,0:T(8,128)(2,1)S(1)}, bf16[2,128,128]{2,1,0:T(8,128)(2,1)S(1)}, u32[]{:S(2)}, u32[]{:S(2)}) collective-permute-start(bf16[2,128,128]{2,1,0:T(8,128)(2,1)S(1)} %get-tuple-element.8), channel_id=1, source_target_pairs={{8,1},{9,2},{10,3},{11,4},{12,5},{13,6},{14,7},{16,9},{17,10},{18,... | collective-permute-start | bytes 196616 | tf_op jit(solution)/shard_map/ppermute | solution.py:119
  41.2 4.0 %copy-start.5 = (bf16[2,128,128]{2,1,0:T(8,128)(2,1)}, bf16[2,128,128]{2,1,0:T(8,128)(2,1)S(1)}, u32[]{:S(2)}) copy-start(bf16[2,128,128]{2,1,0:T(8,128)(2,1)S(1)} %collective-permute-done.5.down_ref) | copy-start | bytes 196612
  45.2 0.6 %copy-start.6 = (bf16[2,128,128]{2,1,0:T(8,128)(2,1)}, bf16[2,128,128]{2,1,0:T(8,128)(2,1)S(1)}, u32[]{:S(2)}) copy-start(bf16[2,128,128]{2,1,0:T(8,128)(2,1)S(1)} %collective-permute-done.6.down_left_ref) | copy-start | bytes 196612
  45.8 0.9 %copy-start.2 = (bf16[8,3,128,128]{3,2,1,0:T(8,128)(2,1)}, bf16[8,3,128,128]{3,2,1,0:T(8,128)(2,1)S(1)}, u32[]{:S(2)}) copy-start(bf16[8,3,128,128]{3,2,1,0:T(8,128)(2,1)S(1)} %collective-permute-done.recv_ref) | copy-start | bytes 2359300

commit v4 on v3

--- a/solution.py
+++ b/solution.py
@@ -22,8 +22,7 @@
 def band_kernel(tile_rows, band_local, half_band, grid_tiles, sent_rows):
     extended = band_local + 2
 
-    def kernel(ids, q_ref, jac_ref, recv_ref, mid_ref, left_ref, right_ref, up_ref, up_right_ref,
-               down_ref, down_left_ref, out_ref):
+    def kernel(ids, q_ref, jac_ref, recv_ref, mid_ref, left_ref, right_ref, up_ref, down_ref, out_ref):
         row_id = ids[0]
         col_id = ids[1]
         first_row = row_id * tile_rows
@@ -32,22 +31,16 @@
         size = jac_ref.shape[-1]
 
         def prior_tile(ext_row, ext_slot):
-            if ext_row == 0:
-                if ext_slot < 2 + band_local:
-                    tile = up_ref[ext_slot - 2]
-                else:
-                    tile = up_right_ref[ext_slot - 2 - band_local]
+            if ext_slot < 2:
+                tile = left_ref[ext_row - 1, band_local - 2 + ext_slot]
+            elif ext_slot >= 2 + band_local:
+                tile = right_ref[ext_row, ext_slot - 2 - band_local]
+            elif ext_row == 0:
+                tile = up_ref[ext_slot - 2]
             elif ext_row == tile_rows + 1:
-                if ext_slot < 2:
-                    tile = down_left_ref[band_local - 2 + ext_slot]
-                else:
-                    tile = down_ref[ext_slot - 2]
-            elif ext_slot < 2:
-                tile = left_ref[ext_row - 1, band_local - 2 + ext_slot]
-            elif ext_slot < 2 + band_local:
+                tile = down_ref[ext_slot - 2]
+            else:
                 tile = mid_ref[ext_row - 1, ext_slot - 2]
-            else:
-                tile = right_ref[ext_row - 1, ext_slot - 2 - band_local]
             column = first_row + ext_row - 1 + low_slot + ext_slot - half_band
             keep = (column >= 0) & (column < grid_tiles)
             return jnp.where(keep, tile, jnp.zeros_like(tile))
@@ -107,20 +100,8 @@
     def flat(a, b):
         return a * col_count + b
 
-    left = lax.ppermute(p_band, "col", [(b, b + 1) for b in range(col_count - 1)])
-    right = lax.ppermute(p_band, "col", [(b + 1, b) for b in range(col_count - 1)])
     up = lax.ppermute(p_band[-1], "row", [(a, a + 1) for a in range(row_count - 1)])
     down = lax.ppermute(p_band[0], "row", [(a + 1, a) for a in range(row_count - 1)])
-    up_right = lax.ppermute(
-        p_band[-1],
-        ("row", "col"),
-        [(flat(a, b), flat(a + 1, b - 1)) for a in range(row_count - 1) for b in range(1, col_count)],
-    )
-    down_left = lax.ppermute(
-        p_band[0],
-        ("row", "col"),
-        [(flat(a, b), flat(a - 1, b + 1)) for a in range(1, row_count) for b in range(col_count - 1)],
-    )
 
     jacobian = assemble(blocks, block_offsets, block_live)
 
@@ -136,15 +117,20 @@
             pairs += [(flat(a, b), flat(a - 1, b)) for a in range(1, row_count)]
     received = lax.ppermute(sent, ("row", "col"), pairs)
 
+    left_payload = jnp.concatenate([p_band, down[None]], axis=0)
+    right_payload = jnp.concatenate([up[None], p_band], axis=0)
+    left = lax.ppermute(left_payload, "col", [(b, b + 1) for b in range(col_count - 1)])
+    right = lax.ppermute(right_payload, "col", [(b + 1, b) for b in range(col_count - 1)])
+
     ids = jnp.stack([row_id, col_id]).astype(jnp.int32)
     vmem = pl.BlockSpec(memory_space=pltpu.MemorySpace.VMEM)
     smem = pl.BlockSpec(memory_space=pltpu.MemorySpace.SMEM)
     return pl.pallas_call(
         band_kernel(tile_rows, band_local, half_band, grid_tiles, sent_rows),
         out_shape=jax.ShapeDtypeStruct(p_band.shape, p_band.dtype),
-        in_specs=[smem] + [vmem] * 10,
+        in_specs=[smem] + [vmem] * 8,
         out_specs=vmem,
-    )(ids, q_var, jacobian, received, p_band, left, right, up, up_right, down, down_left)
+    )(ids, q_var, jacobian, received, p_band, left, right, up, down)
 
 
 def solution(mesh):

time: 52.5 us -> 52.3 us (level)
  starting transfers between devices: 20.2 us -> 18.4 us
  local copies, waits for them, and re-layouts: 2.28 us -> 3.69 us
  other arithmetic: 3.11 us -> 3.66 us
    ppermute x4 -> x2, starting transfers between devices: 11.8 us -> 8.9 us  [the longest x1 6.44 us: shards(): lax.ppermute(left_payload, 'col', [(b, b + 1) for b in range(col_count -...]
    concatenate x0 -> x1, other arithmetic: none -> 1.23 us  [shards(): right_payload = jnp.concatenate([up[None], p_band], axis=0)]
    ppermute x1, starting transfers between devices: 2.65 us -> 3.77 us  [shards(): lax.ppermute(p_band[-1], 'row', [(a, a + 1) for a in range(row_count - 1)])]
    squeeze x1, local copies, waits for them, and re-layouts: 0.01 us -> 0.88 us  [shards(): p_band[-1]]
    and x1, other arithmetic: 0.69 us -> 0.01 us  [assemble(): choose = (block_offsets == target) & alive]
    unnamed x16 -> x18, local copies, waits for them, and re-layouts: 2.17 us -> 2.71 us
    ppermute x4 -> x2, waiting for transfers between devices: 20.9 us -> 20.6 us  [the longest x1 20.6 us: shards(): lax.ppermute(right_payload, 'col', [(b + 1, b) for b in range(col_count -...]
  transfers between devices with their start and end apart: 7 -> 5, of which waited for: 2 -> 1; matrix products, arithmetic and copies ran while one was open for 1% -> 7% of each run, Pallas kernels for 0% -> 0%
where the time goes in v4:
time: 52.3 us; the launch traced here: 52 us
  waiting for transfers between devices  20.7 us (40%)
  starting transfers between devices  18.4 us (35%)
  Pallas kernels  5.41 us (10%)
  local copies, waits for them, and re-layouts  3.69 us (7%)
  other arithmetic  3.66 us (7%)
    ppermute x1, waiting for transfers between devices, shards(): lax.ppermute(right_payload, 'col', [(b + 1, b) for b in range(col_count -...  20.6 us
    ppermute x1, starting transfers between devices, shards(): lax.ppermute(left_payload, 'col', [(b, b + 1) for b in range(col_count -...  6.44 us
    pallas_call x1, Pallas kernels, shards(): pl.pallas_call(band_kernel(tile_rows, band_local, half_band, grid_tiles,...  5.41 us
    ppermute x1, starting transfers between devices, shards(): received = lax.ppermute(sent, ('row', 'col'), pairs)  3.77 us
    ppermute x1, starting transfers between devices, shards(): lax.ppermute(p_band[-1], 'row', [(a, a + 1) for a in range(row_count - 1)])  3.77 us
    unnamed x18, local copies, waits for them, and re-layouts  2.71 us
    ppermute x1, starting transfers between devices, shards(): lax.ppermute(right_payload, 'col', [(b + 1, b) for b in range(col_count -...  2.46 us
    ppermute x1, starting transfers between devices, shards(): lax.ppermute(p_band[0], 'row', [(a + 1, a) for a in range(row_count - 1)])  1.92 us
  transfers between devices with their start and end apart: 5, of which 1 were waited for; matrix products, arithmetic and copies ran while one was open for 7% of the time, Pallas kernels for 0%

profile of v4, /device:TPU:103, one launch (start us, length us, event | category | flops | bytes accessed | tf_op | source)
XLA Modules:
  0.0 52.0 jit_solution(14357901695521678310)
XLA Ops:
  0.0 0.9 %slice_bitcast_fusion = (bf16[2,128,128]{2,1,0:T(8,128)(2,1)S(1)}, bf16[2,128,128]{2,1,0:T(8,128)(2,1)S(1)}) fusion(bf16[10,2,128,128]{3,2,1,0:T(8,128)(2,1)} %mid_ref.1), kind=kLoop, calls=%fused_computation.21 | loop fusion | bytes 262144 | tf_op jit(solution)/shard_map/squeeze | solution.py:103
  0.9 3.8 %collective-permute-start.3 = (bf16[2,128,128]{2,1,0:T(8,128)(2,1)S(1)}, bf16[2,128,128]{2,1,0:T(8,128)(2,1)S(1)}, u32[]{:S(2)}, u32[]{:S(2)}) collective-permute-start(bf16[2,128,128]{2,1,0:T(8,128)(2,1)S(1)} %get-tuple-element.10), channel_id=1, source_target_pairs={{0,8},{8,16},{16,24},{24,32},{32,40},{40,48},{48,56},{56,64},{64,7... | collective-permute-start | bytes 196616 | tf_op jit(solution)/shard_map/ppermute | solution.py:103
  4.7 1.9 %collective-permute-start.1 = (bf16[2,128,128]{2,1,0:T(8,128)(2,1)S(1)}, bf16[2,128,128]{2,1,0:T(8,128)(2,1)S(1)}, u32[]{:S(2)}, u32[]{:S(2)}) collective-permute-start(bf16[2,128,128]{2,1,0:T(8,128)(2,1)S(1)} %get-tuple-element.11), channel_id=1, source_target_pairs={{8,0},{16,8},{24,16},{32,24},{40,32},{48,40},{56,48},{64,56},{72,6... | collective-permute-start | bytes 196616 | tf_op jit(solution)/shard_map/ppermute | solution.py:104
  6.6 0.0 copy-start.7
  6.6 0.0 copy-start.8
  6.6 0.7 %copy-done.7 = s32[10,3]{0,1:T(4,128)S(1)} copy-done((s32[10,3]{0,1:T(4,128)S(1)}, s32[10,3]{0,1:T(4,128)}, u32[]{:S(2)}) %copy-start.7) | copy-done | bytes 144
  7.3 1.7 %fusion.2 = (bf16[10,1,128,128]{3,2,1,0:T(8,128)(2,1)S(1)}, bf16[10,1,128,128]{3,2,1,0:T(8,128)(2,1)S(1)}, bf16[10,1,128,128]{3,2,1,0:T(8,128)(2,1)S(1)}) fusion(pred[10]{0:T(512)(128)(4,1)S(1)} %get-tuple-element.16, pred[10]{0:T(512)(128)(4,1)S(1)} %get-tuple-element.17, pred[10]{0:T(512)(128)(4,1)S(1)} %get-tuple-element.15, ...), kind=kLoop, calls=%fused_computation.14 | loop fusion | flops 3440640 | bytes 1966170 | tf_op jit(solution)/shard_map/convert_element_type | solution.py:18
  9.1 0.1 pad_maximum_fusion.jac_ref
  9.2 0.0 copy-start.1
  9.2 0.1 constant_dynamic-slice_fusion
  9.3 3.8 %collective-permute-start = (bf16[8,3,128,128]{3,2,1,0:T(8,128)(2,1)S(1)}, bf16[8,3,128,128]{3,2,1,0:T(8,128)(2,1)S(1)}, u32[]{:S(2)}, u32[]{:S(2)}) collective-permute-start(bf16[8,3,128,128]{3,2,1,0:T(8,128)(2,1)S(1)} %constant_dynamic-slice_fusion), channel_id=1, source_target_pairs={{0,8},{8,16},{16,24},{24,32},{32,40},{40,48},{48,56},{56,64},{64,7... | collective-permute-start | bytes 2359304 | tf_op jit(solution)/shard_map/ppermute | solution.py:118
  13.1 0.0 collective-permute-done.3.up_ref
  13.1 0.0 collective-permute-done.1.down_ref
  13.1 1.2 %pad_maximum_fusion.2 = (bf16[11,2,128,128]{3,2,1,0:T(8,128)(2,1)}, bf16[11,2,128,128]{3,2,1,0:T(8,128)(2,1)}) fusion(bf16[10,2,128,128]{3,2,1,0:T(8,128)(2,1)S(1)} %copy-done.1, bf16[1,2,128,128]{3,2,1,0:T(8,128)(2,1)S(1)} %bitcast.26, bf16[1,2,128,128]{3,2,1,0:T(8,128)(2,1)S(1)} %bitcast.27), kind=kLoop, calls=%fused_computation.11 | loop fusion | flops 720896 | bytes 2228224 | tf_op jit(solution)/shard_map/concatenate | solution.py:121
  14.4 2.5 %collective-permute-start.4 = (bf16[11,2,128,128]{3,2,1,0:T(8,128)(2,1)}, bf16[11,2,128,128]{3,2,1,0:T(8,128)(2,1)S(1)}, u32[]{:S(2)}, u32[]{:S(2)}) collective-permute-start(bf16[11,2,128,128]{3,2,1,0:T(8,128)(2,1)} %get-tuple-element.8), channel_id=1, source_target_pairs={{1,0},{2,1},{3,2},{4,3},{5,4},{6,5},{7,6},{9,8},{10,9},{11,10},{12... | collective-permute-start | bytes 2162696 | tf_op jit(solution)/shard_map/ppermute | solution.py:123
  16.8 6.4 %collective-permute-start.2 = (bf16[11,2,128,128]{3,2,1,0:T(8,128)(2,1)}, bf16[11,2,128,128]{3,2,1,0:T(8,128)(2,1)S(1)}, u32[]{:S(2)}, u32[]{:S(2)}) collective-permute-start(bf16[11,2,128,128]{3,2,1,0:T(8,128)(2,1)} %get-tuple-element.9), channel_id=1, source_target_pairs={{0,1},{1,2},{2,3},{3,4},{4,5},{5,6},{6,7},{8,9},{9,10},{10,11},{11... | collective-permute-start | bytes 2162696 | tf_op jit(solution)/shard_map/ppermute | solution.py:122
  23.3 0.6 %pad_add_fusion.ids = s32[2]{0:T(128)} fusion(s32[1]{0:T(128)} %bitcast.1, s32[1]{0:T(128)} %bitcast), kind=kLoop, calls=%fused_computation.36 | loop fusion | flops 2 | bytes 16 | tf_op jit(solution)/shard_map/stack | solution.py:125
  23.9 20.6 %collective-permute-done.4.right_ref = bf16[11,2,128,128]{3,2,1,0:T(8,128)(2,1)S(1)} collective-permute-done((bf16[11,2,128,128]{3,2,1,0:T(8,128)(2,1)}, bf16[11,2,128,128]{3,2,1,0:T(8,128)(2,1)S(1)}, u32[]{:S(2)}, u32[]{:S(2)}) %collective-permute-start.4) | collective-permute-done | bytes 720928 | tf_op jit(solution)/shard_map/ppermute | solution.py:123
  44.5 0.0 collective-permute-done.2.left_ref
  44.5 0.0 collective-permute-done.recv_ref
  44.5 0.9 %copy-done.3 = bf16[11,2,128,128]{3,2,1,0:T(8,128)(2,1)} copy-done((bf16[11,2,128,128]{3,2,1,0:T(8,128)(2,1)}, bf16[11,2,128,128]{3,2,1,0:T(8,128)(2,1)S(1)}, u32[]{:S(2)}) %copy-start.3) | copy-done | bytes 720920
  45.4 0.2 copy-done.4
  45.6 0.9 %copy-done.2 = bf16[8,3,128,128]{3,2,1,0:T(8,128)(2,1)} copy-done((bf16[8,3,128,128]{3,2,1,0:T(8,128)(2,1)}, bf16[8,3,128,128]{3,2,1,0:T(8,128)(2,1)S(1)}, u32[]{:S(2)}) %copy-start.2) | copy-done | bytes 786456
  46.5 5.4 %shard_map.55 = bf16[10,2,128,128]{3,2,1,0:T(8,128)(2,1)} custom-call(s32[2]{0:T(128)} %pad_add_fusion.ids, f32[10,128]{1,0:T(8,128)} %q_ref.1, bf16[10,3,128,128]{3,2,1,0:T(8,128)(2,1)} %copy-done, bf16[8,3,128,128]{3,2,1,0:T(8,128)(2,1)} %copy-done.2, bf16[10,2,128,128]{3,2,1,0:T(8,128)(2,1)} %mid_ref.1, bf16[11,2,128,128]{3,2,1,0:T(8,128)(2,1)} %copy-done.4, ...), custom_call_target="tpu_custom_call" | custom-call | tf_op jit(solution)/shard_map/pallas_call | solution.py:128
  (14 shorter events, 0.1 us)
Async XLA Ops:
  0.9 12.2 %collective-permute-start.3 = (bf16[2,128,128]{2,1,0:T(8,128)(2,1)S(1)}, bf16[2,128,128]{2,1,0:T(8,128)(2,1)S(1)}, u32[]{:S(2)}, u32[]{:S(2)}) collective-permute-start(bf16[2,128,128]{2,1,0:T(8,128)(2,1)S(1)} %get-tuple-element.10), channel_id=1, source_target_pairs={{0,8},{8,16},{16,24},{24,32},{32,40},{40,48},{48,56},{56,64},{64,7... | collective-permute-start | bytes 196616 | tf_op jit(solution)/shard_map/ppermute | solution.py:103
  4.7 8.4 %collective-permute-start.1 = (bf16[2,128,128]{2,1,0:T(8,128)(2,1)S(1)}, bf16[2,128,128]{2,1,0:T(8,128)(2,1)S(1)}, u32[]{:S(2)}, u32[]{:S(2)}) collective-permute-start(bf16[2,128,128]{2,1,0:T(8,128)(2,1)S(1)} %get-tuple-element.11), channel_id=1, source_target_pairs={{8,0},{16,8},{24,16},{32,24},{40,32},{48,40},{56,48},{64,56},{72,6... | collective-permute-start | bytes 196616 | tf_op jit(solution)/shard_map/ppermute | solution.py:104
  6.6 0.7 %copy-start.7 = (s32[10,3]{0,1:T(4,128)S(1)}, s32[10,3]{0,1:T(4,128)}, u32[]{:S(2)}) copy-start(s32[10,3]{0,1:T(4,128)} %param.7) | copy-start | bytes 364
  6.6 0.7 %copy-start.8 = (s32[10]{0:T(128)S(1)}, s32[10]{0:T(128)}, u32[]{:S(2)}) copy-start(s32[10]{0:T(128)} %param.8) | copy-start | bytes 124
  9.2 5.2 %copy-start = (bf16[10,3,128,128]{3,2,1,0:T(8,128)(2,1)}, bf16[10,3,128,128]{3,2,1,0:T(8,128)(2,1)S(1)}, u32[]{:S(2)}) copy-start(bf16[10,3,128,128]{3,2,1,0:T(8,128)(2,1)S(1)} %pad_maximum_fusion.jac_ref) | copy-start | bytes 2949124
  9.2 3.9 %copy-start.1 = (bf16[10,2,128,128]{3,2,1,0:T(8,128)(2,1)S(1)}, bf16[10,2,128,128]{3,2,1,0:T(8,128)(2,1)}, u32[]{:S(2)}) copy-start(bf16[10,2,128,128]{3,2,1,0:T(8,128)(2,1)} %mid_ref.1) | copy-start | bytes 1966084
  9.3 35.2 %collective-permute-start = (bf16[8,3,128,128]{3,2,1,0:T(8,128)(2,1)S(1)}, bf16[8,3,128,128]{3,2,1,0:T(8,128)(2,1)S(1)}, u32[]{:S(2)}, u32[]{:S(2)}) collective-permute-start(bf16[8,3,128,128]{3,2,1,0:T(8,128)(2,1)S(1)} %constant_dynamic-slice_fusion), channel_id=1, source_target_pairs={{0,8},{8,16},{16,24},{24,32},{32,40},{40,48},{48,56},{56,64},{64,7... | collective-permute-start | bytes 2359304 | tf_op jit(solution)/shard_map/ppermute | solution.py:118
  13.1 1.3 %copy-start.5 = (bf16[2,128,128]{2,1,0:T(8,128)(2,1)}, bf16[2,128,128]{2,1,0:T(8,128)(2,1)S(1)}, u32[]{:S(2)}) copy-start(bf16[2,128,128]{2,1,0:T(8,128)(2,1)S(1)} %collective-permute-done.3.up_ref) | copy-start | bytes 196612
  13.1 1.3 %copy-start.6 = (bf16[2,128,128]{2,1,0:T(8,128)(2,1)}, bf16[2,128,128]{2,1,0:T(8,128)(2,1)S(1)}, u32[]{:S(2)}) copy-start(bf16[2,128,128]{2,1,0:T(8,128)(2,1)S(1)} %collective-permute-done.1.down_ref) | copy-start | bytes 196612
  14.4 30.1 %collective-permute-start.4 = (bf16[11,2,128,128]{3,2,1,0:T(8,128)(2,1)}, bf16[11,2,128,128]{3,2,1,0:T(8,128)(2,1)S(1)}, u32[]{:S(2)}, u32[]{:S(2)}) collective-permute-start(bf16[11,2,128,128]{3,2,1,0:T(8,128)(2,1)} %get-tuple-element.8), channel_id=1, source_target_pairs={{1,0},{2,1},{3,2},{4,3},{5,4},{6,5},{7,6},{9,8},{10,9},{11,10},{12... | collective-permute-start | bytes 2162696 | tf_op jit(solution)/shard_map/ppermute | solution.py:123
  16.8 27.7 %collective-permute-start.2 = (bf16[11,2,128,128]{3,2,1,0:T(8,128)(2,1)}, bf16[11,2,128,128]{3,2,1,0:T(8,128)(2,1)S(1)}, u32[]{:S(2)}, u32[]{:S(2)}) collective-permute-start(bf16[11,2,128,128]{3,2,1,0:T(8,128)(2,1)} %get-tuple-element.9), channel_id=1, source_target_pairs={{0,1},{1,2},{2,3},{3,4},{4,5},{5,6},{6,7},{8,9},{9,10},{10,11},{11... | collective-permute-start | bytes 2162696 | tf_op jit(solution)/shard_map/ppermute | solution.py:122
  44.5 0.9 %copy-start.3 = (bf16[11,2,128,128]{3,2,1,0:T(8,128)(2,1)}, bf16[11,2,128,128]{3,2,1,0:T(8,128)(2,1)S(1)}, u32[]{:S(2)}) copy-start(bf16[11,2,128,128]{3,2,1,0:T(8,128)(2,1)S(1)} %collective-permute-done.4.right_ref) | copy-start | bytes 2162692
  44.5 1.1 %copy-start.4 = (bf16[11,2,128,128]{3,2,1,0:T(8,128)(2,1)}, bf16[11,2,128,128]{3,2,1,0:T(8,128)(2,1)S(1)}, u32[]{:S(2)}) copy-start(bf16[11,2,128,128]{3,2,1,0:T(8,128)(2,1)S(1)} %collective-permute-done.2.left_ref) | copy-start | bytes 2162692
  45.6 0.9 %copy-start.2 = (bf16[8,3,128,128]{3,2,1,0:T(8,128)(2,1)}, bf16[8,3,128,128]{3,2,1,0:T(8,128)(2,1)S(1)}, u32[]{:S(2)}) copy-start(bf16[8,3,128,128]{3,2,1,0:T(8,128)(2,1)S(1)} %collective-permute-done.recv_ref) | copy-start | bytes 2359300

commit v5 on v4

--- a/solution.py
+++ b/solution.py
@@ -22,7 +22,8 @@
 def band_kernel(tile_rows, band_local, half_band, grid_tiles, sent_rows):
     extended = band_local + 2
 
-    def kernel(ids, q_ref, jac_ref, recv_ref, mid_ref, left_ref, right_ref, up_ref, down_ref, out_ref):
+    def kernel(ids, q_ref, jac_ref, recv_ref, mid_ref, left_ref, right_ref, up_ref, down_ref,
+               up_right_ref, down_left_ref, out_ref):
         row_id = ids[0]
         col_id = ids[1]
         first_row = row_id * tile_rows
@@ -32,9 +33,15 @@
 
         def prior_tile(ext_row, ext_slot):
             if ext_slot < 2:
-                tile = left_ref[ext_row - 1, band_local - 2 + ext_slot]
+                if ext_row == tile_rows + 1:
+                    tile = down_left_ref[band_local - 2 + ext_slot]
+                else:
+                    tile = left_ref[ext_row - 1, band_local - 2 + ext_slot]
             elif ext_slot >= 2 + band_local:
-                tile = right_ref[ext_row, ext_slot - 2 - band_local]
+                if ext_row == 0:
+                    tile = up_right_ref[ext_slot - 2 - band_local]
+                else:
+                    tile = right_ref[ext_row - 1, ext_slot - 2 - band_local]
             elif ext_row == 0:
                 tile = up_ref[ext_slot - 2]
             elif ext_row == tile_rows + 1:
@@ -100,6 +107,8 @@
     def flat(a, b):
         return a * col_count + b
 
+    left = lax.ppermute(p_band, "col", [(b, b + 1) for b in range(col_count - 1)])
+    right = lax.ppermute(p_band, "col", [(b + 1, b) for b in range(col_count - 1)])
     up = lax.ppermute(p_band[-1], "row", [(a, a + 1) for a in range(row_count - 1)])
     down = lax.ppermute(p_band[0], "row", [(a + 1, a) for a in range(row_count - 1)])
 
@@ -117,10 +126,8 @@
             pairs += [(flat(a, b), flat(a - 1, b)) for a in range(1, row_count)]
     received = lax.ppermute(sent, ("row", "col"), pairs)
 
-    left_payload = jnp.concatenate([p_band, down[None]], axis=0)
-    right_payload = jnp.concatenate([up[None], p_band], axis=0)
-    left = lax.ppermute(left_payload, "col", [(b, b + 1) for b in range(col_count - 1)])
-    right = lax.ppermute(right_payload, "col", [(b + 1, b) for b in range(col_count - 1)])
+    down_left = lax.ppermute(down, "col", [(b, b + 1) for b in range(col_count - 1)])
+    up_right = lax.ppermute(up, "col", [(b + 1, b) for b in range(col_count - 1)])
 
     ids = jnp.stack([row_id, col_id]).astype(jnp.int32)
     vmem = pl.BlockSpec(memory_space=pltpu.MemorySpace.VMEM)
@@ -128,9 +135,9 @@
     return pl.pallas_call(
         band_kernel(tile_rows, band_local, half_band, grid_tiles, sent_rows),
         out_shape=jax.ShapeDtypeStruct(p_band.shape, p_band.dtype),
-        in_specs=[smem] + [vmem] * 8,
+        in_specs=[smem] + [vmem] * 10,
         out_specs=vmem,
-    )(ids, q_var, jacobian, received, p_band, left, right, up, down)
+    )(ids, q_var, jacobian, received, p_band, left, right, up, down, up_right, down_left)
 
 
 def solution(mesh):

time: 52.3 us -> 50.5 us (0.966)
  the two profiles are of different devices: /device:TPU:103 before, /device:TPU:126 now
where the time goes in v5:
time: 50.5 us; the launch traced here: 50.2 us
  waiting for transfers between devices  22.1 us (44%)
  starting transfers between devices  17.1 us (34%)
  Pallas kernels  5.39 us (11%)
  other arithmetic  3.11 us (6%)
  local copies, waits for them, and re-layouts  2.27 us (4%)
    ppermute x1, waiting for transfers between devices, shards(): lax.ppermute(p_band[-1], 'row', [(a, a + 1) for a in range(row_count - 1)])  17.9 us
    ppermute x1, starting transfers between devices, shards(): lax.ppermute(p_band, 'col', [(b + 1, b) for b in range(col_count - 1)])  5.41 us
    pallas_call x1, Pallas kernels, shards(): pl.pallas_call(band_kernel(tile_rows, band_local, half_band, grid_tiles,...  5.39 us
    ppermute x1, waiting for transfers between devices, shards(): lax.ppermute(down, 'col', [(b, b + 1) for b in range(col_count - 1)])  4.26 us
    ppermute x1, starting transfers between devices, shards(): lax.ppermute(p_band[0], 'row', [(a + 1, a) for a in range(row_count - 1)])  3.64 us
    ppermute x1, starting transfers between devices, shards(): received = lax.ppermute(sent, ('row', 'col'), pairs)  2.22 us
    unnamed x16, local copies, waits for them, and re-layouts  2.17 us
    ppermute x1, starting transfers between devices, shards(): lax.ppermute(p_band[-1], 'row', [(a, a + 1) for a in range(row_count - 1)])  1.92 us
  transfers between devices with their start and end apart: 7, of which 2 were waited for; matrix products, arithmetic and copies ran while one was open for 1% of the time, Pallas kernels for 0%

profile of v5, /device:TPU:126, one launch (start us, length us, event | category | flops | bytes accessed | tf_op | source)
XLA Modules:
  0.0 50.2 jit_solution(15343207996192765311)
XLA Ops:
  0.0 0.7 %copy-done.7 = s32[10]{0:T(128)S(1)} copy-done((s32[10]{0:T(128)S(1)}, s32[10]{0:T(128)}, u32[]{:S(2)}) %copy-start.7) | copy-done | bytes 64
  0.7 0.7 %fusion.11 = (pred[10,3]{0,1:T(4,128)(4,1)S(1)}, pred[10,3]{0,1:T(4,128)(4,1)S(1)}, pred[10,3]{0,1:T(4,128)(4,1)S(1)}) fusion(s32[10,3]{0,1:T(4,128)} %param.7, s32[10]{0:T(128)S(1)} %copy-done.7), kind=kLoop, calls=%fused_computation.24 | loop fusion | flops 210 | bytes 250 | tf_op jit(solution)/shard_map/and | solution.py:14
  1.4 1.7 %fusion.2 = (bf16[10,1,128,128]{3,2,1,0:T(8,128)(2,1)S(1)}, bf16[10,1,128,128]{3,2,1,0:T(8,128)(2,1)S(1)}, bf16[10,1,128,128]{3,2,1,0:T(8,128)(2,1)S(1)}) fusion(pred[10]{0:T(512)(128)(4,1)S(1)} %get-tuple-element.14, pred[10]{0:T(512)(128)(4,1)S(1)} %get-tuple-element.15, pred[10]{0:T(512)(128)(4,1)S(1)} %get-tuple-element.13, ...), kind=kLoop, calls=%fused_computation.12 | loop fusion | flops 3440640 | bytes 1966170 | tf_op jit(solution)/shard_map/convert_element_type | solution.py:18
  3.1 0.1 pad_maximum_fusion.jac_ref
  3.2 0.0 copy-start.1
  3.3 0.1 constant_dynamic-slice_fusion
  3.3 2.2 %collective-permute-start = (bf16[8,3,128,128]{3,2,1,0:T(8,128)(2,1)S(1)}, bf16[8,3,128,128]{3,2,1,0:T(8,128)(2,1)S(1)}, u32[]{:S(2)}, u32[]{:S(2)}) collective-permute-start(bf16[8,3,128,128]{3,2,1,0:T(8,128)(2,1)S(1)} %constant_dynamic-slice_fusion), channel_id=1, source_target_pairs={{0,8},{8,16},{16,24},{24,32},{32,40},{40,48},{48,56},{56,64},{64,7... | collective-permute-start | bytes 2359304 | tf_op jit(solution)/shard_map/ppermute | solution.py:127
  5.6 1.3 %collective-permute-start.1 = (bf16[10,2,128,128]{3,2,1,0:T(8,128)(2,1)S(1)}, bf16[10,2,128,128]{3,2,1,0:T(8,128)(2,1)}, u32[]{:S(2)}, u32[]{:S(2)}) collective-permute-start(bf16[10,2,128,128]{3,2,1,0:T(8,128)(2,1)S(1)} %copy-done.1), channel_id=1, source_target_pairs={{0,1},{1,2},{2,3},{3,4},{4,5},{5,6},{6,7},{8,9},{9,10},{10,11},{11... | collective-permute-start | bytes 1966088 | tf_op jit(solution)/shard_map/ppermute | solution.py:110
  6.9 5.4 %collective-permute-start.2 = (bf16[10,2,128,128]{3,2,1,0:T(8,128)(2,1)S(1)}, bf16[10,2,128,128]{3,2,1,0:T(8,128)(2,1)}, u32[]{:S(2)}, u32[]{:S(2)}) collective-permute-start(bf16[10,2,128,128]{3,2,1,0:T(8,128)(2,1)S(1)} %copy-done.1), channel_id=1, source_target_pairs={{1,0},{2,1},{3,2},{4,3},{5,4},{6,5},{7,6},{9,8},{10,9},{11,10},{12... | collective-permute-start | bytes 1966088 | tf_op jit(solution)/shard_map/ppermute | solution.py:111
  12.3 1.9 %collective-permute-start.3 = (bf16[2,128,128]{2,1,0:T(8,128)(2,1)S(1)}, bf16[2,128,128]{2,1,0:T(8,128)(2,1)S(1)}, u32[]{:S(2)}, u32[]{:S(2)}) collective-permute-start(bf16[2,128,128]{2,1,0:T(8,128)(2,1)S(1)} %get-tuple-element.9), channel_id=1, source_target_pairs={{0,8},{8,16},{16,24},{24,32},{32,40},{40,48},{48,56},{56,64},{64,7... | collective-permute-start | bytes 196616 | tf_op jit(solution)/shard_map/ppermute | solution.py:112
  14.2 3.6 %collective-permute-start.4 = (bf16[2,128,128]{2,1,0:T(8,128)(2,1)S(1)}, bf16[2,128,128]{2,1,0:T(8,128)(2,1)S(1)}, u32[]{:S(2)}, u32[]{:S(2)}) collective-permute-start(bf16[2,128,128]{2,1,0:T(8,128)(2,1)S(1)} %get-tuple-element.8), channel_id=1, source_target_pairs={{8,0},{16,8},{24,16},{32,24},{40,32},{48,40},{56,48},{64,56},{72,6... | collective-permute-start | bytes 196616 | tf_op jit(solution)/shard_map/ppermute | solution.py:113
  17.9 17.9 %collective-permute-done.3.up_ref = bf16[2,128,128]{2,1,0:T(8,128)(2,1)S(1)} collective-permute-done((bf16[2,128,128]{2,1,0:T(8,128)(2,1)S(1)}, bf16[2,128,128]{2,1,0:T(8,128)(2,1)S(1)}, u32[]{:S(2)}, u32[]{:S(2)}) %collective-permute-start.3) | collective-permute-done | bytes 65568 | tf_op jit(solution)/shard_map/ppermute | solution.py:112
  35.8 1.3 %collective-permute-start.5 = (bf16[2,128,128]{2,1,0:T(8,128)(2,1)S(1)}, bf16[2,128,128]{2,1,0:T(8,128)(2,1)S(1)}, u32[]{:S(2)}, u32[]{:S(2)}) collective-permute-start(bf16[2,128,128]{2,1,0:T(8,128)(2,1)S(1)} %collective-permute-done.3.up_ref), channel_id=1, source_target_pairs={{1,0},{2,1},{3,2},{4,3},{5,4},{6,5},{7,6},{9,8},{10,9},{11,10},{12... | collective-permute-start | bytes 196616 | tf_op jit(solution)/shard_map/ppermute | solution.py:130
  37.0 0.0 collective-permute-done.4.down_ref
  37.1 1.3 %collective-permute-start.6 = (bf16[2,128,128]{2,1,0:T(8,128)(2,1)S(1)}, bf16[2,128,128]{2,1,0:T(8,128)(2,1)S(1)}, u32[]{:S(2)}, u32[]{:S(2)}) collective-permute-start(bf16[2,128,128]{2,1,0:T(8,128)(2,1)S(1)} %collective-permute-done.4.down_ref), channel_id=1, source_target_pairs={{0,1},{1,2},{2,3},{3,4},{4,5},{5,6},{6,7},{8,9},{9,10},{10,11},{11... | collective-permute-start | bytes 196616 | tf_op jit(solution)/shard_map/ppermute | solution.py:129
  38.4 0.6 %pad_add_fusion.ids = s32[2]{0:T(128)} fusion(s32[1]{0:T(128)} %bitcast.1, s32[1]{0:T(128)} %bitcast), kind=kLoop, calls=%fused_computation.34 | loop fusion | flops 2 | bytes 16 | tf_op jit(solution)/shard_map/stack | solution.py:132
  39.0 0.0 collective-permute-done.5.up_right_ref
  39.0 4.3 %collective-permute-done.6.down_left_ref = bf16[2,128,128]{2,1,0:T(8,128)(2,1)S(1)} collective-permute-done((bf16[2,128,128]{2,1,0:T(8,128)(2,1)S(1)}, bf16[2,128,128]{2,1,0:T(8,128)(2,1)S(1)}, u32[]{:S(2)}, u32[]{:S(2)}) %collective-permute-start.6) | collective-permute-done | bytes 65568 | tf_op jit(solution)/shard_map/ppermute | solution.py:129
  43.2 0.0 collective-permute-done.1.left_ref
  43.2 0.0 collective-permute-done.2.right_ref
  43.2 0.0 collective-permute-done.recv_ref
  43.3 0.6 %copy-done.6 = bf16[2,128,128]{2,1,0:T(8,128)(2,1)} copy-done((bf16[2,128,128]{2,1,0:T(8,128)(2,1)}, bf16[2,128,128]{2,1,0:T(8,128)(2,1)S(1)}, u32[]{:S(2)}) %copy-start.6) | copy-done | bytes 65560
  43.8 0.9 %copy-done.2 = bf16[8,3,128,128]{3,2,1,0:T(8,128)(2,1)} copy-done((bf16[8,3,128,128]{3,2,1,0:T(8,128)(2,1)}, bf16[8,3,128,128]{3,2,1,0:T(8,128)(2,1)S(1)}, u32[]{:S(2)}) %copy-start.2) | copy-done | bytes 786456
  44.8 5.4 %shard_map.55 = bf16[10,2,128,128]{3,2,1,0:T(8,128)(2,1)} custom-call(s32[2]{0:T(128)} %pad_add_fusion.ids, f32[10,128]{1,0:T(8,128)} %q_ref.1, bf16[10,3,128,128]{3,2,1,0:T(8,128)(2,1)} %copy-done, bf16[8,3,128,128]{3,2,1,0:T(8,128)(2,1)} %copy-done.2, bf16[10,2,128,128]{3,2,1,0:T(8,128)(2,1)} %mid_ref.1, ...), custom_call_target="tpu_custom_call" | custom-call | tf_op jit(solution)/shard_map/pallas_call | solution.py:135
  (15 shorter events, 0.1 us)
Async XLA Ops:
  0.0 0.7 %copy-start.7 = (s32[10]{0:T(128)S(1)}, s32[10]{0:T(128)}, u32[]{:S(2)}) copy-start(s32[10]{0:T(128)} %param.8) | copy-start | bytes 124
  3.2 40.0 %copy-start = (bf16[10,3,128,128]{3,2,1,0:T(8,128)(2,1)}, bf16[10,3,128,128]{3,2,1,0:T(8,128)(2,1)S(1)}, u32[]{:S(2)}) copy-start(bf16[10,3,128,128]{3,2,1,0:T(8,128)(2,1)S(1)} %pad_maximum_fusion.jac_ref) | copy-start | bytes 2949124
  3.2 2.3 %copy-start.1 = (bf16[10,2,128,128]{3,2,1,0:T(8,128)(2,1)S(1)}, bf16[10,2,128,128]{3,2,1,0:T(8,128)(2,1)}, u32[]{:S(2)}) copy-start(bf16[10,2,128,128]{3,2,1,0:T(8,128)(2,1)} %mid_ref.1) | copy-start | bytes 1966084
  3.3 39.9 %collective-permute-start = (bf16[8,3,128,128]{3,2,1,0:T(8,128)(2,1)S(1)}, bf16[8,3,128,128]{3,2,1,0:T(8,128)(2,1)S(1)}, u32[]{:S(2)}, u32[]{:S(2)}) collective-permute-start(bf16[8,3,128,128]{3,2,1,0:T(8,128)(2,1)S(1)} %constant_dynamic-slice_fusion), channel_id=1, source_target_pairs={{0,8},{8,16},{16,24},{24,32},{32,40},{40,48},{48,56},{56,64},{64,7... | collective-permute-start | bytes 2359304 | tf_op jit(solution)/shard_map/ppermute | solution.py:127
  5.6 37.7 %collective-permute-start.1 = (bf16[10,2,128,128]{3,2,1,0:T(8,128)(2,1)S(1)}, bf16[10,2,128,128]{3,2,1,0:T(8,128)(2,1)}, u32[]{:S(2)}, u32[]{:S(2)}) collective-permute-start(bf16[10,2,128,128]{3,2,1,0:T(8,128)(2,1)S(1)} %copy-done.1), channel_id=1, source_target_pairs={{0,1},{1,2},{2,3},{3,4},{4,5},{5,6},{6,7},{8,9},{9,10},{10,11},{11... | collective-permute-start | bytes 1966088 | tf_op jit(solution)/shard_map/ppermute | solution.py:110
  6.9 36.4 %collective-permute-start.2 = (bf16[10,2,128,128]{3,2,1,0:T(8,128)(2,1)S(1)}, bf16[10,2,128,128]{3,2,1,0:T(8,128)(2,1)}, u32[]{:S(2)}, u32[]{:S(2)}) collective-permute-start(bf16[10,2,128,128]{3,2,1,0:T(8,128)(2,1)S(1)} %copy-done.1), channel_id=1, source_target_pairs={{1,0},{2,1},{3,2},{4,3},{5,4},{6,5},{7,6},{9,8},{10,9},{11,10},{12... | collective-permute-start | bytes 1966088 | tf_op jit(solution)/shard_map/ppermute | solution.py:111
  12.3 23.5 %collective-permute-start.3 = (bf16[2,128,128]{2,1,0:T(8,128)(2,1)S(1)}, bf16[2,128,128]{2,1,0:T(8,128)(2,1)S(1)}, u32[]{:S(2)}, u32[]{:S(2)}) collective-permute-start(bf16[2,128,128]{2,1,0:T(8,128)(2,1)S(1)} %get-tuple-element.9), channel_id=1, source_target_pairs={{0,8},{8,16},{16,24},{24,32},{32,40},{40,48},{48,56},{56,64},{64,7... | collective-permute-start | bytes 196616 | tf_op jit(solution)/shard_map/ppermute | solution.py:112
  14.2 22.8 %collective-permute-start.4 = (bf16[2,128,128]{2,1,0:T(8,128)(2,1)S(1)}, bf16[2,128,128]{2,1,0:T(8,128)(2,1)S(1)}, u32[]{:S(2)}, u32[]{:S(2)}) collective-permute-start(bf16[2,128,128]{2,1,0:T(8,128)(2,1)S(1)} %get-tuple-element.8), channel_id=1, source_target_pairs={{8,0},{16,8},{24,16},{32,24},{40,32},{48,40},{56,48},{64,56},{72,6... | collective-permute-start | bytes 196616 | tf_op jit(solution)/shard_map/ppermute | solution.py:113
  35.8 7.5 %copy-start.3 = (bf16[2,128,128]{2,1,0:T(8,128)(2,1)}, bf16[2,128,128]{2,1,0:T(8,128)(2,1)S(1)}, u32[]{:S(2)}) copy-start(bf16[2,128,128]{2,1,0:T(8,128)(2,1)S(1)} %collective-permute-done.3.up_ref) | copy-start | bytes 196612
  35.8 3.2 %collective-permute-start.5 = (bf16[2,128,128]{2,1,0:T(8,128)(2,1)S(1)}, bf16[2,128,128]{2,1,0:T(8,128)(2,1)S(1)}, u32[]{:S(2)}, u32[]{:S(2)}) collective-permute-start(bf16[2,128,128]{2,1,0:T(8,128)(2,1)S(1)} %collective-permute-done.3.up_ref), channel_id=1, source_target_pairs={{1,0},{2,1},{3,2},{4,3},{5,4},{6,5},{7,6},{9,8},{10,9},{11,10},{12... | collective-permute-start | bytes 196616 | tf_op jit(solution)/shard_map/ppermute | solution.py:130
  37.1 6.2 %copy-start.4 = (bf16[2,128,128]{2,1,0:T(8,128)(2,1)}, bf16[2,128,128]{2,1,0:T(8,128)(2,1)S(1)}, u32[]{:S(2)}) copy-start(bf16[2,128,128]{2,1,0:T(8,128)(2,1)S(1)} %collective-permute-done.4.down_ref) | copy-start | bytes 196612
  37.1 6.2 %collective-permute-start.6 = (bf16[2,128,128]{2,1,0:T(8,128)(2,1)S(1)}, bf16[2,128,128]{2,1,0:T(8,128)(2,1)S(1)}, u32[]{:S(2)}, u32[]{:S(2)}) collective-permute-start(bf16[2,128,128]{2,1,0:T(8,128)(2,1)S(1)} %collective-permute-done.4.down_ref), channel_id=1, source_target_pairs={{0,1},{1,2},{2,3},{3,4},{4,5},{5,6},{6,7},{8,9},{9,10},{10,11},{11... | collective-permute-start | bytes 196616 | tf_op jit(solution)/shard_map/ppermute | solution.py:129
  39.0 4.3 %copy-start.5 = (bf16[2,128,128]{2,1,0:T(8,128)(2,1)}, bf16[2,128,128]{2,1,0:T(8,128)(2,1)S(1)}, u32[]{:S(2)}) copy-start(bf16[2,128,128]{2,1,0:T(8,128)(2,1)S(1)} %collective-permute-done.5.up_right_ref) | copy-start | bytes 196612
  43.2 0.6 %copy-start.6 = (bf16[2,128,128]{2,1,0:T(8,128)(2,1)}, bf16[2,128,128]{2,1,0:T(8,128)(2,1)S(1)}, u32[]{:S(2)}) copy-start(bf16[2,128,128]{2,1,0:T(8,128)(2,1)S(1)} %collective-permute-done.6.down_left_ref) | copy-start | bytes 196612
  43.8 0.9 %copy-start.2 = (bf16[8,3,128,128]{3,2,1,0:T(8,128)(2,1)}, bf16[8,3,128,128]{3,2,1,0:T(8,128)(2,1)S(1)}, u32[]{:S(2)}) copy-start(bf16[8,3,128,128]{3,2,1,0:T(8,128)(2,1)S(1)} %collective-permute-done.recv_ref) | copy-start | bytes 2359300

commit v6 on v5

--- a/solution.py
+++ b/solution.py
@@ -19,11 +19,12 @@
     return jnp.stack(pieces, axis=1)
 
 
-def band_kernel(tile_rows, band_local, half_band, grid_tiles, sent_rows):
+def band_kernel(tile_rows, band_local, half_band, grid_tiles, sent_rows, row_count, col_count):
     extended = band_local + 2
+    window = tile_rows + band_local - 1
 
     def kernel(ids, q_ref, jac_ref, recv_ref, mid_ref, left_ref, right_ref, up_ref, down_ref,
-               up_right_ref, down_left_ref, out_ref):
+               up_right_ref, down_left_ref, out_ref, win_ref):
         row_id = ids[0]
         col_id = ids[1]
         first_row = row_id * tile_rows
@@ -31,7 +32,22 @@
         low_offset = col_id * band_local - half_band
         size = jac_ref.shape[-1]
 
-        def prior_tile(ext_row, ext_slot):
+        for col_value in range(col_count):
+            offset = col_value * band_local - half_band
+
+            @pl.when(col_id == col_value)
+            def _():
+                for position in range(window):
+                    at = offset + position
+                    for g in range(3):
+                        if at < 0:
+                            win_ref[position, g] = recv_ref[sent_rows + at, g]
+                        elif at < tile_rows:
+                            win_ref[position, g] = jac_ref[at, g]
+                        else:
+                            win_ref[position, g] = recv_ref[at - tile_rows, g]
+
+        def prior_tile(ext_row, ext_slot, masked):
             if ext_slot < 2:
                 if ext_row == tile_rows + 1:
                     tile = down_left_ref[band_local - 2 + ext_slot]
@@ -48,48 +64,56 @@
                 tile = down_ref[ext_slot - 2]
             else:
                 tile = mid_ref[ext_row - 1, ext_slot - 2]
+            if not masked:
+                return tile
             column = first_row + ext_row - 1 + low_slot + ext_slot - half_band
             keep = (column >= 0) & (column < grid_tiles)
             return jnp.where(keep, tile, jnp.zeros_like(tile))
 
-        def window_tile(position, g):
-            at = sent_rows + low_offset + position
-            before = recv_ref[jnp.clip(at, 0, sent_rows - 1), g]
-            own = jac_ref[jnp.clip(at - sent_rows, 0, tile_rows - 1), g]
-            after = recv_ref[jnp.clip(at - sent_rows - tile_rows, 0, sent_rows - 1), g]
-            return jnp.where(at < sent_rows, before, jnp.where(at < sent_rows + tile_rows, own, after))
-
         eye = lax.broadcasted_iota(jnp.int32, (size, size), 0) == lax.broadcasted_iota(
             jnp.int32, (size, size), 1
         )
-        for row in range(tile_rows):
-            lhs = jnp.concatenate([jac_ref[row, f] for f in range(3)], axis=1)
-            rhs = jnp.concatenate(
-                [
-                    jnp.concatenate(
-                        [prior_tile(row + f, u - f + 2) for u in range(extended)], axis=1
+
+        def body(masked):
+            for row in range(tile_rows):
+                lhs = jnp.concatenate([jac_ref[row, f] for f in range(3)], axis=1)
+                rhs = jnp.concatenate(
+                    [
+                        jnp.concatenate(
+                            [prior_tile(row + f, u - f + 2, masked) for u in range(extended)], axis=1
+                        )
+                        for f in range(3)
+                    ],
+                    axis=0,
+                )
+                spread = jnp.dot(lhs, rhs, preferred_element_type=jnp.float32).astype(jnp.bfloat16)
+                noise = jnp.where(eye, q_ref[pl.ds(row, 1), :], 0.0)
+                for k in range(band_local):
+                    left_side = spread[:, k * size : (k + 3) * size]
+                    right_side = jnp.concatenate([win_ref[row + k, g] for g in range(3)], axis=1)
+                    total = lax.dot_general(
+                        left_side,
+                        right_side,
+                        (((1,), (1,)), ((), ())),
+                        preferred_element_type=jnp.float32,
                     )
-                    for f in range(3)
-                ],
-                axis=0,
-            )
-            spread = jnp.dot(lhs, rhs, preferred_element_type=jnp.float32).astype(jnp.bfloat16)
-            for k in range(band_local):
-                left_side = spread[:, k * size : (k + 3) * size]
-                right_side = jnp.concatenate([window_tile(row + k, g) for g in range(3)], axis=1)
-                total = lax.dot_general(
-                    left_side,
-                    right_side,
-                    (((1,), (1,)), ((), ())),
-                    preferred_element_type=jnp.float32,
-                )
-                on_diagonal = low_offset + k == 0
-                noise = jnp.where(eye & on_diagonal, q_ref[pl.ds(row, 1), :], 0.0)
-                total = total + noise
-                column = first_row + row + low_offset + k
-                keep = (column >= 0) & (column < grid_tiles)
-                total = jnp.where(keep, total, jnp.zeros_like(total))
-                out_ref[row, k] = total.astype(out_ref.dtype)
+                    on_diagonal = (low_offset + k == 0).astype(jnp.float32)
+                    total = total + noise * on_diagonal
+                    if masked:
+                        column = first_row + row + low_offset + k
+                        keep = (column >= 0) & (column < grid_tiles)
+                        total = jnp.where(keep, total, jnp.zeros_like(total))
+                    out_ref[row, k] = total.astype(out_ref.dtype)
+
+        edge = (row_id == 0) | (row_id == row_count - 1)
+
+        @pl.when(edge)
+        def _():
+            body(True)
+
+        @pl.when(jnp.logical_not(edge))
+        def _():
+            body(False)
 
     return kernel
 
@@ -133,10 +157,11 @@
     vmem = pl.BlockSpec(memory_space=pltpu.MemorySpace.VMEM)
     smem = pl.BlockSpec(memory_space=pltpu.MemorySpace.SMEM)
     return pl.pallas_call(
-        band_kernel(tile_rows, band_local, half_band, grid_tiles, sent_rows),
+        band_kernel(tile_rows, band_local, half_band, grid_tiles, sent_rows, row_count, col_count),
         out_shape=jax.ShapeDtypeStruct(p_band.shape, p_band.dtype),
         in_specs=[smem] + [vmem] * 10,
         out_specs=vmem,
+        scratch_shapes=[pltpu.VMEM((tile_rows + band_local - 1, 3, tile_size, tile_size), p_band.dtype)],
     )(ids, q_var, jacobian, received, p_band, left, right, up, down, up_right, down_left)
 
 

time: 50.5 us -> 50.6 us (level)
  no operation moved by 1% of the time
where the time goes in v6:
time: 50.6 us; the launch traced here: 50.3 us
  waiting for transfers between devices  22.1 us (44%)
  starting transfers between devices  17.1 us (34%)
  Pallas kernels  5.48 us (11%)
  other arithmetic  3.11 us (6%)
  local copies, waits for them, and re-layouts  2.27 us (4%)
    ppermute x1, waiting for transfers between devices, shards(): lax.ppermute(p_band[-1], 'row', [(a, a + 1) for a in range(row_count - 1)])  17.9 us
    pallas_call x1, Pallas kernels, shards(): pl.pallas_call(band_kernel(tile_rows, band_local, half_band, grid_tiles,...  5.48 us
    ppermute x1, starting transfers between devices, shards(): lax.ppermute(p_band, 'col', [(b + 1, b) for b in range(col_count - 1)])  5.41 us
    ppermute x1, waiting for transfers between devices, shards(): lax.ppermute(down, 'col', [(b, b + 1) for b in range(col_count - 1)])  4.26 us
    ppermute x1, starting transfers between devices, shards(): lax.ppermute(p_band[0], 'row', [(a + 1, a) for a in range(row_count - 1)])  3.64 us
    ppermute x1, starting transfers between devices, shards(): received = lax.ppermute(sent, ('row', 'col'), pairs)  2.22 us
    unnamed x16, local copies, waits for them, and re-layouts  2.17 us
    ppermute x1, starting transfers between devices, shards(): lax.ppermute(p_band[-1], 'row', [(a, a + 1) for a in range(row_count - 1)])  1.92 us
  transfers between devices with their start and end apart: 7, of which 2 were waited for; matrix products, arithmetic and copies ran while one was open for 1% of the time, Pallas kernels for 0%

profile of v6, /device:TPU:126, one launch (start us, length us, event | category | flops | bytes accessed | tf_op | source)
XLA Modules:
  0.0 50.3 jit_solution(12356015483724104865)
XLA Ops:
  0.0 0.7 %copy-done.7 = s32[10]{0:T(128)S(1)} copy-done((s32[10]{0:T(128)S(1)}, s32[10]{0:T(128)}, u32[]{:S(2)}) %copy-start.7) | copy-done | bytes 64
  0.7 0.7 %fusion.11 = (pred[10,3]{0,1:T(4,128)(4,1)S(1)}, pred[10,3]{0,1:T(4,128)(4,1)S(1)}, pred[10,3]{0,1:T(4,128)(4,1)S(1)}) fusion(s32[10,3]{0,1:T(4,128)} %param.7, s32[10]{0:T(128)S(1)} %copy-done.7), kind=kLoop, calls=%fused_computation.24 | loop fusion | flops 210 | bytes 250 | tf_op jit(solution)/shard_map/and | solution.py:14
  1.4 1.7 %fusion.2 = (bf16[10,1,128,128]{3,2,1,0:T(8,128)(2,1)S(1)}, bf16[10,1,128,128]{3,2,1,0:T(8,128)(2,1)S(1)}, bf16[10,1,128,128]{3,2,1,0:T(8,128)(2,1)S(1)}) fusion(pred[10]{0:T(512)(128)(4,1)S(1)} %get-tuple-element.14, pred[10]{0:T(512)(128)(4,1)S(1)} %get-tuple-element.15, pred[10]{0:T(512)(128)(4,1)S(1)} %get-tuple-element.13, ...), kind=kLoop, calls=%fused_computation.12 | loop fusion | flops 3440640 | bytes 1966170 | tf_op jit(solution)/shard_map/convert_element_type | solution.py:18
  3.1 0.1 pad_maximum_fusion.jac_ref
  3.2 0.0 copy-start.1
  3.3 0.1 constant_dynamic-slice_fusion
  3.3 2.2 %collective-permute-start = (bf16[8,3,128,128]{3,2,1,0:T(8,128)(2,1)S(1)}, bf16[8,3,128,128]{3,2,1,0:T(8,128)(2,1)S(1)}, u32[]{:S(2)}, u32[]{:S(2)}) collective-permute-start(bf16[8,3,128,128]{3,2,1,0:T(8,128)(2,1)S(1)} %constant_dynamic-slice_fusion), channel_id=1, source_target_pairs={{0,8},{8,16},{16,24},{24,32},{32,40},{40,48},{48,56},{56,64},{64,7... | collective-permute-start | bytes 2359304 | tf_op jit(solution)/shard_map/ppermute | solution.py:151
  5.6 1.3 %collective-permute-start.1 = (bf16[10,2,128,128]{3,2,1,0:T(8,128)(2,1)S(1)}, bf16[10,2,128,128]{3,2,1,0:T(8,128)(2,1)}, u32[]{:S(2)}, u32[]{:S(2)}) collective-permute-start(bf16[10,2,128,128]{3,2,1,0:T(8,128)(2,1)S(1)} %copy-done.1), channel_id=1, source_target_pairs={{0,1},{1,2},{2,3},{3,4},{4,5},{5,6},{6,7},{8,9},{9,10},{10,11},{11... | collective-permute-start | bytes 1966088 | tf_op jit(solution)/shard_map/ppermute | solution.py:134
  6.9 5.4 %collective-permute-start.2 = (bf16[10,2,128,128]{3,2,1,0:T(8,128)(2,1)S(1)}, bf16[10,2,128,128]{3,2,1,0:T(8,128)(2,1)}, u32[]{:S(2)}, u32[]{:S(2)}) collective-permute-start(bf16[10,2,128,128]{3,2,1,0:T(8,128)(2,1)S(1)} %copy-done.1), channel_id=1, source_target_pairs={{1,0},{2,1},{3,2},{4,3},{5,4},{6,5},{7,6},{9,8},{10,9},{11,10},{12... | collective-permute-start | bytes 1966088 | tf_op jit(solution)/shard_map/ppermute | solution.py:135
  12.3 1.9 %collective-permute-start.3 = (bf16[2,128,128]{2,1,0:T(8,128)(2,1)S(1)}, bf16[2,128,128]{2,1,0:T(8,128)(2,1)S(1)}, u32[]{:S(2)}, u32[]{:S(2)}) collective-permute-start(bf16[2,128,128]{2,1,0:T(8,128)(2,1)S(1)} %get-tuple-element.9), channel_id=1, source_target_pairs={{0,8},{8,16},{16,24},{24,32},{32,40},{40,48},{48,56},{56,64},{64,7... | collective-permute-start | bytes 196616 | tf_op jit(solution)/shard_map/ppermute | solution.py:136
  14.2 3.6 %collective-permute-start.4 = (bf16[2,128,128]{2,1,0:T(8,128)(2,1)S(1)}, bf16[2,128,128]{2,1,0:T(8,128)(2,1)S(1)}, u32[]{:S(2)}, u32[]{:S(2)}) collective-permute-start(bf16[2,128,128]{2,1,0:T(8,128)(2,1)S(1)} %get-tuple-element.8), channel_id=1, source_target_pairs={{8,0},{16,8},{24,16},{32,24},{40,32},{48,40},{56,48},{64,56},{72,6... | collective-permute-start | bytes 196616 | tf_op jit(solution)/shard_map/ppermute | solution.py:137
  17.9 17.9 %collective-permute-done.3.up_ref = bf16[2,128,128]{2,1,0:T(8,128)(2,1)S(1)} collective-permute-done((bf16[2,128,128]{2,1,0:T(8,128)(2,1)S(1)}, bf16[2,128,128]{2,1,0:T(8,128)(2,1)S(1)}, u32[]{:S(2)}, u32[]{:S(2)}) %collective-permute-start.3) | collective-permute-done | bytes 65568 | tf_op jit(solution)/shard_map/ppermute | solution.py:136
  35.8 1.3 %collective-permute-start.5 = (bf16[2,128,128]{2,1,0:T(8,128)(2,1)S(1)}, bf16[2,128,128]{2,1,0:T(8,128)(2,1)S(1)}, u32[]{:S(2)}, u32[]{:S(2)}) collective-permute-start(bf16[2,128,128]{2,1,0:T(8,128)(2,1)S(1)} %collective-permute-done.3.up_ref), channel_id=1, source_target_pairs={{1,0},{2,1},{3,2},{4,3},{5,4},{6,5},{7,6},{9,8},{10,9},{11,10},{12... | collective-permute-start | bytes 196616 | tf_op jit(solution)/shard_map/ppermute | solution.py:154
  37.0 0.0 collective-permute-done.4.down_ref
  37.1 1.3 %collective-permute-start.6 = (bf16[2,128,128]{2,1,0:T(8,128)(2,1)S(1)}, bf16[2,128,128]{2,1,0:T(8,128)(2,1)S(1)}, u32[]{:S(2)}, u32[]{:S(2)}) collective-permute-start(bf16[2,128,128]{2,1,0:T(8,128)(2,1)S(1)} %collective-permute-done.4.down_ref), channel_id=1, source_target_pairs={{0,1},{1,2},{2,3},{3,4},{4,5},{5,6},{6,7},{8,9},{9,10},{10,11},{11... | collective-permute-start | bytes 196616 | tf_op jit(solution)/shard_map/ppermute | solution.py:153
  38.4 0.6 %pad_add_fusion.ids = s32[2]{0:T(128)} fusion(s32[1]{0:T(128)} %bitcast.1, s32[1]{0:T(128)} %bitcast), kind=kLoop, calls=%fused_computation.34 | loop fusion | flops 2 | bytes 16 | tf_op jit(solution)/shard_map/stack | solution.py:156
  39.0 0.0 collective-permute-done.5.up_right_ref
  39.0 4.3 %collective-permute-done.6.down_left_ref = bf16[2,128,128]{2,1,0:T(8,128)(2,1)S(1)} collective-permute-done((bf16[2,128,128]{2,1,0:T(8,128)(2,1)S(1)}, bf16[2,128,128]{2,1,0:T(8,128)(2,1)S(1)}, u32[]{:S(2)}, u32[]{:S(2)}) %collective-permute-start.6) | collective-permute-done | bytes 65568 | tf_op jit(solution)/shard_map/ppermute | solution.py:153
  43.2 0.0 collective-permute-done.1.left_ref
  43.2 0.0 collective-permute-done.2.right_ref
  43.2 0.0 collective-permute-done.recv_ref
  43.3 0.6 %copy-done.6 = bf16[2,128,128]{2,1,0:T(8,128)(2,1)} copy-done((bf16[2,128,128]{2,1,0:T(8,128)(2,1)}, bf16[2,128,128]{2,1,0:T(8,128)(2,1)S(1)}, u32[]{:S(2)}) %copy-start.6) | copy-done | bytes 65560
  43.8 0.9 %copy-done.2 = bf16[8,3,128,128]{3,2,1,0:T(8,128)(2,1)} copy-done((bf16[8,3,128,128]{3,2,1,0:T(8,128)(2,1)}, bf16[8,3,128,128]{3,2,1,0:T(8,128)(2,1)S(1)}, u32[]{:S(2)}) %copy-start.2) | copy-done | bytes 786456
  44.8 5.5 %shard_map.55 = bf16[10,2,128,128]{3,2,1,0:T(8,128)(2,1)} custom-call(s32[2]{0:T(128)} %pad_add_fusion.ids, f32[10,128]{1,0:T(8,128)} %q_ref.1, bf16[10,3,128,128]{3,2,1,0:T(8,128)(2,1)} %copy-done, bf16[8,3,128,128]{3,2,1,0:T(8,128)(2,1)} %copy-done.2, bf16[10,2,128,128]{3,2,1,0:T(8,128)(2,1)} %mid_ref.1, ...), custom_call_target="tpu_custom_call" | custom-call | tf_op jit(solution)/shard_map/pallas_call | solution.py:159
  (15 shorter events, 0.1 us)
Async XLA Ops:
  0.0 0.7 %copy-start.7 = (s32[10]{0:T(128)S(1)}, s32[10]{0:T(128)}, u32[]{:S(2)}) copy-start(s32[10]{0:T(128)} %param.8) | copy-start | bytes 124
  3.2 40.0 %copy-start = (bf16[10,3,128,128]{3,2,1,0:T(8,128)(2,1)}, bf16[10,3,128,128]{3,2,1,0:T(8,128)(2,1)S(1)}, u32[]{:S(2)}) copy-start(bf16[10,3,128,128]{3,2,1,0:T(8,128)(2,1)S(1)} %pad_maximum_fusion.jac_ref) | copy-start | bytes 2949124
  3.2 2.3 %copy-start.1 = (bf16[10,2,128,128]{3,2,1,0:T(8,128)(2,1)S(1)}, bf16[10,2,128,128]{3,2,1,0:T(8,128)(2,1)}, u32[]{:S(2)}) copy-start(bf16[10,2,128,128]{3,2,1,0:T(8,128)(2,1)} %mid_ref.1) | copy-start | bytes 1966084
  3.3 39.9 %collective-permute-start = (bf16[8,3,128,128]{3,2,1,0:T(8,128)(2,1)S(1)}, bf16[8,3,128,128]{3,2,1,0:T(8,128)(2,1)S(1)}, u32[]{:S(2)}, u32[]{:S(2)}) collective-permute-start(bf16[8,3,128,128]{3,2,1,0:T(8,128)(2,1)S(1)} %constant_dynamic-slice_fusion), channel_id=1, source_target_pairs={{0,8},{8,16},{16,24},{24,32},{32,40},{40,48},{48,56},{56,64},{64,7... | collective-permute-start | bytes 2359304 | tf_op jit(solution)/shard_map/ppermute | solution.py:151
  5.6 37.7 %collective-permute-start.1 = (bf16[10,2,128,128]{3,2,1,0:T(8,128)(2,1)S(1)}, bf16[10,2,128,128]{3,2,1,0:T(8,128)(2,1)}, u32[]{:S(2)}, u32[]{:S(2)}) collective-permute-start(bf16[10,2,128,128]{3,2,1,0:T(8,128)(2,1)S(1)} %copy-done.1), channel_id=1, source_target_pairs={{0,1},{1,2},{2,3},{3,4},{4,5},{5,6},{6,7},{8,9},{9,10},{10,11},{11... | collective-permute-start | bytes 1966088 | tf_op jit(solution)/shard_map/ppermute | solution.py:134
  6.9 36.4 %collective-permute-start.2 = (bf16[10,2,128,128]{3,2,1,0:T(8,128)(2,1)S(1)}, bf16[10,2,128,128]{3,2,1,0:T(8,128)(2,1)}, u32[]{:S(2)}, u32[]{:S(2)}) collective-permute-start(bf16[10,2,128,128]{3,2,1,0:T(8,128)(2,1)S(1)} %copy-done.1), channel_id=1, source_target_pairs={{1,0},{2,1},{3,2},{4,3},{5,4},{6,5},{7,6},{9,8},{10,9},{11,10},{12... | collective-permute-start | bytes 1966088 | tf_op jit(solution)/shard_map/ppermute | solution.py:135
  12.3 23.5 %collective-permute-start.3 = (bf16[2,128,128]{2,1,0:T(8,128)(2,1)S(1)}, bf16[2,128,128]{2,1,0:T(8,128)(2,1)S(1)}, u32[]{:S(2)}, u32[]{:S(2)}) collective-permute-start(bf16[2,128,128]{2,1,0:T(8,128)(2,1)S(1)} %get-tuple-element.9), channel_id=1, source_target_pairs={{0,8},{8,16},{16,24},{24,32},{32,40},{40,48},{48,56},{56,64},{64,7... | collective-permute-start | bytes 196616 | tf_op jit(solution)/shard_map/ppermute | solution.py:136
  14.2 22.8 %collective-permute-start.4 = (bf16[2,128,128]{2,1,0:T(8,128)(2,1)S(1)}, bf16[2,128,128]{2,1,0:T(8,128)(2,1)S(1)}, u32[]{:S(2)}, u32[]{:S(2)}) collective-permute-start(bf16[2,128,128]{2,1,0:T(8,128)(2,1)S(1)} %get-tuple-element.8), channel_id=1, source_target_pairs={{8,0},{16,8},{24,16},{32,24},{40,32},{48,40},{56,48},{64,56},{72,6... | collective-permute-start | bytes 196616 | tf_op jit(solution)/shard_map/ppermute | solution.py:137
  35.8 7.5 %copy-start.3 = (bf16[2,128,128]{2,1,0:T(8,128)(2,1)}, bf16[2,128,128]{2,1,0:T(8,128)(2,1)S(1)}, u32[]{:S(2)}) copy-start(bf16[2,128,128]{2,1,0:T(8,128)(2,1)S(1)} %collective-permute-done.3.up_ref) | copy-start | bytes 196612
  35.8 3.2 %collective-permute-start.5 = (bf16[2,128,128]{2,1,0:T(8,128)(2,1)S(1)}, bf16[2,128,128]{2,1,0:T(8,128)(2,1)S(1)}, u32[]{:S(2)}, u32[]{:S(2)}) collective-permute-start(bf16[2,128,128]{2,1,0:T(8,128)(2,1)S(1)} %collective-permute-done.3.up_ref), channel_id=1, source_target_pairs={{1,0},{2,1},{3,2},{4,3},{5,4},{6,5},{7,6},{9,8},{10,9},{11,10},{12... | collective-permute-start | bytes 196616 | tf_op jit(solution)/shard_map/ppermute | solution.py:154
  37.1 6.2 %copy-start.4 = (bf16[2,128,128]{2,1,0:T(8,128)(2,1)}, bf16[2,128,128]{2,1,0:T(8,128)(2,1)S(1)}, u32[]{:S(2)}) copy-start(bf16[2,128,128]{2,1,0:T(8,128)(2,1)S(1)} %collective-permute-done.4.down_ref) | copy-start | bytes 196612
  37.1 6.2 %collective-permute-start.6 = (bf16[2,128,128]{2,1,0:T(8,128)(2,1)S(1)}, bf16[2,128,128]{2,1,0:T(8,128)(2,1)S(1)}, u32[]{:S(2)}, u32[]{:S(2)}) collective-permute-start(bf16[2,128,128]{2,1,0:T(8,128)(2,1)S(1)} %collective-permute-done.4.down_ref), channel_id=1, source_target_pairs={{0,1},{1,2},{2,3},{3,4},{4,5},{5,6},{6,7},{8,9},{9,10},{10,11},{11... | collective-permute-start | bytes 196616 | tf_op jit(solution)/shard_map/ppermute | solution.py:153
  39.0 4.3 %copy-start.5 = (bf16[2,128,128]{2,1,0:T(8,128)(2,1)}, bf16[2,128,128]{2,1,0:T(8,128)(2,1)S(1)}, u32[]{:S(2)}) copy-start(bf16[2,128,128]{2,1,0:T(8,128)(2,1)S(1)} %collective-permute-done.5.up_right_ref) | copy-start | bytes 196612
  43.2 0.6 %copy-start.6 = (bf16[2,128,128]{2,1,0:T(8,128)(2,1)}, bf16[2,128,128]{2,1,0:T(8,128)(2,1)S(1)}, u32[]{:S(2)}) copy-start(bf16[2,128,128]{2,1,0:T(8,128)(2,1)S(1)} %collective-permute-done.6.down_left_ref) | copy-start | bytes 196612
  43.8 0.9 %copy-start.2 = (bf16[8,3,128,128]{3,2,1,0:T(8,128)(2,1)}, bf16[8,3,128,128]{3,2,1,0:T(8,128)(2,1)S(1)}, u32[]{:S(2)}) copy-start(bf16[8,3,128,128]{3,2,1,0:T(8,128)(2,1)S(1)} %collective-permute-done.recv_ref) | copy-start | bytes 2359300

commit v7 on v6

--- a/solution.py
+++ b/solution.py
@@ -133,22 +133,39 @@
 
     left = lax.ppermute(p_band, "col", [(b, b + 1) for b in range(col_count - 1)])
     right = lax.ppermute(p_band, "col", [(b + 1, b) for b in range(col_count - 1)])
-    up = lax.ppermute(p_band[-1], "row", [(a, a + 1) for a in range(row_count - 1)])
-    down = lax.ppermute(p_band[0], "row", [(a + 1, a) for a in range(row_count - 1)])
-
-    jacobian = assemble(blocks, block_offsets, block_live)
+    meta = jnp.zeros((tile_size, tile_size), p_band.dtype)
+    meta = meta.at[0, : tile_rows * 3].set(block_offsets.reshape(-1).astype(p_band.dtype))
+    meta = meta.at[1, :tile_rows].set(block_live.astype(p_band.dtype))
+    up_all = lax.ppermute(
+        jnp.concatenate([p_band[-1], meta[None]], axis=0), "row", [(a, a + 1) for a in range(row_count - 1)]
+    )
+    down_all = lax.ppermute(
+        jnp.concatenate([p_band[0], meta[None]], axis=0), "row", [(a + 1, a) for a in range(row_count - 1)]
+    )
+    up = up_all[:band_local]
+    down = down_all[:band_local]
 
     sent_rows = half_band
     lower_half = col_id < col_count // 2
     send_start = jnp.where(lower_half, tile_rows - sent_rows, 0)
-    sent = lax.dynamic_slice_in_dim(jacobian, send_start, sent_rows, 0)
+    sent = lax.dynamic_slice_in_dim(blocks, send_start, sent_rows, 0)
     pairs = []
     for b in range(col_count):
         if b * band_local - half_band < 0:
             pairs += [(flat(a, b), flat(a + 1, b)) for a in range(row_count - 1)]
         else:
             pairs += [(flat(a, b), flat(a - 1, b)) for a in range(1, row_count)]
-    received = lax.ppermute(sent, ("row", "col"), pairs)
+    received_blocks = lax.ppermute(sent, ("row", "col"), pairs)
+
+    jacobian = assemble(blocks, block_offsets, block_live)
+    received_meta = jnp.where(lower_half, up_all[band_local], down_all[band_local]).astype(jnp.float32)
+    received_offsets = jnp.round(received_meta[0, : tile_rows * 3]).astype(jnp.int32).reshape(tile_rows, 3)
+    received_live = jnp.round(received_meta[1, :tile_rows]).astype(jnp.int32)
+    received = assemble(
+        received_blocks,
+        lax.dynamic_slice_in_dim(received_offsets, send_start, sent_rows, 0),
+        lax.dynamic_slice_in_dim(received_live, send_start, sent_rows, 0),
+    )
 
     down_left = lax.ppermute(down, "col", [(b, b + 1) for b in range(col_count - 1)])
     up_right = lax.ppermute(up, "col", [(b + 1, b) for b in range(col_count - 1)])

time: 50.6 us -> 50.9 us (level)
  the two profiles are of different devices: /device:TPU:126 before, /device:TPU:158 now
where the time goes in v7:
time: 50.9 us; the launch traced here: 50.5 us
  waiting for transfers between devices  18.9 us (37%)
  starting transfers between devices  16.9 us (33%)
  Pallas kernels  5.48 us (11%)
  other arithmetic  4.49 us (9%)
  local copies, waits for them, and re-layouts  4.48 us (9%)
    ppermute x1, waiting for transfers between devices, shards(): lax.ppermute(jnp.concatenate([p_band[-1], meta[None]], axis=0), 'row', [(...  16.1 us
    pallas_call x1, Pallas kernels, shards(): pl.pallas_call(band_kernel(tile_rows, band_local, half_band, grid_tiles,...  5.48 us
    ppermute x1, starting transfers between devices, shards(): lax.ppermute(p_band, 'col', [(b + 1, b) for b in range(col_count - 1)])  5.43 us
    ppermute x1, starting transfers between devices, shards(): lax.ppermute(jnp.concatenate([p_band[0], meta[None]], axis=0), 'row', [(a...  3.64 us
    ppermute x1, waiting for transfers between devices, shards(): lax.ppermute(down, 'col', [(b, b + 1) for b in range(col_count - 1)])  2.77 us
    another operation x2, other arithmetic, assemble(): return jnp.stack(pieces, axis=1)  2.05 us
    ppermute x1, starting transfers between devices, shards(): received_blocks = lax.ppermute(sent, ('row', 'col'), pairs)  1.92 us
    ppermute x1, starting transfers between devices, shards(): lax.ppermute(jnp.concatenate([p_band[-1], meta[None]], axis=0), 'row', [(...  1.91 us
  transfers between devices with their start and end apart: 7, of which 2 were waited for; matrix products, arithmetic and copies ran while one was open for 15% of the time, Pallas kernels for 0%

profile of v7, /device:TPU:158, one launch (start us, length us, event | category | flops | bytes accessed | tf_op | source)
XLA Modules:
  0.0 50.5 jit_solution(15746708130351987208)
XLA Ops:
  0.0 1.4 %collective-permute-start.3 = (bf16[10,2,128,128]{3,2,1,0:T(8,128)(2,1)}, bf16[10,2,128,128]{3,2,1,0:T(8,128)(2,1)S(1)}, u32[]{:S(2)}, u32[]{:S(2)}) collective-permute-start(bf16[10,2,128,128]{3,2,1,0:T(8,128)(2,1)} %mid_ref.1), channel_id=1, source_target_pairs={{0,1},{1,2},{2,3},{3,4},{4,5},{5,6},{6,7},{8,9},{9,10},{10,11},{11... | collective-permute-start | bytes 1966088 | tf_op jit(solution)/shard_map/ppermute | solution.py:134
  1.4 5.4 %collective-permute-start.4 = (bf16[10,2,128,128]{3,2,1,0:T(8,128)(2,1)}, bf16[10,2,128,128]{3,2,1,0:T(8,128)(2,1)}, u32[]{:S(2)}, u32[]{:S(2)}) collective-permute-start(bf16[10,2,128,128]{3,2,1,0:T(8,128)(2,1)} %mid_ref.1), channel_id=1, source_target_pairs={{1,0},{2,1},{3,2},{4,3},{5,4},{6,5},{7,6},{9,8},{10,9},{11,10},{12... | collective-permute-start | bytes 1966088 | tf_op jit(solution)/shard_map/ppermute | solution.py:135
  6.8 0.9 %slice_bitcast_fusion.1 = (bf16[2,128,128]{2,1,0:T(8,128)(2,1)S(1)}, bf16[2,128,128]{2,1,0:T(8,128)(2,1)S(1)}) fusion(bf16[10,2,128,128]{3,2,1,0:T(8,128)(2,1)} %mid_ref.1), kind=kLoop, calls=%fused_computation.41 | loop fusion | bytes 262144 | tf_op jit(solution)/shard_map/squeeze | solution.py:140
  7.8 0.1 copy.7
  8.0 0.6 %copy-done.7 = s32[10]{0:T(128)S(1)} copy-done((s32[10]{0:T(128)S(1)}, s32[10]{0:T(128)}, u32[]{:S(2)}) %copy-start.7) | copy-done | bytes 64
  8.7 0.7 %pad_maximum_fusion.3 = (bf16[3,128,128]{2,1,0:T(8,128)(2,1)}, bf16[3,128,128]{2,1,0:T(8,128)(2,1)S(1)}) fusion(bf16[1,128,128]{2,1,0:T(8,128)(2,1)S(1)} %scatter.9, bf16[2,128,128]{2,1,0:T(8,128)(2,1)S(1)} %get-tuple-element.44, bf16[2,128,128]{2,1,0:T(8,128)(2,1)S(1)} %get-tuple-element.45), kind=kLoop, calls=%fused_computation.39 | loop fusion | flops 98304 | bytes 360448 | tf_op jit(solution)/shard_map/concatenate | solution.py:140
  9.4 1.9 %collective-permute-start = (bf16[3,128,128]{2,1,0:T(8,128)(2,1)}, bf16[3,128,128]{2,1,0:T(8,128)(2,1)S(1)}, u32[]{:S(2)}, u32[]{:S(2)}) collective-permute-start(bf16[3,128,128]{2,1,0:T(8,128)(2,1)} %get-tuple-element.46), channel_id=1, source_target_pairs={{0,8},{8,16},{16,24},{24,32},{32,40},{40,48},{48,56},{56,64},{64,7... | collective-permute-start | bytes 294920 | tf_op jit(solution)/shard_map/ppermute | solution.py:139
  11.3 3.6 %collective-permute-start.1 = (bf16[3,128,128]{2,1,0:T(8,128)(2,1)S(1)}, bf16[3,128,128]{2,1,0:T(8,128)(2,1)S(1)}, u32[]{:S(2)}, u32[]{:S(2)}) collective-permute-start(bf16[3,128,128]{2,1,0:T(8,128)(2,1)S(1)} %get-tuple-element.47), channel_id=1, source_target_pairs={{8,0},{16,8},{24,16},{32,24},{40,32},{48,40},{56,48},{64,56},{72,6... | collective-permute-start | bytes 294920 | tf_op jit(solution)/shard_map/ppermute | solution.py:142
  15.0 1.2 %constant_dynamic-slice_fusion = bf16[8,3,128,128]{3,2,1,0:T(8,128)(2,1)S(1)} fusion(bf16[10,3,128,128]{3,2,1,0:T(8,128)(2,1)} %param.10, s32[]{:T(128)S(6)} %select_n.101), kind=kLoop, calls=%fused_computation.72 | loop fusion | bytes 1572868 | tf_op jit(solution)/shard_map/dynamic_slice | solution.py:151
  16.1 1.9 %collective-permute-start.2 = (bf16[8,3,128,128]{3,2,1,0:T(8,128)(2,1)S(1)}, bf16[8,3,128,128]{3,2,1,0:T(8,128)(2,1)S(1)}, u32[]{:S(2)}, u32[]{:S(2)}) collective-permute-start(bf16[8,3,128,128]{3,2,1,0:T(8,128)(2,1)S(1)} %constant_dynamic-slice_fusion), channel_id=1, source_target_pairs={{0,8},{8,16},{16,24},{24,32},{32,40},{40,48},{48,56},{56,64},{64,7... | collective-permute-start | bytes 2359304 | tf_op jit(solution)/shard_map/ppermute | solution.py:158
  18.1 0.5 %fusion.2 = (bf16[10,1,128,128]{3,2,1,0:T(8,128)(2,1)S(1)}, bf16[10,1,128,128]{3,2,1,0:T(8,128)(2,1)S(1)}, bf16[10,1,128,128]{3,2,1,0:T(8,128)(2,1)S(1)}) fusion(pred[10]{0:T(512)(128)(4,1)S(1)} %get-tuple-element.55, pred[10]{0:T(512)(128)(4,1)S(1)} %get-tuple-element.56, pred[10]{0:T(512)(128)(4,1)S(1)} %get-tuple-element.54, ...), kind=kLoop, calls=%fused_computation.22 | loop fusion | flops 3440640 | bytes 1966170 | tf_op jit(solution)/shard_map/convert_element_type | solution.py:18
  18.7 1.1 %pad_maximum_fusion.jac_ref = bf16[10,3,128,128]{3,2,1,0:T(8,128)(2,1)} fusion(bf16[10,1,128,128]{3,2,1,0:T(8,128)(2,1)S(1)} %get-tuple-element.39, bf16[10,1,128,128]{3,2,1,0:T(8,128)(2,1)S(1)} %get-tuple-element.40, bf16[10,1,128,128]{3,2,1,0:T(8,128)(2,1)S(1)} %get-tuple-element.38), kind=kLoop, calls=%fused_computation | loop fusion | flops 983040 | bytes 1966080 | tf_op jit(solution)/shard_map/stack | solution.py:19
  19.8 0.6 %pad_add_fusion.ids = s32[2]{0:T(128)} fusion(s32[1]{0:T(128)} %bitcast.1, s32[1]{0:T(128)} %bitcast), kind=kLoop, calls=%fused_computation.80 | loop fusion | flops 2 | bytes 16 | tf_op jit(solution)/shard_map/stack | solution.py:173
  20.4 16.1 %collective-permute-done = bf16[3,128,128]{2,1,0:T(8,128)(2,1)S(1)} collective-permute-done((bf16[3,128,128]{2,1,0:T(8,128)(2,1)}, bf16[3,128,128]{2,1,0:T(8,128)(2,1)S(1)}, u32[]{:S(2)}, u32[]{:S(2)}) %collective-permute-start) | collective-permute-done | bytes 98336 | tf_op jit(solution)/shard_map/ppermute | solution.py:139
  36.7 1.3 %collective-permute-start.5 = (bf16[2,128,128]{2,1,0:T(8,128)(2,1)S(1)}, bf16[2,128,128]{2,1,0:T(8,128)(2,1)S(1)}, u32[]{:S(2)}, u32[]{:S(2)}) collective-permute-start(bf16[2,128,128]{2,1,0:T(8,128)(2,1)S(1)} %slice.182.up_ref), channel_id=1, source_target_pairs={{1,0},{2,1},{3,2},{4,3},{5,4},{6,5},{7,6},{9,8},{10,9},{11,10},{12... | collective-permute-start | bytes 196616 | tf_op jit(solution)/shard_map/ppermute | solution.py:171
  38.0 1.3 %collective-permute-start.6 = (bf16[2,128,128]{2,1,0:T(8,128)(2,1)S(1)}, bf16[2,128,128]{2,1,0:T(8,128)(2,1)S(1)}, u32[]{:S(2)}, u32[]{:S(2)}) collective-permute-start(bf16[2,128,128]{2,1,0:T(8,128)(2,1)S(1)} %slice.183.down_ref), channel_id=1, source_target_pairs={{0,1},{1,2},{2,3},{3,4},{4,5},{5,6},{6,7},{8,9},{9,10},{10,11},{11... | collective-permute-start | bytes 196616 | tf_op jit(solution)/shard_map/ppermute | solution.py:170
  39.5 0.2 slice_reduce_fusion.8
  39.7 0.3 slice_reduce_fusion.2
  39.9 0.5 fusion.11
  40.4 1.0 %pad_maximum_fusion.1.recv_ref = bf16[8,3,128,128]{3,2,1,0:T(8,128)(2,1)} fusion(bf16[8,1,128,128]{3,2,1,0:T(8,128)(2,1)S(1)} %get-tuple-element.42, bf16[8,1,128,128]{3,2,1,0:T(8,128)(2,1)S(1)} %get-tuple-element.43, bf16[8,1,128,128]{3,2,1,0:T(8,128)(2,1)S(1)} %get-tuple-element.41), kind=kLoop, calls=%fused_computation.10 | loop fusion | flops 786432 | bytes 1572864 | tf_op jit(solution)/shard_map/stack | solution.py:19
  41.4 2.8 %collective-permute-done.6.down_left_ref = bf16[2,128,128]{2,1,0:T(8,128)(2,1)S(1)} collective-permute-done((bf16[2,128,128]{2,1,0:T(8,128)(2,1)S(1)}, bf16[2,128,128]{2,1,0:T(8,128)(2,1)S(1)}, u32[]{:S(2)}, u32[]{:S(2)}) %collective-permute-start.6) | collective-permute-done | bytes 65568 | tf_op jit(solution)/shard_map/ppermute | solution.py:170
  44.2 0.6 %copy-done.5 = bf16[2,128,128]{2,1,0:T(8,128)(2,1)} copy-done((bf16[2,128,128]{2,1,0:T(8,128)(2,1)}, bf16[2,128,128]{2,1,0:T(8,128)(2,1)S(1)}, u32[]{:S(2)}) %copy-start.5) | copy-done | bytes 65560
  44.8 0.2 copy-done.1
  45.0 5.5 %shard_map.55 = bf16[10,2,128,128]{3,2,1,0:T(8,128)(2,1)} custom-call(s32[2]{0:T(128)} %pad_add_fusion.ids, f32[10,128]{1,0:T(8,128)} %q_ref.1, bf16[10,3,128,128]{3,2,1,0:T(8,128)(2,1)} %pad_maximum_fusion.jac_ref, bf16[8,3,128,128]{3,2,1,0:T(8,128)(2,1)} %pad_maximum_fusion.1.recv_ref, bf16[10,2,128,128]{3,2,1,0:T(8,128)(2,1)} %mid_ref.1, ...), custom_call_target="tpu_custom_call" | custom-call | tf_op jit(solution)/shard_map/pallas_call | solution.py:176
  (34 shorter events, 0.5 us)
Async XLA Ops:
  0.0 7.7 %copy-start.6 = (s32[10,3]{0,1:T(4,128)S(1)}, s32[10,3]{0,1:T(4,128)}, u32[]{:S(2)}) copy-start(s32[10,3]{0,1:T(4,128)} %param.11) | copy-start | bytes 364
  0.0 44.2 %collective-permute-start.3 = (bf16[10,2,128,128]{3,2,1,0:T(8,128)(2,1)}, bf16[10,2,128,128]{3,2,1,0:T(8,128)(2,1)S(1)}, u32[]{:S(2)}, u32[]{:S(2)}) collective-permute-start(bf16[10,2,128,128]{3,2,1,0:T(8,128)(2,1)} %mid_ref.1), channel_id=1, source_target_pairs={{0,1},{1,2},{2,3},{3,4},{4,5},{5,6},{6,7},{8,9},{9,10},{10,11},{11... | collective-permute-start | bytes 1966088 | tf_op jit(solution)/shard_map/ppermute | solution.py:134
  1.4 42.8 %collective-permute-start.4 = (bf16[10,2,128,128]{3,2,1,0:T(8,128)(2,1)}, bf16[10,2,128,128]{3,2,1,0:T(8,128)(2,1)}, u32[]{:S(2)}, u32[]{:S(2)}) collective-permute-start(bf16[10,2,128,128]{3,2,1,0:T(8,128)(2,1)} %mid_ref.1), channel_id=1, source_target_pairs={{1,0},{2,1},{3,2},{4,3},{5,4},{6,5},{7,6},{9,8},{10,9},{11,10},{12... | collective-permute-start | bytes 1966088 | tf_op jit(solution)/shard_map/ppermute | solution.py:135
  7.9 0.7 %copy-start.7 = (s32[10]{0:T(128)S(1)}, s32[10]{0:T(128)}, u32[]{:S(2)}) copy-start(s32[10]{0:T(128)} %param.12) | copy-start | bytes 124
  8.7 9.4 %copy-start = (bf16[10,3,128,128]{3,2,1,0:T(8,128)(2,1)S(1)}, bf16[10,3,128,128]{3,2,1,0:T(8,128)(2,1)}, u32[]{:S(2)}) copy-start(bf16[10,3,128,128]{3,2,1,0:T(8,128)(2,1)} %param.10) | copy-start | bytes 2949124
  9.4 27.2 %collective-permute-start = (bf16[3,128,128]{2,1,0:T(8,128)(2,1)}, bf16[3,128,128]{2,1,0:T(8,128)(2,1)S(1)}, u32[]{:S(2)}, u32[]{:S(2)}) collective-permute-start(bf16[3,128,128]{2,1,0:T(8,128)(2,1)} %get-tuple-element.46), channel_id=1, source_target_pairs={{0,8},{8,16},{16,24},{24,32},{32,40},{40,48},{48,56},{56,64},{64,7... | collective-permute-start | bytes 294920 | tf_op jit(solution)/shard_map/ppermute | solution.py:139
  11.3 25.3 %collective-permute-start.1 = (bf16[3,128,128]{2,1,0:T(8,128)(2,1)S(1)}, bf16[3,128,128]{2,1,0:T(8,128)(2,1)S(1)}, u32[]{:S(2)}, u32[]{:S(2)}) collective-permute-start(bf16[3,128,128]{2,1,0:T(8,128)(2,1)S(1)} %get-tuple-element.47), channel_id=1, source_target_pairs={{8,0},{16,8},{24,16},{32,24},{40,32},{48,40},{56,48},{64,56},{72,6... | collective-permute-start | bytes 294920 | tf_op jit(solution)/shard_map/ppermute | solution.py:142
  16.1 23.8 %collective-permute-start.2 = (bf16[8,3,128,128]{3,2,1,0:T(8,128)(2,1)S(1)}, bf16[8,3,128,128]{3,2,1,0:T(8,128)(2,1)S(1)}, u32[]{:S(2)}, u32[]{:S(2)}) collective-permute-start(bf16[8,3,128,128]{3,2,1,0:T(8,128)(2,1)S(1)} %constant_dynamic-slice_fusion), channel_id=1, source_target_pairs={{0,8},{8,16},{16,24},{24,32},{32,40},{40,48},{48,56},{56,64},{64,7... | collective-permute-start | bytes 2359304 | tf_op jit(solution)/shard_map/ppermute | solution.py:158
  36.7 1.3 %copy-start.2 = (bf16[2,128,128]{2,1,0:T(8,128)(2,1)}, bf16[2,128,128]{2,1,0:T(8,128)(2,1)S(1)}, u32[]{:S(2)}) copy-start(bf16[2,128,128]{2,1,0:T(8,128)(2,1)S(1)} %slice.182.up_ref) | copy-start | bytes 196612
  36.7 4.7 %collective-permute-start.5 = (bf16[2,128,128]{2,1,0:T(8,128)(2,1)S(1)}, bf16[2,128,128]{2,1,0:T(8,128)(2,1)S(1)}, u32[]{:S(2)}, u32[]{:S(2)}) collective-permute-start(bf16[2,128,128]{2,1,0:T(8,128)(2,1)S(1)} %slice.182.up_ref), channel_id=1, source_target_pairs={{1,0},{2,1},{3,2},{4,3},{5,4},{6,5},{7,6},{9,8},{10,9},{11,10},{12... | collective-permute-start | bytes 196616 | tf_op jit(solution)/shard_map/ppermute | solution.py:171
  38.0 2.4 %copy-start.3 = (bf16[2,128,128]{2,1,0:T(8,128)(2,1)}, bf16[2,128,128]{2,1,0:T(8,128)(2,1)S(1)}, u32[]{:S(2)}) copy-start(bf16[2,128,128]{2,1,0:T(8,128)(2,1)S(1)} %slice.183.down_ref) | copy-start | bytes 196612
  38.0 6.2 %collective-permute-start.6 = (bf16[2,128,128]{2,1,0:T(8,128)(2,1)S(1)}, bf16[2,128,128]{2,1,0:T(8,128)(2,1)S(1)}, u32[]{:S(2)}, u32[]{:S(2)}) collective-permute-start(bf16[2,128,128]{2,1,0:T(8,128)(2,1)S(1)} %slice.183.down_ref), channel_id=1, source_target_pairs={{0,1},{1,2},{2,3},{3,4},{4,5},{5,6},{6,7},{8,9},{9,10},{10,11},{11... | collective-permute-start | bytes 196616 | tf_op jit(solution)/shard_map/ppermute | solution.py:170
  41.4 2.8 %copy-start.4 = (bf16[2,128,128]{2,1,0:T(8,128)(2,1)}, bf16[2,128,128]{2,1,0:T(8,128)(2,1)S(1)}, u32[]{:S(2)}) copy-start(bf16[2,128,128]{2,1,0:T(8,128)(2,1)S(1)} %collective-permute-done.5.up_right_ref) | copy-start | bytes 196612
  44.2 0.6 %copy-start.5 = (bf16[2,128,128]{2,1,0:T(8,128)(2,1)}, bf16[2,128,128]{2,1,0:T(8,128)(2,1)S(1)}, u32[]{:S(2)}) copy-start(bf16[2,128,128]{2,1,0:T(8,128)(2,1)S(1)} %collective-permute-done.6.down_left_ref) | copy-start | bytes 196612
  44.2 0.9 %copy-start.1 = (bf16[10,2,128,128]{3,2,1,0:T(8,128)(2,1)}, bf16[10,2,128,128]{3,2,1,0:T(8,128)(2,1)S(1)}, u32[]{:S(2)}) copy-start(bf16[10,2,128,128]{3,2,1,0:T(8,128)(2,1)S(1)} %collective-permute-done.3.left_ref) | copy-start | bytes 1966084

commit v8 on v7

--- a/solution.py
+++ b/solution.py
@@ -155,6 +155,7 @@
             pairs += [(flat(a, b), flat(a + 1, b)) for a in range(row_count - 1)]
         else:
             pairs += [(flat(a, b), flat(a - 1, b)) for a in range(1, row_count)]
+    sent, _ = lax.optimization_barrier((sent, (up_all, down_all)))
     received_blocks = lax.ppermute(sent, ("row", "col"), pairs)
 
     jacobian = assemble(blocks, block_offsets, block_live)

time: 50.9 us -> 58.8 us (1.16)
  the two profiles are of different devices: /device:TPU:158 before, /device:TPU:151 now
where the time goes in v8:
time: 58.8 us; the launch traced here: 58.4 us
  waiting for transfers between devices  27.4 us (47%)
  starting transfers between devices  16 us (27%)
  Pallas kernels  5.48 us (9%)
  local copies, waits for them, and re-layouts  5.35 us (9%)
  other arithmetic  3.86 us (7%)
    ppermute x1, waiting for transfers between devices, shards(): lax.ppermute(jnp.concatenate([p_band[-1], meta[None]], axis=0), 'row', [(...  18.6 us
    ppermute x1, waiting for transfers between devices, shards(): received_blocks = lax.ppermute(sent, ('row', 'col'), pairs)  8.74 us
    pallas_call x1, Pallas kernels, shards(): pl.pallas_call(band_kernel(tile_rows, band_local, half_band, grid_tiles,...  5.48 us
    ppermute x1, starting transfers between devices, shards(): lax.ppermute(jnp.concatenate([p_band[-1], meta[None]], axis=0), 'row', [(...  4.16 us
    ppermute x1, starting transfers between devices, shards(): lax.ppermute(p_band, 'col', [(b + 1, b) for b in range(col_count - 1)])  4.03 us
    unnamed x18, local copies, waits for them, and re-layouts  2.37 us
    another operation x2, other arithmetic, assemble(): return jnp.stack(pieces, axis=1)  2.05 us
    ppermute x1, starting transfers between devices, shards(): lax.ppermute(jnp.concatenate([p_band[0], meta[None]], axis=0), 'row', [(a...  1.92 us
  transfers between devices with their start and end apart: 7, of which 2 were waited for; matrix products, arithmetic and copies ran while one was open for 12% of the time, Pallas kernels for 0%

profile of v8, /device:TPU:151, one launch (start us, length us, event | category | flops | bytes accessed | tf_op | source)
XLA Modules:
  0.0 58.4 jit_solution(10707214343845464998)
XLA Ops:
  0.0 1.4 %collective-permute-start.3 = (bf16[10,2,128,128]{3,2,1,0:T(8,128)(2,1)}, bf16[10,2,128,128]{3,2,1,0:T(8,128)(2,1)S(1)}, u32[]{:S(2)}, u32[]{:S(2)}) collective-permute-start(bf16[10,2,128,128]{3,2,1,0:T(8,128)(2,1)} %mid_ref.1), channel_id=1, source_target_pairs={{0,1},{1,2},{2,3},{3,4},{4,5},{5,6},{6,7},{8,9},{9,10},{10,11},{11... | collective-permute-start | bytes 1966088 | tf_op jit(solution)/shard_map/ppermute | solution.py:134
  1.4 4.0 %collective-permute-start.4 = (bf16[10,2,128,128]{3,2,1,0:T(8,128)(2,1)}, bf16[10,2,128,128]{3,2,1,0:T(8,128)(2,1)S(1)}, u32[]{:S(2)}, u32[]{:S(2)}) collective-permute-start(bf16[10,2,128,128]{3,2,1,0:T(8,128)(2,1)} %mid_ref.1), channel_id=1, source_target_pairs={{1,0},{2,1},{3,2},{4,3},{5,4},{6,5},{7,6},{9,8},{10,9},{11,10},{12... | collective-permute-start | bytes 1966088 | tf_op jit(solution)/shard_map/ppermute | solution.py:135
  5.5 0.9 %slice_bitcast_fusion.1 = (bf16[2,128,128]{2,1,0:T(8,128)(2,1)S(1)}, bf16[2,128,128]{2,1,0:T(8,128)(2,1)S(1)}) fusion(bf16[10,2,128,128]{3,2,1,0:T(8,128)(2,1)} %mid_ref.1), kind=kLoop, calls=%fused_computation.41 | loop fusion | bytes 262144 | tf_op jit(solution)/shard_map/squeeze | solution.py:140
  6.4 0.1 copy.7
  6.6 0.6 %copy-done.8 = s32[10]{0:T(128)S(1)} copy-done((s32[10]{0:T(128)S(1)}, s32[10]{0:T(128)}, u32[]{:S(2)}) %copy-start.8) | copy-done | bytes 64
  7.4 4.2 %collective-permute-start = (bf16[3,128,128]{2,1,0:T(8,128)(2,1)S(1)}, bf16[3,128,128]{2,1,0:T(8,128)(2,1)S(1)}, u32[]{:S(2)}, u32[]{:S(2)}) collective-permute-start(bf16[3,128,128]{2,1,0:T(8,128)(2,1)S(1)} %get-tuple-element.48), channel_id=1, source_target_pairs={{0,8},{8,16},{16,24},{24,32},{32,40},{40,48},{48,56},{56,64},{64,7... | collective-permute-start | bytes 294920 | tf_op jit(solution)/shard_map/ppermute | solution.py:139
  11.5 1.9 %collective-permute-start.1 = (bf16[3,128,128]{2,1,0:T(8,128)(2,1)S(1)}, bf16[3,128,128]{2,1,0:T(8,128)(2,1)S(1)}, u32[]{:S(2)}, u32[]{:S(2)}) collective-permute-start(bf16[3,128,128]{2,1,0:T(8,128)(2,1)S(1)} %get-tuple-element.49), channel_id=1, source_target_pairs={{8,0},{16,8},{24,16},{32,24},{40,32},{48,40},{56,48},{64,56},{72,6... | collective-permute-start | bytes 294920 | tf_op jit(solution)/shard_map/ppermute | solution.py:142
  13.5 1.2 %constant_dynamic-slice_fusion = bf16[8,3,128,128]{3,2,1,0:T(8,128)(2,1)S(1)} fusion(bf16[10,3,128,128]{3,2,1,0:T(8,128)(2,1)} %param.10, s32[]{:T(128)S(6)} %select_n.101), kind=kLoop, calls=%fused_computation.72 | loop fusion | bytes 1572868 | tf_op jit(solution)/shard_map/dynamic_slice | solution.py:151
  14.7 0.5 fusion.2
  15.3 1.1 %pad_maximum_fusion.jac_ref = bf16[10,3,128,128]{3,2,1,0:T(8,128)(2,1)} fusion(bf16[10,1,128,128]{3,2,1,0:T(8,128)(2,1)S(1)} %get-tuple-element.41, bf16[10,1,128,128]{3,2,1,0:T(8,128)(2,1)S(1)} %get-tuple-element.42, bf16[10,1,128,128]{3,2,1,0:T(8,128)(2,1)S(1)} %get-tuple-element.40), kind=kLoop, calls=%fused_computation | loop fusion | flops 983040 | bytes 1966080 | tf_op jit(solution)/shard_map/stack | solution.py:19
  16.3 0.6 %pad_add_fusion.ids = s32[2]{0:T(128)} fusion(s32[1]{0:T(128)} %bitcast.1, s32[1]{0:T(128)} %bitcast), kind=kLoop, calls=%fused_computation.80 | loop fusion | flops 2 | bytes 16 | tf_op jit(solution)/shard_map/stack | solution.py:174
  17.0 18.6 %collective-permute-done = bf16[3,128,128]{2,1,0:T(8,128)(2,1)S(1)} collective-permute-done((bf16[3,128,128]{2,1,0:T(8,128)(2,1)S(1)}, bf16[3,128,128]{2,1,0:T(8,128)(2,1)S(1)}, u32[]{:S(2)}, u32[]{:S(2)}) %collective-permute-start) | collective-permute-done | bytes 98336 | tf_op jit(solution)/shard_map/ppermute | solution.py:139
  35.6 1.9 %collective-permute-start.2 = (bf16[8,3,128,128]{3,2,1,0:T(8,128)(2,1)S(1)}, bf16[8,3,128,128]{3,2,1,0:T(8,128)(2,1)S(1)}, u32[]{:S(2)}, u32[]{:S(2)}) collective-permute-start(bf16[8,3,128,128]{3,2,1,0:T(8,128)(2,1)S(1)} %constant_dynamic-slice_fusion), channel_id=1, source_target_pairs={{0,8},{8,16},{16,24},{24,32},{32,40},{40,48},{48,56},{56,64},{64,7... | collective-permute-start | bytes 2359304 | tf_op jit(solution)/shard_map/ppermute | solution.py:159
  37.7 1.3 %collective-permute-start.5 = (bf16[2,128,128]{2,1,0:T(8,128)(2,1)S(1)}, bf16[2,128,128]{2,1,0:T(8,128)(2,1)S(1)}, u32[]{:S(2)}, u32[]{:S(2)}) collective-permute-start(bf16[2,128,128]{2,1,0:T(8,128)(2,1)S(1)} %slice.182.up_ref), channel_id=1, source_target_pairs={{1,0},{2,1},{3,2},{4,3},{5,4},{6,5},{7,6},{9,8},{10,9},{11,10},{12... | collective-permute-start | bytes 196616 | tf_op jit(solution)/shard_map/ppermute | solution.py:172
  39.0 1.3 %collective-permute-start.6 = (bf16[2,128,128]{2,1,0:T(8,128)(2,1)S(1)}, bf16[2,128,128]{2,1,0:T(8,128)(2,1)S(1)}, u32[]{:S(2)}, u32[]{:S(2)}) collective-permute-start(bf16[2,128,128]{2,1,0:T(8,128)(2,1)S(1)} %slice.183.down_ref), channel_id=1, source_target_pairs={{0,1},{1,2},{2,3},{3,4},{4,5},{5,6},{6,7},{8,9},{9,10},{10,11},{11... | collective-permute-start | bytes 196616 | tf_op jit(solution)/shard_map/ppermute | solution.py:171
  40.5 0.2 slice_reduce_fusion.8
  40.7 0.3 slice_reduce_fusion.2
  40.9 8.7 %collective-permute-done.2 = bf16[8,3,128,128]{3,2,1,0:T(8,128)(2,1)S(1)} collective-permute-done((bf16[8,3,128,128]{3,2,1,0:T(8,128)(2,1)S(1)}, bf16[8,3,128,128]{3,2,1,0:T(8,128)(2,1)S(1)}, u32[]{:S(2)}, u32[]{:S(2)}) %collective-permute-start.2) | collective-permute-done | bytes 786464 | tf_op jit(solution)/shard_map/ppermute | solution.py:159
  49.7 0.5 fusion.11
  50.2 1.0 %pad_maximum_fusion.1.recv_ref = bf16[8,3,128,128]{3,2,1,0:T(8,128)(2,1)} fusion(bf16[8,1,128,128]{3,2,1,0:T(8,128)(2,1)S(1)} %get-tuple-element.44, bf16[8,1,128,128]{3,2,1,0:T(8,128)(2,1)S(1)} %get-tuple-element.45, bf16[8,1,128,128]{3,2,1,0:T(8,128)(2,1)S(1)} %get-tuple-element.43), kind=kLoop, calls=%fused_computation.10 | loop fusion | flops 786432 | bytes 1572864 | tf_op jit(solution)/shard_map/stack | solution.py:19
  51.2 0.6 copy-done.5
  51.8 0.3 copy-done.1
  52.1 0.8 %copy-done.2 = bf16[10,2,128,128]{3,2,1,0:T(8,128)(2,1)} copy-done((bf16[10,2,128,128]{3,2,1,0:T(8,128)(2,1)}, bf16[10,2,128,128]{3,2,1,0:T(8,128)(2,1)S(1)}, u32[]{:S(2)}) %copy-start.2) | copy-done | bytes 655384
  52.9 5.5 %shard_map.55 = bf16[10,2,128,128]{3,2,1,0:T(8,128)(2,1)} custom-call(s32[2]{0:T(128)} %pad_add_fusion.ids, f32[10,128]{1,0:T(8,128)} %q_ref.1, bf16[10,3,128,128]{3,2,1,0:T(8,128)(2,1)} %pad_maximum_fusion.jac_ref, bf16[8,3,128,128]{3,2,1,0:T(8,128)(2,1)} %pad_maximum_fusion.1.recv_ref, bf16[10,2,128,128]{3,2,1,0:T(8,128)(2,1)} %mid_ref.1, ...), custom_call_target="tpu_custom_call" | custom-call | tf_op jit(solution)/shard_map/pallas_call | solution.py:177
  (36 shorter events, 0.6 us)
Async XLA Ops:
  0.0 6.4 %copy-start.7 = (s32[10,3]{0,1:T(4,128)S(1)}, s32[10,3]{0,1:T(4,128)}, u32[]{:S(2)}) copy-start(s32[10,3]{0,1:T(4,128)} %param.11) | copy-start | bytes 364
  0.0 51.2 %collective-permute-start.3 = (bf16[10,2,128,128]{3,2,1,0:T(8,128)(2,1)}, bf16[10,2,128,128]{3,2,1,0:T(8,128)(2,1)S(1)}, u32[]{:S(2)}, u32[]{:S(2)}) collective-permute-start(bf16[10,2,128,128]{3,2,1,0:T(8,128)(2,1)} %mid_ref.1), channel_id=1, source_target_pairs={{0,1},{1,2},{2,3},{3,4},{4,5},{5,6},{6,7},{8,9},{9,10},{10,11},{11... | collective-permute-start | bytes 1966088 | tf_op jit(solution)/shard_map/ppermute | solution.py:134
  1.4 49.8 %collective-permute-start.4 = (bf16[10,2,128,128]{3,2,1,0:T(8,128)(2,1)}, bf16[10,2,128,128]{3,2,1,0:T(8,128)(2,1)S(1)}, u32[]{:S(2)}, u32[]{:S(2)}) collective-permute-start(bf16[10,2,128,128]{3,2,1,0:T(8,128)(2,1)} %mid_ref.1), channel_id=1, source_target_pairs={{1,0},{2,1},{3,2},{4,3},{5,4},{6,5},{7,6},{9,8},{10,9},{11,10},{12... | collective-permute-start | bytes 1966088 | tf_op jit(solution)/shard_map/ppermute | solution.py:135
  6.6 0.7 %copy-start.8 = (s32[10]{0:T(128)S(1)}, s32[10]{0:T(128)}, u32[]{:S(2)}) copy-start(s32[10]{0:T(128)} %param.12) | copy-start | bytes 124
  7.3 7.4 %copy-start = (bf16[10,3,128,128]{3,2,1,0:T(8,128)(2,1)S(1)}, bf16[10,3,128,128]{3,2,1,0:T(8,128)(2,1)}, u32[]{:S(2)}) copy-start(bf16[10,3,128,128]{3,2,1,0:T(8,128)(2,1)} %param.10) | copy-start | bytes 2949124
  7.4 28.3 %collective-permute-start = (bf16[3,128,128]{2,1,0:T(8,128)(2,1)S(1)}, bf16[3,128,128]{2,1,0:T(8,128)(2,1)S(1)}, u32[]{:S(2)}, u32[]{:S(2)}) collective-permute-start(bf16[3,128,128]{2,1,0:T(8,128)(2,1)S(1)} %get-tuple-element.48), channel_id=1, source_target_pairs={{0,8},{8,16},{16,24},{24,32},{32,40},{40,48},{48,56},{56,64},{64,7... | collective-permute-start | bytes 294920 | tf_op jit(solution)/shard_map/ppermute | solution.py:139
  11.5 24.1 %collective-permute-start.1 = (bf16[3,128,128]{2,1,0:T(8,128)(2,1)S(1)}, bf16[3,128,128]{2,1,0:T(8,128)(2,1)S(1)}, u32[]{:S(2)}, u32[]{:S(2)}) collective-permute-start(bf16[3,128,128]{2,1,0:T(8,128)(2,1)S(1)} %get-tuple-element.49), channel_id=1, source_target_pairs={{8,0},{16,8},{24,16},{32,24},{40,32},{48,40},{56,48},{64,56},{72,6... | collective-permute-start | bytes 294920 | tf_op jit(solution)/shard_map/ppermute | solution.py:142
  35.6 14.0 %collective-permute-start.2 = (bf16[8,3,128,128]{3,2,1,0:T(8,128)(2,1)S(1)}, bf16[8,3,128,128]{3,2,1,0:T(8,128)(2,1)S(1)}, u32[]{:S(2)}, u32[]{:S(2)}) collective-permute-start(bf16[8,3,128,128]{3,2,1,0:T(8,128)(2,1)S(1)} %constant_dynamic-slice_fusion), channel_id=1, source_target_pairs={{0,8},{8,16},{16,24},{24,32},{32,40},{40,48},{48,56},{56,64},{64,7... | collective-permute-start | bytes 2359304 | tf_op jit(solution)/shard_map/ppermute | solution.py:159
  37.7 1.3 %copy-start.3 = (bf16[2,128,128]{2,1,0:T(8,128)(2,1)}, bf16[2,128,128]{2,1,0:T(8,128)(2,1)S(1)}, u32[]{:S(2)}) copy-start(bf16[2,128,128]{2,1,0:T(8,128)(2,1)S(1)} %slice.182.up_ref) | copy-start | bytes 196612
  37.7 13.5 %collective-permute-start.5 = (bf16[2,128,128]{2,1,0:T(8,128)(2,1)S(1)}, bf16[2,128,128]{2,1,0:T(8,128)(2,1)S(1)}, u32[]{:S(2)}, u32[]{:S(2)}) collective-permute-start(bf16[2,128,128]{2,1,0:T(8,128)(2,1)S(1)} %slice.182.up_ref), channel_id=1, source_target_pairs={{1,0},{2,1},{3,2},{4,3},{5,4},{6,5},{7,6},{9,8},{10,9},{11,10},{12... | collective-permute-start | bytes 196616 | tf_op jit(solution)/shard_map/ppermute | solution.py:172
  39.0 11.1 %copy-start.4 = (bf16[2,128,128]{2,1,0:T(8,128)(2,1)}, bf16[2,128,128]{2,1,0:T(8,128)(2,1)S(1)}, u32[]{:S(2)}) copy-start(bf16[2,128,128]{2,1,0:T(8,128)(2,1)S(1)} %slice.183.down_ref) | copy-start | bytes 196612
  39.0 12.1 %collective-permute-start.6 = (bf16[2,128,128]{2,1,0:T(8,128)(2,1)S(1)}, bf16[2,128,128]{2,1,0:T(8,128)(2,1)S(1)}, u32[]{:S(2)}, u32[]{:S(2)}) collective-permute-start(bf16[2,128,128]{2,1,0:T(8,128)(2,1)S(1)} %slice.183.down_ref), channel_id=1, source_target_pairs={{0,1},{1,2},{2,3},{3,4},{4,5},{5,6},{6,7},{8,9},{9,10},{10,11},{11... | collective-permute-start | bytes 196616 | tf_op jit(solution)/shard_map/ppermute | solution.py:171
  51.2 0.6 %copy-start.5 = (bf16[2,128,128]{2,1,0:T(8,128)(2,1)}, bf16[2,128,128]{2,1,0:T(8,128)(2,1)S(1)}, u32[]{:S(2)}) copy-start(bf16[2,128,128]{2,1,0:T(8,128)(2,1)S(1)} %collective-permute-done.5.up_right_ref) | copy-start | bytes 196612
  51.2 0.6 %copy-start.6 = (bf16[2,128,128]{2,1,0:T(8,128)(2,1)}, bf16[2,128,128]{2,1,0:T(8,128)(2,1)S(1)}, u32[]{:S(2)}) copy-start(bf16[2,128,128]{2,1,0:T(8,128)(2,1)S(1)} %collective-permute-done.6.down_left_ref) | copy-start | bytes 196612
  51.2 0.9 %copy-start.1 = (bf16[10,2,128,128]{3,2,1,0:T(8,128)(2,1)}, bf16[10,2,128,128]{3,2,1,0:T(8,128)(2,1)S(1)}, u32[]{:S(2)}) copy-start(bf16[10,2,128,128]{3,2,1,0:T(8,128)(2,1)S(1)} %collective-permute-done.3.left_ref) | copy-start | bytes 1966084
  52.1 0.8 %copy-start.2 = (bf16[10,2,128,128]{3,2,1,0:T(8,128)(2,1)}, bf16[10,2,128,128]{3,2,1,0:T(8,128)(2,1)S(1)}, u32[]{:S(2)}) copy-start(bf16[10,2,128,128]{3,2,1,0:T(8,128)(2,1)S(1)} %collective-permute-done.4.right_ref) | copy-start | bytes 1966084

commit v9 on v8

--- a/solution.py
+++ b/solution.py
@@ -24,7 +24,7 @@
     window = tile_rows + band_local - 1
 
     def kernel(ids, q_ref, jac_ref, recv_ref, mid_ref, left_ref, right_ref, up_ref, down_ref,
-               up_right_ref, down_left_ref, out_ref, win_ref):
+               out_ref, win_ref):
         row_id = ids[0]
         col_id = ids[1]
         first_row = row_id * tile_rows
@@ -49,15 +49,9 @@
 
         def prior_tile(ext_row, ext_slot, masked):
             if ext_slot < 2:
-                if ext_row == tile_rows + 1:
-                    tile = down_left_ref[band_local - 2 + ext_slot]
-                else:
-                    tile = left_ref[ext_row - 1, band_local - 2 + ext_slot]
+                tile = left_ref[ext_row - 1, band_local - 2 + ext_slot]
             elif ext_slot >= 2 + band_local:
-                if ext_row == 0:
-                    tile = up_right_ref[ext_slot - 2 - band_local]
-                else:
-                    tile = right_ref[ext_row - 1, ext_slot - 2 - band_local]
+                tile = right_ref[ext_row, ext_slot - 2 - band_local]
             elif ext_row == 0:
                 tile = up_ref[ext_slot - 2]
             elif ext_row == tile_rows + 1:
@@ -131,8 +125,6 @@
     def flat(a, b):
         return a * col_count + b
 
-    left = lax.ppermute(p_band, "col", [(b, b + 1) for b in range(col_count - 1)])
-    right = lax.ppermute(p_band, "col", [(b + 1, b) for b in range(col_count - 1)])
     meta = jnp.zeros((tile_size, tile_size), p_band.dtype)
     meta = meta.at[0, : tile_rows * 3].set(block_offsets.reshape(-1).astype(p_band.dtype))
     meta = meta.at[1, :tile_rows].set(block_live.astype(p_band.dtype))
@@ -155,6 +147,10 @@
             pairs += [(flat(a, b), flat(a + 1, b)) for a in range(row_count - 1)]
         else:
             pairs += [(flat(a, b), flat(a - 1, b)) for a in range(1, row_count)]
+    left_payload = jnp.concatenate([p_band, down[None]], axis=0)
+    right_payload = jnp.concatenate([up[None], p_band], axis=0)
+    left = lax.ppermute(left_payload, "col", [(b, b + 1) for b in range(col_count - 1)])
+    right = lax.ppermute(right_payload, "col", [(b + 1, b) for b in range(col_count - 1)])
     sent, _ = lax.optimization_barrier((sent, (up_all, down_all)))
     received_blocks = lax.ppermute(sent, ("row", "col"), pairs)
 
@@ -168,19 +164,16 @@
         lax.dynamic_slice_in_dim(received_live, send_start, sent_rows, 0),
     )
 
-    down_left = lax.ppermute(down, "col", [(b, b + 1) for b in range(col_count - 1)])
-    up_right = lax.ppermute(up, "col", [(b + 1, b) for b in range(col_count - 1)])
-
     ids = jnp.stack([row_id, col_id]).astype(jnp.int32)
     vmem = pl.BlockSpec(memory_space=pltpu.MemorySpace.VMEM)
     smem = pl.BlockSpec(memory_space=pltpu.MemorySpace.SMEM)
     return pl.pallas_call(
         band_kernel(tile_rows, band_local, half_band, grid_tiles, sent_rows, row_count, col_count),
         out_shape=jax.ShapeDtypeStruct(p_band.shape, p_band.dtype),
-        in_specs=[smem] + [vmem] * 10,
+        in_specs=[smem] + [vmem] * 8,
         out_specs=vmem,
         scratch_shapes=[pltpu.VMEM((tile_rows + band_local - 1, 3, tile_size, tile_size), p_band.dtype)],
-    )(ids, q_var, jacobian, received, p_band, left, right, up, down, up_right, down_left)
+    )(ids, q_var, jacobian, received, p_band, left, right, up, down)
 
 
 def solution(mesh):

time: 58.8 us -> 57.4 us (0.976)
  the two profiles are of different devices: /device:TPU:151 before, /device:TPU:121 now
where the time goes in v9:
time: 57.4 us; the launch traced here: 57.1 us
  waiting for transfers between devices  22.3 us (39%)
  starting transfers between devices  17.4 us (30%)
  other arithmetic  6.4 us (11%)
  Pallas kernels  5.49 us (10%)
  local copies, waits for them, and re-layouts  5.23 us (9%)
    ppermute x1, waiting for transfers between devices, shards(): lax.ppermute(right_payload, 'col', [(b + 1, b) for b in range(col_count -...  9.63 us
    ppermute x1, waiting for transfers between devices, shards(): lax.ppermute(left_payload, 'col', [(b, b + 1) for b in range(col_count -...  7.85 us
    ppermute x1, starting transfers between devices, shards(): lax.ppermute(right_payload, 'col', [(b + 1, b) for b in range(col_count -...  6.05 us
    ppermute x1, starting transfers between devices, shards(): lax.ppermute(jnp.concatenate([p_band[-1], meta[None]], axis=0), 'row', [(...  5.63 us
    pallas_call x1, Pallas kernels, shards(): pl.pallas_call(band_kernel(tile_rows, band_local, half_band, grid_tiles,...  5.49 us
    ppermute x1, waiting for transfers between devices, shards(): lax.ppermute(jnp.concatenate([p_band[0], meta[None]], axis=0), 'row', [(a...  2.55 us
    ppermute x1, waiting for transfers between devices, shards(): received_blocks = lax.ppermute(sent, ('row', 'col'), pairs)  2.3 us
    another operation x2, other arithmetic, assemble(): return jnp.stack(pieces, axis=1)  2.05 us
  transfers between devices with their start and end apart: 5, of which 4 were waited for; matrix products, arithmetic and copies ran while one was open for 14% of the time, Pallas kernels for 0%

profile of v9, /device:TPU:121, one launch (start us, length us, event | category | flops | bytes accessed | tf_op | source)
XLA Modules:
  0.0 57.1 jit_solution(9587084998075638168)
XLA Ops:
  0.0 0.7 %convert_bitcast_fusion = bf16[1,1,10]{2,1,0:T(2,128)(2,1)S(1)} fusion(s32[10]{0:T(128)} %param.12), kind=kLoop, calls=%fused_computation.83 | loop fusion | flops 10 | bytes 60 | tf_op jit(solution)/shard_map/broadcast_in_dim | solution.py:132
  0.7 0.7 %convert_element_type.109 = bf16[10,3]{0,1:T(4,128)(2,1)S(1)} convert(s32[10,3]{0,1:T(4,128)} %param.11) | non-fusion elementwise | flops 30 | bytes 180 | tf_op jit(solution)/shard_map/convert_element_type | solution.py:129
  1.6 0.9 %slice_bitcast_fusion.1 = (bf16[2,128,128]{2,1,0:T(8,128)(2,1)S(1)}, bf16[2,128,128]{2,1,0:T(8,128)(2,1)S(1)}) fusion(bf16[10,2,128,128]{3,2,1,0:T(8,128)(2,1)} %mid_ref.1), kind=kLoop, calls=%fused_computation.43 | loop fusion | bytes 262144 | tf_op jit(solution)/shard_map/squeeze | solution.py:132
  2.7 5.6 %collective-permute-start = (bf16[3,128,128]{2,1,0:T(8,128)(2,1)S(1)}, bf16[3,128,128]{2,1,0:T(8,128)(2,1)S(1)}, u32[]{:S(2)}, u32[]{:S(2)}) collective-permute-start(bf16[3,128,128]{2,1,0:T(8,128)(2,1)S(1)} %get-tuple-element.54), channel_id=1, source_target_pairs={{0,8},{8,16},{16,24},{24,32},{32,40},{40,48},{48,56},{56,64},{64,7... | collective-permute-start | bytes 294920 | tf_op jit(solution)/shard_map/ppermute | solution.py:131
  8.3 1.9 %collective-permute-start.1 = (bf16[3,128,128]{2,1,0:T(8,128)(2,1)S(1)}, bf16[3,128,128]{2,1,0:T(8,128)(2,1)S(1)}, u32[]{:S(2)}, u32[]{:S(2)}) collective-permute-start(bf16[3,128,128]{2,1,0:T(8,128)(2,1)S(1)} %get-tuple-element.55), channel_id=1, source_target_pairs={{8,0},{16,8},{24,16},{32,24},{40,32},{48,40},{56,48},{64,56},{72,6... | collective-permute-start | bytes 294920 | tf_op jit(solution)/shard_map/ppermute | solution.py:134
  10.3 1.2 %constant_dynamic-slice_fusion = bf16[8,3,128,128]{3,2,1,0:T(8,128)(2,1)S(1)} fusion(bf16[10,3,128,128]{3,2,1,0:T(8,128)(2,1)} %param.10, s32[]{:T(128)S(6)} %select_n.101), kind=kLoop, calls=%fused_computation.74 | loop fusion | bytes 1572868 | tf_op jit(solution)/shard_map/dynamic_slice | solution.py:143
  11.5 0.5 fusion.2
  12.1 1.1 %pad_maximum_fusion.jac_ref = bf16[10,3,128,128]{3,2,1,0:T(8,128)(2,1)} fusion(bf16[10,1,128,128]{3,2,1,0:T(8,128)(2,1)S(1)} %get-tuple-element.41, bf16[10,1,128,128]{3,2,1,0:T(8,128)(2,1)S(1)} %get-tuple-element.42, bf16[10,1,128,128]{3,2,1,0:T(8,128)(2,1)S(1)} %get-tuple-element.40), kind=kLoop, calls=%fused_computation | loop fusion | flops 983040 | bytes 1966080 | tf_op jit(solution)/shard_map/stack | solution.py:19
  13.2 0.6 %pad_add_fusion.ids = s32[2]{0:T(128)} fusion(s32[1]{0:T(128)} %bitcast.1, s32[1]{0:T(128)} %bitcast), kind=kLoop, calls=%fused_computation.82 | loop fusion | flops 2 | bytes 16 | tf_op jit(solution)/shard_map/stack | solution.py:167
  13.8 2.5 %collective-permute-done.1 = bf16[3,128,128]{2,1,0:T(8,128)(2,1)S(1)} collective-permute-done((bf16[3,128,128]{2,1,0:T(8,128)(2,1)S(1)}, bf16[3,128,128]{2,1,0:T(8,128)(2,1)S(1)}, u32[]{:S(2)}, u32[]{:S(2)}) %collective-permute-start.1) | collective-permute-done | bytes 98336 | tf_op jit(solution)/shard_map/ppermute | solution.py:134
  16.4 1.9 %collective-permute-start.2 = (bf16[8,3,128,128]{3,2,1,0:T(8,128)(2,1)S(1)}, bf16[8,3,128,128]{3,2,1,0:T(8,128)(2,1)S(1)}, u32[]{:S(2)}, u32[]{:S(2)}) collective-permute-start(bf16[8,3,128,128]{3,2,1,0:T(8,128)(2,1)S(1)} %constant_dynamic-slice_fusion), channel_id=1, source_target_pairs={{0,8},{8,16},{16,24},{24,32},{32,40},{40,48},{48,56},{56,64},{64,7... | collective-permute-start | bytes 2359304 | tf_op jit(solution)/shard_map/ppermute | solution.py:155
  18.3 0.6 %fusion.30 = (bf16[2,128,128]{2,1,0:T(8,128)(2,1)}, bf16[1,2,128,128]{3,2,1,0:T(8,128)(2,1)S(1)}) fusion(bf16[3,128,128]{2,1,0:T(8,128)(2,1)S(1)} %collective-permute-done.1), kind=kLoop, calls=%fused_computation.86 | loop fusion | bytes 196608 | tf_op jit(solution)/shard_map/slice | solution.py:138
  18.9 0.6 %fusion.31 = (bf16[2,128,128]{2,1,0:T(8,128)(2,1)}, bf16[1,2,128,128]{3,2,1,0:T(8,128)(2,1)S(1)}) fusion(bf16[3,128,128]{2,1,0:T(8,128)(2,1)S(1)} %collective-permute-done), kind=kLoop, calls=%fused_computation.87 | loop fusion | bytes 196608 | tf_op jit(solution)/shard_map/slice | solution.py:137
  19.6 1.2 %pad_maximum_fusion.3 = (bf16[11,2,128,128]{3,2,1,0:T(8,128)(2,1)}, bf16[11,2,128,128]{3,2,1,0:T(8,128)(2,1)}) fusion(bf16[10,2,128,128]{3,2,1,0:T(8,128)(2,1)S(1)} %copy-done.1, bf16[1,2,128,128]{3,2,1,0:T(8,128)(2,1)S(1)} %get-tuple-element.53, bf16[1,2,128,128]{3,2,1,0:T(8,128)(2,1)S(1)} %get-tuple-element.51), kind=kLoop, calls=%fused_computation.21 | loop fusion | flops 720896 | bytes 2228224 | tf_op jit(solution)/shard_map/concatenate | solution.py:151
  20.9 6.0 %collective-permute-start.4 = (bf16[11,2,128,128]{3,2,1,0:T(8,128)(2,1)}, bf16[11,2,128,128]{3,2,1,0:T(8,128)(2,1)S(1)}, u32[]{:S(2)}, u32[]{:S(2)}) collective-permute-start(bf16[11,2,128,128]{3,2,1,0:T(8,128)(2,1)} %get-tuple-element.46), channel_id=1, source_target_pairs={{1,0},{2,1},{3,2},{4,3},{5,4},{6,5},{7,6},{9,8},{10,9},{11,10},{12... | collective-permute-start | bytes 2162696 | tf_op jit(solution)/shard_map/ppermute | solution.py:153
  26.9 1.9 %collective-permute-start.3 = (bf16[11,2,128,128]{3,2,1,0:T(8,128)(2,1)}, bf16[11,2,128,128]{3,2,1,0:T(8,128)(2,1)S(1)}, u32[]{:S(2)}, u32[]{:S(2)}) collective-permute-start(bf16[11,2,128,128]{3,2,1,0:T(8,128)(2,1)} %get-tuple-element.47), channel_id=1, source_target_pairs={{0,1},{1,2},{2,3},{3,4},{4,5},{5,6},{6,7},{8,9},{9,10},{10,11},{11... | collective-permute-start | bytes 2162696 | tf_op jit(solution)/shard_map/ppermute | solution.py:152
  29.2 0.3 slice_reduce_fusion.2
  29.5 2.3 %collective-permute-done.2 = bf16[8,3,128,128]{3,2,1,0:T(8,128)(2,1)S(1)} collective-permute-done((bf16[8,3,128,128]{3,2,1,0:T(8,128)(2,1)S(1)}, bf16[8,3,128,128]{3,2,1,0:T(8,128)(2,1)S(1)}, u32[]{:S(2)}, u32[]{:S(2)}) %collective-permute-start.2) | collective-permute-done | bytes 786464 | tf_op jit(solution)/shard_map/ppermute | solution.py:155
  31.8 0.5 fusion.11
  32.2 1.0 %pad_maximum_fusion.1.recv_ref = bf16[8,3,128,128]{3,2,1,0:T(8,128)(2,1)} fusion(bf16[8,1,128,128]{3,2,1,0:T(8,128)(2,1)S(1)} %get-tuple-element.44, bf16[8,1,128,128]{3,2,1,0:T(8,128)(2,1)S(1)} %get-tuple-element.45, bf16[8,1,128,128]{3,2,1,0:T(8,128)(2,1)S(1)} %get-tuple-element.43), kind=kLoop, calls=%fused_computation.10 | loop fusion | flops 786432 | bytes 1572864 | tf_op jit(solution)/shard_map/stack | solution.py:19
  33.2 9.6 %collective-permute-done.4.right_ref = bf16[11,2,128,128]{3,2,1,0:T(8,128)(2,1)S(1)} collective-permute-done((bf16[11,2,128,128]{3,2,1,0:T(8,128)(2,1)}, bf16[11,2,128,128]{3,2,1,0:T(8,128)(2,1)S(1)}, u32[]{:S(2)}, u32[]{:S(2)}) %collective-permute-start.4) | collective-permute-done | bytes 720928 | tf_op jit(solution)/shard_map/ppermute | solution.py:153
  42.9 7.8 %collective-permute-done.3.left_ref = bf16[11,2,128,128]{3,2,1,0:T(8,128)(2,1)S(1)} collective-permute-done((bf16[11,2,128,128]{3,2,1,0:T(8,128)(2,1)}, bf16[11,2,128,128]{3,2,1,0:T(8,128)(2,1)S(1)}, u32[]{:S(2)}, u32[]{:S(2)}) %collective-permute-start.3) | collective-permute-done | bytes 720928 | tf_op jit(solution)/shard_map/ppermute | solution.py:152
  50.7 0.9 %copy-done.3 = bf16[11,2,128,128]{3,2,1,0:T(8,128)(2,1)} copy-done((bf16[11,2,128,128]{3,2,1,0:T(8,128)(2,1)}, bf16[11,2,128,128]{3,2,1,0:T(8,128)(2,1)S(1)}, u32[]{:S(2)}) %copy-start.3) | copy-done | bytes 720920
  51.6 5.5 %shard_map.55 = bf16[10,2,128,128]{3,2,1,0:T(8,128)(2,1)} custom-call(s32[2]{0:T(128)} %pad_add_fusion.ids, f32[10,128]{1,0:T(8,128)} %q_ref.1, bf16[10,3,128,128]{3,2,1,0:T(8,128)(2,1)} %pad_maximum_fusion.jac_ref, bf16[8,3,128,128]{3,2,1,0:T(8,128)(2,1)} %pad_maximum_fusion.1.recv_ref, bf16[10,2,128,128]{3,2,1,0:T(8,128)(2,1)} %mid_ref.1, ...), custom_call_target="tpu_custom_call" | custom-call | tf_op jit(solution)/shard_map/pallas_call | solution.py:170
  (27 shorter events, 0.9 us)
Async XLA Ops:
  1.6 8.7 %copy-start.5 = (s32[10]{0:T(128)S(1)}, s32[10]{0:T(128)}, u32[]{:S(2)}) copy-start(s32[10]{0:T(128)} %param.12) | copy-start | bytes 124
  2.6 7.6 %copy-start.4 = (s32[10,3]{0,1:T(4,128)S(1)}, s32[10,3]{0,1:T(4,128)}, u32[]{:S(2)}) copy-start(s32[10,3]{0,1:T(4,128)} %param.11) | copy-start | bytes 364
  2.6 8.9 %copy-start = (bf16[10,3,128,128]{3,2,1,0:T(8,128)(2,1)S(1)}, bf16[10,3,128,128]{3,2,1,0:T(8,128)(2,1)}, u32[]{:S(2)}) copy-start(bf16[10,3,128,128]{3,2,1,0:T(8,128)(2,1)} %param.10) | copy-start | bytes 2949124
  2.7 11.1 %collective-permute-start = (bf16[3,128,128]{2,1,0:T(8,128)(2,1)S(1)}, bf16[3,128,128]{2,1,0:T(8,128)(2,1)S(1)}, u32[]{:S(2)}, u32[]{:S(2)}) collective-permute-start(bf16[3,128,128]{2,1,0:T(8,128)(2,1)S(1)} %get-tuple-element.54), channel_id=1, source_target_pairs={{0,8},{8,16},{16,24},{24,32},{32,40},{40,48},{48,56},{56,64},{64,7... | collective-permute-start | bytes 294920 | tf_op jit(solution)/shard_map/ppermute | solution.py:131
  8.3 8.0 %collective-permute-start.1 = (bf16[3,128,128]{2,1,0:T(8,128)(2,1)S(1)}, bf16[3,128,128]{2,1,0:T(8,128)(2,1)S(1)}, u32[]{:S(2)}, u32[]{:S(2)}) collective-permute-start(bf16[3,128,128]{2,1,0:T(8,128)(2,1)S(1)} %get-tuple-element.55), channel_id=1, source_target_pairs={{8,0},{16,8},{24,16},{32,24},{40,32},{48,40},{56,48},{64,56},{72,6... | collective-permute-start | bytes 294920 | tf_op jit(solution)/shard_map/ppermute | solution.py:134
  12.1 7.5 %copy-start.1 = (bf16[10,2,128,128]{3,2,1,0:T(8,128)(2,1)S(1)}, bf16[10,2,128,128]{3,2,1,0:T(8,128)(2,1)}, u32[]{:S(2)}) copy-start(bf16[10,2,128,128]{3,2,1,0:T(8,128)(2,1)} %mid_ref.1) | copy-start | bytes 1966084
  16.4 15.4 %collective-permute-start.2 = (bf16[8,3,128,128]{3,2,1,0:T(8,128)(2,1)S(1)}, bf16[8,3,128,128]{3,2,1,0:T(8,128)(2,1)S(1)}, u32[]{:S(2)}, u32[]{:S(2)}) collective-permute-start(bf16[8,3,128,128]{3,2,1,0:T(8,128)(2,1)S(1)} %constant_dynamic-slice_fusion), channel_id=1, source_target_pairs={{0,8},{8,16},{16,24},{24,32},{32,40},{40,48},{48,56},{56,64},{64,7... | collective-permute-start | bytes 2359304 | tf_op jit(solution)/shard_map/ppermute | solution.py:155
  20.9 22.0 %collective-permute-start.4 = (bf16[11,2,128,128]{3,2,1,0:T(8,128)(2,1)}, bf16[11,2,128,128]{3,2,1,0:T(8,128)(2,1)S(1)}, u32[]{:S(2)}, u32[]{:S(2)}) collective-permute-start(bf16[11,2,128,128]{3,2,1,0:T(8,128)(2,1)} %get-tuple-element.46), channel_id=1, source_target_pairs={{1,0},{2,1},{3,2},{4,3},{5,4},{6,5},{7,6},{9,8},{10,9},{11,10},{12... | collective-permute-start | bytes 2162696 | tf_op jit(solution)/shard_map/ppermute | solution.py:153
  26.9 23.8 %collective-permute-start.3 = (bf16[11,2,128,128]{3,2,1,0:T(8,128)(2,1)}, bf16[11,2,128,128]{3,2,1,0:T(8,128)(2,1)S(1)}, u32[]{:S(2)}, u32[]{:S(2)}) collective-permute-start(bf16[11,2,128,128]{3,2,1,0:T(8,128)(2,1)} %get-tuple-element.47), channel_id=1, source_target_pairs={{0,1},{1,2},{2,3},{3,4},{4,5},{5,6},{6,7},{8,9},{9,10},{10,11},{11... | collective-permute-start | bytes 2162696 | tf_op jit(solution)/shard_map/ppermute | solution.py:152
  42.9 7.9 %copy-start.2 = (bf16[11,2,128,128]{3,2,1,0:T(8,128)(2,1)}, bf16[11,2,128,128]{3,2,1,0:T(8,128)(2,1)S(1)}, u32[]{:S(2)}) copy-start(bf16[11,2,128,128]{3,2,1,0:T(8,128)(2,1)S(1)} %collective-permute-done.4.right_ref) | copy-start | bytes 2162692
  50.7 0.9 %copy-start.3 = (bf16[11,2,128,128]{3,2,1,0:T(8,128)(2,1)}, bf16[11,2,128,128]{3,2,1,0:T(8,128)(2,1)S(1)}, u32[]{:S(2)}) copy-start(bf16[11,2,128,128]{3,2,1,0:T(8,128)(2,1)S(1)} %collective-permute-done.3.left_ref) | copy-start | bytes 2162692

commit v10 on v7

--- a/solution.py
+++ b/solution.py
@@ -76,27 +76,28 @@
 
         def body(masked):
             for row in range(tile_rows):
-                lhs = jnp.concatenate([jac_ref[row, f] for f in range(3)], axis=1)
-                rhs = jnp.concatenate(
-                    [
-                        jnp.concatenate(
-                            [prior_tile(row + f, u - f + 2, masked) for u in range(extended)], axis=1
+                spread = []
+                for u in range(extended):
+                    acc = None
+                    for f in range(3):
+                        term = jnp.dot(
+                            jac_ref[row, f],
+                            prior_tile(row + f, u - f + 2, masked),
+                            preferred_element_type=jnp.float32,
                         )
-                        for f in range(3)
-                    ],
-                    axis=0,
-                )
-                spread = jnp.dot(lhs, rhs, preferred_element_type=jnp.float32).astype(jnp.bfloat16)
+                        acc = term if acc is None else acc + term
+                    spread.append(acc.astype(jnp.bfloat16))
                 noise = jnp.where(eye, q_ref[pl.ds(row, 1), :], 0.0)
                 for k in range(band_local):
-                    left_side = spread[:, k * size : (k + 3) * size]
-                    right_side = jnp.concatenate([win_ref[row + k, g] for g in range(3)], axis=1)
-                    total = lax.dot_general(
-                        left_side,
-                        right_side,
-                        (((1,), (1,)), ((), ())),
-                        preferred_element_type=jnp.float32,
-                    )
+                    total = None
+                    for g in range(3):
+                        term = lax.dot_general(
+                            spread[k + g],
+                            win_ref[row + k, g],
+                            (((1,), (1,)), ((), ())),
+                            preferred_element_type=jnp.float32,
+                        )
+                        total = term if total is None else total + term
                     on_diagonal = (low_offset + k == 0).astype(jnp.float32)
                     total = total + noise * on_diagonal
                     if masked:

time: 50.9 us -> 51.5 us (1.012)
  the two profiles are of different devices: /device:TPU:158 before, /device:TPU:478 now
where the time goes in v10:
time: 51.5 us; the launch traced here: 51.2 us
  waiting for transfers between devices  18.9 us (37%)
  starting transfers between devices  16.9 us (33%)
  Pallas kernels  6.11 us (12%)
  other arithmetic  4.49 us (9%)
  local copies, waits for them, and re-layouts  4.48 us (9%)
    ppermute x1, waiting for transfers between devices, shards(): lax.ppermute(jnp.concatenate([p_band[-1], meta[None]], axis=0), 'row', [(...  16.1 us
    pallas_call x1, Pallas kernels, shards(): pl.pallas_call(band_kernel(tile_rows, band_local, half_band, grid_tiles,...  6.11 us
    ppermute x1, starting transfers between devices, shards(): lax.ppermute(p_band, 'col', [(b + 1, b) for b in range(col_count - 1)])  5.43 us
    ppermute x1, starting transfers between devices, shards(): lax.ppermute(jnp.concatenate([p_band[0], meta[None]], axis=0), 'row', [(a...  3.64 us
    ppermute x1, waiting for transfers between devices, shards(): lax.ppermute(down, 'col', [(b, b + 1) for b in range(col_count - 1)])  2.77 us
    another operation x2, other arithmetic, assemble(): return jnp.stack(pieces, axis=1)  2.05 us
    ppermute x1, starting transfers between devices, shards(): received_blocks = lax.ppermute(sent, ('row', 'col'), pairs)  1.92 us
    ppermute x1, starting transfers between devices, shards(): lax.ppermute(jnp.concatenate([p_band[-1], meta[None]], axis=0), 'row', [(...  1.91 us
  transfers between devices with their start and end apart: 7, of which 2 were waited for; matrix products, arithmetic and copies ran while one was open for 15% of the time, Pallas kernels for 0%

profile of v10, /device:TPU:478, one launch (start us, length us, event | category | flops | bytes accessed | tf_op | source)
XLA Modules:
  0.0 51.2 jit_solution(14819519537526935545)
XLA Ops:
  0.0 1.4 %collective-permute-start.3 = (bf16[10,2,128,128]{3,2,1,0:T(8,128)(2,1)}, bf16[10,2,128,128]{3,2,1,0:T(8,128)(2,1)S(1)}, u32[]{:S(2)}, u32[]{:S(2)}) collective-permute-start(bf16[10,2,128,128]{3,2,1,0:T(8,128)(2,1)} %mid_ref.1), channel_id=1, source_target_pairs={{0,1},{1,2},{2,3},{3,4},{4,5},{5,6},{6,7},{8,9},{9,10},{10,11},{11... | collective-permute-start | bytes 1966088 | tf_op jit(solution)/shard_map/ppermute | solution.py:135
  1.4 5.4 %collective-permute-start.4 = (bf16[10,2,128,128]{3,2,1,0:T(8,128)(2,1)}, bf16[10,2,128,128]{3,2,1,0:T(8,128)(2,1)}, u32[]{:S(2)}, u32[]{:S(2)}) collective-permute-start(bf16[10,2,128,128]{3,2,1,0:T(8,128)(2,1)} %mid_ref.1), channel_id=1, source_target_pairs={{1,0},{2,1},{3,2},{4,3},{5,4},{6,5},{7,6},{9,8},{10,9},{11,10},{12... | collective-permute-start | bytes 1966088 | tf_op jit(solution)/shard_map/ppermute | solution.py:136
  6.8 0.9 %slice_bitcast_fusion.1 = (bf16[2,128,128]{2,1,0:T(8,128)(2,1)S(1)}, bf16[2,128,128]{2,1,0:T(8,128)(2,1)S(1)}) fusion(bf16[10,2,128,128]{3,2,1,0:T(8,128)(2,1)} %mid_ref.1), kind=kLoop, calls=%fused_computation.41 | loop fusion | bytes 262144 | tf_op jit(solution)/shard_map/squeeze | solution.py:141
  7.8 0.1 copy.7
  8.0 0.6 %copy-done.7 = s32[10]{0:T(128)S(1)} copy-done((s32[10]{0:T(128)S(1)}, s32[10]{0:T(128)}, u32[]{:S(2)}) %copy-start.7) | copy-done | bytes 64
  8.7 0.7 %pad_maximum_fusion.3 = (bf16[3,128,128]{2,1,0:T(8,128)(2,1)}, bf16[3,128,128]{2,1,0:T(8,128)(2,1)S(1)}) fusion(bf16[1,128,128]{2,1,0:T(8,128)(2,1)S(1)} %scatter.9, bf16[2,128,128]{2,1,0:T(8,128)(2,1)S(1)} %get-tuple-element.44, bf16[2,128,128]{2,1,0:T(8,128)(2,1)S(1)} %get-tuple-element.45), kind=kLoop, calls=%fused_computation.39 | loop fusion | flops 98304 | bytes 360448 | tf_op jit(solution)/shard_map/concatenate | solution.py:141
  9.4 1.9 %collective-permute-start = (bf16[3,128,128]{2,1,0:T(8,128)(2,1)}, bf16[3,128,128]{2,1,0:T(8,128)(2,1)S(1)}, u32[]{:S(2)}, u32[]{:S(2)}) collective-permute-start(bf16[3,128,128]{2,1,0:T(8,128)(2,1)} %get-tuple-element.46), channel_id=1, source_target_pairs={{0,8},{8,16},{16,24},{24,32},{32,40},{40,48},{48,56},{56,64},{64,7... | collective-permute-start | bytes 294920 | tf_op jit(solution)/shard_map/ppermute | solution.py:140
  11.3 3.6 %collective-permute-start.1 = (bf16[3,128,128]{2,1,0:T(8,128)(2,1)S(1)}, bf16[3,128,128]{2,1,0:T(8,128)(2,1)S(1)}, u32[]{:S(2)}, u32[]{:S(2)}) collective-permute-start(bf16[3,128,128]{2,1,0:T(8,128)(2,1)S(1)} %get-tuple-element.47), channel_id=1, source_target_pairs={{8,0},{16,8},{24,16},{32,24},{40,32},{48,40},{56,48},{64,56},{72,6... | collective-permute-start | bytes 294920 | tf_op jit(solution)/shard_map/ppermute | solution.py:143
  15.0 1.2 %constant_dynamic-slice_fusion = bf16[8,3,128,128]{3,2,1,0:T(8,128)(2,1)S(1)} fusion(bf16[10,3,128,128]{3,2,1,0:T(8,128)(2,1)} %param.10, s32[]{:T(128)S(6)} %select_n.101), kind=kLoop, calls=%fused_computation.72 | loop fusion | bytes 1572868 | tf_op jit(solution)/shard_map/dynamic_slice | solution.py:152
  16.1 1.9 %collective-permute-start.2 = (bf16[8,3,128,128]{3,2,1,0:T(8,128)(2,1)S(1)}, bf16[8,3,128,128]{3,2,1,0:T(8,128)(2,1)S(1)}, u32[]{:S(2)}, u32[]{:S(2)}) collective-permute-start(bf16[8,3,128,128]{3,2,1,0:T(8,128)(2,1)S(1)} %constant_dynamic-slice_fusion), channel_id=1, source_target_pairs={{0,8},{8,16},{16,24},{24,32},{32,40},{40,48},{48,56},{56,64},{64,7... | collective-permute-start | bytes 2359304 | tf_op jit(solution)/shard_map/ppermute | solution.py:159
  18.1 0.5 %fusion.2 = (bf16[10,1,128,128]{3,2,1,0:T(8,128)(2,1)S(1)}, bf16[10,1,128,128]{3,2,1,0:T(8,128)(2,1)S(1)}, bf16[10,1,128,128]{3,2,1,0:T(8,128)(2,1)S(1)}) fusion(pred[10]{0:T(512)(128)(4,1)S(1)} %get-tuple-element.55, pred[10]{0:T(512)(128)(4,1)S(1)} %get-tuple-element.56, pred[10]{0:T(512)(128)(4,1)S(1)} %get-tuple-element.54, ...), kind=kLoop, calls=%fused_computation.22 | loop fusion | flops 3440640 | bytes 1966170 | tf_op jit(solution)/shard_map/convert_element_type | solution.py:18
  18.7 1.1 %pad_maximum_fusion.jac_ref = bf16[10,3,128,128]{3,2,1,0:T(8,128)(2,1)} fusion(bf16[10,1,128,128]{3,2,1,0:T(8,128)(2,1)S(1)} %get-tuple-element.39, bf16[10,1,128,128]{3,2,1,0:T(8,128)(2,1)S(1)} %get-tuple-element.40, bf16[10,1,128,128]{3,2,1,0:T(8,128)(2,1)S(1)} %get-tuple-element.38), kind=kLoop, calls=%fused_computation | loop fusion | flops 983040 | bytes 1966080 | tf_op jit(solution)/shard_map/stack | solution.py:19
  19.8 0.6 %pad_add_fusion.ids = s32[2]{0:T(128)} fusion(s32[1]{0:T(128)} %bitcast.1, s32[1]{0:T(128)} %bitcast), kind=kLoop, calls=%fused_computation.80 | loop fusion | flops 2 | bytes 16 | tf_op jit(solution)/shard_map/stack | solution.py:174
  20.4 16.1 %collective-permute-done = bf16[3,128,128]{2,1,0:T(8,128)(2,1)S(1)} collective-permute-done((bf16[3,128,128]{2,1,0:T(8,128)(2,1)}, bf16[3,128,128]{2,1,0:T(8,128)(2,1)S(1)}, u32[]{:S(2)}, u32[]{:S(2)}) %collective-permute-start) | collective-permute-done | bytes 98336 | tf_op jit(solution)/shard_map/ppermute | solution.py:140
  36.7 1.3 %collective-permute-start.5 = (bf16[2,128,128]{2,1,0:T(8,128)(2,1)S(1)}, bf16[2,128,128]{2,1,0:T(8,128)(2,1)S(1)}, u32[]{:S(2)}, u32[]{:S(2)}) collective-permute-start(bf16[2,128,128]{2,1,0:T(8,128)(2,1)S(1)} %slice.182.up_ref), channel_id=1, source_target_pairs={{1,0},{2,1},{3,2},{4,3},{5,4},{6,5},{7,6},{9,8},{10,9},{11,10},{12... | collective-permute-start | bytes 196616 | tf_op jit(solution)/shard_map/ppermute | solution.py:172
  38.0 1.3 %collective-permute-start.6 = (bf16[2,128,128]{2,1,0:T(8,128)(2,1)S(1)}, bf16[2,128,128]{2,1,0:T(8,128)(2,1)S(1)}, u32[]{:S(2)}, u32[]{:S(2)}) collective-permute-start(bf16[2,128,128]{2,1,0:T(8,128)(2,1)S(1)} %slice.183.down_ref), channel_id=1, source_target_pairs={{0,1},{1,2},{2,3},{3,4},{4,5},{5,6},{6,7},{8,9},{9,10},{10,11},{11... | collective-permute-start | bytes 196616 | tf_op jit(solution)/shard_map/ppermute | solution.py:171
  39.5 0.2 slice_reduce_fusion.8
  39.7 0.3 slice_reduce_fusion.2
  39.9 0.5 fusion.11
  40.4 1.0 %pad_maximum_fusion.1.recv_ref = bf16[8,3,128,128]{3,2,1,0:T(8,128)(2,1)} fusion(bf16[8,1,128,128]{3,2,1,0:T(8,128)(2,1)S(1)} %get-tuple-element.42, bf16[8,1,128,128]{3,2,1,0:T(8,128)(2,1)S(1)} %get-tuple-element.43, bf16[8,1,128,128]{3,2,1,0:T(8,128)(2,1)S(1)} %get-tuple-element.41), kind=kLoop, calls=%fused_computation.10 | loop fusion | flops 786432 | bytes 1572864 | tf_op jit(solution)/shard_map/stack | solution.py:19
  41.4 2.8 %collective-permute-done.6.down_left_ref = bf16[2,128,128]{2,1,0:T(8,128)(2,1)S(1)} collective-permute-done((bf16[2,128,128]{2,1,0:T(8,128)(2,1)S(1)}, bf16[2,128,128]{2,1,0:T(8,128)(2,1)S(1)}, u32[]{:S(2)}, u32[]{:S(2)}) %collective-permute-start.6) | collective-permute-done | bytes 65568 | tf_op jit(solution)/shard_map/ppermute | solution.py:171
  44.2 0.6 %copy-done.5 = bf16[2,128,128]{2,1,0:T(8,128)(2,1)} copy-done((bf16[2,128,128]{2,1,0:T(8,128)(2,1)}, bf16[2,128,128]{2,1,0:T(8,128)(2,1)S(1)}, u32[]{:S(2)}) %copy-start.5) | copy-done | bytes 65560
  44.8 0.2 copy-done.1
  45.0 6.1 %shard_map.55 = bf16[10,2,128,128]{3,2,1,0:T(8,128)(2,1)} custom-call(s32[2]{0:T(128)} %pad_add_fusion.ids, f32[10,128]{1,0:T(8,128)} %q_ref.1, bf16[10,3,128,128]{3,2,1,0:T(8,128)(2,1)} %pad_maximum_fusion.jac_ref, bf16[8,3,128,128]{3,2,1,0:T(8,128)(2,1)} %pad_maximum_fusion.1.recv_ref, bf16[10,2,128,128]{3,2,1,0:T(8,128)(2,1)} %mid_ref.1, ...), custom_call_target="tpu_custom_call" | custom-call | tf_op jit(solution)/shard_map/pallas_call | solution.py:177
  (34 shorter events, 0.5 us)
Async XLA Ops:
  0.0 7.7 %copy-start.6 = (s32[10,3]{0,1:T(4,128)S(1)}, s32[10,3]{0,1:T(4,128)}, u32[]{:S(2)}) copy-start(s32[10,3]{0,1:T(4,128)} %param.11) | copy-start | bytes 364
  0.0 44.2 %collective-permute-start.3 = (bf16[10,2,128,128]{3,2,1,0:T(8,128)(2,1)}, bf16[10,2,128,128]{3,2,1,0:T(8,128)(2,1)S(1)}, u32[]{:S(2)}, u32[]{:S(2)}) collective-permute-start(bf16[10,2,128,128]{3,2,1,0:T(8,128)(2,1)} %mid_ref.1), channel_id=1, source_target_pairs={{0,1},{1,2},{2,3},{3,4},{4,5},{5,6},{6,7},{8,9},{9,10},{10,11},{11... | collective-permute-start | bytes 1966088 | tf_op jit(solution)/shard_map/ppermute | solution.py:135
  1.4 42.8 %collective-permute-start.4 = (bf16[10,2,128,128]{3,2,1,0:T(8,128)(2,1)}, bf16[10,2,128,128]{3,2,1,0:T(8,128)(2,1)}, u32[]{:S(2)}, u32[]{:S(2)}) collective-permute-start(bf16[10,2,128,128]{3,2,1,0:T(8,128)(2,1)} %mid_ref.1), channel_id=1, source_target_pairs={{1,0},{2,1},{3,2},{4,3},{5,4},{6,5},{7,6},{9,8},{10,9},{11,10},{12... | collective-permute-start | bytes 1966088 | tf_op jit(solution)/shard_map/ppermute | solution.py:136
  7.9 0.7 %copy-start.7 = (s32[10]{0:T(128)S(1)}, s32[10]{0:T(128)}, u32[]{:S(2)}) copy-start(s32[10]{0:T(128)} %param.12) | copy-start | bytes 124
  8.7 9.4 %copy-start = (bf16[10,3,128,128]{3,2,1,0:T(8,128)(2,1)S(1)}, bf16[10,3,128,128]{3,2,1,0:T(8,128)(2,1)}, u32[]{:S(2)}) copy-start(bf16[10,3,128,128]{3,2,1,0:T(8,128)(2,1)} %param.10) | copy-start | bytes 2949124
  9.4 27.2 %collective-permute-start = (bf16[3,128,128]{2,1,0:T(8,128)(2,1)}, bf16[3,128,128]{2,1,0:T(8,128)(2,1)S(1)}, u32[]{:S(2)}, u32[]{:S(2)}) collective-permute-start(bf16[3,128,128]{2,1,0:T(8,128)(2,1)} %get-tuple-element.46), channel_id=1, source_target_pairs={{0,8},{8,16},{16,24},{24,32},{32,40},{40,48},{48,56},{56,64},{64,7... | collective-permute-start | bytes 294920 | tf_op jit(solution)/shard_map/ppermute | solution.py:140
  11.3 25.3 %collective-permute-start.1 = (bf16[3,128,128]{2,1,0:T(8,128)(2,1)S(1)}, bf16[3,128,128]{2,1,0:T(8,128)(2,1)S(1)}, u32[]{:S(2)}, u32[]{:S(2)}) collective-permute-start(bf16[3,128,128]{2,1,0:T(8,128)(2,1)S(1)} %get-tuple-element.47), channel_id=1, source_target_pairs={{8,0},{16,8},{24,16},{32,24},{40,32},{48,40},{56,48},{64,56},{72,6... | collective-permute-start | bytes 294920 | tf_op jit(solution)/shard_map/ppermute | solution.py:143
  16.1 23.8 %collective-permute-start.2 = (bf16[8,3,128,128]{3,2,1,0:T(8,128)(2,1)S(1)}, bf16[8,3,128,128]{3,2,1,0:T(8,128)(2,1)S(1)}, u32[]{:S(2)}, u32[]{:S(2)}) collective-permute-start(bf16[8,3,128,128]{3,2,1,0:T(8,128)(2,1)S(1)} %constant_dynamic-slice_fusion), channel_id=1, source_target_pairs={{0,8},{8,16},{16,24},{24,32},{32,40},{40,48},{48,56},{56,64},{64,7... | collective-permute-start | bytes 2359304 | tf_op jit(solution)/shard_map/ppermute | solution.py:159
  36.7 1.3 %copy-start.2 = (bf16[2,128,128]{2,1,0:T(8,128)(2,1)}, bf16[2,128,128]{2,1,0:T(8,128)(2,1)S(1)}, u32[]{:S(2)}) copy-start(bf16[2,128,128]{2,1,0:T(8,128)(2,1)S(1)} %slice.182.up_ref) | copy-start | bytes 196612
  36.7 4.7 %collective-permute-start.5 = (bf16[2,128,128]{2,1,0:T(8,128)(2,1)S(1)}, bf16[2,128,128]{2,1,0:T(8,128)(2,1)S(1)}, u32[]{:S(2)}, u32[]{:S(2)}) collective-permute-start(bf16[2,128,128]{2,1,0:T(8,128)(2,1)S(1)} %slice.182.up_ref), channel_id=1, source_target_pairs={{1,0},{2,1},{3,2},{4,3},{5,4},{6,5},{7,6},{9,8},{10,9},{11,10},{12... | collective-permute-start | bytes 196616 | tf_op jit(solution)/shard_map/ppermute | solution.py:172
  38.0 2.4 %copy-start.3 = (bf16[2,128,128]{2,1,0:T(8,128)(2,1)}, bf16[2,128,128]{2,1,0:T(8,128)(2,1)S(1)}, u32[]{:S(2)}) copy-start(bf16[2,128,128]{2,1,0:T(8,128)(2,1)S(1)} %slice.183.down_ref) | copy-start | bytes 196612
  38.0 6.2 %collective-permute-start.6 = (bf16[2,128,128]{2,1,0:T(8,128)(2,1)S(1)}, bf16[2,128,128]{2,1,0:T(8,128)(2,1)S(1)}, u32[]{:S(2)}, u32[]{:S(2)}) collective-permute-start(bf16[2,128,128]{2,1,0:T(8,128)(2,1)S(1)} %slice.183.down_ref), channel_id=1, source_target_pairs={{0,1},{1,2},{2,3},{3,4},{4,5},{5,6},{6,7},{8,9},{9,10},{10,11},{11... | collective-permute-start | bytes 196616 | tf_op jit(solution)/shard_map/ppermute | solution.py:171
  41.4 2.8 %copy-start.4 = (bf16[2,128,128]{2,1,0:T(8,128)(2,1)}, bf16[2,128,128]{2,1,0:T(8,128)(2,1)S(1)}, u32[]{:S(2)}) copy-start(bf16[2,128,128]{2,1,0:T(8,128)(2,1)S(1)} %collective-permute-done.5.up_right_ref) | copy-start | bytes 196612
  44.2 0.6 %copy-start.5 = (bf16[2,128,128]{2,1,0:T(8,128)(2,1)}, bf16[2,128,128]{2,1,0:T(8,128)(2,1)S(1)}, u32[]{:S(2)}) copy-start(bf16[2,128,128]{2,1,0:T(8,128)(2,1)S(1)} %collective-permute-done.6.down_left_ref) | copy-start | bytes 196612
  44.2 0.9 %copy-start.1 = (bf16[10,2,128,128]{3,2,1,0:T(8,128)(2,1)}, bf16[10,2,128,128]{3,2,1,0:T(8,128)(2,1)S(1)}, u32[]{:S(2)}) copy-start(bf16[10,2,128,128]{3,2,1,0:T(8,128)(2,1)S(1)} %collective-permute-done.3.left_ref) | copy-start | bytes 1966084

commit v11 on v7

--- a/solution.py
+++ b/solution.py
@@ -24,7 +24,7 @@
     window = tile_rows + band_local - 1
 
     def kernel(ids, q_ref, jac_ref, recv_ref, mid_ref, left_ref, right_ref, up_ref, down_ref,
-               up_right_ref, down_left_ref, out_ref, win_ref):
+               up_right_ref, down_left_ref, out_ref, win_ref, spread_ref):
         row_id = ids[0]
         col_id = ids[1]
         first_row = row_id * tile_rows
@@ -86,18 +86,27 @@
                     ],
                     axis=0,
                 )
-                spread = jnp.dot(lhs, rhs, preferred_element_type=jnp.float32).astype(jnp.bfloat16)
-                noise = jnp.where(eye, q_ref[pl.ds(row, 1), :], 0.0)
-                for k in range(band_local):
-                    left_side = spread[:, k * size : (k + 3) * size]
-                    right_side = jnp.concatenate([win_ref[row + k, g] for g in range(3)], axis=1)
-                    total = lax.dot_general(
-                        left_side,
-                        right_side,
-                        (((1,), (1,)), ((), ())),
-                        preferred_element_type=jnp.float32,
-                    )
+                spread_ref[row] = jnp.dot(lhs, rhs, preferred_element_type=jnp.float32).astype(
+                    jnp.bfloat16
+                )
+            for position in range(window):
+                members = [
+                    (position - k, k) for k in range(band_local) if 0 <= position - k < tile_rows
+                ]
+                left_side = jnp.concatenate(
+                    [spread_ref[row, :, k * size : (k + 3) * size] for row, k in members], axis=0
+                )
+                right_side = jnp.concatenate([win_ref[position, g] for g in range(3)], axis=1)
+                product = lax.dot_general(
+                    left_side,
+                    right_side,
+                    (((1,), (1,)), ((), ())),
+                    preferred_element_type=jnp.float32,
+                )
+                for index, (row, k) in enumerate(members):
+                    total = product[index * size : (index + 1) * size]
                     on_diagonal = (low_offset + k == 0).astype(jnp.float32)
+                    noise = jnp.where(eye, q_ref[pl.ds(row, 1), :], 0.0)
                     total = total + noise * on_diagonal
                     if masked:
                         column = first_row + row + low_offset + k
@@ -178,7 +187,10 @@
         out_shape=jax.ShapeDtypeStruct(p_band.shape, p_band.dtype),
         in_specs=[smem] + [vmem] * 10,
         out_specs=vmem,
-        scratch_shapes=[pltpu.VMEM((tile_rows + band_local - 1, 3, tile_size, tile_size), p_band.dtype)],
+        scratch_shapes=[
+            pltpu.VMEM((tile_rows + band_local - 1, 3, tile_size, tile_size), p_band.dtype),
+            pltpu.VMEM((tile_rows, tile_size, (band_local + 2) * tile_size), p_band.dtype),
+        ],
     )(ids, q_var, jacobian, received, p_band, left, right, up, down, up_right, down_left)
 
 

time: 50.9 us -> 49.8 us (0.978)
  the two profiles are of different devices: /device:TPU:158 before, /device:TPU:222 now
where the time goes in v11:
time: 49.8 us; the launch traced here: 49.4 us
  waiting for transfers between devices  18.9 us (38%)
  starting transfers between devices  16.9 us (34%)
  other arithmetic  4.49 us (9%)
  local copies, waits for them, and re-layouts  4.48 us (9%)
  Pallas kernels  4.4 us (9%)
    ppermute x1, waiting for transfers between devices, shards(): lax.ppermute(jnp.concatenate([p_band[-1], meta[None]], axis=0), 'row', [(...  16.1 us
    ppermute x1, starting transfers between devices, shards(): lax.ppermute(p_band, 'col', [(b + 1, b) for b in range(col_count - 1)])  5.43 us
    pallas_call x1, Pallas kernels, shards(): pl.pallas_call(band_kernel(tile_rows, band_local, half_band, grid_tiles,...  4.4 us
    ppermute x1, starting transfers between devices, shards(): lax.ppermute(jnp.concatenate([p_band[0], meta[None]], axis=0), 'row', [(a...  3.64 us
    ppermute x1, waiting for transfers between devices, shards(): lax.ppermute(down, 'col', [(b, b + 1) for b in range(col_count - 1)])  2.77 us
    another operation x2, other arithmetic, assemble(): return jnp.stack(pieces, axis=1)  2.05 us
    ppermute x1, starting transfers between devices, shards(): received_blocks = lax.ppermute(sent, ('row', 'col'), pairs)  1.92 us
    ppermute x1, starting transfers between devices, shards(): lax.ppermute(jnp.concatenate([p_band[-1], meta[None]], axis=0), 'row', [(...  1.91 us
  transfers between devices with their start and end apart: 7, of which 2 were waited for; matrix products, arithmetic and copies ran while one was open for 15% of the time, Pallas kernels for 0%

profile of v11, /device:TPU:222, one launch (start us, length us, event | category | flops | bytes accessed | tf_op | source)
XLA Modules:
  0.0 49.4 jit_solution(4233566310421395777)
XLA Ops:
  0.0 1.4 %collective-permute-start.3 = (bf16[10,2,128,128]{3,2,1,0:T(8,128)(2,1)}, bf16[10,2,128,128]{3,2,1,0:T(8,128)(2,1)S(1)}, u32[]{:S(2)}, u32[]{:S(2)}) collective-permute-start(bf16[10,2,128,128]{3,2,1,0:T(8,128)(2,1)} %mid_ref.1), channel_id=1, source_target_pairs={{0,1},{1,2},{2,3},{3,4},{4,5},{5,6},{6,7},{8,9},{9,10},{10,11},{11... | collective-permute-start | bytes 1966088 | tf_op jit(solution)/shard_map/ppermute | solution.py:143
  1.4 5.4 %collective-permute-start.4 = (bf16[10,2,128,128]{3,2,1,0:T(8,128)(2,1)}, bf16[10,2,128,128]{3,2,1,0:T(8,128)(2,1)}, u32[]{:S(2)}, u32[]{:S(2)}) collective-permute-start(bf16[10,2,128,128]{3,2,1,0:T(8,128)(2,1)} %mid_ref.1), channel_id=1, source_target_pairs={{1,0},{2,1},{3,2},{4,3},{5,4},{6,5},{7,6},{9,8},{10,9},{11,10},{12... | collective-permute-start | bytes 1966088 | tf_op jit(solution)/shard_map/ppermute | solution.py:144
  6.8 0.9 %slice_bitcast_fusion.1 = (bf16[2,128,128]{2,1,0:T(8,128)(2,1)S(1)}, bf16[2,128,128]{2,1,0:T(8,128)(2,1)S(1)}) fusion(bf16[10,2,128,128]{3,2,1,0:T(8,128)(2,1)} %mid_ref.1), kind=kLoop, calls=%fused_computation.41 | loop fusion | bytes 262144 | tf_op jit(solution)/shard_map/squeeze | solution.py:149
  7.8 0.1 copy.7
  8.0 0.6 %copy-done.7 = s32[10]{0:T(128)S(1)} copy-done((s32[10]{0:T(128)S(1)}, s32[10]{0:T(128)}, u32[]{:S(2)}) %copy-start.7) | copy-done | bytes 64
  8.7 0.7 %pad_maximum_fusion.3 = (bf16[3,128,128]{2,1,0:T(8,128)(2,1)}, bf16[3,128,128]{2,1,0:T(8,128)(2,1)S(1)}) fusion(bf16[1,128,128]{2,1,0:T(8,128)(2,1)S(1)} %scatter.9, bf16[2,128,128]{2,1,0:T(8,128)(2,1)S(1)} %get-tuple-element.44, bf16[2,128,128]{2,1,0:T(8,128)(2,1)S(1)} %get-tuple-element.45), kind=kLoop, calls=%fused_computation.39 | loop fusion | flops 98304 | bytes 360448 | tf_op jit(solution)/shard_map/concatenate | solution.py:149
  9.4 1.9 %collective-permute-start = (bf16[3,128,128]{2,1,0:T(8,128)(2,1)}, bf16[3,128,128]{2,1,0:T(8,128)(2,1)S(1)}, u32[]{:S(2)}, u32[]{:S(2)}) collective-permute-start(bf16[3,128,128]{2,1,0:T(8,128)(2,1)} %get-tuple-element.46), channel_id=1, source_target_pairs={{0,8},{8,16},{16,24},{24,32},{32,40},{40,48},{48,56},{56,64},{64,7... | collective-permute-start | bytes 294920 | tf_op jit(solution)/shard_map/ppermute | solution.py:148
  11.3 3.6 %collective-permute-start.1 = (bf16[3,128,128]{2,1,0:T(8,128)(2,1)S(1)}, bf16[3,128,128]{2,1,0:T(8,128)(2,1)S(1)}, u32[]{:S(2)}, u32[]{:S(2)}) collective-permute-start(bf16[3,128,128]{2,1,0:T(8,128)(2,1)S(1)} %get-tuple-element.47), channel_id=1, source_target_pairs={{8,0},{16,8},{24,16},{32,24},{40,32},{48,40},{56,48},{64,56},{72,6... | collective-permute-start | bytes 294920 | tf_op jit(solution)/shard_map/ppermute | solution.py:151
  15.0 1.2 %constant_dynamic-slice_fusion = bf16[8,3,128,128]{3,2,1,0:T(8,128)(2,1)S(1)} fusion(bf16[10,3,128,128]{3,2,1,0:T(8,128)(2,1)} %param.10, s32[]{:T(128)S(6)} %select_n.101), kind=kLoop, calls=%fused_computation.72 | loop fusion | bytes 1572868 | tf_op jit(solution)/shard_map/dynamic_slice | solution.py:160
  16.1 1.9 %collective-permute-start.2 = (bf16[8,3,128,128]{3,2,1,0:T(8,128)(2,1)S(1)}, bf16[8,3,128,128]{3,2,1,0:T(8,128)(2,1)S(1)}, u32[]{:S(2)}, u32[]{:S(2)}) collective-permute-start(bf16[8,3,128,128]{3,2,1,0:T(8,128)(2,1)S(1)} %constant_dynamic-slice_fusion), channel_id=1, source_target_pairs={{0,8},{8,16},{16,24},{24,32},{32,40},{40,48},{48,56},{56,64},{64,7... | collective-permute-start | bytes 2359304 | tf_op jit(solution)/shard_map/ppermute | solution.py:167
  18.1 0.5 %fusion.2 = (bf16[10,1,128,128]{3,2,1,0:T(8,128)(2,1)S(1)}, bf16[10,1,128,128]{3,2,1,0:T(8,128)(2,1)S(1)}, bf16[10,1,128,128]{3,2,1,0:T(8,128)(2,1)S(1)}) fusion(pred[10]{0:T(512)(128)(4,1)S(1)} %get-tuple-element.55, pred[10]{0:T(512)(128)(4,1)S(1)} %get-tuple-element.56, pred[10]{0:T(512)(128)(4,1)S(1)} %get-tuple-element.54, ...), kind=kLoop, calls=%fused_computation.22 | loop fusion | flops 3440640 | bytes 1966170 | tf_op jit(solution)/shard_map/convert_element_type | solution.py:18
  18.7 1.1 %pad_maximum_fusion.jac_ref = bf16[10,3,128,128]{3,2,1,0:T(8,128)(2,1)} fusion(bf16[10,1,128,128]{3,2,1,0:T(8,128)(2,1)S(1)} %get-tuple-element.39, bf16[10,1,128,128]{3,2,1,0:T(8,128)(2,1)S(1)} %get-tuple-element.40, bf16[10,1,128,128]{3,2,1,0:T(8,128)(2,1)S(1)} %get-tuple-element.38), kind=kLoop, calls=%fused_computation | loop fusion | flops 983040 | bytes 1966080 | tf_op jit(solution)/shard_map/stack | solution.py:19
  19.8 0.6 %pad_add_fusion.ids = s32[2]{0:T(128)} fusion(s32[1]{0:T(128)} %bitcast.1, s32[1]{0:T(128)} %bitcast), kind=kLoop, calls=%fused_computation.80 | loop fusion | flops 2 | bytes 16 | tf_op jit(solution)/shard_map/stack | solution.py:182
  20.4 16.1 %collective-permute-done = bf16[3,128,128]{2,1,0:T(8,128)(2,1)S(1)} collective-permute-done((bf16[3,128,128]{2,1,0:T(8,128)(2,1)}, bf16[3,128,128]{2,1,0:T(8,128)(2,1)S(1)}, u32[]{:S(2)}, u32[]{:S(2)}) %collective-permute-start) | collective-permute-done | bytes 98336 | tf_op jit(solution)/shard_map/ppermute | solution.py:148
  36.7 1.3 %collective-permute-start.5 = (bf16[2,128,128]{2,1,0:T(8,128)(2,1)S(1)}, bf16[2,128,128]{2,1,0:T(8,128)(2,1)S(1)}, u32[]{:S(2)}, u32[]{:S(2)}) collective-permute-start(bf16[2,128,128]{2,1,0:T(8,128)(2,1)S(1)} %slice.182.up_ref), channel_id=1, source_target_pairs={{1,0},{2,1},{3,2},{4,3},{5,4},{6,5},{7,6},{9,8},{10,9},{11,10},{12... | collective-permute-start | bytes 196616 | tf_op jit(solution)/shard_map/ppermute | solution.py:180
  38.0 1.3 %collective-permute-start.6 = (bf16[2,128,128]{2,1,0:T(8,128)(2,1)S(1)}, bf16[2,128,128]{2,1,0:T(8,128)(2,1)S(1)}, u32[]{:S(2)}, u32[]{:S(2)}) collective-permute-start(bf16[2,128,128]{2,1,0:T(8,128)(2,1)S(1)} %slice.183.down_ref), channel_id=1, source_target_pairs={{0,1},{1,2},{2,3},{3,4},{4,5},{5,6},{6,7},{8,9},{9,10},{10,11},{11... | collective-permute-start | bytes 196616 | tf_op jit(solution)/shard_map/ppermute | solution.py:179
  39.5 0.2 slice_reduce_fusion.8
  39.7 0.3 slice_reduce_fusion.2
  39.9 0.5 fusion.11
  40.4 1.0 %pad_maximum_fusion.1.recv_ref = bf16[8,3,128,128]{3,2,1,0:T(8,128)(2,1)} fusion(bf16[8,1,128,128]{3,2,1,0:T(8,128)(2,1)S(1)} %get-tuple-element.42, bf16[8,1,128,128]{3,2,1,0:T(8,128)(2,1)S(1)} %get-tuple-element.43, bf16[8,1,128,128]{3,2,1,0:T(8,128)(2,1)S(1)} %get-tuple-element.41), kind=kLoop, calls=%fused_computation.10 | loop fusion | flops 786432 | bytes 1572864 | tf_op jit(solution)/shard_map/stack | solution.py:19
  41.4 2.8 %collective-permute-done.6.down_left_ref = bf16[2,128,128]{2,1,0:T(8,128)(2,1)S(1)} collective-permute-done((bf16[2,128,128]{2,1,0:T(8,128)(2,1)S(1)}, bf16[2,128,128]{2,1,0:T(8,128)(2,1)S(1)}, u32[]{:S(2)}, u32[]{:S(2)}) %collective-permute-start.6) | collective-permute-done | bytes 65568 | tf_op jit(solution)/shard_map/ppermute | solution.py:179
  44.2 0.6 %copy-done.5 = bf16[2,128,128]{2,1,0:T(8,128)(2,1)} copy-done((bf16[2,128,128]{2,1,0:T(8,128)(2,1)}, bf16[2,128,128]{2,1,0:T(8,128)(2,1)S(1)}, u32[]{:S(2)}) %copy-start.5) | copy-done | bytes 65560
  44.8 0.2 copy-done.1
  45.0 4.4 %shard_map.55 = bf16[10,2,128,128]{3,2,1,0:T(8,128)(2,1)} custom-call(s32[2]{0:T(128)} %pad_add_fusion.ids, f32[10,128]{1,0:T(8,128)} %q_ref.1, bf16[10,3,128,128]{3,2,1,0:T(8,128)(2,1)} %pad_maximum_fusion.jac_ref, bf16[8,3,128,128]{3,2,1,0:T(8,128)(2,1)} %pad_maximum_fusion.1.recv_ref, bf16[10,2,128,128]{3,2,1,0:T(8,128)(2,1)} %mid_ref.1, ...), custom_call_target="tpu_custom_call" | custom-call | tf_op jit(solution)/shard_map/pallas_call | solution.py:185
  (34 shorter events, 0.5 us)
Async XLA Ops:
  0.0 7.7 %copy-start.6 = (s32[10,3]{0,1:T(4,128)S(1)}, s32[10,3]{0,1:T(4,128)}, u32[]{:S(2)}) copy-start(s32[10,3]{0,1:T(4,128)} %param.11) | copy-start | bytes 364
  0.0 44.2 %collective-permute-start.3 = (bf16[10,2,128,128]{3,2,1,0:T(8,128)(2,1)}, bf16[10,2,128,128]{3,2,1,0:T(8,128)(2,1)S(1)}, u32[]{:S(2)}, u32[]{:S(2)}) collective-permute-start(bf16[10,2,128,128]{3,2,1,0:T(8,128)(2,1)} %mid_ref.1), channel_id=1, source_target_pairs={{0,1},{1,2},{2,3},{3,4},{4,5},{5,6},{6,7},{8,9},{9,10},{10,11},{11... | collective-permute-start | bytes 1966088 | tf_op jit(solution)/shard_map/ppermute | solution.py:143
  1.4 42.8 %collective-permute-start.4 = (bf16[10,2,128,128]{3,2,1,0:T(8,128)(2,1)}, bf16[10,2,128,128]{3,2,1,0:T(8,128)(2,1)}, u32[]{:S(2)}, u32[]{:S(2)}) collective-permute-start(bf16[10,2,128,128]{3,2,1,0:T(8,128)(2,1)} %mid_ref.1), channel_id=1, source_target_pairs={{1,0},{2,1},{3,2},{4,3},{5,4},{6,5},{7,6},{9,8},{10,9},{11,10},{12... | collective-permute-start | bytes 1966088 | tf_op jit(solution)/shard_map/ppermute | solution.py:144
  7.9 0.7 %copy-start.7 = (s32[10]{0:T(128)S(1)}, s32[10]{0:T(128)}, u32[]{:S(2)}) copy-start(s32[10]{0:T(128)} %param.12) | copy-start | bytes 124
  8.7 9.4 %copy-start = (bf16[10,3,128,128]{3,2,1,0:T(8,128)(2,1)S(1)}, bf16[10,3,128,128]{3,2,1,0:T(8,128)(2,1)}, u32[]{:S(2)}) copy-start(bf16[10,3,128,128]{3,2,1,0:T(8,128)(2,1)} %param.10) | copy-start | bytes 2949124
  9.4 27.2 %collective-permute-start = (bf16[3,128,128]{2,1,0:T(8,128)(2,1)}, bf16[3,128,128]{2,1,0:T(8,128)(2,1)S(1)}, u32[]{:S(2)}, u32[]{:S(2)}) collective-permute-start(bf16[3,128,128]{2,1,0:T(8,128)(2,1)} %get-tuple-element.46), channel_id=1, source_target_pairs={{0,8},{8,16},{16,24},{24,32},{32,40},{40,48},{48,56},{56,64},{64,7... | collective-permute-start | bytes 294920 | tf_op jit(solution)/shard_map/ppermute | solution.py:148
  11.3 25.3 %collective-permute-start.1 = (bf16[3,128,128]{2,1,0:T(8,128)(2,1)S(1)}, bf16[3,128,128]{2,1,0:T(8,128)(2,1)S(1)}, u32[]{:S(2)}, u32[]{:S(2)}) collective-permute-start(bf16[3,128,128]{2,1,0:T(8,128)(2,1)S(1)} %get-tuple-element.47), channel_id=1, source_target_pairs={{8,0},{16,8},{24,16},{32,24},{40,32},{48,40},{56,48},{64,56},{72,6... | collective-permute-start | bytes 294920 | tf_op jit(solution)/shard_map/ppermute | solution.py:151
  16.1 23.8 %collective-permute-start.2 = (bf16[8,3,128,128]{3,2,1,0:T(8,128)(2,1)S(1)}, bf16[8,3,128,128]{3,2,1,0:T(8,128)(2,1)S(1)}, u32[]{:S(2)}, u32[]{:S(2)}) collective-permute-start(bf16[8,3,128,128]{3,2,1,0:T(8,128)(2,1)S(1)} %constant_dynamic-slice_fusion), channel_id=1, source_target_pairs={{0,8},{8,16},{16,24},{24,32},{32,40},{40,48},{48,56},{56,64},{64,7... | collective-permute-start | bytes 2359304 | tf_op jit(solution)/shard_map/ppermute | solution.py:167
  36.7 1.3 %copy-start.2 = (bf16[2,128,128]{2,1,0:T(8,128)(2,1)}, bf16[2,128,128]{2,1,0:T(8,128)(2,1)S(1)}, u32[]{:S(2)}) copy-start(bf16[2,128,128]{2,1,0:T(8,128)(2,1)S(1)} %slice.182.up_ref) | copy-start | bytes 196612
  36.7 4.7 %collective-permute-start.5 = (bf16[2,128,128]{2,1,0:T(8,128)(2,1)S(1)}, bf16[2,128,128]{2,1,0:T(8,128)(2,1)S(1)}, u32[]{:S(2)}, u32[]{:S(2)}) collective-permute-start(bf16[2,128,128]{2,1,0:T(8,128)(2,1)S(1)} %slice.182.up_ref), channel_id=1, source_target_pairs={{1,0},{2,1},{3,2},{4,3},{5,4},{6,5},{7,6},{9,8},{10,9},{11,10},{12... | collective-permute-start | bytes 196616 | tf_op jit(solution)/shard_map/ppermute | solution.py:180
  38.0 2.4 %copy-start.3 = (bf16[2,128,128]{2,1,0:T(8,128)(2,1)}, bf16[2,128,128]{2,1,0:T(8,128)(2,1)S(1)}, u32[]{:S(2)}) copy-start(bf16[2,128,128]{2,1,0:T(8,128)(2,1)S(1)} %slice.183.down_ref) | copy-start | bytes 196612
  38.0 6.2 %collective-permute-start.6 = (bf16[2,128,128]{2,1,0:T(8,128)(2,1)S(1)}, bf16[2,128,128]{2,1,0:T(8,128)(2,1)S(1)}, u32[]{:S(2)}, u32[]{:S(2)}) collective-permute-start(bf16[2,128,128]{2,1,0:T(8,128)(2,1)S(1)} %slice.183.down_ref), channel_id=1, source_target_pairs={{0,1},{1,2},{2,3},{3,4},{4,5},{5,6},{6,7},{8,9},{9,10},{10,11},{11... | collective-permute-start | bytes 196616 | tf_op jit(solution)/shard_map/ppermute | solution.py:179
  41.4 2.8 %copy-start.4 = (bf16[2,128,128]{2,1,0:T(8,128)(2,1)}, bf16[2,128,128]{2,1,0:T(8,128)(2,1)S(1)}, u32[]{:S(2)}) copy-start(bf16[2,128,128]{2,1,0:T(8,128)(2,1)S(1)} %collective-permute-done.5.up_right_ref) | copy-start | bytes 196612
  44.2 0.6 %copy-start.5 = (bf16[2,128,128]{2,1,0:T(8,128)(2,1)}, bf16[2,128,128]{2,1,0:T(8,128)(2,1)S(1)}, u32[]{:S(2)}) copy-start(bf16[2,128,128]{2,1,0:T(8,128)(2,1)S(1)} %collective-permute-done.6.down_left_ref) | copy-start | bytes 196612
  44.2 0.9 %copy-start.1 = (bf16[10,2,128,128]{3,2,1,0:T(8,128)(2,1)}, bf16[10,2,128,128]{3,2,1,0:T(8,128)(2,1)S(1)}, u32[]{:S(2)}) copy-start(bf16[10,2,128,128]{3,2,1,0:T(8,128)(2,1)S(1)} %collective-permute-done.3.left_ref) | copy-start | bytes 1966084

commit v12 on v11

--- a/solution.py
+++ b/solution.py
@@ -24,7 +24,7 @@
     window = tile_rows + band_local - 1
 
     def kernel(ids, q_ref, jac_ref, recv_ref, mid_ref, left_ref, right_ref, up_ref, down_ref,
-               up_right_ref, down_left_ref, out_ref, win_ref, spread_ref):
+               up_right_ref, down_left_ref, out_ref, win_ref, spread_ref, flipped_ref):
         row_id = ids[0]
         col_id = ids[1]
         first_row = row_id * tile_rows
@@ -75,36 +75,39 @@
         )
 
         def body(masked):
+            for ext_row in range(tile_rows + 2):
+                for ext_slot in range(extended + 2):
+                    used = any(
+                        0 <= ext_row - f < tile_rows and 0 <= ext_slot + f - 2 < extended
+                        for f in range(3)
+                    )
+                    if used:
+                        flipped_ref[ext_row, ext_slot] = prior_tile(ext_row, ext_slot, masked).T
             for row in range(tile_rows):
-                lhs = jnp.concatenate([jac_ref[row, f] for f in range(3)], axis=1)
-                rhs = jnp.concatenate(
+                lhs = jnp.concatenate(
                     [
                         jnp.concatenate(
-                            [prior_tile(row + f, u - f + 2, masked) for u in range(extended)], axis=1
+                            [flipped_ref[row + f, u - f + 2] for f in range(3)], axis=1
                         )
-                        for f in range(3)
+                        for u in range(extended)
                     ],
                     axis=0,
                 )
-                spread_ref[row] = jnp.dot(lhs, rhs, preferred_element_type=jnp.float32).astype(
-                    jnp.bfloat16
-                )
+                rhs = jnp.concatenate([jac_ref[row, f] for f in range(3)], axis=1)
+                spread_ref[row] = lax.dot_general(
+                    lhs, rhs, (((1,), (1,)), ((), ())), preferred_element_type=jnp.float32
+                ).astype(jnp.bfloat16)
             for position in range(window):
                 members = [
                     (position - k, k) for k in range(band_local) if 0 <= position - k < tile_rows
                 ]
-                left_side = jnp.concatenate(
-                    [spread_ref[row, :, k * size : (k + 3) * size] for row, k in members], axis=0
+                left_side = jnp.concatenate([win_ref[position, g] for g in range(3)], axis=1)
+                right_side = jnp.concatenate(
+                    [spread_ref[row, k * size : (k + 3) * size, :] for row, k in members], axis=1
                 )
-                right_side = jnp.concatenate([win_ref[position, g] for g in range(3)], axis=1)
-                product = lax.dot_general(
-                    left_side,
-                    right_side,
-                    (((1,), (1,)), ((), ())),
-                    preferred_element_type=jnp.float32,
-                )
+                product = jnp.dot(left_side, right_side, preferred_element_type=jnp.float32)
                 for index, (row, k) in enumerate(members):
-                    total = product[index * size : (index + 1) * size]
+                    total = product[:, index * size : (index + 1) * size].T
                     on_diagonal = (low_offset + k == 0).astype(jnp.float32)
                     noise = jnp.where(eye, q_ref[pl.ds(row, 1), :], 0.0)
                     total = total + noise * on_diagonal
@@ -189,7 +192,8 @@
         out_specs=vmem,
         scratch_shapes=[
             pltpu.VMEM((tile_rows + band_local - 1, 3, tile_size, tile_size), p_band.dtype),
-            pltpu.VMEM((tile_rows, tile_size, (band_local + 2) * tile_size), p_band.dtype),
+            pltpu.VMEM((tile_rows, (band_local + 2) * tile_size, tile_size), p_band.dtype),
+            pltpu.VMEM((tile_rows + 2, band_local + 4, tile_size, tile_size), p_band.dtype),
         ],
     )(ids, q_var, jacobian, received, p_band, left, right, up, down, up_right, down_left)
 

time: 49.8 us -> 50.2 us (level)
  the two profiles are of different devices: /device:TPU:222 before, /device:TPU:478 now
where the time goes in v12:
time: 50.2 us; the launch traced here: 49.8 us
  waiting for transfers between devices  18.9 us (38%)
  starting transfers between devices  16.9 us (34%)
  Pallas kernels  4.73 us (9%)
  other arithmetic  4.49 us (9%)
  local copies, waits for them, and re-layouts  4.48 us (9%)
    ppermute x1, waiting for transfers between devices, shards(): lax.ppermute(jnp.concatenate([p_band[-1], meta[None]], axis=0), 'row', [(...  16.1 us
    ppermute x1, starting transfers between devices, shards(): lax.ppermute(p_band, 'col', [(b + 1, b) for b in range(col_count - 1)])  5.43 us
    pallas_call x1, Pallas kernels, shards(): pl.pallas_call(band_kernel(tile_rows, band_local, half_band, grid_tiles,...  4.73 us
    ppermute x1, starting transfers between devices, shards(): lax.ppermute(jnp.concatenate([p_band[0], meta[None]], axis=0), 'row', [(a...  3.64 us
    ppermute x1, waiting for transfers between devices, shards(): lax.ppermute(down, 'col', [(b, b + 1) for b in range(col_count - 1)])  2.77 us
    another operation x2, other arithmetic, assemble(): return jnp.stack(pieces, axis=1)  2.05 us
    ppermute x1, starting transfers between devices, shards(): received_blocks = lax.ppermute(sent, ('row', 'col'), pairs)  1.92 us
    ppermute x1, starting transfers between devices, shards(): lax.ppermute(jnp.concatenate([p_band[-1], meta[None]], axis=0), 'row', [(...  1.91 us
  transfers between devices with their start and end apart: 7, of which 2 were waited for; matrix products, arithmetic and copies ran while one was open for 15% of the time, Pallas kernels for 0%

profile of v12, /device:TPU:478, one launch (start us, length us, event | category | flops | bytes accessed | tf_op | source)
XLA Modules:
  0.0 49.8 jit_solution(16376032283862020892)
XLA Ops:
  0.0 1.4 %collective-permute-start.3 = (bf16[10,2,128,128]{3,2,1,0:T(8,128)(2,1)}, bf16[10,2,128,128]{3,2,1,0:T(8,128)(2,1)S(1)}, u32[]{:S(2)}, u32[]{:S(2)}) collective-permute-start(bf16[10,2,128,128]{3,2,1,0:T(8,128)(2,1)} %mid_ref.1), channel_id=1, source_target_pairs={{0,1},{1,2},{2,3},{3,4},{4,5},{5,6},{6,7},{8,9},{9,10},{10,11},{11... | collective-permute-start | bytes 1966088 | tf_op jit(solution)/shard_map/ppermute | solution.py:146
  1.4 5.4 %collective-permute-start.4 = (bf16[10,2,128,128]{3,2,1,0:T(8,128)(2,1)}, bf16[10,2,128,128]{3,2,1,0:T(8,128)(2,1)}, u32[]{:S(2)}, u32[]{:S(2)}) collective-permute-start(bf16[10,2,128,128]{3,2,1,0:T(8,128)(2,1)} %mid_ref.1), channel_id=1, source_target_pairs={{1,0},{2,1},{3,2},{4,3},{5,4},{6,5},{7,6},{9,8},{10,9},{11,10},{12... | collective-permute-start | bytes 1966088 | tf_op jit(solution)/shard_map/ppermute | solution.py:147
  6.8 0.9 %slice_bitcast_fusion.1 = (bf16[2,128,128]{2,1,0:T(8,128)(2,1)S(1)}, bf16[2,128,128]{2,1,0:T(8,128)(2,1)S(1)}) fusion(bf16[10,2,128,128]{3,2,1,0:T(8,128)(2,1)} %mid_ref.1), kind=kLoop, calls=%fused_computation.41 | loop fusion | bytes 262144 | tf_op jit(solution)/shard_map/squeeze | solution.py:152
  7.8 0.1 copy.7
  8.0 0.6 %copy-done.7 = s32[10]{0:T(128)S(1)} copy-done((s32[10]{0:T(128)S(1)}, s32[10]{0:T(128)}, u32[]{:S(2)}) %copy-start.7) | copy-done | bytes 64
  8.7 0.7 %pad_maximum_fusion.3 = (bf16[3,128,128]{2,1,0:T(8,128)(2,1)}, bf16[3,128,128]{2,1,0:T(8,128)(2,1)S(1)}) fusion(bf16[1,128,128]{2,1,0:T(8,128)(2,1)S(1)} %scatter.9, bf16[2,128,128]{2,1,0:T(8,128)(2,1)S(1)} %get-tuple-element.44, bf16[2,128,128]{2,1,0:T(8,128)(2,1)S(1)} %get-tuple-element.45), kind=kLoop, calls=%fused_computation.39 | loop fusion | flops 98304 | bytes 360448 | tf_op jit(solution)/shard_map/concatenate | solution.py:152
  9.4 1.9 %collective-permute-start = (bf16[3,128,128]{2,1,0:T(8,128)(2,1)}, bf16[3,128,128]{2,1,0:T(8,128)(2,1)S(1)}, u32[]{:S(2)}, u32[]{:S(2)}) collective-permute-start(bf16[3,128,128]{2,1,0:T(8,128)(2,1)} %get-tuple-element.46), channel_id=1, source_target_pairs={{0,8},{8,16},{16,24},{24,32},{32,40},{40,48},{48,56},{56,64},{64,7... | collective-permute-start | bytes 294920 | tf_op jit(solution)/shard_map/ppermute | solution.py:151
  11.3 3.6 %collective-permute-start.1 = (bf16[3,128,128]{2,1,0:T(8,128)(2,1)S(1)}, bf16[3,128,128]{2,1,0:T(8,128)(2,1)S(1)}, u32[]{:S(2)}, u32[]{:S(2)}) collective-permute-start(bf16[3,128,128]{2,1,0:T(8,128)(2,1)S(1)} %get-tuple-element.47), channel_id=1, source_target_pairs={{8,0},{16,8},{24,16},{32,24},{40,32},{48,40},{56,48},{64,56},{72,6... | collective-permute-start | bytes 294920 | tf_op jit(solution)/shard_map/ppermute | solution.py:154
  15.0 1.2 %constant_dynamic-slice_fusion = bf16[8,3,128,128]{3,2,1,0:T(8,128)(2,1)S(1)} fusion(bf16[10,3,128,128]{3,2,1,0:T(8,128)(2,1)} %param.10, s32[]{:T(128)S(6)} %select_n.101), kind=kLoop, calls=%fused_computation.72 | loop fusion | bytes 1572868 | tf_op jit(solution)/shard_map/dynamic_slice | solution.py:163
  16.1 1.9 %collective-permute-start.2 = (bf16[8,3,128,128]{3,2,1,0:T(8,128)(2,1)S(1)}, bf16[8,3,128,128]{3,2,1,0:T(8,128)(2,1)S(1)}, u32[]{:S(2)}, u32[]{:S(2)}) collective-permute-start(bf16[8,3,128,128]{3,2,1,0:T(8,128)(2,1)S(1)} %constant_dynamic-slice_fusion), channel_id=1, source_target_pairs={{0,8},{8,16},{16,24},{24,32},{32,40},{40,48},{48,56},{56,64},{64,7... | collective-permute-start | bytes 2359304 | tf_op jit(solution)/shard_map/ppermute | solution.py:170
  18.1 0.5 %fusion.2 = (bf16[10,1,128,128]{3,2,1,0:T(8,128)(2,1)S(1)}, bf16[10,1,128,128]{3,2,1,0:T(8,128)(2,1)S(1)}, bf16[10,1,128,128]{3,2,1,0:T(8,128)(2,1)S(1)}) fusion(pred[10]{0:T(512)(128)(4,1)S(1)} %get-tuple-element.55, pred[10]{0:T(512)(128)(4,1)S(1)} %get-tuple-element.56, pred[10]{0:T(512)(128)(4,1)S(1)} %get-tuple-element.54, ...), kind=kLoop, calls=%fused_computation.22 | loop fusion | flops 3440640 | bytes 1966170 | tf_op jit(solution)/shard_map/convert_element_type | solution.py:18
  18.7 1.1 %pad_maximum_fusion.jac_ref = bf16[10,3,128,128]{3,2,1,0:T(8,128)(2,1)} fusion(bf16[10,1,128,128]{3,2,1,0:T(8,128)(2,1)S(1)} %get-tuple-element.39, bf16[10,1,128,128]{3,2,1,0:T(8,128)(2,1)S(1)} %get-tuple-element.40, bf16[10,1,128,128]{3,2,1,0:T(8,128)(2,1)S(1)} %get-tuple-element.38), kind=kLoop, calls=%fused_computation | loop fusion | flops 983040 | bytes 1966080 | tf_op jit(solution)/shard_map/stack | solution.py:19
  19.8 0.6 %pad_add_fusion.ids = s32[2]{0:T(128)} fusion(s32[1]{0:T(128)} %bitcast.1, s32[1]{0:T(128)} %bitcast), kind=kLoop, calls=%fused_computation.80 | loop fusion | flops 2 | bytes 16 | tf_op jit(solution)/shard_map/stack | solution.py:185
  20.4 16.1 %collective-permute-done = bf16[3,128,128]{2,1,0:T(8,128)(2,1)S(1)} collective-permute-done((bf16[3,128,128]{2,1,0:T(8,128)(2,1)}, bf16[3,128,128]{2,1,0:T(8,128)(2,1)S(1)}, u32[]{:S(2)}, u32[]{:S(2)}) %collective-permute-start) | collective-permute-done | bytes 98336 | tf_op jit(solution)/shard_map/ppermute | solution.py:151
  36.7 1.3 %collective-permute-start.5 = (bf16[2,128,128]{2,1,0:T(8,128)(2,1)S(1)}, bf16[2,128,128]{2,1,0:T(8,128)(2,1)S(1)}, u32[]{:S(2)}, u32[]{:S(2)}) collective-permute-start(bf16[2,128,128]{2,1,0:T(8,128)(2,1)S(1)} %slice.182.up_ref), channel_id=1, source_target_pairs={{1,0},{2,1},{3,2},{4,3},{5,4},{6,5},{7,6},{9,8},{10,9},{11,10},{12... | collective-permute-start | bytes 196616 | tf_op jit(solution)/shard_map/ppermute | solution.py:183
  38.0 1.3 %collective-permute-start.6 = (bf16[2,128,128]{2,1,0:T(8,128)(2,1)S(1)}, bf16[2,128,128]{2,1,0:T(8,128)(2,1)S(1)}, u32[]{:S(2)}, u32[]{:S(2)}) collective-permute-start(bf16[2,128,128]{2,1,0:T(8,128)(2,1)S(1)} %slice.183.down_ref), channel_id=1, source_target_pairs={{0,1},{1,2},{2,3},{3,4},{4,5},{5,6},{6,7},{8,9},{9,10},{10,11},{11... | collective-permute-start | bytes 196616 | tf_op jit(solution)/shard_map/ppermute | solution.py:182
  39.5 0.2 slice_reduce_fusion.8
  39.7 0.3 slice_reduce_fusion.2
  39.9 0.5 fusion.11
  40.4 1.0 %pad_maximum_fusion.1.recv_ref = bf16[8,3,128,128]{3,2,1,0:T(8,128)(2,1)} fusion(bf16[8,1,128,128]{3,2,1,0:T(8,128)(2,1)S(1)} %get-tuple-element.42, bf16[8,1,128,128]{3,2,1,0:T(8,128)(2,1)S(1)} %get-tuple-element.43, bf16[8,1,128,128]{3,2,1,0:T(8,128)(2,1)S(1)} %get-tuple-element.41), kind=kLoop, calls=%fused_computation.10 | loop fusion | flops 786432 | bytes 1572864 | tf_op jit(solution)/shard_map/stack | solution.py:19
  41.4 2.8 %collective-permute-done.6.down_left_ref = bf16[2,128,128]{2,1,0:T(8,128)(2,1)S(1)} collective-permute-done((bf16[2,128,128]{2,1,0:T(8,128)(2,1)S(1)}, bf16[2,128,128]{2,1,0:T(8,128)(2,1)S(1)}, u32[]{:S(2)}, u32[]{:S(2)}) %collective-permute-start.6) | collective-permute-done | bytes 65568 | tf_op jit(solution)/shard_map/ppermute | solution.py:182
  44.2 0.6 %copy-done.5 = bf16[2,128,128]{2,1,0:T(8,128)(2,1)} copy-done((bf16[2,128,128]{2,1,0:T(8,128)(2,1)}, bf16[2,128,128]{2,1,0:T(8,128)(2,1)S(1)}, u32[]{:S(2)}) %copy-start.5) | copy-done | bytes 65560
  44.8 0.2 copy-done.1
  45.0 4.7 %shard_map.55 = bf16[10,2,128,128]{3,2,1,0:T(8,128)(2,1)} custom-call(s32[2]{0:T(128)} %pad_add_fusion.ids, f32[10,128]{1,0:T(8,128)} %q_ref.1, bf16[10,3,128,128]{3,2,1,0:T(8,128)(2,1)} %pad_maximum_fusion.jac_ref, bf16[8,3,128,128]{3,2,1,0:T(8,128)(2,1)} %pad_maximum_fusion.1.recv_ref, bf16[10,2,128,128]{3,2,1,0:T(8,128)(2,1)} %mid_ref.1, ...), custom_call_target="tpu_custom_call" | custom-call | tf_op jit(solution)/shard_map/pallas_call | solution.py:188
  (34 shorter events, 0.5 us)
Async XLA Ops:
  0.0 7.7 %copy-start.6 = (s32[10,3]{0,1:T(4,128)S(1)}, s32[10,3]{0,1:T(4,128)}, u32[]{:S(2)}) copy-start(s32[10,3]{0,1:T(4,128)} %param.11) | copy-start | bytes 364
  0.0 44.2 %collective-permute-start.3 = (bf16[10,2,128,128]{3,2,1,0:T(8,128)(2,1)}, bf16[10,2,128,128]{3,2,1,0:T(8,128)(2,1)S(1)}, u32[]{:S(2)}, u32[]{:S(2)}) collective-permute-start(bf16[10,2,128,128]{3,2,1,0:T(8,128)(2,1)} %mid_ref.1), channel_id=1, source_target_pairs={{0,1},{1,2},{2,3},{3,4},{4,5},{5,6},{6,7},{8,9},{9,10},{10,11},{11... | collective-permute-start | bytes 1966088 | tf_op jit(solution)/shard_map/ppermute | solution.py:146
  1.4 42.8 %collective-permute-start.4 = (bf16[10,2,128,128]{3,2,1,0:T(8,128)(2,1)}, bf16[10,2,128,128]{3,2,1,0:T(8,128)(2,1)}, u32[]{:S(2)}, u32[]{:S(2)}) collective-permute-start(bf16[10,2,128,128]{3,2,1,0:T(8,128)(2,1)} %mid_ref.1), channel_id=1, source_target_pairs={{1,0},{2,1},{3,2},{4,3},{5,4},{6,5},{7,6},{9,8},{10,9},{11,10},{12... | collective-permute-start | bytes 1966088 | tf_op jit(solution)/shard_map/ppermute | solution.py:147
  7.9 0.7 %copy-start.7 = (s32[10]{0:T(128)S(1)}, s32[10]{0:T(128)}, u32[]{:S(2)}) copy-start(s32[10]{0:T(128)} %param.12) | copy-start | bytes 124
  8.7 9.4 %copy-start = (bf16[10,3,128,128]{3,2,1,0:T(8,128)(2,1)S(1)}, bf16[10,3,128,128]{3,2,1,0:T(8,128)(2,1)}, u32[]{:S(2)}) copy-start(bf16[10,3,128,128]{3,2,1,0:T(8,128)(2,1)} %param.10) | copy-start | bytes 2949124
  9.4 27.2 %collective-permute-start = (bf16[3,128,128]{2,1,0:T(8,128)(2,1)}, bf16[3,128,128]{2,1,0:T(8,128)(2,1)S(1)}, u32[]{:S(2)}, u32[]{:S(2)}) collective-permute-start(bf16[3,128,128]{2,1,0:T(8,128)(2,1)} %get-tuple-element.46), channel_id=1, source_target_pairs={{0,8},{8,16},{16,24},{24,32},{32,40},{40,48},{48,56},{56,64},{64,7... | collective-permute-start | bytes 294920 | tf_op jit(solution)/shard_map/ppermute | solution.py:151
  11.3 25.3 %collective-permute-start.1 = (bf16[3,128,128]{2,1,0:T(8,128)(2,1)S(1)}, bf16[3,128,128]{2,1,0:T(8,128)(2,1)S(1)}, u32[]{:S(2)}, u32[]{:S(2)}) collective-permute-start(bf16[3,128,128]{2,1,0:T(8,128)(2,1)S(1)} %get-tuple-element.47), channel_id=1, source_target_pairs={{8,0},{16,8},{24,16},{32,24},{40,32},{48,40},{56,48},{64,56},{72,6... | collective-permute-start | bytes 294920 | tf_op jit(solution)/shard_map/ppermute | solution.py:154
  16.1 23.8 %collective-permute-start.2 = (bf16[8,3,128,128]{3,2,1,0:T(8,128)(2,1)S(1)}, bf16[8,3,128,128]{3,2,1,0:T(8,128)(2,1)S(1)}, u32[]{:S(2)}, u32[]{:S(2)}) collective-permute-start(bf16[8,3,128,128]{3,2,1,0:T(8,128)(2,1)S(1)} %constant_dynamic-slice_fusion), channel_id=1, source_target_pairs={{0,8},{8,16},{16,24},{24,32},{32,40},{40,48},{48,56},{56,64},{64,7... | collective-permute-start | bytes 2359304 | tf_op jit(solution)/shard_map/ppermute | solution.py:170
  36.7 1.3 %copy-start.2 = (bf16[2,128,128]{2,1,0:T(8,128)(2,1)}, bf16[2,128,128]{2,1,0:T(8,128)(2,1)S(1)}, u32[]{:S(2)}) copy-start(bf16[2,128,128]{2,1,0:T(8,128)(2,1)S(1)} %slice.182.up_ref) | copy-start | bytes 196612
  36.7 4.7 %collective-permute-start.5 = (bf16[2,128,128]{2,1,0:T(8,128)(2,1)S(1)}, bf16[2,128,128]{2,1,0:T(8,128)(2,1)S(1)}, u32[]{:S(2)}, u32[]{:S(2)}) collective-permute-start(bf16[2,128,128]{2,1,0:T(8,128)(2,1)S(1)} %slice.182.up_ref), channel_id=1, source_target_pairs={{1,0},{2,1},{3,2},{4,3},{5,4},{6,5},{7,6},{9,8},{10,9},{11,10},{12... | collective-permute-start | bytes 196616 | tf_op jit(solution)/shard_map/ppermute | solution.py:183
  38.0 2.4 %copy-start.3 = (bf16[2,128,128]{2,1,0:T(8,128)(2,1)}, bf16[2,128,128]{2,1,0:T(8,128)(2,1)S(1)}, u32[]{:S(2)}) copy-start(bf16[2,128,128]{2,1,0:T(8,128)(2,1)S(1)} %slice.183.down_ref) | copy-start | bytes 196612
  38.0 6.2 %collective-permute-start.6 = (bf16[2,128,128]{2,1,0:T(8,128)(2,1)S(1)}, bf16[2,128,128]{2,1,0:T(8,128)(2,1)S(1)}, u32[]{:S(2)}, u32[]{:S(2)}) collective-permute-start(bf16[2,128,128]{2,1,0:T(8,128)(2,1)S(1)} %slice.183.down_ref), channel_id=1, source_target_pairs={{0,1},{1,2},{2,3},{3,4},{4,5},{5,6},{6,7},{8,9},{9,10},{10,11},{11... | collective-permute-start | bytes 196616 | tf_op jit(solution)/shard_map/ppermute | solution.py:182
  41.4 2.8 %copy-start.4 = (bf16[2,128,128]{2,1,0:T(8,128)(2,1)}, bf16[2,128,128]{2,1,0:T(8,128)(2,1)S(1)}, u32[]{:S(2)}) copy-start(bf16[2,128,128]{2,1,0:T(8,128)(2,1)S(1)} %collective-permute-done.5.up_right_ref) | copy-start | bytes 196612
  44.2 0.6 %copy-start.5 = (bf16[2,128,128]{2,1,0:T(8,128)(2,1)}, bf16[2,128,128]{2,1,0:T(8,128)(2,1)S(1)}, u32[]{:S(2)}) copy-start(bf16[2,128,128]{2,1,0:T(8,128)(2,1)S(1)} %collective-permute-done.6.down_left_ref) | copy-start | bytes 196612
  44.2 0.9 %copy-start.1 = (bf16[10,2,128,128]{3,2,1,0:T(8,128)(2,1)}, bf16[10,2,128,128]{3,2,1,0:T(8,128)(2,1)S(1)}, u32[]{:S(2)}) copy-start(bf16[10,2,128,128]{3,2,1,0:T(8,128)(2,1)S(1)} %collective-permute-done.3.left_ref) | copy-start | bytes 1966084

commit v13 on v12

--- a/solution.py
+++ b/solution.py
@@ -94,20 +94,29 @@
                     axis=0,
                 )
                 rhs = jnp.concatenate([jac_ref[row, f] for f in range(3)], axis=1)
-                spread_ref[row] = lax.dot_general(
+                flipped_spread = lax.dot_general(
                     lhs, rhs, (((1,), (1,)), ((), ())), preferred_element_type=jnp.float32
                 ).astype(jnp.bfloat16)
+                for u in range(extended):
+                    spread_ref[row, :, u * size : (u + 1) * size] = flipped_spread[
+                        u * size : (u + 1) * size
+                    ].T
             for position in range(window):
                 members = [
                     (position - k, k) for k in range(band_local) if 0 <= position - k < tile_rows
                 ]
-                left_side = jnp.concatenate([win_ref[position, g] for g in range(3)], axis=1)
-                right_side = jnp.concatenate(
-                    [spread_ref[row, k * size : (k + 3) * size, :] for row, k in members], axis=1
+                left_side = jnp.concatenate(
+                    [spread_ref[row, :, k * size : (k + 3) * size] for row, k in members], axis=0
                 )
-                product = jnp.dot(left_side, right_side, preferred_element_type=jnp.float32)
+                right_side = jnp.concatenate([win_ref[position, g] for g in range(3)], axis=1)
+                product = lax.dot_general(
+                    left_side,
+                    right_side,
+                    (((1,), (1,)), ((), ())),
+                    preferred_element_type=jnp.float32,
+                )
                 for index, (row, k) in enumerate(members):
-                    total = product[:, index * size : (index + 1) * size].T
+                    total = product[index * size : (index + 1) * size]
                     on_diagonal = (low_offset + k == 0).astype(jnp.float32)
                     noise = jnp.where(eye, q_ref[pl.ds(row, 1), :], 0.0)
                     total = total + noise * on_diagonal
@@ -192,7 +201,7 @@
         out_specs=vmem,
         scratch_shapes=[
             pltpu.VMEM((tile_rows + band_local - 1, 3, tile_size, tile_size), p_band.dtype),
-            pltpu.VMEM((tile_rows, (band_local + 2) * tile_size, tile_size), p_band.dtype),
+            pltpu.VMEM((tile_rows, tile_size, (band_local + 2) * tile_size), p_band.dtype),
             pltpu.VMEM((tile_rows + 2, band_local + 4, tile_size, tile_size), p_band.dtype),
         ],
     )(ids, q_var, jacobian, received, p_band, left, right, up, down, up_right, down_left)

time: 50.2 us -> 50.2 us (level)
  no operation moved by 1% of the time
where the time goes in v13:
time: 50.2 us; the launch traced here: 49.8 us
  waiting for transfers between devices  18.9 us (38%)
  starting transfers between devices  16.9 us (34%)
  Pallas kernels  4.8 us (10%)
  other arithmetic  4.49 us (9%)
  local copies, waits for them, and re-layouts  4.48 us (9%)
    ppermute x1, waiting for transfers between devices, shards(): lax.ppermute(jnp.concatenate([p_band[-1], meta[None]], axis=0), 'row', [(...  16.1 us
    ppermute x1, starting transfers between devices, shards(): lax.ppermute(p_band, 'col', [(b + 1, b) for b in range(col_count - 1)])  5.43 us
    pallas_call x1, Pallas kernels, shards(): pl.pallas_call(band_kernel(tile_rows, band_local, half_band, grid_tiles,...  4.8 us
    ppermute x1, starting transfers between devices, shards(): lax.ppermute(jnp.concatenate([p_band[0], meta[None]], axis=0), 'row', [(a...  3.64 us
    ppermute x1, waiting for transfers between devices, shards(): lax.ppermute(down, 'col', [(b, b + 1) for b in range(col_count - 1)])  2.77 us
    another operation x2, other arithmetic, assemble(): return jnp.stack(pieces, axis=1)  2.05 us
    ppermute x1, starting transfers between devices, shards(): received_blocks = lax.ppermute(sent, ('row', 'col'), pairs)  1.92 us
    ppermute x1, starting transfers between devices, shards(): lax.ppermute(jnp.concatenate([p_band[-1], meta[None]], axis=0), 'row', [(...  1.91 us
  transfers between devices with their start and end apart: 7, of which 2 were waited for; matrix products, arithmetic and copies ran while one was open for 15% of the time, Pallas kernels for 0%

profile of v13, /device:TPU:478, one launch (start us, length us, event | category | flops | bytes accessed | tf_op | source)
XLA Modules:
  0.0 49.8 jit_solution(17477730305948327738)
XLA Ops:
  0.0 1.4 %collective-permute-start.3 = (bf16[10,2,128,128]{3,2,1,0:T(8,128)(2,1)}, bf16[10,2,128,128]{3,2,1,0:T(8,128)(2,1)S(1)}, u32[]{:S(2)}, u32[]{:S(2)}) collective-permute-start(bf16[10,2,128,128]{3,2,1,0:T(8,128)(2,1)} %mid_ref.1), channel_id=1, source_target_pairs={{0,1},{1,2},{2,3},{3,4},{4,5},{5,6},{6,7},{8,9},{9,10},{10,11},{11... | collective-permute-start | bytes 1966088 | tf_op jit(solution)/shard_map/ppermute | solution.py:155
  1.4 5.4 %collective-permute-start.4 = (bf16[10,2,128,128]{3,2,1,0:T(8,128)(2,1)}, bf16[10,2,128,128]{3,2,1,0:T(8,128)(2,1)}, u32[]{:S(2)}, u32[]{:S(2)}) collective-permute-start(bf16[10,2,128,128]{3,2,1,0:T(8,128)(2,1)} %mid_ref.1), channel_id=1, source_target_pairs={{1,0},{2,1},{3,2},{4,3},{5,4},{6,5},{7,6},{9,8},{10,9},{11,10},{12... | collective-permute-start | bytes 1966088 | tf_op jit(solution)/shard_map/ppermute | solution.py:156
  6.8 0.9 %slice_bitcast_fusion.1 = (bf16[2,128,128]{2,1,0:T(8,128)(2,1)S(1)}, bf16[2,128,128]{2,1,0:T(8,128)(2,1)S(1)}) fusion(bf16[10,2,128,128]{3,2,1,0:T(8,128)(2,1)} %mid_ref.1), kind=kLoop, calls=%fused_computation.41 | loop fusion | bytes 262144 | tf_op jit(solution)/shard_map/squeeze | solution.py:161
  7.8 0.1 copy.7
  8.0 0.6 %copy-done.7 = s32[10]{0:T(128)S(1)} copy-done((s32[10]{0:T(128)S(1)}, s32[10]{0:T(128)}, u32[]{:S(2)}) %copy-start.7) | copy-done | bytes 64
  8.7 0.7 %pad_maximum_fusion.3 = (bf16[3,128,128]{2,1,0:T(8,128)(2,1)}, bf16[3,128,128]{2,1,0:T(8,128)(2,1)S(1)}) fusion(bf16[1,128,128]{2,1,0:T(8,128)(2,1)S(1)} %scatter.9, bf16[2,128,128]{2,1,0:T(8,128)(2,1)S(1)} %get-tuple-element.44, bf16[2,128,128]{2,1,0:T(8,128)(2,1)S(1)} %get-tuple-element.45), kind=kLoop, calls=%fused_computation.39 | loop fusion | flops 98304 | bytes 360448 | tf_op jit(solution)/shard_map/concatenate | solution.py:161
  9.4 1.9 %collective-permute-start = (bf16[3,128,128]{2,1,0:T(8,128)(2,1)}, bf16[3,128,128]{2,1,0:T(8,128)(2,1)S(1)}, u32[]{:S(2)}, u32[]{:S(2)}) collective-permute-start(bf16[3,128,128]{2,1,0:T(8,128)(2,1)} %get-tuple-element.46), channel_id=1, source_target_pairs={{0,8},{8,16},{16,24},{24,32},{32,40},{40,48},{48,56},{56,64},{64,7... | collective-permute-start | bytes 294920 | tf_op jit(solution)/shard_map/ppermute | solution.py:160
  11.3 3.6 %collective-permute-start.1 = (bf16[3,128,128]{2,1,0:T(8,128)(2,1)S(1)}, bf16[3,128,128]{2,1,0:T(8,128)(2,1)S(1)}, u32[]{:S(2)}, u32[]{:S(2)}) collective-permute-start(bf16[3,128,128]{2,1,0:T(8,128)(2,1)S(1)} %get-tuple-element.47), channel_id=1, source_target_pairs={{8,0},{16,8},{24,16},{32,24},{40,32},{48,40},{56,48},{64,56},{72,6... | collective-permute-start | bytes 294920 | tf_op jit(solution)/shard_map/ppermute | solution.py:163
  15.0 1.2 %constant_dynamic-slice_fusion = bf16[8,3,128,128]{3,2,1,0:T(8,128)(2,1)S(1)} fusion(bf16[10,3,128,128]{3,2,1,0:T(8,128)(2,1)} %param.10, s32[]{:T(128)S(6)} %select_n.101), kind=kLoop, calls=%fused_computation.72 | loop fusion | bytes 1572868 | tf_op jit(solution)/shard_map/dynamic_slice | solution.py:172
  16.1 1.9 %collective-permute-start.2 = (bf16[8,3,128,128]{3,2,1,0:T(8,128)(2,1)S(1)}, bf16[8,3,128,128]{3,2,1,0:T(8,128)(2,1)S(1)}, u32[]{:S(2)}, u32[]{:S(2)}) collective-permute-start(bf16[8,3,128,128]{3,2,1,0:T(8,128)(2,1)S(1)} %constant_dynamic-slice_fusion), channel_id=1, source_target_pairs={{0,8},{8,16},{16,24},{24,32},{32,40},{40,48},{48,56},{56,64},{64,7... | collective-permute-start | bytes 2359304 | tf_op jit(solution)/shard_map/ppermute | solution.py:179
  18.1 0.5 %fusion.2 = (bf16[10,1,128,128]{3,2,1,0:T(8,128)(2,1)S(1)}, bf16[10,1,128,128]{3,2,1,0:T(8,128)(2,1)S(1)}, bf16[10,1,128,128]{3,2,1,0:T(8,128)(2,1)S(1)}) fusion(pred[10]{0:T(512)(128)(4,1)S(1)} %get-tuple-element.55, pred[10]{0:T(512)(128)(4,1)S(1)} %get-tuple-element.56, pred[10]{0:T(512)(128)(4,1)S(1)} %get-tuple-element.54, ...), kind=kLoop, calls=%fused_computation.22 | loop fusion | flops 3440640 | bytes 1966170 | tf_op jit(solution)/shard_map/convert_element_type | solution.py:18
  18.7 1.1 %pad_maximum_fusion.jac_ref = bf16[10,3,128,128]{3,2,1,0:T(8,128)(2,1)} fusion(bf16[10,1,128,128]{3,2,1,0:T(8,128)(2,1)S(1)} %get-tuple-element.39, bf16[10,1,128,128]{3,2,1,0:T(8,128)(2,1)S(1)} %get-tuple-element.40, bf16[10,1,128,128]{3,2,1,0:T(8,128)(2,1)S(1)} %get-tuple-element.38), kind=kLoop, calls=%fused_computation | loop fusion | flops 983040 | bytes 1966080 | tf_op jit(solution)/shard_map/stack | solution.py:19
  19.8 0.6 %pad_add_fusion.ids = s32[2]{0:T(128)} fusion(s32[1]{0:T(128)} %bitcast.1, s32[1]{0:T(128)} %bitcast), kind=kLoop, calls=%fused_computation.80 | loop fusion | flops 2 | bytes 16 | tf_op jit(solution)/shard_map/stack | solution.py:194
  20.4 16.1 %collective-permute-done = bf16[3,128,128]{2,1,0:T(8,128)(2,1)S(1)} collective-permute-done((bf16[3,128,128]{2,1,0:T(8,128)(2,1)}, bf16[3,128,128]{2,1,0:T(8,128)(2,1)S(1)}, u32[]{:S(2)}, u32[]{:S(2)}) %collective-permute-start) | collective-permute-done | bytes 98336 | tf_op jit(solution)/shard_map/ppermute | solution.py:160
  36.7 1.3 %collective-permute-start.5 = (bf16[2,128,128]{2,1,0:T(8,128)(2,1)S(1)}, bf16[2,128,128]{2,1,0:T(8,128)(2,1)S(1)}, u32[]{:S(2)}, u32[]{:S(2)}) collective-permute-start(bf16[2,128,128]{2,1,0:T(8,128)(2,1)S(1)} %slice.182.up_ref), channel_id=1, source_target_pairs={{1,0},{2,1},{3,2},{4,3},{5,4},{6,5},{7,6},{9,8},{10,9},{11,10},{12... | collective-permute-start | bytes 196616 | tf_op jit(solution)/shard_map/ppermute | solution.py:192
  38.0 1.3 %collective-permute-start.6 = (bf16[2,128,128]{2,1,0:T(8,128)(2,1)S(1)}, bf16[2,128,128]{2,1,0:T(8,128)(2,1)S(1)}, u32[]{:S(2)}, u32[]{:S(2)}) collective-permute-start(bf16[2,128,128]{2,1,0:T(8,128)(2,1)S(1)} %slice.183.down_ref), channel_id=1, source_target_pairs={{0,1},{1,2},{2,3},{3,4},{4,5},{5,6},{6,7},{8,9},{9,10},{10,11},{11... | collective-permute-start | bytes 196616 | tf_op jit(solution)/shard_map/ppermute | solution.py:191
  39.5 0.2 slice_reduce_fusion.8
  39.7 0.3 slice_reduce_fusion.2
  39.9 0.5 fusion.11
  40.4 1.0 %pad_maximum_fusion.1.recv_ref = bf16[8,3,128,128]{3,2,1,0:T(8,128)(2,1)} fusion(bf16[8,1,128,128]{3,2,1,0:T(8,128)(2,1)S(1)} %get-tuple-element.42, bf16[8,1,128,128]{3,2,1,0:T(8,128)(2,1)S(1)} %get-tuple-element.43, bf16[8,1,128,128]{3,2,1,0:T(8,128)(2,1)S(1)} %get-tuple-element.41), kind=kLoop, calls=%fused_computation.10 | loop fusion | flops 786432 | bytes 1572864 | tf_op jit(solution)/shard_map/stack | solution.py:19
  41.4 2.8 %collective-permute-done.6.down_left_ref = bf16[2,128,128]{2,1,0:T(8,128)(2,1)S(1)} collective-permute-done((bf16[2,128,128]{2,1,0:T(8,128)(2,1)S(1)}, bf16[2,128,128]{2,1,0:T(8,128)(2,1)S(1)}, u32[]{:S(2)}, u32[]{:S(2)}) %collective-permute-start.6) | collective-permute-done | bytes 65568 | tf_op jit(solution)/shard_map/ppermute | solution.py:191
  44.2 0.6 %copy-done.5 = bf16[2,128,128]{2,1,0:T(8,128)(2,1)} copy-done((bf16[2,128,128]{2,1,0:T(8,128)(2,1)}, bf16[2,128,128]{2,1,0:T(8,128)(2,1)S(1)}, u32[]{:S(2)}) %copy-start.5) | copy-done | bytes 65560
  44.8 0.2 copy-done.1
  45.0 4.8 %shard_map.55 = bf16[10,2,128,128]{3,2,1,0:T(8,128)(2,1)} custom-call(s32[2]{0:T(128)} %pad_add_fusion.ids, f32[10,128]{1,0:T(8,128)} %q_ref.1, bf16[10,3,128,128]{3,2,1,0:T(8,128)(2,1)} %pad_maximum_fusion.jac_ref, bf16[8,3,128,128]{3,2,1,0:T(8,128)(2,1)} %pad_maximum_fusion.1.recv_ref, bf16[10,2,128,128]{3,2,1,0:T(8,128)(2,1)} %mid_ref.1, ...), custom_call_target="tpu_custom_call" | custom-call | tf_op jit(solution)/shard_map/pallas_call | solution.py:197
  (34 shorter events, 0.5 us)
Async XLA Ops:
  0.0 7.7 %copy-start.6 = (s32[10,3]{0,1:T(4,128)S(1)}, s32[10,3]{0,1:T(4,128)}, u32[]{:S(2)}) copy-start(s32[10,3]{0,1:T(4,128)} %param.11) | copy-start | bytes 364
  0.0 44.2 %collective-permute-start.3 = (bf16[10,2,128,128]{3,2,1,0:T(8,128)(2,1)}, bf16[10,2,128,128]{3,2,1,0:T(8,128)(2,1)S(1)}, u32[]{:S(2)}, u32[]{:S(2)}) collective-permute-start(bf16[10,2,128,128]{3,2,1,0:T(8,128)(2,1)} %mid_ref.1), channel_id=1, source_target_pairs={{0,1},{1,2},{2,3},{3,4},{4,5},{5,6},{6,7},{8,9},{9,10},{10,11},{11... | collective-permute-start | bytes 1966088 | tf_op jit(solution)/shard_map/ppermute | solution.py:155
  1.4 42.8 %collective-permute-start.4 = (bf16[10,2,128,128]{3,2,1,0:T(8,128)(2,1)}, bf16[10,2,128,128]{3,2,1,0:T(8,128)(2,1)}, u32[]{:S(2)}, u32[]{:S(2)}) collective-permute-start(bf16[10,2,128,128]{3,2,1,0:T(8,128)(2,1)} %mid_ref.1), channel_id=1, source_target_pairs={{1,0},{2,1},{3,2},{4,3},{5,4},{6,5},{7,6},{9,8},{10,9},{11,10},{12... | collective-permute-start | bytes 1966088 | tf_op jit(solution)/shard_map/ppermute | solution.py:156
  7.9 0.7 %copy-start.7 = (s32[10]{0:T(128)S(1)}, s32[10]{0:T(128)}, u32[]{:S(2)}) copy-start(s32[10]{0:T(128)} %param.12) | copy-start | bytes 124
  8.7 9.4 %copy-start = (bf16[10,3,128,128]{3,2,1,0:T(8,128)(2,1)S(1)}, bf16[10,3,128,128]{3,2,1,0:T(8,128)(2,1)}, u32[]{:S(2)}) copy-start(bf16[10,3,128,128]{3,2,1,0:T(8,128)(2,1)} %param.10) | copy-start | bytes 2949124
  9.4 27.2 %collective-permute-start = (bf16[3,128,128]{2,1,0:T(8,128)(2,1)}, bf16[3,128,128]{2,1,0:T(8,128)(2,1)S(1)}, u32[]{:S(2)}, u32[]{:S(2)}) collective-permute-start(bf16[3,128,128]{2,1,0:T(8,128)(2,1)} %get-tuple-element.46), channel_id=1, source_target_pairs={{0,8},{8,16},{16,24},{24,32},{32,40},{40,48},{48,56},{56,64},{64,7... | collective-permute-start | bytes 294920 | tf_op jit(solution)/shard_map/ppermute | solution.py:160
  11.3 25.3 %collective-permute-start.1 = (bf16[3,128,128]{2,1,0:T(8,128)(2,1)S(1)}, bf16[3,128,128]{2,1,0:T(8,128)(2,1)S(1)}, u32[]{:S(2)}, u32[]{:S(2)}) collective-permute-start(bf16[3,128,128]{2,1,0:T(8,128)(2,1)S(1)} %get-tuple-element.47), channel_id=1, source_target_pairs={{8,0},{16,8},{24,16},{32,24},{40,32},{48,40},{56,48},{64,56},{72,6... | collective-permute-start | bytes 294920 | tf_op jit(solution)/shard_map/ppermute | solution.py:163
  16.1 23.8 %collective-permute-start.2 = (bf16[8,3,128,128]{3,2,1,0:T(8,128)(2,1)S(1)}, bf16[8,3,128,128]{3,2,1,0:T(8,128)(2,1)S(1)}, u32[]{:S(2)}, u32[]{:S(2)}) collective-permute-start(bf16[8,3,128,128]{3,2,1,0:T(8,128)(2,1)S(1)} %constant_dynamic-slice_fusion), channel_id=1, source_target_pairs={{0,8},{8,16},{16,24},{24,32},{32,40},{40,48},{48,56},{56,64},{64,7... | collective-permute-start | bytes 2359304 | tf_op jit(solution)/shard_map/ppermute | solution.py:179
  36.7 1.3 %copy-start.2 = (bf16[2,128,128]{2,1,0:T(8,128)(2,1)}, bf16[2,128,128]{2,1,0:T(8,128)(2,1)S(1)}, u32[]{:S(2)}) copy-start(bf16[2,128,128]{2,1,0:T(8,128)(2,1)S(1)} %slice.182.up_ref) | copy-start | bytes 196612
  36.7 4.7 %collective-permute-start.5 = (bf16[2,128,128]{2,1,0:T(8,128)(2,1)S(1)}, bf16[2,128,128]{2,1,0:T(8,128)(2,1)S(1)}, u32[]{:S(2)}, u32[]{:S(2)}) collective-permute-start(bf16[2,128,128]{2,1,0:T(8,128)(2,1)S(1)} %slice.182.up_ref), channel_id=1, source_target_pairs={{1,0},{2,1},{3,2},{4,3},{5,4},{6,5},{7,6},{9,8},{10,9},{11,10},{12... | collective-permute-start | bytes 196616 | tf_op jit(solution)/shard_map/ppermute | solution.py:192
  38.0 2.4 %copy-start.3 = (bf16[2,128,128]{2,1,0:T(8,128)(2,1)}, bf16[2,128,128]{2,1,0:T(8,128)(2,1)S(1)}, u32[]{:S(2)}) copy-start(bf16[2,128,128]{2,1,0:T(8,128)(2,1)S(1)} %slice.183.down_ref) | copy-start | bytes 196612
  38.0 6.2 %collective-permute-start.6 = (bf16[2,128,128]{2,1,0:T(8,128)(2,1)S(1)}, bf16[2,128,128]{2,1,0:T(8,128)(2,1)S(1)}, u32[]{:S(2)}, u32[]{:S(2)}) collective-permute-start(bf16[2,128,128]{2,1,0:T(8,128)(2,1)S(1)} %slice.183.down_ref), channel_id=1, source_target_pairs={{0,1},{1,2},{2,3},{3,4},{4,5},{5,6},{6,7},{8,9},{9,10},{10,11},{11... | collective-permute-start | bytes 196616 | tf_op jit(solution)/shard_map/ppermute | solution.py:191
  41.4 2.8 %copy-start.4 = (bf16[2,128,128]{2,1,0:T(8,128)(2,1)}, bf16[2,128,128]{2,1,0:T(8,128)(2,1)S(1)}, u32[]{:S(2)}) copy-start(bf16[2,128,128]{2,1,0:T(8,128)(2,1)S(1)} %collective-permute-done.5.up_right_ref) | copy-start | bytes 196612
  44.2 0.6 %copy-start.5 = (bf16[2,128,128]{2,1,0:T(8,128)(2,1)}, bf16[2,128,128]{2,1,0:T(8,128)(2,1)S(1)}, u32[]{:S(2)}) copy-start(bf16[2,128,128]{2,1,0:T(8,128)(2,1)S(1)} %collective-permute-done.6.down_left_ref) | copy-start | bytes 196612
  44.2 0.9 %copy-start.1 = (bf16[10,2,128,128]{3,2,1,0:T(8,128)(2,1)}, bf16[10,2,128,128]{3,2,1,0:T(8,128)(2,1)S(1)}, u32[]{:S(2)}) copy-start(bf16[10,2,128,128]{3,2,1,0:T(8,128)(2,1)S(1)} %collective-permute-done.3.left_ref) | copy-start | bytes 1966084

commit v14 on v11

--- a/solution.py
+++ b/solution.py
@@ -142,38 +142,35 @@
 
     left = lax.ppermute(p_band, "col", [(b, b + 1) for b in range(col_count - 1)])
     right = lax.ppermute(p_band, "col", [(b + 1, b) for b in range(col_count - 1)])
-    meta = jnp.zeros((tile_size, tile_size), p_band.dtype)
-    meta = meta.at[0, : tile_rows * 3].set(block_offsets.reshape(-1).astype(p_band.dtype))
-    meta = meta.at[1, :tile_rows].set(block_live.astype(p_band.dtype))
-    up_all = lax.ppermute(
-        jnp.concatenate([p_band[-1], meta[None]], axis=0), "row", [(a, a + 1) for a in range(row_count - 1)]
-    )
-    down_all = lax.ppermute(
-        jnp.concatenate([p_band[0], meta[None]], axis=0), "row", [(a + 1, a) for a in range(row_count - 1)]
-    )
-    up = up_all[:band_local]
-    down = down_all[:band_local]
+    up = lax.ppermute(p_band[-1], "row", [(a, a + 1) for a in range(row_count - 1)])
+    down = lax.ppermute(p_band[0], "row", [(a + 1, a) for a in range(row_count - 1)])
 
     sent_rows = half_band
     lower_half = col_id < col_count // 2
     send_start = jnp.where(lower_half, tile_rows - sent_rows, 0)
-    sent = lax.dynamic_slice_in_dim(blocks, send_start, sent_rows, 0)
+    sent_offsets = lax.dynamic_slice_in_dim(block_offsets, send_start, sent_rows, 0)
+    sent_live = lax.dynamic_slice_in_dim(block_live, send_start, sent_rows, 0)
+    meta = jnp.zeros((tile_size, tile_size), blocks.dtype)
+    meta = meta.at[0, : sent_rows * 3].set(sent_offsets.reshape(-1).astype(blocks.dtype))
+    meta = meta.at[1, :sent_rows].set(sent_live.astype(blocks.dtype))
+    sent_tiles = lax.dynamic_slice_in_dim(blocks, send_start, sent_rows, 0).reshape(
+        (sent_rows * 3, tile_size, tile_size)
+    )
+    sent = jnp.concatenate([sent_tiles, meta[None]], axis=0)
     pairs = []
     for b in range(col_count):
         if b * band_local - half_band < 0:
             pairs += [(flat(a, b), flat(a + 1, b)) for a in range(row_count - 1)]
         else:
             pairs += [(flat(a, b), flat(a - 1, b)) for a in range(1, row_count)]
-    received_blocks = lax.ppermute(sent, ("row", "col"), pairs)
+    received_all = lax.ppermute(sent, ("row", "col"), pairs)
 
     jacobian = assemble(blocks, block_offsets, block_live)
-    received_meta = jnp.where(lower_half, up_all[band_local], down_all[band_local]).astype(jnp.float32)
-    received_offsets = jnp.round(received_meta[0, : tile_rows * 3]).astype(jnp.int32).reshape(tile_rows, 3)
-    received_live = jnp.round(received_meta[1, :tile_rows]).astype(jnp.int32)
+    received_meta = received_all[sent_rows * 3].astype(jnp.float32)
     received = assemble(
-        received_blocks,
-        lax.dynamic_slice_in_dim(received_offsets, send_start, sent_rows, 0),
-        lax.dynamic_slice_in_dim(received_live, send_start, sent_rows, 0),
+        received_all[: sent_rows * 3].reshape((sent_rows, 3, tile_size, tile_size)),
+        jnp.round(received_meta[0, : sent_rows * 3]).astype(jnp.int32).reshape(sent_rows, 3),
+        jnp.round(received_meta[1, :sent_rows]).astype(jnp.int32),
     )
 
     down_left = lax.ppermute(down, "col", [(b, b + 1) for b in range(col_count - 1)])

time: 49.8 us -> 49.2 us (0.988)
  the two profiles are of different devices: /device:TPU:222 before, /device:TPU:414 now
where the time goes in v14:
time: 49.2 us; the launch traced here: 48.8 us
  starting transfers between devices  16.9 us (34%)
  waiting for transfers between devices  16.7 us (34%)
  local copies, waits for them, and re-layouts  6.49 us (13%)
  Pallas kernels  4.4 us (9%)
  other arithmetic  4.05 us (8%)
    ppermute x1, waiting for transfers between devices, shards(): lax.ppermute(p_band[-1], 'row', [(a, a + 1) for a in range(row_count - 1)])  14.3 us
    ppermute x1, starting transfers between devices, shards(): lax.ppermute(p_band, 'col', [(b + 1, b) for b in range(col_count - 1)])  5.43 us
    pallas_call x1, Pallas kernels, shards(): pl.pallas_call(band_kernel(tile_rows, band_local, half_band, grid_tiles,...  4.4 us
    ppermute x1, starting transfers between devices, shards(): lax.ppermute(p_band[0], 'row', [(a + 1, a) for a in range(row_count - 1)])  3.16 us
    unnamed x20, local copies, waits for them, and re-layouts  2.78 us
    ppermute x1, waiting for transfers between devices, shards(): lax.ppermute(down, 'col', [(b, b + 1) for b in range(col_count - 1)])  2.46 us
    ppermute x1, starting transfers between devices, shards(): lax.ppermute(p_band[-1], 'row', [(a, a + 1) for a in range(row_count - 1)])  2.41 us
    another operation x2, other arithmetic, assemble(): return jnp.stack(pieces, axis=1)  2.05 us
  transfers between devices with their start and end apart: 7, of which 2 were waited for; matrix products, arithmetic and copies ran while one was open for 16% of the time, Pallas kernels for 0%

profile of v14, /device:TPU:414, one launch (start us, length us, event | category | flops | bytes accessed | tf_op | source)
XLA Modules:
  0.0 48.8 jit_solution(883798183262491523)
XLA Ops:
  0.0 1.3 %collective-permute-start.1 = (bf16[10,2,128,128]{3,2,1,0:T(8,128)(2,1)}, bf16[10,2,128,128]{3,2,1,0:T(8,128)(2,1)S(1)}, u32[]{:S(2)}, u32[]{:S(2)}) collective-permute-start(bf16[10,2,128,128]{3,2,1,0:T(8,128)(2,1)} %mid_ref.1), channel_id=1, source_target_pairs={{0,1},{1,2},{2,3},{3,4},{4,5},{5,6},{6,7},{8,9},{9,10},{10,11},{11... | collective-permute-start | bytes 1966088 | tf_op jit(solution)/shard_map/ppermute | solution.py:143
  1.3 5.4 %collective-permute-start.2 = (bf16[10,2,128,128]{3,2,1,0:T(8,128)(2,1)}, bf16[10,2,128,128]{3,2,1,0:T(8,128)(2,1)}, u32[]{:S(2)}, u32[]{:S(2)}) collective-permute-start(bf16[10,2,128,128]{3,2,1,0:T(8,128)(2,1)} %mid_ref.1), channel_id=1, source_target_pairs={{1,0},{2,1},{3,2},{4,3},{5,4},{6,5},{7,6},{9,8},{10,9},{11,10},{12... | collective-permute-start | bytes 1966088 | tf_op jit(solution)/shard_map/ppermute | solution.py:144
  6.7 0.7 %copy-done.6 = s32[10,3]{0,1:T(4,128)S(1)} copy-done((s32[10,3]{0,1:T(4,128)S(1)}, s32[10,3]{0,1:T(4,128)}, u32[]{:S(2)}) %copy-start.6) | copy-done | bytes 144
  7.7 0.7 %copy-done.9 = s32[10]{0:T(128)S(1)} copy-done((s32[10]{0:T(128)S(1)}, s32[10]{0:T(128)}, u32[]{:S(2)}) %copy-start.9) | copy-done | bytes 64
  8.4 1.2 %constant_dynamic-slice_fusion = bf16[8,3,128,128]{3,2,1,0:T(8,128)(2,1)S(1)} fusion(bf16[10,3,128,128]{3,2,1,0:T(8,128)(2,1)} %param.10, s32[]{:T(128)S(6)} %select_n.90), kind=kLoop, calls=%fused_computation.81 | loop fusion | bytes 1572868 | tf_op jit(solution)/shard_map/dynamic_slice | solution.py:156
  9.8 2.1 %collective-permute-start = (bf16[25,128,128]{2,1,0:T(8,128)(2,1)S(1)}, bf16[25,128,128]{2,1,0:T(8,128)(2,1)S(1)}, u32[]{:S(2)}, u32[]{:S(2)}) collective-permute-start(bf16[25,128,128]{2,1,0:T(8,128)(2,1)S(1)} %pad_maximum_fusion.1), channel_id=1, source_target_pairs={{0,8},{8,16},{16,24},{24,32},{32,40},{40,48},{48,56},{56,64},{64,7... | collective-permute-start | bytes 2457608 | tf_op jit(solution)/shard_map/ppermute | solution.py:166
  11.9 0.9 %slice_bitcast_fusion = (bf16[2,128,128]{2,1,0:T(8,128)(2,1)S(1)}, bf16[2,128,128]{2,1,0:T(8,128)(2,1)S(1)}) fusion(bf16[10,2,128,128]{3,2,1,0:T(8,128)(2,1)} %mid_ref.1), kind=kLoop, calls=%fused_computation.39 | loop fusion | bytes 262144 | tf_op jit(solution)/shard_map/squeeze | solution.py:146
  12.8 2.4 %collective-permute-start.3 = (bf16[2,128,128]{2,1,0:T(8,128)(2,1)S(1)}, bf16[2,128,128]{2,1,0:T(8,128)(2,1)S(1)}, u32[]{:S(2)}, u32[]{:S(2)}) collective-permute-start(bf16[2,128,128]{2,1,0:T(8,128)(2,1)S(1)} %get-tuple-element.48), channel_id=1, source_target_pairs={{0,8},{8,16},{16,24},{24,32},{32,40},{40,48},{48,56},{56,64},{64,7... | collective-permute-start | bytes 196616 | tf_op jit(solution)/shard_map/ppermute | solution.py:145
  15.2 3.2 %collective-permute-start.4 = (bf16[2,128,128]{2,1,0:T(8,128)(2,1)S(1)}, bf16[2,128,128]{2,1,0:T(8,128)(2,1)S(1)}, u32[]{:S(2)}, u32[]{:S(2)}) collective-permute-start(bf16[2,128,128]{2,1,0:T(8,128)(2,1)S(1)} %get-tuple-element.47), channel_id=1, source_target_pairs={{8,0},{16,8},{24,16},{32,24},{40,32},{48,40},{56,48},{64,56},{72,6... | collective-permute-start | bytes 196616 | tf_op jit(solution)/shard_map/ppermute | solution.py:146
  18.4 0.5 %slice_bitcast_fusion.11 = (pred[10]{0:T(512)(128)(4,1)S(1)}, pred[10]{0:T(512)(128)(4,1)}, pred[10]{0:T(512)(128)(4,1)}) fusion(pred[10,3]{0,1:T(4,128)(4,1)S(1)} %get-tuple-element.49), kind=kLoop, calls=%fused_computation.73 | loop fusion | bytes 60 | tf_op jit(solution)/shard_map/jit(_where)/broadcast_in_dim | solution.py:17
  19.0 0.5 %copy-done.7 = pred[10]{0:T(512)(128)(4,1)S(1)} copy-done((pred[10]{0:T(512)(128)(4,1)S(1)}, pred[10]{0:T(512)(128)(4,1)}, u32[]{:S(2)}) %copy-start.7) | copy-done | bytes 34
  19.5 0.5 %fusion.2 = (bf16[10,1,128,128]{3,2,1,0:T(8,128)(2,1)S(1)}, bf16[10,1,128,128]{3,2,1,0:T(8,128)(2,1)S(1)}, bf16[10,1,128,128]{3,2,1,0:T(8,128)(2,1)S(1)}) fusion(pred[10]{0:T(512)(128)(4,1)S(1)} %copy-done.7, pred[10]{0:T(512)(128)(4,1)S(1)} %copy-done.8, pred[10]{0:T(512)(128)(4,1)S(1)} %get-tuple-element.55, bf16[10,3,128,128]{3,2,1,0:T(8,128)(2,1)S(1)} %copy-done, ...), kind=kLoop, calls=%fused_computation.23 | loop fusion | flops 3440640 | bytes 1966170 | tf_op jit(solution)/shard_map/convert_element_type | solution.py:18
  20.1 1.1 %pad_maximum_fusion.jac_ref = bf16[10,3,128,128]{3,2,1,0:T(8,128)(2,1)} fusion(bf16[10,1,128,128]{3,2,1,0:T(8,128)(2,1)S(1)} %get-tuple-element.42, bf16[10,1,128,128]{3,2,1,0:T(8,128)(2,1)S(1)} %get-tuple-element.43, bf16[10,1,128,128]{3,2,1,0:T(8,128)(2,1)S(1)} %get-tuple-element.41), kind=kLoop, calls=%fused_computation | loop fusion | flops 983040 | bytes 1966080 | tf_op jit(solution)/shard_map/stack | solution.py:19
  21.1 0.6 %pad_add_fusion.ids = s32[2]{0:T(128)} fusion(s32[1]{0:T(128)} %bitcast.1, s32[1]{0:T(128)} %bitcast), kind=kLoop, calls=%fused_computation.79 | loop fusion | flops 2 | bytes 16 | tf_op jit(solution)/shard_map/stack | solution.py:179
  21.8 14.3 %collective-permute-done.3.up_ref = bf16[2,128,128]{2,1,0:T(8,128)(2,1)S(1)} collective-permute-done((bf16[2,128,128]{2,1,0:T(8,128)(2,1)S(1)}, bf16[2,128,128]{2,1,0:T(8,128)(2,1)S(1)}, u32[]{:S(2)}, u32[]{:S(2)}) %collective-permute-start.3) | collective-permute-done | bytes 65568 | tf_op jit(solution)/shard_map/ppermute | solution.py:145
  36.1 1.3 %collective-permute-start.5 = (bf16[2,128,128]{2,1,0:T(8,128)(2,1)S(1)}, bf16[2,128,128]{2,1,0:T(8,128)(2,1)S(1)}, u32[]{:S(2)}, u32[]{:S(2)}) collective-permute-start(bf16[2,128,128]{2,1,0:T(8,128)(2,1)S(1)} %collective-permute-done.3.up_ref), channel_id=1, source_target_pairs={{1,0},{2,1},{3,2},{4,3},{5,4},{6,5},{7,6},{9,8},{10,9},{11,10},{12... | collective-permute-start | bytes 196616 | tf_op jit(solution)/shard_map/ppermute | solution.py:177
  37.4 1.3 %collective-permute-start.6 = (bf16[2,128,128]{2,1,0:T(8,128)(2,1)S(1)}, bf16[2,128,128]{2,1,0:T(8,128)(2,1)S(1)}, u32[]{:S(2)}, u32[]{:S(2)}) collective-permute-start(bf16[2,128,128]{2,1,0:T(8,128)(2,1)S(1)} %collective-permute-done.4.down_ref), channel_id=1, source_target_pairs={{0,1},{1,2},{2,3},{3,4},{4,5},{5,6},{6,7},{8,9},{9,10},{10,11},{11... | collective-permute-start | bytes 196616 | tf_op jit(solution)/shard_map/ppermute | solution.py:176
  39.3 0.3 slice_reduce_fusion.2
  39.6 0.5 fusion.11
  40.1 1.0 %pad_maximum_fusion.2.recv_ref = bf16[8,3,128,128]{3,2,1,0:T(8,128)(2,1)} fusion(bf16[8,1,128,128]{3,2,1,0:T(8,128)(2,1)S(1)} %get-tuple-element.45, bf16[8,1,128,128]{3,2,1,0:T(8,128)(2,1)S(1)} %get-tuple-element.46, bf16[8,1,128,128]{3,2,1,0:T(8,128)(2,1)S(1)} %get-tuple-element.44), kind=kLoop, calls=%fused_computation.11 | loop fusion | flops 786432 | bytes 1572864 | tf_op jit(solution)/shard_map/stack | solution.py:19
  41.1 2.5 %collective-permute-done.6.down_left_ref = bf16[2,128,128]{2,1,0:T(8,128)(2,1)S(1)} collective-permute-done((bf16[2,128,128]{2,1,0:T(8,128)(2,1)S(1)}, bf16[2,128,128]{2,1,0:T(8,128)(2,1)S(1)}, u32[]{:S(2)}, u32[]{:S(2)}) %collective-permute-start.6) | collective-permute-done | bytes 65568 | tf_op jit(solution)/shard_map/ppermute | solution.py:176
  43.6 0.6 %copy-done.5 = bf16[2,128,128]{2,1,0:T(8,128)(2,1)} copy-done((bf16[2,128,128]{2,1,0:T(8,128)(2,1)}, bf16[2,128,128]{2,1,0:T(8,128)(2,1)S(1)}, u32[]{:S(2)}) %copy-start.5) | copy-done | bytes 65560
  44.2 0.2 copy-done.1
  44.4 4.4 %shard_map.55 = bf16[10,2,128,128]{3,2,1,0:T(8,128)(2,1)} custom-call(s32[2]{0:T(128)} %pad_add_fusion.ids, f32[10,128]{1,0:T(8,128)} %q_ref.1, bf16[10,3,128,128]{3,2,1,0:T(8,128)(2,1)} %pad_maximum_fusion.jac_ref, bf16[8,3,128,128]{3,2,1,0:T(8,128)(2,1)} %pad_maximum_fusion.2.recv_ref, bf16[10,2,128,128]{3,2,1,0:T(8,128)(2,1)} %mid_ref.1, ...), custom_call_target="tpu_custom_call" | custom-call | tf_op jit(solution)/shard_map/pallas_call | solution.py:182
  (38 shorter events, 1.3 us)
Async XLA Ops:
  0.0 43.5 %collective-permute-start.1 = (bf16[10,2,128,128]{3,2,1,0:T(8,128)(2,1)}, bf16[10,2,128,128]{3,2,1,0:T(8,128)(2,1)S(1)}, u32[]{:S(2)}, u32[]{:S(2)}) collective-permute-start(bf16[10,2,128,128]{3,2,1,0:T(8,128)(2,1)} %mid_ref.1), channel_id=1, source_target_pairs={{0,1},{1,2},{2,3},{3,4},{4,5},{5,6},{6,7},{8,9},{9,10},{10,11},{11... | collective-permute-start | bytes 1966088 | tf_op jit(solution)/shard_map/ppermute | solution.py:143
  1.3 42.3 %collective-permute-start.2 = (bf16[10,2,128,128]{3,2,1,0:T(8,128)(2,1)}, bf16[10,2,128,128]{3,2,1,0:T(8,128)(2,1)}, u32[]{:S(2)}, u32[]{:S(2)}) collective-permute-start(bf16[10,2,128,128]{3,2,1,0:T(8,128)(2,1)} %mid_ref.1), channel_id=1, source_target_pairs={{1,0},{2,1},{3,2},{4,3},{5,4},{6,5},{7,6},{9,8},{10,9},{11,10},{12... | collective-permute-start | bytes 1966088 | tf_op jit(solution)/shard_map/ppermute | solution.py:144
  6.7 0.7 %copy-start.6 = (s32[10,3]{0,1:T(4,128)S(1)}, s32[10,3]{0,1:T(4,128)}, u32[]{:S(2)}) copy-start(s32[10,3]{0,1:T(4,128)} %param.11) | copy-start | bytes 364
  7.7 0.7 %copy-start.9 = (s32[10]{0:T(128)S(1)}, s32[10]{0:T(128)}, u32[]{:S(2)}) copy-start(s32[10]{0:T(128)} %param.12) | copy-start | bytes 124
  9.6 9.4 %copy-start = (bf16[10,3,128,128]{3,2,1,0:T(8,128)(2,1)S(1)}, bf16[10,3,128,128]{3,2,1,0:T(8,128)(2,1)}, u32[]{:S(2)}) copy-start(bf16[10,3,128,128]{3,2,1,0:T(8,128)(2,1)} %param.10) | copy-start | bytes 2949124
  9.8 28.8 %collective-permute-start = (bf16[25,128,128]{2,1,0:T(8,128)(2,1)S(1)}, bf16[25,128,128]{2,1,0:T(8,128)(2,1)S(1)}, u32[]{:S(2)}, u32[]{:S(2)}) collective-permute-start(bf16[25,128,128]{2,1,0:T(8,128)(2,1)S(1)} %pad_maximum_fusion.1), channel_id=1, source_target_pairs={{0,8},{8,16},{16,24},{24,32},{32,40},{40,48},{48,56},{56,64},{64,7... | collective-permute-start | bytes 2457608 | tf_op jit(solution)/shard_map/ppermute | solution.py:166
  12.8 23.3 %collective-permute-start.3 = (bf16[2,128,128]{2,1,0:T(8,128)(2,1)S(1)}, bf16[2,128,128]{2,1,0:T(8,128)(2,1)S(1)}, u32[]{:S(2)}, u32[]{:S(2)}) collective-permute-start(bf16[2,128,128]{2,1,0:T(8,128)(2,1)S(1)} %get-tuple-element.48), channel_id=1, source_target_pairs={{0,8},{8,16},{16,24},{24,32},{32,40},{40,48},{48,56},{56,64},{64,7... | collective-permute-start | bytes 196616 | tf_op jit(solution)/shard_map/ppermute | solution.py:145
  15.2 22.2 %collective-permute-start.4 = (bf16[2,128,128]{2,1,0:T(8,128)(2,1)S(1)}, bf16[2,128,128]{2,1,0:T(8,128)(2,1)S(1)}, u32[]{:S(2)}, u32[]{:S(2)}) collective-permute-start(bf16[2,128,128]{2,1,0:T(8,128)(2,1)S(1)} %get-tuple-element.47), channel_id=1, source_target_pairs={{8,0},{16,8},{24,16},{32,24},{40,32},{48,40},{56,48},{64,56},{72,6... | collective-permute-start | bytes 196616 | tf_op jit(solution)/shard_map/ppermute | solution.py:146
  18.9 0.6 %copy-start.7 = (pred[10]{0:T(512)(128)(4,1)S(1)}, pred[10]{0:T(512)(128)(4,1)}, u32[]{:S(2)}) copy-start(pred[10]{0:T(512)(128)(4,1)} %get-tuple-element.56) | copy-start | bytes 34
  18.9 0.6 %copy-start.8 = (pred[10]{0:T(512)(128)(4,1)S(1)}, pred[10]{0:T(512)(128)(4,1)}, u32[]{:S(2)}) copy-start(pred[10]{0:T(512)(128)(4,1)} %get-tuple-element.57) | copy-start | bytes 34
  36.1 3.1 %copy-start.2 = (bf16[2,128,128]{2,1,0:T(8,128)(2,1)}, bf16[2,128,128]{2,1,0:T(8,128)(2,1)S(1)}, u32[]{:S(2)}) copy-start(bf16[2,128,128]{2,1,0:T(8,128)(2,1)S(1)} %collective-permute-done.3.up_ref) | copy-start | bytes 196612
  36.1 5.0 %collective-permute-start.5 = (bf16[2,128,128]{2,1,0:T(8,128)(2,1)S(1)}, bf16[2,128,128]{2,1,0:T(8,128)(2,1)S(1)}, u32[]{:S(2)}, u32[]{:S(2)}) collective-permute-start(bf16[2,128,128]{2,1,0:T(8,128)(2,1)S(1)} %collective-permute-done.3.up_ref), channel_id=1, source_target_pairs={{1,0},{2,1},{3,2},{4,3},{5,4},{6,5},{7,6},{9,8},{10,9},{11,10},{12... | collective-permute-start | bytes 196616 | tf_op jit(solution)/shard_map/ppermute | solution.py:177
  37.4 1.8 %copy-start.3 = (bf16[2,128,128]{2,1,0:T(8,128)(2,1)}, bf16[2,128,128]{2,1,0:T(8,128)(2,1)S(1)}, u32[]{:S(2)}) copy-start(bf16[2,128,128]{2,1,0:T(8,128)(2,1)S(1)} %collective-permute-done.4.down_ref) | copy-start | bytes 196612
  37.4 6.2 %collective-permute-start.6 = (bf16[2,128,128]{2,1,0:T(8,128)(2,1)S(1)}, bf16[2,128,128]{2,1,0:T(8,128)(2,1)S(1)}, u32[]{:S(2)}, u32[]{:S(2)}) collective-permute-start(bf16[2,128,128]{2,1,0:T(8,128)(2,1)S(1)} %collective-permute-done.4.down_ref), channel_id=1, source_target_pairs={{0,1},{1,2},{2,3},{3,4},{4,5},{5,6},{6,7},{8,9},{9,10},{10,11},{11... | collective-permute-start | bytes 196616 | tf_op jit(solution)/shard_map/ppermute | solution.py:176
  41.1 2.5 %copy-start.4 = (bf16[2,128,128]{2,1,0:T(8,128)(2,1)}, bf16[2,128,128]{2,1,0:T(8,128)(2,1)S(1)}, u32[]{:S(2)}) copy-start(bf16[2,128,128]{2,1,0:T(8,128)(2,1)S(1)} %collective-permute-done.5.up_right_ref) | copy-start | bytes 196612
  43.5 0.6 %copy-start.5 = (bf16[2,128,128]{2,1,0:T(8,128)(2,1)}, bf16[2,128,128]{2,1,0:T(8,128)(2,1)S(1)}, u32[]{:S(2)}) copy-start(bf16[2,128,128]{2,1,0:T(8,128)(2,1)S(1)} %collective-permute-done.6.down_left_ref) | copy-start | bytes 196612
  43.5 0.9 %copy-start.1 = (bf16[10,2,128,128]{3,2,1,0:T(8,128)(2,1)}, bf16[10,2,128,128]{3,2,1,0:T(8,128)(2,1)S(1)}, u32[]{:S(2)}) copy-start(bf16[10,2,128,128]{3,2,1,0:T(8,128)(2,1)S(1)} %collective-permute-done.1.left_ref) | copy-start | bytes 1966084

commit v15 on v14

--- a/solution.py
+++ b/solution.py
@@ -19,12 +19,22 @@
     return jnp.stack(pieces, axis=1)
 
 
-def band_kernel(tile_rows, band_local, half_band, grid_tiles, sent_rows, row_count, col_count):
+def band_kernel(tile_rows, band_local, half_band, grid_tiles, sent_rows, row_count, col_count, inner):
     extended = band_local + 2
     window = tile_rows + band_local - 1
+    inner_rows = range(1, tile_rows - 1)
+
+    def inner_kernel(ids, jac_ref, mid_ref, left_ref, right_ref, out_ref):
+        kernel(ids, None, jac_ref, None, mid_ref, left_ref, right_ref, None, None, None, None, None,
+               out_ref, None, None)
+
+    def final_kernel(ids, q_ref, jac_ref, recv_ref, mid_ref, left_ref, right_ref, up_ref, down_ref,
+                     up_right_ref, down_left_ref, inner_ref, out_ref, win_ref, spread_ref):
+        kernel(ids, q_ref, jac_ref, recv_ref, mid_ref, left_ref, right_ref, up_ref, down_ref,
+               up_right_ref, down_left_ref, inner_ref, out_ref, win_ref, spread_ref)
 
     def kernel(ids, q_ref, jac_ref, recv_ref, mid_ref, left_ref, right_ref, up_ref, down_ref,
-               up_right_ref, down_left_ref, out_ref, win_ref, spread_ref):
+               up_right_ref, down_left_ref, inner_ref, out_ref, win_ref, spread_ref):
         row_id = ids[0]
         col_id = ids[1]
         first_row = row_id * tile_rows
@@ -32,7 +42,7 @@
         low_offset = col_id * band_local - half_band
         size = jac_ref.shape[-1]
 
-        for col_value in range(col_count):
+        for col_value in range(0 if inner else col_count):
             offset = col_value * band_local - half_band
 
             @pl.when(col_id == col_value)
@@ -74,8 +84,17 @@
             jnp.int32, (size, size), 1
         )
 
+        def spread_rows(row):
+            if inner:
+                return out_ref.at[row - 1]
+            if row in inner_rows:
+                return inner_ref.at[row - 1]
+            return spread_ref.at[row]
+
         def body(masked):
             for row in range(tile_rows):
+                if (row in inner_rows) != inner:
+                    continue
                 lhs = jnp.concatenate([jac_ref[row, f] for f in range(3)], axis=1)
                 rhs = jnp.concatenate(
                     [
@@ -86,15 +105,17 @@
                     ],
                     axis=0,
                 )
-                spread_ref[row] = jnp.dot(lhs, rhs, preferred_element_type=jnp.float32).astype(
+                spread_rows(row)[...] = jnp.dot(lhs, rhs, preferred_element_type=jnp.float32).astype(
                     jnp.bfloat16
                 )
+            if inner:
+                return
             for position in range(window):
                 members = [
                     (position - k, k) for k in range(band_local) if 0 <= position - k < tile_rows
                 ]
                 left_side = jnp.concatenate(
-                    [spread_ref[row, :, k * size : (k + 3) * size] for row, k in members], axis=0
+                    [spread_rows(row)[:, k * size : (k + 3) * size] for row, k in members], axis=0
                 )
                 right_side = jnp.concatenate([win_ref[position, g] for g in range(3)], axis=1)
                 product = lax.dot_general(
@@ -124,7 +145,7 @@
         def _():
             body(False)
 
-    return kernel
+    return inner_kernel if inner else final_kernel
 
 
 def shards(p_band, blocks, block_offsets, block_live, q_var):
@@ -179,16 +200,24 @@
     ids = jnp.stack([row_id, col_id]).astype(jnp.int32)
     vmem = pl.BlockSpec(memory_space=pltpu.MemorySpace.VMEM)
     smem = pl.BlockSpec(memory_space=pltpu.MemorySpace.SMEM)
+    sizes = (tile_rows, band_local, half_band, grid_tiles, sent_rows, row_count, col_count)
+    spread_row = (tile_size, (band_local + 2) * tile_size)
+    inner_spread = pl.pallas_call(
+        band_kernel(*sizes, True),
+        out_shape=jax.ShapeDtypeStruct((tile_rows - 2,) + spread_row, p_band.dtype),
+        in_specs=[smem] + [vmem] * 4,
+        out_specs=vmem,
+    )(ids, jacobian, p_band, left, right)
     return pl.pallas_call(
-        band_kernel(tile_rows, band_local, half_band, grid_tiles, sent_rows, row_count, col_count),
+        band_kernel(*sizes, False),
         out_shape=jax.ShapeDtypeStruct(p_band.shape, p_band.dtype),
-        in_specs=[smem] + [vmem] * 10,
+        in_specs=[smem] + [vmem] * 11,
         out_specs=vmem,
         scratch_shapes=[
             pltpu.VMEM((tile_rows + band_local - 1, 3, tile_size, tile_size), p_band.dtype),
-            pltpu.VMEM((tile_rows, tile_size, (band_local + 2) * tile_size), p_band.dtype),
+            pltpu.VMEM((tile_rows,) + spread_row, p_band.dtype),
         ],
-    )(ids, q_var, jacobian, received, p_band, left, right, up, down, up_right, down_left)
+    )(ids, q_var, jacobian, received, p_band, left, right, up, down, up_right, down_left, inner_spread)
 
 
 def solution(mesh):

time: 49.2 us -> 50.5 us (1.026)
  the two profiles are of different devices: /device:TPU:414 before, /device:TPU:280 now
where the time goes in v15:
time: 50.5 us; the launch traced here: 50 us
  starting transfers between devices  24.3 us (48%)
  Pallas kernels  7.77 us (15%)
  local copies, waits for them, and re-layouts  7.11 us (14%)
  other arithmetic  5.7 us (11%)
  waiting for transfers between devices  4.88 us (10%)
    ppermute x1, starting transfers between devices, shards(): lax.ppermute(up, 'col', [(b + 1, b) for b in range(col_count - 1)])  7.63 us
    ppermute x1, starting transfers between devices, shards(): lax.ppermute(p_band, 'col', [(b + 1, b) for b in range(col_count - 1)])  5.33 us
    ppermute x1, waiting for transfers between devices, shards(): lax.ppermute(p_band, 'col', [(b, b + 1) for b in range(col_count - 1)])  4.87 us
    pallas_call x1, Pallas kernels, shards(): pl.pallas_call(band_kernel(*sizes, False), out_shape=jax.ShapeDtypeStruct...  4.27 us
    pallas_call x1, Pallas kernels, shards(): pl.pallas_call(band_kernel(*sizes, True), out_shape=jax.ShapeDtypeStruct(...  3.5 us
    ppermute x1, starting transfers between devices, shards(): received_all = lax.ppermute(sent, ('row', 'col'), pairs)  3.15 us
    unnamed x18, local copies, waits for them, and re-layouts  2.73 us
    ppermute x1, starting transfers between devices, shards(): lax.ppermute(p_band[-1], 'row', [(a, a + 1) for a in range(row_count - 1)])  2.41 us
  transfers between devices with their start and end apart: 7, of which 1 were waited for; matrix products, arithmetic and copies ran while one was open for 20% of the time, Pallas kernels for 7%

profile of v15, /device:TPU:280, one launch (start us, length us, event | category | flops | bytes accessed | tf_op | source)
XLA Modules:
  0.0 50.0 jit_solution(686660340693204058)
XLA Ops:
  0.0 5.3 %collective-permute-start.2 = (bf16[10,2,128,128]{3,2,1,0:T(8,128)(2,1)}, bf16[10,2,128,128]{3,2,1,0:T(8,128)(2,1)S(1)}, u32[]{:S(2)}, u32[]{:S(2)}) collective-permute-start(bf16[10,2,128,128]{3,2,1,0:T(8,128)(2,1)} %mid_ref.3), channel_id=1, source_target_pairs={{1,0},{2,1},{3,2},{4,3},{5,4},{6,5},{7,6},{9,8},{10,9},{11,10},{12... | collective-permute-start | bytes 1966088 | tf_op jit(solution)/shard_map/ppermute | solution.py:165
  5.3 1.9 %collective-permute-start.1 = (bf16[10,2,128,128]{3,2,1,0:T(8,128)(2,1)}, bf16[10,2,128,128]{3,2,1,0:T(8,128)(2,1)S(1)}, u32[]{:S(2)}, u32[]{:S(2)}) collective-permute-start(bf16[10,2,128,128]{3,2,1,0:T(8,128)(2,1)} %mid_ref.3), channel_id=1, source_target_pairs={{0,1},{1,2},{2,3},{3,4},{4,5},{5,6},{6,7},{8,9},{9,10},{10,11},{11... | collective-permute-start | bytes 1966088 | tf_op jit(solution)/shard_map/ppermute | solution.py:164
  7.3 0.9 %slice_bitcast_fusion = (bf16[2,128,128]{2,1,0:T(8,128)(2,1)S(1)}, bf16[2,128,128]{2,1,0:T(8,128)(2,1)S(1)}) fusion(bf16[10,2,128,128]{3,2,1,0:T(8,128)(2,1)} %mid_ref.3), kind=kLoop, calls=%fused_computation.39 | loop fusion | bytes 262144 | tf_op jit(solution)/shard_map/squeeze | solution.py:167
  8.2 1.9 %collective-permute-start.4 = (bf16[2,128,128]{2,1,0:T(8,128)(2,1)S(1)}, bf16[2,128,128]{2,1,0:T(8,128)(2,1)S(1)}, u32[]{:S(2)}, u32[]{:S(2)}) collective-permute-start(bf16[2,128,128]{2,1,0:T(8,128)(2,1)S(1)} %get-tuple-element.47), channel_id=1, source_target_pairs={{8,0},{16,8},{24,16},{32,24},{40,32},{48,40},{56,48},{64,56},{72,6... | collective-permute-start | bytes 196616 | tf_op jit(solution)/shard_map/ppermute | solution.py:167
  10.1 2.4 %collective-permute-start.3 = (bf16[2,128,128]{2,1,0:T(8,128)(2,1)S(1)}, bf16[2,128,128]{2,1,0:T(8,128)(2,1)S(1)}, u32[]{:S(2)}, u32[]{:S(2)}) collective-permute-start(bf16[2,128,128]{2,1,0:T(8,128)(2,1)S(1)} %get-tuple-element.48), channel_id=1, source_target_pairs={{0,8},{8,16},{16,24},{24,32},{32,40},{40,48},{48,56},{56,64},{64,7... | collective-permute-start | bytes 196616 | tf_op jit(solution)/shard_map/ppermute | solution.py:166
  12.5 0.6 %copy-done.8 = s32[10]{0:T(128)S(1)} copy-done((s32[10]{0:T(128)S(1)}, s32[10]{0:T(128)}, u32[]{:S(2)}) %copy-start.8) | copy-done | bytes 64
  13.5 1.2 %constant_dynamic-slice_fusion = bf16[8,3,128,128]{3,2,1,0:T(8,128)(2,1)S(1)} fusion(bf16[10,3,128,128]{3,2,1,0:T(8,128)(2,1)} %param.10, s32[]{:T(128)S(6)} %select_n.90), kind=kLoop, calls=%fused_computation.81 | loop fusion | bytes 1572868 | tf_op jit(solution)/shard_map/dynamic_slice | solution.py:177
  14.9 1.0 %pad_maximum_fusion.1 = bf16[25,128,128]{2,1,0:T(8,128)(2,1)} fusion(bf16[1,128,128]{2,1,0:T(8,128)(2,1)S(1)} %scatter.9, bf16[24,128,128]{2,1,0:T(8,128)(2,1)S(1)} %bitcast.38), kind=kLoop, calls=%fused_computation.10 | loop fusion | flops 409600 | bytes 1638400 | tf_op jit(solution)/shard_map/concatenate | solution.py:180
  15.9 3.1 %collective-permute-start = (bf16[25,128,128]{2,1,0:T(8,128)(2,1)}, bf16[25,128,128]{2,1,0:T(8,128)(2,1)}, u32[]{:S(2)}, u32[]{:S(2)}) collective-permute-start(bf16[25,128,128]{2,1,0:T(8,128)(2,1)} %pad_maximum_fusion.1), channel_id=1, source_target_pairs={{0,8},{8,16},{16,24},{24,32},{32,40},{40,48},{48,56},{56,64},{64,7... | collective-permute-start | bytes 2457608 | tf_op jit(solution)/shard_map/ppermute | solution.py:187
  19.1 0.5 %fusion.2 = (bf16[10,1,128,128]{3,2,1,0:T(8,128)(2,1)S(1)}, bf16[10,1,128,128]{3,2,1,0:T(8,128)(2,1)S(1)}, bf16[10,1,128,128]{3,2,1,0:T(8,128)(2,1)S(1)}) fusion(pred[10]{0:T(512)(128)(4,1)S(1)} %get-tuple-element.56, pred[10]{0:T(512)(128)(4,1)S(1)} %get-tuple-element.57, pred[10]{0:T(512)(128)(4,1)S(1)} %get-tuple-element.55, ...), kind=kLoop, calls=%fused_computation.23 | loop fusion | flops 3440640 | bytes 1966170 | tf_op jit(solution)/shard_map/convert_element_type | solution.py:18
  19.7 1.1 %pad_maximum_fusion.jac_ref = bf16[10,3,128,128]{3,2,1,0:T(8,128)(2,1)} fusion(bf16[10,1,128,128]{3,2,1,0:T(8,128)(2,1)S(1)} %get-tuple-element.42, bf16[10,1,128,128]{3,2,1,0:T(8,128)(2,1)S(1)} %get-tuple-element.43, bf16[10,1,128,128]{3,2,1,0:T(8,128)(2,1)S(1)} %get-tuple-element.41), kind=kLoop, calls=%fused_computation | loop fusion | flops 983040 | bytes 1966080 | tf_op jit(solution)/shard_map/stack | solution.py:19
  20.8 0.6 %pad_add_fusion.ids = s32[2]{0:T(128)} fusion(s32[1]{0:T(128)} %bitcast.1, s32[1]{0:T(128)} %bitcast), kind=kLoop, calls=%fused_computation.79 | loop fusion | flops 2 | bytes 16 | tf_op jit(solution)/shard_map/stack | solution.py:200
  21.4 2.0 %collective-permute-start.6 = (bf16[2,128,128]{2,1,0:T(8,128)(2,1)S(1)}, bf16[2,128,128]{2,1,0:T(8,128)(2,1)S(1)}, u32[]{:S(2)}, u32[]{:S(2)}) collective-permute-start(bf16[2,128,128]{2,1,0:T(8,128)(2,1)S(1)} %collective-permute-done.4.down_ref), channel_id=1, source_target_pairs={{0,1},{1,2},{2,3},{3,4},{4,5},{5,6},{6,7},{8,9},{9,10},{10,11},{11... | collective-permute-start | bytes 196616 | tf_op jit(solution)/shard_map/ppermute | solution.py:197
  23.4 7.6 %collective-permute-start.5 = (bf16[2,128,128]{2,1,0:T(8,128)(2,1)S(1)}, bf16[2,128,128]{2,1,0:T(8,128)(2,1)S(1)}, u32[]{:S(2)}, u32[]{:S(2)}) collective-permute-start(bf16[2,128,128]{2,1,0:T(8,128)(2,1)S(1)} %collective-permute-done.3.up_ref), channel_id=1, source_target_pairs={{1,0},{2,1},{3,2},{4,3},{5,4},{6,5},{7,6},{9,8},{10,9},{11,10},{12... | collective-permute-start | bytes 196616 | tf_op jit(solution)/shard_map/ppermute | solution.py:198
  31.0 4.9 %collective-permute-done.1.left_ref = bf16[10,2,128,128]{3,2,1,0:T(8,128)(2,1)S(1)} collective-permute-done((bf16[10,2,128,128]{3,2,1,0:T(8,128)(2,1)}, bf16[10,2,128,128]{3,2,1,0:T(8,128)(2,1)S(1)}, u32[]{:S(2)}, u32[]{:S(2)}) %collective-permute-start.1) | collective-permute-done | bytes 655392 | tf_op jit(solution)/shard_map/ppermute | solution.py:164
  35.9 0.8 %copy-done.2 = bf16[10,2,128,128]{3,2,1,0:T(8,128)(2,1)} copy-done((bf16[10,2,128,128]{3,2,1,0:T(8,128)(2,1)}, bf16[10,2,128,128]{3,2,1,0:T(8,128)(2,1)S(1)}, u32[]{:S(2)}) %copy-start.2) | copy-done | bytes 655384
  36.7 3.5 %shard_map.55.inner_ref = bf16[8,128,512]{2,1,0:T(8,128)(2,1)} custom-call(s32[2]{0:T(128)} %pad_add_fusion.ids, bf16[10,3,128,128]{3,2,1,0:T(8,128)(2,1)} %pad_maximum_fusion.jac_ref, bf16[10,2,128,128]{3,2,1,0:T(8,128)(2,1)} %mid_ref.3, bf16[10,2,128,128]{3,2,1,0:T(8,128)(2,1)} %copy-done.2, bf16[10,2,128,128]{3,2,1,0:T(8,128)(2,1)} %copy-done.1), custom_call_target="tpu_custom_call" | custom-call | tf_op jit(solution)/shard_map/pallas_call | solution.py:205
  40.3 0.8 %fusion.18 = f32[128,128]{1,0:T(8,128)S(1)} fusion(bf16[25,128,128]{2,1,0:T(8,128)(2,1)} %collective-permute-done), kind=kLoop, calls=%fused_computation.42 | loop fusion | flops 16384 | bytes 98304 | tf_op jit(solution)/shard_map/convert_element_type | solution.py:190
  41.8 1.2 %slice.170 = bf16[24,128,128]{2,1,0:T(8,128)(2,1)S(1)} slice(bf16[25,128,128]{2,1,0:T(8,128)(2,1)} %collective-permute-done), slice={[0:24], [0:128], [0:128]} | slice | bytes 1572864 | tf_op jit(solution)/shard_map/slice | solution.py:192
  43.1 0.5 fusion.11
  43.5 1.0 %pad_maximum_fusion.2.recv_ref = bf16[8,3,128,128]{3,2,1,0:T(8,128)(2,1)} fusion(bf16[8,1,128,128]{3,2,1,0:T(8,128)(2,1)S(1)} %get-tuple-element.45, bf16[8,1,128,128]{3,2,1,0:T(8,128)(2,1)S(1)} %get-tuple-element.46, bf16[8,1,128,128]{3,2,1,0:T(8,128)(2,1)S(1)} %get-tuple-element.44), kind=kLoop, calls=%fused_computation.11 | loop fusion | flops 786432 | bytes 1572864 | tf_op jit(solution)/shard_map/stack | solution.py:19
  44.5 0.6 %copy-done.5 = bf16[2,128,128]{2,1,0:T(8,128)(2,1)} copy-done((bf16[2,128,128]{2,1,0:T(8,128)(2,1)}, bf16[2,128,128]{2,1,0:T(8,128)(2,1)S(1)}, u32[]{:S(2)}) %copy-start.5) | copy-done | bytes 65560
  45.1 0.6 %copy-done.6 = bf16[2,128,128]{2,1,0:T(8,128)(2,1)} copy-done((bf16[2,128,128]{2,1,0:T(8,128)(2,1)}, bf16[2,128,128]{2,1,0:T(8,128)(2,1)S(1)}, u32[]{:S(2)}) %copy-start.6) | copy-done | bytes 65560
  45.7 4.3 %shard_map.56 = bf16[10,2,128,128]{3,2,1,0:T(8,128)(2,1)} custom-call(s32[2]{0:T(128)} %pad_add_fusion.ids, f32[10,128]{1,0:T(8,128)} %q_ref.1, bf16[10,3,128,128]{3,2,1,0:T(8,128)(2,1)} %pad_maximum_fusion.jac_ref, bf16[8,3,128,128]{3,2,1,0:T(8,128)(2,1)} %pad_maximum_fusion.2.recv_ref, bf16[10,2,128,128]{3,2,1,0:T(8,128)(2,1)} %mid_ref.3, ...), custom_call_target="tpu_custom_call" | custom-call | tf_op jit(solution)/shard_map/pallas_call | solution.py:211
  (37 shorter events, 1.4 us)
Async XLA Ops:
  0.0 31.0 %collective-permute-start.2 = (bf16[10,2,128,128]{3,2,1,0:T(8,128)(2,1)}, bf16[10,2,128,128]{3,2,1,0:T(8,128)(2,1)S(1)}, u32[]{:S(2)}, u32[]{:S(2)}) collective-permute-start(bf16[10,2,128,128]{3,2,1,0:T(8,128)(2,1)} %mid_ref.3), channel_id=1, source_target_pairs={{1,0},{2,1},{3,2},{4,3},{5,4},{6,5},{7,6},{9,8},{10,9},{11,10},{12... | collective-permute-start | bytes 1966088 | tf_op jit(solution)/shard_map/ppermute | solution.py:165
  5.3 30.6 %collective-permute-start.1 = (bf16[10,2,128,128]{3,2,1,0:T(8,128)(2,1)}, bf16[10,2,128,128]{3,2,1,0:T(8,128)(2,1)S(1)}, u32[]{:S(2)}, u32[]{:S(2)}) collective-permute-start(bf16[10,2,128,128]{3,2,1,0:T(8,128)(2,1)} %mid_ref.3), channel_id=1, source_target_pairs={{0,1},{1,2},{2,3},{3,4},{4,5},{5,6},{6,7},{8,9},{9,10},{10,11},{11... | collective-permute-start | bytes 1966088 | tf_op jit(solution)/shard_map/ppermute | solution.py:164
  8.2 13.2 %collective-permute-start.4 = (bf16[2,128,128]{2,1,0:T(8,128)(2,1)S(1)}, bf16[2,128,128]{2,1,0:T(8,128)(2,1)S(1)}, u32[]{:S(2)}, u32[]{:S(2)}) collective-permute-start(bf16[2,128,128]{2,1,0:T(8,128)(2,1)S(1)} %get-tuple-element.47), channel_id=1, source_target_pairs={{8,0},{16,8},{24,16},{32,24},{40,32},{48,40},{56,48},{64,56},{72,6... | collective-permute-start | bytes 196616 | tf_op jit(solution)/shard_map/ppermute | solution.py:167
  10.1 13.3 %collective-permute-start.3 = (bf16[2,128,128]{2,1,0:T(8,128)(2,1)S(1)}, bf16[2,128,128]{2,1,0:T(8,128)(2,1)S(1)}, u32[]{:S(2)}, u32[]{:S(2)}) collective-permute-start(bf16[2,128,128]{2,1,0:T(8,128)(2,1)S(1)} %get-tuple-element.48), channel_id=1, source_target_pairs={{0,8},{8,16},{16,24},{24,32},{32,40},{40,48},{48,56},{56,64},{64,7... | collective-permute-start | bytes 196616 | tf_op jit(solution)/shard_map/ppermute | solution.py:166
  12.5 0.7 %copy-start.8 = (s32[10]{0:T(128)S(1)}, s32[10]{0:T(128)}, u32[]{:S(2)}) copy-start(s32[10]{0:T(128)} %param.12) | copy-start | bytes 124
  12.5 0.7 %copy-start.7 = (s32[10,3]{0,1:T(4,128)S(1)}, s32[10,3]{0,1:T(4,128)}, u32[]{:S(2)}) copy-start(s32[10,3]{0,1:T(4,128)} %param.11) | copy-start | bytes 364
  14.7 4.4 %copy-start = (bf16[10,3,128,128]{3,2,1,0:T(8,128)(2,1)S(1)}, bf16[10,3,128,128]{3,2,1,0:T(8,128)(2,1)}, u32[]{:S(2)}) copy-start(bf16[10,3,128,128]{3,2,1,0:T(8,128)(2,1)} %param.10) | copy-start | bytes 2949124
  15.9 24.4 %collective-permute-start = (bf16[25,128,128]{2,1,0:T(8,128)(2,1)}, bf16[25,128,128]{2,1,0:T(8,128)(2,1)}, u32[]{:S(2)}, u32[]{:S(2)}) collective-permute-start(bf16[25,128,128]{2,1,0:T(8,128)(2,1)} %pad_maximum_fusion.1), channel_id=1, source_target_pairs={{0,8},{8,16},{16,24},{24,32},{32,40},{40,48},{48,56},{56,64},{64,7... | collective-permute-start | bytes 2457608 | tf_op jit(solution)/shard_map/ppermute | solution.py:187
  21.4 18.9 %copy-start.3 = (bf16[2,128,128]{2,1,0:T(8,128)(2,1)}, bf16[2,128,128]{2,1,0:T(8,128)(2,1)S(1)}, u32[]{:S(2)}) copy-start(bf16[2,128,128]{2,1,0:T(8,128)(2,1)S(1)} %collective-permute-done.4.down_ref) | copy-start | bytes 196612
  21.4 23.1 %collective-permute-start.6 = (bf16[2,128,128]{2,1,0:T(8,128)(2,1)S(1)}, bf16[2,128,128]{2,1,0:T(8,128)(2,1)S(1)}, u32[]{:S(2)}, u32[]{:S(2)}) collective-permute-start(bf16[2,128,128]{2,1,0:T(8,128)(2,1)S(1)} %collective-permute-done.4.down_ref), channel_id=1, source_target_pairs={{0,1},{1,2},{2,3},{3,4},{4,5},{5,6},{6,7},{8,9},{9,10},{10,11},{11... | collective-permute-start | bytes 196616 | tf_op jit(solution)/shard_map/ppermute | solution.py:197
  23.4 16.9 %copy-start.4 = (bf16[2,128,128]{2,1,0:T(8,128)(2,1)}, bf16[2,128,128]{2,1,0:T(8,128)(2,1)S(1)}, u32[]{:S(2)}) copy-start(bf16[2,128,128]{2,1,0:T(8,128)(2,1)S(1)} %collective-permute-done.3.up_ref) | copy-start | bytes 196612
  23.4 21.1 %collective-permute-start.5 = (bf16[2,128,128]{2,1,0:T(8,128)(2,1)S(1)}, bf16[2,128,128]{2,1,0:T(8,128)(2,1)S(1)}, u32[]{:S(2)}, u32[]{:S(2)}) collective-permute-start(bf16[2,128,128]{2,1,0:T(8,128)(2,1)S(1)} %collective-permute-done.3.up_ref), channel_id=1, source_target_pairs={{1,0},{2,1},{3,2},{4,3},{5,4},{6,5},{7,6},{9,8},{10,9},{11,10},{12... | collective-permute-start | bytes 196616 | tf_op jit(solution)/shard_map/ppermute | solution.py:198
  31.0 4.9 %copy-start.1 = (bf16[10,2,128,128]{3,2,1,0:T(8,128)(2,1)}, bf16[10,2,128,128]{3,2,1,0:T(8,128)(2,1)S(1)}, u32[]{:S(2)}) copy-start(bf16[10,2,128,128]{3,2,1,0:T(8,128)(2,1)S(1)} %collective-permute-done.2.right_ref) | copy-start | bytes 1966084
  35.9 0.8 %copy-start.2 = (bf16[10,2,128,128]{3,2,1,0:T(8,128)(2,1)}, bf16[10,2,128,128]{3,2,1,0:T(8,128)(2,1)S(1)}, u32[]{:S(2)}) copy-start(bf16[10,2,128,128]{3,2,1,0:T(8,128)(2,1)S(1)} %collective-permute-done.1.left_ref) | copy-start | bytes 1966084
  44.5 0.6 %copy-start.5 = (bf16[2,128,128]{2,1,0:T(8,128)(2,1)}, bf16[2,128,128]{2,1,0:T(8,128)(2,1)S(1)}, u32[]{:S(2)}) copy-start(bf16[2,128,128]{2,1,0:T(8,128)(2,1)S(1)} %collective-permute-done.6.down_left_ref) | copy-start | bytes 196612
  45.1 0.6 %copy-start.6 = (bf16[2,128,128]{2,1,0:T(8,128)(2,1)}, bf16[2,128,128]{2,1,0:T(8,128)(2,1)S(1)}, u32[]{:S(2)}) copy-start(bf16[2,128,128]{2,1,0:T(8,128)(2,1)S(1)} %collective-permute-done.5.up_right_ref) | copy-start | bytes 196612

commit v16 on v14

--- a/solution.py
+++ b/solution.py
@@ -23,8 +23,10 @@
     extended = band_local + 2
     window = tile_rows + band_local - 1
 
-    def kernel(ids, q_ref, jac_ref, recv_ref, mid_ref, left_ref, right_ref, up_ref, down_ref,
-               up_right_ref, down_left_ref, out_ref, win_ref, spread_ref):
+    half_rows = tile_rows // 2
+
+    def kernel(ids, q_ref, jac_ref, recv_ref, mid_ref, left_ref, left_late_ref, right_ref,
+               right_late_ref, up_ref, down_ref, out_ref, win_ref, spread_ref):
         row_id = ids[0]
         col_id = ids[1]
         first_row = row_id * tile_rows
@@ -48,16 +50,17 @@
                             win_ref[position, g] = recv_ref[at - tile_rows, g]
 
         def prior_tile(ext_row, ext_slot, masked):
+            at = ext_row - 1
             if ext_slot < 2:
-                if ext_row == tile_rows + 1:
-                    tile = down_left_ref[band_local - 2 + ext_slot]
+                if at < half_rows:
+                    tile = left_ref[at, band_local - 2 + ext_slot]
                 else:
-                    tile = left_ref[ext_row - 1, band_local - 2 + ext_slot]
+                    tile = left_late_ref[at - half_rows, band_local - 2 + ext_slot]
             elif ext_slot >= 2 + band_local:
-                if ext_row == 0:
-                    tile = up_right_ref[ext_slot - 2 - band_local]
+                if 0 <= at < half_rows:
+                    tile = right_ref[at, ext_slot - 2 - band_local]
                 else:
-                    tile = right_ref[ext_row - 1, ext_slot - 2 - band_local]
+                    tile = right_late_ref[max(at - half_rows + 1, 0), ext_slot - 2 - band_local]
             elif ext_row == 0:
                 tile = up_ref[ext_slot - 2]
             elif ext_row == tile_rows + 1:
@@ -140,8 +143,10 @@
     def flat(a, b):
         return a * col_count + b
 
-    left = lax.ppermute(p_band, "col", [(b, b + 1) for b in range(col_count - 1)])
-    right = lax.ppermute(p_band, "col", [(b + 1, b) for b in range(col_count - 1)])
+    half_rows = tile_rows // 2
+    early = p_band[:half_rows]
+    left = lax.ppermute(early, "col", [(b, b + 1) for b in range(col_count - 1)])
+    right = lax.ppermute(early, "col", [(b + 1, b) for b in range(col_count - 1)])
     up = lax.ppermute(p_band[-1], "row", [(a, a + 1) for a in range(row_count - 1)])
     down = lax.ppermute(p_band[0], "row", [(a + 1, a) for a in range(row_count - 1)])
 
@@ -173,8 +178,16 @@
         jnp.round(received_meta[1, :sent_rows]).astype(jnp.int32),
     )
 
-    down_left = lax.ppermute(down, "col", [(b, b + 1) for b in range(col_count - 1)])
-    up_right = lax.ppermute(up, "col", [(b + 1, b) for b in range(col_count - 1)])
+    left_late = lax.ppermute(
+        jnp.concatenate([p_band[half_rows:], down[None]], axis=0),
+        "col",
+        [(b, b + 1) for b in range(col_count - 1)],
+    )
+    right_late = lax.ppermute(
+        jnp.concatenate([up[None], p_band[half_rows:]], axis=0),
+        "col",
+        [(b + 1, b) for b in range(col_count - 1)],
+    )
 
     ids = jnp.stack([row_id, col_id]).astype(jnp.int32)
     vmem = pl.BlockSpec(memory_space=pltpu.MemorySpace.VMEM)
@@ -188,7 +201,7 @@
             pltpu.VMEM((tile_rows + band_local - 1, 3, tile_size, tile_size), p_band.dtype),
             pltpu.VMEM((tile_rows, tile_size, (band_local + 2) * tile_size), p_band.dtype),
         ],
-    )(ids, q_var, jacobian, received, p_band, left, right, up, down, up_right, down_left)
+    )(ids, q_var, jacobian, received, p_band, left, left_late, right, right_late, up, down)
 
 
 def solution(mesh):

time: 49.2 us -> 57.2 us (1.16)
  the two profiles are of different devices: /device:TPU:414 before, /device:TPU:238 now
where the time goes in v16:
time: 57.2 us; the launch traced here: 56.8 us
  starting transfers between devices  27.1 us (47%)
  waiting for transfers between devices  13.5 us (24%)
  local copies, waits for them, and re-layouts  6.66 us (12%)
  other arithmetic  5.03 us (9%)
  Pallas kernels  4.4 us (8%)
    ppermute x1, starting transfers between devices, shards(): lax.ppermute(jnp.concatenate([p_band[half_rows:], down[None]], axis=0), '...  9.39 us
    ppermute x1, waiting for transfers between devices, shards(): lax.ppermute(jnp.concatenate([up[None], p_band[half_rows:]], axis=0), 'co...  7.73 us
    pallas_call x1, Pallas kernels, shards(): pl.pallas_call(band_kernel(tile_rows, band_local, half_band, grid_tiles,...  4.4 us
    ppermute x1, starting transfers between devices, shards(): lax.ppermute(p_band[-1], 'row', [(a, a + 1) for a in range(row_count - 1)])  4.2 us
    ppermute x1, starting transfers between devices, shards(): lax.ppermute(early, 'col', [(b, b + 1) for b in range(col_count - 1)])  4.11 us
    ppermute x1, starting transfers between devices, shards(): lax.ppermute(p_band[0], 'row', [(a + 1, a) for a in range(row_count - 1)])  3.64 us
    ppermute x1, waiting for transfers between devices, shards(): lax.ppermute(jnp.concatenate([p_band[half_rows:], down[None]], axis=0), '...  3.45 us
    unnamed x16, local copies, waits for them, and re-layouts  2.64 us
  transfers between devices with their start and end apart: 7, of which 4 were waited for; matrix products, arithmetic and copies ran while one was open for 13% of the time, Pallas kernels for 0%

profile of v16, /device:TPU:238, one launch (start us, length us, event | category | flops | bytes accessed | tf_op | source)
XLA Modules:
  0.0 56.8 jit_solution(15608885340807587096)
XLA Ops:
  0.0 1.9 %fusion.28 = (bf16[5,2,128,128]{3,2,1,0:T(8,128)(2,1)S(1)}, bf16[5,2,128,128]{3,2,1,0:T(8,128)(2,1)}) fusion(bf16[10,2,128,128]{3,2,1,0:T(8,128)(2,1)} %mid_ref.1), kind=kLoop, calls=%fused_computation.84 | loop fusion | bytes 1310720 | tf_op jit(solution)/shard_map/slice | solution.py:182
  1.9 4.1 %collective-permute-start.1 = (bf16[5,2,128,128]{3,2,1,0:T(8,128)(2,1)}, bf16[5,2,128,128]{3,2,1,0:T(8,128)(2,1)S(1)}, u32[]{:S(2)}, u32[]{:S(2)}) collective-permute-start(bf16[5,2,128,128]{3,2,1,0:T(8,128)(2,1)} %get-tuple-element.50), channel_id=1, source_target_pairs={{0,1},{1,2},{2,3},{3,4},{4,5},{5,6},{6,7},{8,9},{9,10},{10,11},{11... | collective-permute-start | bytes 983048 | tf_op jit(solution)/shard_map/ppermute | solution.py:148
  6.0 1.9 %collective-permute-start.4 = (bf16[5,2,128,128]{3,2,1,0:T(8,128)(2,1)}, bf16[5,2,128,128]{3,2,1,0:T(8,128)(2,1)}, u32[]{:S(2)}, u32[]{:S(2)}) collective-permute-start(bf16[5,2,128,128]{3,2,1,0:T(8,128)(2,1)} %get-tuple-element.50), channel_id=1, source_target_pairs={{1,0},{2,1},{3,2},{4,3},{5,4},{6,5},{7,6},{9,8},{10,9},{11,10},{12... | collective-permute-start | bytes 983048 | tf_op jit(solution)/shard_map/ppermute | solution.py:149
  8.0 0.7 %copy-done.6 = s32[10,3]{0,1:T(4,128)S(1)} copy-done((s32[10,3]{0,1:T(4,128)S(1)}, s32[10,3]{0,1:T(4,128)}, u32[]{:S(2)}) %copy-start.6) | copy-done | bytes 144
  8.9 0.7 %copy-done.7 = s32[10]{0:T(128)S(1)} copy-done((s32[10]{0:T(128)S(1)}, s32[10]{0:T(128)}, u32[]{:S(2)}) %copy-start.7) | copy-done | bytes 64
  9.9 1.0 %pad_maximum_fusion.1 = bf16[25,128,128]{2,1,0:T(8,128)(2,1)} fusion(bf16[1,128,128]{2,1,0:T(8,128)(2,1)S(1)} %scatter.9, bf16[24,128,128]{2,1,0:T(8,128)(2,1)S(1)} %bitcast.40), kind=kLoop, calls=%fused_computation.10 | loop fusion | flops 409600 | bytes 1638400 | tf_op jit(solution)/shard_map/concatenate | solution.py:164
  10.9 1.9 %collective-permute-start = (bf16[25,128,128]{2,1,0:T(8,128)(2,1)}, bf16[25,128,128]{2,1,0:T(8,128)(2,1)S(1)}, u32[]{:S(2)}, u32[]{:S(2)}) collective-permute-start(bf16[25,128,128]{2,1,0:T(8,128)(2,1)} %pad_maximum_fusion.1), channel_id=1, source_target_pairs={{0,8},{8,16},{16,24},{24,32},{32,40},{40,48},{48,56},{56,64},{64,7... | collective-permute-start | bytes 2457608 | tf_op jit(solution)/shard_map/ppermute | solution.py:171
  12.8 0.9 %slice_bitcast_fusion = (bf16[2,128,128]{2,1,0:T(8,128)(2,1)S(1)}, bf16[2,128,128]{2,1,0:T(8,128)(2,1)S(1)}) fusion(bf16[10,2,128,128]{3,2,1,0:T(8,128)(2,1)} %mid_ref.1), kind=kLoop, calls=%fused_computation.41 | loop fusion | bytes 262144 | tf_op jit(solution)/shard_map/squeeze | solution.py:150
  13.7 3.6 %collective-permute-start.2 = (bf16[2,128,128]{2,1,0:T(8,128)(2,1)S(1)}, bf16[2,128,128]{2,1,0:T(8,128)(2,1)S(1)}, u32[]{:S(2)}, u32[]{:S(2)}) collective-permute-start(bf16[2,128,128]{2,1,0:T(8,128)(2,1)S(1)} %get-tuple-element.48), channel_id=1, source_target_pairs={{8,0},{16,8},{24,16},{32,24},{40,32},{48,40},{56,48},{64,56},{72,6... | collective-permute-start | bytes 196616 | tf_op jit(solution)/shard_map/ppermute | solution.py:151
  17.4 4.2 %collective-permute-start.5 = (bf16[2,128,128]{2,1,0:T(8,128)(2,1)S(1)}, bf16[2,128,128]{2,1,0:T(8,128)(2,1)S(1)}, u32[]{:S(2)}, u32[]{:S(2)}) collective-permute-start(bf16[2,128,128]{2,1,0:T(8,128)(2,1)S(1)} %get-tuple-element.47), channel_id=1, source_target_pairs={{0,8},{8,16},{16,24},{24,32},{32,40},{40,48},{48,56},{56,64},{64,7... | collective-permute-start | bytes 196616 | tf_op jit(solution)/shard_map/ppermute | solution.py:150
  21.6 0.5 fusion.2
  22.2 1.1 %pad_maximum_fusion.jac_ref = bf16[10,3,128,128]{3,2,1,0:T(8,128)(2,1)} fusion(bf16[10,1,128,128]{3,2,1,0:T(8,128)(2,1)S(1)} %get-tuple-element.42, bf16[10,1,128,128]{3,2,1,0:T(8,128)(2,1)S(1)} %get-tuple-element.43, bf16[10,1,128,128]{3,2,1,0:T(8,128)(2,1)S(1)} %get-tuple-element.41), kind=kLoop, calls=%fused_computation | loop fusion | flops 983040 | bytes 1966080 | tf_op jit(solution)/shard_map/stack | solution.py:19
  23.3 0.6 %pad_add_fusion.ids = s32[2]{0:T(128)} fusion(s32[1]{0:T(128)} %bitcast.1, s32[1]{0:T(128)} %bitcast), kind=kLoop, calls=%fused_computation.81 | loop fusion | flops 2 | bytes 16 | tf_op jit(solution)/shard_map/stack | solution.py:192
  23.9 2.1 %collective-permute-done.2.down_ref = bf16[2,128,128]{2,1,0:T(8,128)(2,1)S(1)} collective-permute-done((bf16[2,128,128]{2,1,0:T(8,128)(2,1)S(1)}, bf16[2,128,128]{2,1,0:T(8,128)(2,1)S(1)}, u32[]{:S(2)}, u32[]{:S(2)}) %collective-permute-start.2) | collective-permute-done | bytes 65568 | tf_op jit(solution)/shard_map/ppermute | solution.py:151
  26.2 0.4 copy-done.4
  26.8 9.4 %collective-permute-start.3 = (bf16[6,2,128,128]{3,2,1,0:T(8,128)(2,1)S(1)}, bf16[6,2,128,128]{3,2,1,0:T(8,128)(2,1)S(1)}, u32[]{:S(2)}, u32[]{:S(2)}) collective-permute-start(bf16[6,2,128,128]{3,2,1,0:T(8,128)(2,1)S(1)} %get-tuple-element.52), channel_id=1, source_target_pairs={{0,1},{1,2},{2,3},{3,4},{4,5},{5,6},{6,7},{8,9},{9,10},{10,11},{11... | collective-permute-start | bytes 1179656 | tf_op jit(solution)/shard_map/ppermute | solution.py:181
  36.2 1.9 %collective-permute-start.6 = (bf16[6,2,128,128]{3,2,1,0:T(8,128)(2,1)S(1)}, bf16[6,2,128,128]{3,2,1,0:T(8,128)(2,1)S(1)}, u32[]{:S(2)}, u32[]{:S(2)}) collective-permute-start(bf16[6,2,128,128]{3,2,1,0:T(8,128)(2,1)S(1)} %get-tuple-element.51), channel_id=1, source_target_pairs={{1,0},{2,1},{3,2},{4,3},{5,4},{6,5},{7,6},{9,8},{10,9},{11,10},{12... | collective-permute-start | bytes 1179656 | tf_op jit(solution)/shard_map/ppermute | solution.py:186
  38.5 0.3 slice_reduce_fusion.2
  39.0 0.5 fusion.11
  39.5 1.0 %pad_maximum_fusion.2.recv_ref = bf16[8,3,128,128]{3,2,1,0:T(8,128)(2,1)} fusion(bf16[8,1,128,128]{3,2,1,0:T(8,128)(2,1)S(1)} %get-tuple-element.45, bf16[8,1,128,128]{3,2,1,0:T(8,128)(2,1)S(1)} %get-tuple-element.46, bf16[8,1,128,128]{3,2,1,0:T(8,128)(2,1)S(1)} %get-tuple-element.44), kind=kLoop, calls=%fused_computation.11 | loop fusion | flops 786432 | bytes 1572864 | tf_op jit(solution)/shard_map/stack | solution.py:19
  40.5 3.5 %collective-permute-done.3.left_late_ref = bf16[6,2,128,128]{3,2,1,0:T(8,128)(2,1)S(1)} collective-permute-done((bf16[6,2,128,128]{3,2,1,0:T(8,128)(2,1)S(1)}, bf16[6,2,128,128]{3,2,1,0:T(8,128)(2,1)S(1)}, u32[]{:S(2)}, u32[]{:S(2)}) %collective-permute-start.3) | collective-permute-done | bytes 393248 | tf_op jit(solution)/shard_map/ppermute | solution.py:181
  44.0 7.7 %collective-permute-done.6.right_late_ref = bf16[6,2,128,128]{3,2,1,0:T(8,128)(2,1)S(1)} collective-permute-done((bf16[6,2,128,128]{3,2,1,0:T(8,128)(2,1)S(1)}, bf16[6,2,128,128]{3,2,1,0:T(8,128)(2,1)S(1)}, u32[]{:S(2)}, u32[]{:S(2)}) %collective-permute-start.6) | collective-permute-done | bytes 393248 | tf_op jit(solution)/shard_map/ppermute | solution.py:186
  51.7 0.7 %copy-done.2 = bf16[6,2,128,128]{3,2,1,0:T(8,128)(2,1)} copy-done((bf16[6,2,128,128]{3,2,1,0:T(8,128)(2,1)}, bf16[6,2,128,128]{3,2,1,0:T(8,128)(2,1)S(1)}, u32[]{:S(2)}) %copy-start.2) | copy-done | bytes 393240
  52.4 4.4 %shard_map.55 = bf16[10,2,128,128]{3,2,1,0:T(8,128)(2,1)} custom-call(s32[2]{0:T(128)} %pad_add_fusion.ids, f32[10,128]{1,0:T(8,128)} %q_ref.1, bf16[10,3,128,128]{3,2,1,0:T(8,128)(2,1)} %pad_maximum_fusion.jac_ref, bf16[8,3,128,128]{3,2,1,0:T(8,128)(2,1)} %pad_maximum_fusion.2.recv_ref, bf16[10,2,128,128]{3,2,1,0:T(8,128)(2,1)} %mid_ref.1, ...), custom_call_target="tpu_custom_call" | custom-call | tf_op jit(solution)/shard_map/pallas_call | solution.py:195
  (36 shorter events, 1.7 us)
Async XLA Ops:
  0.0 9.7 %copy-start = (bf16[10,3,128,128]{3,2,1,0:T(8,128)(2,1)S(1)}, bf16[10,3,128,128]{3,2,1,0:T(8,128)(2,1)}, u32[]{:S(2)}) copy-start(bf16[10,3,128,128]{3,2,1,0:T(8,128)(2,1)} %param.10) | copy-start | bytes 2949124
  1.9 38.6 %collective-permute-start.1 = (bf16[5,2,128,128]{3,2,1,0:T(8,128)(2,1)}, bf16[5,2,128,128]{3,2,1,0:T(8,128)(2,1)S(1)}, u32[]{:S(2)}, u32[]{:S(2)}) collective-permute-start(bf16[5,2,128,128]{3,2,1,0:T(8,128)(2,1)} %get-tuple-element.50), channel_id=1, source_target_pairs={{0,1},{1,2},{2,3},{3,4},{4,5},{5,6},{6,7},{8,9},{9,10},{10,11},{11... | collective-permute-start | bytes 983048 | tf_op jit(solution)/shard_map/ppermute | solution.py:148
  6.0 34.5 %collective-permute-start.4 = (bf16[5,2,128,128]{3,2,1,0:T(8,128)(2,1)}, bf16[5,2,128,128]{3,2,1,0:T(8,128)(2,1)}, u32[]{:S(2)}, u32[]{:S(2)}) collective-permute-start(bf16[5,2,128,128]{3,2,1,0:T(8,128)(2,1)} %get-tuple-element.50), channel_id=1, source_target_pairs={{1,0},{2,1},{3,2},{4,3},{5,4},{6,5},{7,6},{9,8},{10,9},{11,10},{12... | collective-permute-start | bytes 983048 | tf_op jit(solution)/shard_map/ppermute | solution.py:149
  8.0 0.7 %copy-start.6 = (s32[10,3]{0,1:T(4,128)S(1)}, s32[10,3]{0,1:T(4,128)}, u32[]{:S(2)}) copy-start(s32[10,3]{0,1:T(4,128)} %param.11) | copy-start | bytes 364
  8.9 0.7 %copy-start.7 = (s32[10]{0:T(128)S(1)}, s32[10]{0:T(128)}, u32[]{:S(2)}) copy-start(s32[10]{0:T(128)} %param.12) | copy-start | bytes 124
  10.9 27.2 %collective-permute-start = (bf16[25,128,128]{2,1,0:T(8,128)(2,1)}, bf16[25,128,128]{2,1,0:T(8,128)(2,1)S(1)}, u32[]{:S(2)}, u32[]{:S(2)}) collective-permute-start(bf16[25,128,128]{2,1,0:T(8,128)(2,1)} %pad_maximum_fusion.1), channel_id=1, source_target_pairs={{0,8},{8,16},{16,24},{24,32},{32,40},{40,48},{48,56},{56,64},{64,7... | collective-permute-start | bytes 2457608 | tf_op jit(solution)/shard_map/ppermute | solution.py:171
  13.7 12.3 %collective-permute-start.2 = (bf16[2,128,128]{2,1,0:T(8,128)(2,1)S(1)}, bf16[2,128,128]{2,1,0:T(8,128)(2,1)S(1)}, u32[]{:S(2)}, u32[]{:S(2)}) collective-permute-start(bf16[2,128,128]{2,1,0:T(8,128)(2,1)S(1)} %get-tuple-element.48), channel_id=1, source_target_pairs={{8,0},{16,8},{24,16},{32,24},{40,32},{48,40},{56,48},{64,56},{72,6... | collective-permute-start | bytes 196616 | tf_op jit(solution)/shard_map/ppermute | solution.py:151
  17.4 8.8 %collective-permute-start.5 = (bf16[2,128,128]{2,1,0:T(8,128)(2,1)S(1)}, bf16[2,128,128]{2,1,0:T(8,128)(2,1)S(1)}, u32[]{:S(2)}, u32[]{:S(2)}) collective-permute-start(bf16[2,128,128]{2,1,0:T(8,128)(2,1)S(1)} %get-tuple-element.47), channel_id=1, source_target_pairs={{0,8},{8,16},{16,24},{24,32},{32,40},{40,48},{48,56},{56,64},{64,7... | collective-permute-start | bytes 196616 | tf_op jit(solution)/shard_map/ppermute | solution.py:150
  26.0 0.6 %copy-start.4 = (bf16[2,128,128]{2,1,0:T(8,128)(2,1)}, bf16[2,128,128]{2,1,0:T(8,128)(2,1)S(1)}, u32[]{:S(2)}) copy-start(bf16[2,128,128]{2,1,0:T(8,128)(2,1)S(1)} %collective-permute-done.2.down_ref) | copy-start | bytes 196612
  26.2 0.6 %copy-start.5 = (bf16[2,128,128]{2,1,0:T(8,128)(2,1)}, bf16[2,128,128]{2,1,0:T(8,128)(2,1)S(1)}, u32[]{:S(2)}) copy-start(bf16[2,128,128]{2,1,0:T(8,128)(2,1)S(1)} %collective-permute-done.5.up_ref) | copy-start | bytes 196612
  26.8 17.2 %collective-permute-start.3 = (bf16[6,2,128,128]{3,2,1,0:T(8,128)(2,1)S(1)}, bf16[6,2,128,128]{3,2,1,0:T(8,128)(2,1)S(1)}, u32[]{:S(2)}, u32[]{:S(2)}) collective-permute-start(bf16[6,2,128,128]{3,2,1,0:T(8,128)(2,1)S(1)} %get-tuple-element.52), channel_id=1, source_target_pairs={{0,1},{1,2},{2,3},{3,4},{4,5},{5,6},{6,7},{8,9},{9,10},{10,11},{11... | collective-permute-start | bytes 1179656 | tf_op jit(solution)/shard_map/ppermute | solution.py:181
  36.2 15.5 %collective-permute-start.6 = (bf16[6,2,128,128]{3,2,1,0:T(8,128)(2,1)S(1)}, bf16[6,2,128,128]{3,2,1,0:T(8,128)(2,1)S(1)}, u32[]{:S(2)}, u32[]{:S(2)}) collective-permute-start(bf16[6,2,128,128]{3,2,1,0:T(8,128)(2,1)S(1)} %get-tuple-element.51), channel_id=1, source_target_pairs={{1,0},{2,1},{3,2},{4,3},{5,4},{6,5},{7,6},{9,8},{10,9},{11,10},{12... | collective-permute-start | bytes 1179656 | tf_op jit(solution)/shard_map/ppermute | solution.py:186
  40.5 11.2 %copy-start.3 = (bf16[5,2,128,128]{3,2,1,0:T(8,128)(2,1)}, bf16[5,2,128,128]{3,2,1,0:T(8,128)(2,1)S(1)}, u32[]{:S(2)}) copy-start(bf16[5,2,128,128]{3,2,1,0:T(8,128)(2,1)S(1)} %collective-permute-done.1.left_ref) | copy-start | bytes 983044
  44.0 7.7 %copy-start.1 = (bf16[6,2,128,128]{3,2,1,0:T(8,128)(2,1)}, bf16[6,2,128,128]{3,2,1,0:T(8,128)(2,1)S(1)}, u32[]{:S(2)}) copy-start(bf16[6,2,128,128]{3,2,1,0:T(8,128)(2,1)S(1)} %collective-permute-done.3.left_late_ref) | copy-start | bytes 1179652
  51.7 0.7 %copy-start.2 = (bf16[6,2,128,128]{3,2,1,0:T(8,128)(2,1)}, bf16[6,2,128,128]{3,2,1,0:T(8,128)(2,1)S(1)}, u32[]{:S(2)}) copy-start(bf16[6,2,128,128]{3,2,1,0:T(8,128)(2,1)S(1)} %collective-permute-done.6.right_late_ref) | copy-start | bytes 1179652

commit v17 on v14

--- a/solution.py
+++ b/solution.py
@@ -142,8 +142,6 @@
 
     left = lax.ppermute(p_band, "col", [(b, b + 1) for b in range(col_count - 1)])
     right = lax.ppermute(p_band, "col", [(b + 1, b) for b in range(col_count - 1)])
-    up = lax.ppermute(p_band[-1], "row", [(a, a + 1) for a in range(row_count - 1)])
-    down = lax.ppermute(p_band[0], "row", [(a + 1, a) for a in range(row_count - 1)])
 
     sent_rows = half_band
     lower_half = col_id < col_count // 2
@@ -156,7 +154,9 @@
     sent_tiles = lax.dynamic_slice_in_dim(blocks, send_start, sent_rows, 0).reshape(
         (sent_rows * 3, tile_size, tile_size)
     )
-    sent = jnp.concatenate([sent_tiles, meta[None]], axis=0)
+    with_rows = lax.dynamic_slice_in_dim(p_band, jnp.where(lower_half, tile_rows - 1, 0), 1, 0)[0]
+    alone_rows = lax.dynamic_slice_in_dim(p_band, jnp.where(lower_half, 0, tile_rows - 1), 1, 0)[0]
+    sent = jnp.concatenate([sent_tiles, meta[None], with_rows], axis=0)
     pairs = []
     for b in range(col_count):
         if b * band_local - half_band < 0:
@@ -164,6 +164,10 @@
         else:
             pairs += [(flat(a, b), flat(a - 1, b)) for a in range(1, row_count)]
     received_all = lax.ppermute(sent, ("row", "col"), pairs)
+    received_alone = lax.ppermute(alone_rows, ("row", "col"), [(t, f) for f, t in pairs])
+    received_with = received_all[sent_rows * 3 + 1 :]
+    up = jnp.where(lower_half, received_with, received_alone)
+    down = jnp.where(lower_half, received_alone, received_with)
 
     jacobian = assemble(blocks, block_offsets, block_live)
     received_meta = received_all[sent_rows * 3].astype(jnp.float32)

time: 49.2 us -> 49.4 us (level)
  the two profiles are of different devices: /device:TPU:414 before, /device:TPU:501 now
where the time goes in v17:
time: 49.4 us; the launch traced here: 49 us
  starting transfers between devices  27 us (55%)
  waiting for transfers between devices  7.17 us (15%)
  local copies, waits for them, and re-layouts  6.06 us (12%)
  Pallas kernels  4.4 us (9%)
  other arithmetic  4.12 us (8%)
    ppermute x1, starting transfers between devices, shards(): lax.ppermute(down, 'col', [(b, b + 1) for b in range(col_count - 1)])  13.6 us
    ppermute x1, waiting for transfers between devices, shards(): received_all = lax.ppermute(sent, ('row', 'col'), pairs)  7.15 us
    pallas_call x1, Pallas kernels, shards(): pl.pallas_call(band_kernel(tile_rows, band_local, half_band, grid_tiles,...  4.4 us
    ppermute x1, starting transfers between devices, shards(): received_all = lax.ppermute(sent, ('row', 'col'), pairs)  3.14 us
    ppermute x1, starting transfers between devices, shards(): lax.ppermute(p_band, 'col', [(b, b + 1) for b in range(col_count - 1)])  2.82 us
    ppermute x1, starting transfers between devices, shards(): lax.ppermute(alone_rows, ('row', 'col'), [(t, f) for f, t in pairs])  2.81 us
    unnamed x18, local copies, waits for them, and re-layouts  2.78 us
    ppermute x1, starting transfers between devices, shards(): lax.ppermute(p_band, 'col', [(b + 1, b) for b in range(col_count - 1)])  2.46 us
  transfers between devices with their start and end apart: 6, of which 1 were waited for; matrix products, arithmetic and copies ran while one was open for 15% of the time, Pallas kernels for 0%

profile of v17, /device:TPU:501, one launch (start us, length us, event | category | flops | bytes accessed | tf_op | source)
XLA Modules:
  0.0 49.0 jit_solution(7136752186965080468)
XLA Ops:
  0.0 2.8 %collective-permute-start.1 = (bf16[10,2,128,128]{3,2,1,0:T(8,128)(2,1)}, bf16[10,2,128,128]{3,2,1,0:T(8,128)(2,1)S(1)}, u32[]{:S(2)}, u32[]{:S(2)}) collective-permute-start(bf16[10,2,128,128]{3,2,1,0:T(8,128)(2,1)} %mid_ref.1), channel_id=1, source_target_pairs={{0,1},{1,2},{2,3},{3,4},{4,5},{5,6},{6,7},{8,9},{9,10},{10,11},{11... | collective-permute-start | bytes 1966088 | tf_op jit(solution)/shard_map/ppermute | solution.py:143
  2.8 2.5 %collective-permute-start.2 = (bf16[10,2,128,128]{3,2,1,0:T(8,128)(2,1)}, bf16[10,2,128,128]{3,2,1,0:T(8,128)(2,1)}, u32[]{:S(2)}, u32[]{:S(2)}) collective-permute-start(bf16[10,2,128,128]{3,2,1,0:T(8,128)(2,1)} %mid_ref.1), channel_id=1, source_target_pairs={{1,0},{2,1},{3,2},{4,3},{5,4},{6,5},{7,6},{9,8},{10,9},{11,10},{12... | collective-permute-start | bytes 1966088 | tf_op jit(solution)/shard_map/ppermute | solution.py:144
  5.3 0.7 %copy-done.6 = s32[10,3]{0,1:T(4,128)S(1)} copy-done((s32[10,3]{0,1:T(4,128)S(1)}, s32[10,3]{0,1:T(4,128)}, u32[]{:S(2)}) %copy-start.6) | copy-done | bytes 144
  6.1 0.1 copy.7
  6.3 0.7 %copy-done.7 = s32[10]{0:T(128)S(1)} copy-done((s32[10]{0:T(128)S(1)}, s32[10]{0:T(128)}, u32[]{:S(2)}) %copy-start.7) | copy-done | bytes 64
  7.0 1.2 %constant_dynamic-slice_fusion = bf16[8,3,128,128]{3,2,1,0:T(8,128)(2,1)S(1)} fusion(bf16[10,3,128,128]{3,2,1,0:T(8,128)(2,1)} %param.10, s32[]{:T(128)S(6)} %select_n.110), kind=kLoop, calls=%fused_computation.76 | loop fusion | bytes 1572868 | tf_op jit(solution)/shard_map/dynamic_slice | solution.py:154
  8.2 1.0 %dynamic-slice_bitcast_fusion = (bf16[2,128,128]{2,1,0:T(8,128)(2,1)S(1)}, bf16[2,128,128]{2,1,0:T(8,128)(2,1)S(1)}) fusion(bf16[10,2,128,128]{3,2,1,0:T(8,128)(2,1)} %mid_ref.1, s32[]{:T(128)S(6)} %select_n.122, s32[]{:T(128)S(6)} %select_n.111), kind=kLoop, calls=%fused_computation.39 | loop fusion | bytes 262152 | tf_op jit(solution)/shard_map/squeeze | solution.py:158
  9.2 0.2 scatter.9
  9.3 0.1 pad_maximum_fusion.1
  9.5 3.1 %collective-permute-start = (bf16[27,128,128]{2,1,0:T(8,128)(2,1)S(1)}, bf16[27,128,128]{2,1,0:T(8,128)(2,1)S(1)}, u32[]{:S(2)}, u32[]{:S(2)}) collective-permute-start(bf16[27,128,128]{2,1,0:T(8,128)(2,1)S(1)} %pad_maximum_fusion.1), channel_id=1, source_target_pairs={{0,8},{8,16},{16,24},{24,32},{32,40},{40,48},{48,56},{56,64},{64,7... | collective-permute-start | bytes 2654216 | tf_op jit(solution)/shard_map/ppermute | solution.py:166
  12.6 2.8 %collective-permute-start.3 = (bf16[2,128,128]{2,1,0:T(8,128)(2,1)S(1)}, bf16[2,128,128]{2,1,0:T(8,128)(2,1)S(1)}, u32[]{:S(2)}, u32[]{:S(2)}) collective-permute-start(bf16[2,128,128]{2,1,0:T(8,128)(2,1)S(1)} %get-tuple-element.49), channel_id=1, source_target_pairs={{8,0},{16,8},{24,16},{32,24},{40,32},{48,40},{56,48},{64,56},{72,6... | collective-permute-start | bytes 196616 | tf_op jit(solution)/shard_map/ppermute | solution.py:167
  15.5 0.6 %pad_add_fusion.ids = s32[2]{0:T(128)} fusion(s32[1]{0:T(128)} %bitcast.1, s32[1]{0:T(128)} %bitcast), kind=kLoop, calls=%fused_computation.82 | loop fusion | flops 2 | bytes 16 | tf_op jit(solution)/shard_map/stack | solution.py:183
  16.1 0.5 %fusion.2 = (bf16[10,1,128,128]{3,2,1,0:T(8,128)(2,1)S(1)}, bf16[10,1,128,128]{3,2,1,0:T(8,128)(2,1)S(1)}, bf16[10,1,128,128]{3,2,1,0:T(8,128)(2,1)S(1)}) fusion(pred[10]{0:T(512)(128)(4,1)S(1)} %get-tuple-element.58, pred[10]{0:T(512)(128)(4,1)S(1)} %get-tuple-element.59, pred[10]{0:T(512)(128)(4,1)S(1)} %get-tuple-element.57, ...), kind=kLoop, calls=%fused_computation.23 | loop fusion | flops 3440640 | bytes 1966170 | tf_op jit(solution)/shard_map/convert_element_type | solution.py:18
  16.7 1.1 %pad_maximum_fusion.jac_ref = bf16[10,3,128,128]{3,2,1,0:T(8,128)(2,1)} fusion(bf16[10,1,128,128]{3,2,1,0:T(8,128)(2,1)S(1)} %get-tuple-element.42, bf16[10,1,128,128]{3,2,1,0:T(8,128)(2,1)S(1)} %get-tuple-element.43, bf16[10,1,128,128]{3,2,1,0:T(8,128)(2,1)S(1)} %get-tuple-element.41), kind=kLoop, calls=%fused_computation | loop fusion | flops 983040 | bytes 1966080 | tf_op jit(solution)/shard_map/stack | solution.py:19
  17.8 7.2 %collective-permute-done = bf16[27,128,128]{2,1,0:T(8,128)(2,1)S(1)} collective-permute-done((bf16[27,128,128]{2,1,0:T(8,128)(2,1)S(1)}, bf16[27,128,128]{2,1,0:T(8,128)(2,1)S(1)}, u32[]{:S(2)}, u32[]{:S(2)}) %collective-permute-start) | collective-permute-done | bytes 884768 | tf_op jit(solution)/shard_map/ppermute | solution.py:166
  25.3 2.2 %collective-permute-start.4 = (bf16[2,128,128]{2,1,0:T(8,128)(2,1)S(1)}, bf16[2,128,128]{2,1,0:T(8,128)(2,1)S(1)}, u32[]{:S(2)}, u32[]{:S(2)}) collective-permute-start(bf16[2,128,128]{2,1,0:T(8,128)(2,1)S(1)} %get-tuple-element.45.up_ref), channel_id=1, source_target_pairs={{1,0},{2,1},{3,2},{4,3},{5,4},{6,5},{7,6},{9,8},{10,9},{11,10},{12... | collective-permute-start | bytes 196616 | tf_op jit(solution)/shard_map/ppermute | solution.py:181
  27.4 13.6 %collective-permute-start.5 = (bf16[2,128,128]{2,1,0:T(8,128)(2,1)S(1)}, bf16[2,128,128]{2,1,0:T(8,128)(2,1)S(1)}, u32[]{:S(2)}, u32[]{:S(2)}) collective-permute-start(bf16[2,128,128]{2,1,0:T(8,128)(2,1)S(1)} %get-tuple-element.44.down_ref), channel_id=1, source_target_pairs={{0,1},{1,2},{2,3},{3,4},{4,5},{5,6},{6,7},{8,9},{9,10},{10,11},{11... | collective-permute-start | bytes 196616 | tf_op jit(solution)/shard_map/ppermute | solution.py:180
  41.2 0.2 slice_reduce_fusion.8
  41.4 0.3 slice_reduce_fusion.2
  41.7 0.5 fusion.11
  42.1 1.0 %pad_maximum_fusion.2.recv_ref = bf16[8,3,128,128]{3,2,1,0:T(8,128)(2,1)} fusion(bf16[8,1,128,128]{3,2,1,0:T(8,128)(2,1)S(1)} %get-tuple-element.47, bf16[8,1,128,128]{3,2,1,0:T(8,128)(2,1)S(1)} %get-tuple-element.48, bf16[8,1,128,128]{3,2,1,0:T(8,128)(2,1)S(1)} %get-tuple-element.46), kind=kLoop, calls=%fused_computation.11 | loop fusion | flops 786432 | bytes 1572864 | tf_op jit(solution)/shard_map/stack | solution.py:19
  43.2 0.8 %copy-done.1 = bf16[10,2,128,128]{3,2,1,0:T(8,128)(2,1)} copy-done((bf16[10,2,128,128]{3,2,1,0:T(8,128)(2,1)}, bf16[10,2,128,128]{3,2,1,0:T(8,128)(2,1)S(1)}, u32[]{:S(2)}) %copy-start.1) | copy-done | bytes 655384
  44.0 0.6 %copy-done.5 = bf16[2,128,128]{2,1,0:T(8,128)(2,1)} copy-done((bf16[2,128,128]{2,1,0:T(8,128)(2,1)}, bf16[2,128,128]{2,1,0:T(8,128)(2,1)S(1)}, u32[]{:S(2)}) %copy-start.5) | copy-done | bytes 65560
  44.6 4.4 %shard_map.55 = bf16[10,2,128,128]{3,2,1,0:T(8,128)(2,1)} custom-call(s32[2]{0:T(128)} %pad_add_fusion.ids, f32[10,128]{1,0:T(8,128)} %q_ref.1, bf16[10,3,128,128]{3,2,1,0:T(8,128)(2,1)} %pad_maximum_fusion.jac_ref, bf16[8,3,128,128]{3,2,1,0:T(8,128)(2,1)} %pad_maximum_fusion.2.recv_ref, bf16[10,2,128,128]{3,2,1,0:T(8,128)(2,1)} %mid_ref.1, ...), custom_call_target="tpu_custom_call" | custom-call | tf_op jit(solution)/shard_map/pallas_call | solution.py:186
  (35 shorter events, 0.8 us)
Async XLA Ops:
  0.0 43.1 %collective-permute-start.1 = (bf16[10,2,128,128]{3,2,1,0:T(8,128)(2,1)}, bf16[10,2,128,128]{3,2,1,0:T(8,128)(2,1)S(1)}, u32[]{:S(2)}, u32[]{:S(2)}) collective-permute-start(bf16[10,2,128,128]{3,2,1,0:T(8,128)(2,1)} %mid_ref.1), channel_id=1, source_target_pairs={{0,1},{1,2},{2,3},{3,4},{4,5},{5,6},{6,7},{8,9},{9,10},{10,11},{11... | collective-permute-start | bytes 1966088 | tf_op jit(solution)/shard_map/ppermute | solution.py:143
  2.8 40.3 %collective-permute-start.2 = (bf16[10,2,128,128]{3,2,1,0:T(8,128)(2,1)}, bf16[10,2,128,128]{3,2,1,0:T(8,128)(2,1)}, u32[]{:S(2)}, u32[]{:S(2)}) collective-permute-start(bf16[10,2,128,128]{3,2,1,0:T(8,128)(2,1)} %mid_ref.1), channel_id=1, source_target_pairs={{1,0},{2,1},{3,2},{4,3},{5,4},{6,5},{7,6},{9,8},{10,9},{11,10},{12... | collective-permute-start | bytes 1966088 | tf_op jit(solution)/shard_map/ppermute | solution.py:144
  5.3 0.7 %copy-start.6 = (s32[10,3]{0,1:T(4,128)S(1)}, s32[10,3]{0,1:T(4,128)}, u32[]{:S(2)}) copy-start(s32[10,3]{0,1:T(4,128)} %param.11) | copy-start | bytes 364
  6.2 0.7 %copy-start.7 = (s32[10]{0:T(128)S(1)}, s32[10]{0:T(128)}, u32[]{:S(2)}) copy-start(s32[10]{0:T(128)} %param.12) | copy-start | bytes 124
  8.2 8.0 %copy-start = (bf16[10,3,128,128]{3,2,1,0:T(8,128)(2,1)S(1)}, bf16[10,3,128,128]{3,2,1,0:T(8,128)(2,1)}, u32[]{:S(2)}) copy-start(bf16[10,3,128,128]{3,2,1,0:T(8,128)(2,1)} %param.10) | copy-start | bytes 2949124
  9.4 6.0 %copy-start.8 = (s32[10]{0:T(128)S(1)}, s32[10]{0:T(128)}, u32[]{:S(2)}) copy-start(s32[10]{0:T(128)} %param.12) | copy-start | bytes 124
  9.5 15.5 %collective-permute-start = (bf16[27,128,128]{2,1,0:T(8,128)(2,1)S(1)}, bf16[27,128,128]{2,1,0:T(8,128)(2,1)S(1)}, u32[]{:S(2)}, u32[]{:S(2)}) collective-permute-start(bf16[27,128,128]{2,1,0:T(8,128)(2,1)S(1)} %pad_maximum_fusion.1), channel_id=1, source_target_pairs={{0,8},{8,16},{16,24},{24,32},{32,40},{40,48},{48,56},{56,64},{64,7... | collective-permute-start | bytes 2654216 | tf_op jit(solution)/shard_map/ppermute | solution.py:166
  12.6 12.6 %collective-permute-start.3 = (bf16[2,128,128]{2,1,0:T(8,128)(2,1)S(1)}, bf16[2,128,128]{2,1,0:T(8,128)(2,1)S(1)}, u32[]{:S(2)}, u32[]{:S(2)}) collective-permute-start(bf16[2,128,128]{2,1,0:T(8,128)(2,1)S(1)} %get-tuple-element.49), channel_id=1, source_target_pairs={{8,0},{16,8},{24,16},{32,24},{40,32},{48,40},{56,48},{64,56},{72,6... | collective-permute-start | bytes 196616 | tf_op jit(solution)/shard_map/ppermute | solution.py:167
  25.3 16.0 %copy-start.2 = (bf16[2,128,128]{2,1,0:T(8,128)(2,1)}, bf16[2,128,128]{2,1,0:T(8,128)(2,1)S(1)}, u32[]{:S(2)}) copy-start(bf16[2,128,128]{2,1,0:T(8,128)(2,1)S(1)} %get-tuple-element.44.down_ref) | copy-start | bytes 196612
  25.3 16.0 %copy-start.3 = (bf16[2,128,128]{2,1,0:T(8,128)(2,1)}, bf16[2,128,128]{2,1,0:T(8,128)(2,1)S(1)}, u32[]{:S(2)}) copy-start(bf16[2,128,128]{2,1,0:T(8,128)(2,1)S(1)} %get-tuple-element.45.up_ref) | copy-start | bytes 196612
  25.3 17.9 %collective-permute-start.4 = (bf16[2,128,128]{2,1,0:T(8,128)(2,1)S(1)}, bf16[2,128,128]{2,1,0:T(8,128)(2,1)S(1)}, u32[]{:S(2)}, u32[]{:S(2)}) collective-permute-start(bf16[2,128,128]{2,1,0:T(8,128)(2,1)S(1)} %get-tuple-element.45.up_ref), channel_id=1, source_target_pairs={{1,0},{2,1},{3,2},{4,3},{5,4},{6,5},{7,6},{9,8},{10,9},{11,10},{12... | collective-permute-start | bytes 196616 | tf_op jit(solution)/shard_map/ppermute | solution.py:181
  27.4 15.7 %collective-permute-start.5 = (bf16[2,128,128]{2,1,0:T(8,128)(2,1)S(1)}, bf16[2,128,128]{2,1,0:T(8,128)(2,1)S(1)}, u32[]{:S(2)}, u32[]{:S(2)}) collective-permute-start(bf16[2,128,128]{2,1,0:T(8,128)(2,1)S(1)} %get-tuple-element.44.down_ref), channel_id=1, source_target_pairs={{0,1},{1,2},{2,3},{3,4},{4,5},{5,6},{6,7},{8,9},{9,10},{10,11},{11... | collective-permute-start | bytes 196616 | tf_op jit(solution)/shard_map/ppermute | solution.py:180
  43.1 0.8 %copy-start.1 = (bf16[10,2,128,128]{3,2,1,0:T(8,128)(2,1)}, bf16[10,2,128,128]{3,2,1,0:T(8,128)(2,1)S(1)}, u32[]{:S(2)}) copy-start(bf16[10,2,128,128]{3,2,1,0:T(8,128)(2,1)S(1)} %collective-permute-done.1.left_ref) | copy-start | bytes 1966084
  43.2 0.8 %copy-start.4 = (bf16[2,128,128]{2,1,0:T(8,128)(2,1)}, bf16[2,128,128]{2,1,0:T(8,128)(2,1)S(1)}, u32[]{:S(2)}) copy-start(bf16[2,128,128]{2,1,0:T(8,128)(2,1)S(1)} %collective-permute-done.4.up_right_ref) | copy-start | bytes 196612
  44.0 0.6 %copy-start.5 = (bf16[2,128,128]{2,1,0:T(8,128)(2,1)}, bf16[2,128,128]{2,1,0:T(8,128)(2,1)S(1)}, u32[]{:S(2)}) copy-start(bf16[2,128,128]{2,1,0:T(8,128)(2,1)S(1)} %collective-permute-done.5.down_left_ref) | copy-start | bytes 196612

commit v18 on v14

--- a/solution.py
+++ b/solution.py
@@ -52,12 +52,12 @@
                 if ext_row == tile_rows + 1:
                     tile = down_left_ref[band_local - 2 + ext_slot]
                 else:
-                    tile = left_ref[ext_row - 1, band_local - 2 + ext_slot]
+                    tile = left_ref[(ext_row - 1) * band_local + band_local - 2 + ext_slot - 1]
             elif ext_slot >= 2 + band_local:
                 if ext_row == 0:
                     tile = up_right_ref[ext_slot - 2 - band_local]
                 else:
-                    tile = right_ref[ext_row - 1, ext_slot - 2 - band_local]
+                    tile = right_ref[(ext_row - 1) * band_local + ext_slot - 2 - band_local]
             elif ext_row == 0:
                 tile = up_ref[ext_slot - 2]
             elif ext_row == tile_rows + 1:
@@ -140,8 +140,9 @@
     def flat(a, b):
         return a * col_count + b
 
-    left = lax.ppermute(p_band, "col", [(b, b + 1) for b in range(col_count - 1)])
-    right = lax.ppermute(p_band, "col", [(b + 1, b) for b in range(col_count - 1)])
+    flat_band = p_band.reshape((tile_rows * band_local, tile_size, tile_size))
+    left = lax.ppermute(flat_band[1:], "col", [(b, b + 1) for b in range(col_count - 1)])
+    right = lax.ppermute(flat_band[:-1], "col", [(b + 1, b) for b in range(col_count - 1)])
     up = lax.ppermute(p_band[-1], "row", [(a, a + 1) for a in range(row_count - 1)])
     down = lax.ppermute(p_band[0], "row", [(a + 1, a) for a in range(row_count - 1)])
 

time: 49.2 us -> 49.8 us (1.012)
  the two profiles are of different devices: /device:TPU:414 before, /device:TPU:358 now
where the time goes in v18:
time: 49.8 us; the launch traced here: 49.4 us
  starting transfers between devices  22.8 us (46%)
  waiting for transfers between devices  11.8 us (24%)
  local copies, waits for them, and re-layouts  6.04 us (12%)
  Pallas kernels  4.38 us (9%)
  other arithmetic  4.05 us (8%)
    ppermute x1, waiting for transfers between devices, shards(): lax.ppermute(up, 'col', [(b + 1, b) for b in range(col_count - 1)])  7.13 us
    ppermute x1, starting transfers between devices, shards(): lax.ppermute(flat_band[1:], 'col', [(b, b + 1) for b in range(col_count -...  6.72 us
    ppermute x1, waiting for transfers between devices, shards(): lax.ppermute(down, 'col', [(b, b + 1) for b in range(col_count - 1)])  4.67 us
    pallas_call x1, Pallas kernels, shards(): pl.pallas_call(band_kernel(tile_rows, band_local, half_band, grid_tiles,...  4.38 us
    ppermute x1, starting transfers between devices, shards(): lax.ppermute(down, 'col', [(b, b + 1) for b in range(col_count - 1)])  3.5 us
    ppermute x1, starting transfers between devices, shards(): lax.ppermute(p_band[0], 'row', [(a + 1, a) for a in range(row_count - 1)])  3.37 us
    ppermute x1, starting transfers between devices, shards(): lax.ppermute(flat_band[:-1], 'col', [(b + 1, b) for b in range(col_count...  2.72 us
    ppermute x1, starting transfers between devices, shards(): lax.ppermute(up, 'col', [(b + 1, b) for b in range(col_count - 1)])  2.33 us
  transfers between devices with their start and end apart: 7, of which 2 were waited for; matrix products, arithmetic and copies ran while one was open for 16% of the time, Pallas kernels for 0%

profile of v18, /device:TPU:358, one launch (start us, length us, event | category | flops | bytes accessed | tf_op | source)
XLA Modules:
  0.0 49.4 jit_solution(15265392634646291449)
XLA Ops:
  0.0 0.9 %slice_bitcast_fusion = (bf16[2,128,128]{2,1,0:T(8,128)(2,1)S(1)}, bf16[2,128,128]{2,1,0:T(8,128)(2,1)S(1)}) fusion(bf16[10,2,128,128]{3,2,1,0:T(8,128)(2,1)} %mid_ref.1), kind=kLoop, calls=%fused_computation.39 | loop fusion | bytes 262144 | tf_op jit(solution)/shard_map/squeeze | solution.py:147
  0.9 3.4 %collective-permute-start.4 = (bf16[2,128,128]{2,1,0:T(8,128)(2,1)S(1)}, bf16[2,128,128]{2,1,0:T(8,128)(2,1)S(1)}, u32[]{:S(2)}, u32[]{:S(2)}) collective-permute-start(bf16[2,128,128]{2,1,0:T(8,128)(2,1)S(1)} %get-tuple-element.47), channel_id=1, source_target_pairs={{8,0},{16,8},{24,16},{32,24},{40,32},{48,40},{56,48},{64,56},{72,6... | collective-permute-start | bytes 196616 | tf_op jit(solution)/shard_map/ppermute | solution.py:147
  4.3 1.9 %collective-permute-start.3 = (bf16[2,128,128]{2,1,0:T(8,128)(2,1)S(1)}, bf16[2,128,128]{2,1,0:T(8,128)(2,1)S(1)}, u32[]{:S(2)}, u32[]{:S(2)}) collective-permute-start(bf16[2,128,128]{2,1,0:T(8,128)(2,1)S(1)} %get-tuple-element.48), channel_id=1, source_target_pairs={{0,8},{8,16},{16,24},{24,32},{32,40},{40,48},{48,56},{56,64},{64,7... | collective-permute-start | bytes 196616 | tf_op jit(solution)/shard_map/ppermute | solution.py:146
  6.2 0.6 %copy-done.8 = s32[10]{0:T(128)S(1)} copy-done((s32[10]{0:T(128)S(1)}, s32[10]{0:T(128)}, u32[]{:S(2)}) %copy-start.8) | copy-done | bytes 64
  7.2 1.2 %constant_dynamic-slice_fusion = bf16[8,3,128,128]{3,2,1,0:T(8,128)(2,1)S(1)} fusion(bf16[10,3,128,128]{3,2,1,0:T(8,128)(2,1)} %param.10, s32[]{:T(128)S(6)} %select_n.90), kind=kLoop, calls=%fused_computation.81 | loop fusion | bytes 1572868 | tf_op jit(solution)/shard_map/dynamic_slice | solution.py:157
  8.4 0.2 scatter.9
  8.7 2.3 %collective-permute-start = (bf16[25,128,128]{2,1,0:T(8,128)(2,1)S(1)}, bf16[25,128,128]{2,1,0:T(8,128)(2,1)S(1)}, u32[]{:S(2)}, u32[]{:S(2)}) collective-permute-start(bf16[25,128,128]{2,1,0:T(8,128)(2,1)S(1)} %pad_maximum_fusion.1), channel_id=1, source_target_pairs={{0,8},{8,16},{16,24},{24,32},{32,40},{40,48},{48,56},{56,64},{64,7... | collective-permute-start | bytes 2457608 | tf_op jit(solution)/shard_map/ppermute | solution.py:167
  11.0 1.3 %fusion.28 = (bf16[19,128,128]{2,1,0:T(8,128)(2,1)}, bf16[19,128,128]{2,1,0:T(8,128)(2,1)}) fusion(bf16[20,128,128]{2,1,0:T(8,128)(2,1)S(1)} %bitcast.38), kind=kLoop, calls=%fused_computation.82 | loop fusion | bytes 2490368 | tf_op jit(solution)/shard_map/slice | solution.py:145
  12.3 2.7 %collective-permute-start.2 = (bf16[19,128,128]{2,1,0:T(8,128)(2,1)}, bf16[19,128,128]{2,1,0:T(8,128)(2,1)S(1)}, u32[]{:S(2)}, u32[]{:S(2)}) collective-permute-start(bf16[19,128,128]{2,1,0:T(8,128)(2,1)} %get-tuple-element.49), channel_id=1, source_target_pairs={{1,0},{2,1},{3,2},{4,3},{5,4},{6,5},{7,6},{9,8},{10,9},{11,10},{12... | collective-permute-start | bytes 1867784 | tf_op jit(solution)/shard_map/ppermute | solution.py:145
  15.0 6.7 %collective-permute-start.1 = (bf16[19,128,128]{2,1,0:T(8,128)(2,1)}, bf16[19,128,128]{2,1,0:T(8,128)(2,1)}, u32[]{:S(2)}, u32[]{:S(2)}) collective-permute-start(bf16[19,128,128]{2,1,0:T(8,128)(2,1)} %get-tuple-element.50), channel_id=1, source_target_pairs={{0,1},{1,2},{2,3},{3,4},{4,5},{5,6},{6,7},{8,9},{9,10},{10,11},{11... | collective-permute-start | bytes 1867784 | tf_op jit(solution)/shard_map/ppermute | solution.py:144
  21.8 0.5 %fusion.2 = (bf16[10,1,128,128]{3,2,1,0:T(8,128)(2,1)S(1)}, bf16[10,1,128,128]{3,2,1,0:T(8,128)(2,1)S(1)}, bf16[10,1,128,128]{3,2,1,0:T(8,128)(2,1)S(1)}) fusion(pred[10]{0:T(512)(128)(4,1)S(1)} %get-tuple-element.58, pred[10]{0:T(512)(128)(4,1)S(1)} %get-tuple-element.59, pred[10]{0:T(512)(128)(4,1)S(1)} %get-tuple-element.57, ...), kind=kLoop, calls=%fused_computation.23 | loop fusion | flops 3440640 | bytes 1966170 | tf_op jit(solution)/shard_map/convert_element_type | solution.py:18
  22.4 1.1 %pad_maximum_fusion.jac_ref = bf16[10,3,128,128]{3,2,1,0:T(8,128)(2,1)} fusion(bf16[10,1,128,128]{3,2,1,0:T(8,128)(2,1)S(1)} %get-tuple-element.42, bf16[10,1,128,128]{3,2,1,0:T(8,128)(2,1)S(1)} %get-tuple-element.43, bf16[10,1,128,128]{3,2,1,0:T(8,128)(2,1)S(1)} %get-tuple-element.41), kind=kLoop, calls=%fused_computation | loop fusion | flops 983040 | bytes 1966080 | tf_op jit(solution)/shard_map/stack | solution.py:19
  23.4 0.6 %pad_add_fusion.ids = s32[2]{0:T(128)} fusion(s32[1]{0:T(128)} %bitcast.1, s32[1]{0:T(128)} %bitcast), kind=kLoop, calls=%fused_computation.79 | loop fusion | flops 2 | bytes 16 | tf_op jit(solution)/shard_map/stack | solution.py:180
  24.1 3.5 %collective-permute-start.6 = (bf16[2,128,128]{2,1,0:T(8,128)(2,1)S(1)}, bf16[2,128,128]{2,1,0:T(8,128)(2,1)S(1)}, u32[]{:S(2)}, u32[]{:S(2)}) collective-permute-start(bf16[2,128,128]{2,1,0:T(8,128)(2,1)S(1)} %collective-permute-done.4.down_ref), channel_id=1, source_target_pairs={{0,1},{1,2},{2,3},{3,4},{4,5},{5,6},{6,7},{8,9},{9,10},{10,11},{11... | collective-permute-start | bytes 196616 | tf_op jit(solution)/shard_map/ppermute | solution.py:177
  27.6 2.3 %collective-permute-start.5 = (bf16[2,128,128]{2,1,0:T(8,128)(2,1)S(1)}, bf16[2,128,128]{2,1,0:T(8,128)(2,1)S(1)}, u32[]{:S(2)}, u32[]{:S(2)}) collective-permute-start(bf16[2,128,128]{2,1,0:T(8,128)(2,1)S(1)} %collective-permute-done.3.up_ref), channel_id=1, source_target_pairs={{1,0},{2,1},{3,2},{4,3},{5,4},{6,5},{7,6},{9,8},{10,9},{11,10},{12... | collective-permute-start | bytes 196616 | tf_op jit(solution)/shard_map/ppermute | solution.py:178
  30.4 0.2 slice_reduce_fusion.8
  30.6 0.3 slice_reduce_fusion.2
  30.9 0.5 fusion.11
  31.4 1.0 %pad_maximum_fusion.2.recv_ref = bf16[8,3,128,128]{3,2,1,0:T(8,128)(2,1)} fusion(bf16[8,1,128,128]{3,2,1,0:T(8,128)(2,1)S(1)} %get-tuple-element.45, bf16[8,1,128,128]{3,2,1,0:T(8,128)(2,1)S(1)} %get-tuple-element.46, bf16[8,1,128,128]{3,2,1,0:T(8,128)(2,1)S(1)} %get-tuple-element.44), kind=kLoop, calls=%fused_computation.11 | loop fusion | flops 786432 | bytes 1572864 | tf_op jit(solution)/shard_map/stack | solution.py:19
  32.4 4.7 %collective-permute-done.6.down_left_ref = bf16[2,128,128]{2,1,0:T(8,128)(2,1)S(1)} collective-permute-done((bf16[2,128,128]{2,1,0:T(8,128)(2,1)S(1)}, bf16[2,128,128]{2,1,0:T(8,128)(2,1)S(1)}, u32[]{:S(2)}, u32[]{:S(2)}) %collective-permute-start.6) | collective-permute-done | bytes 65568 | tf_op jit(solution)/shard_map/ppermute | solution.py:177
  37.0 7.1 %collective-permute-done.5.up_right_ref = bf16[2,128,128]{2,1,0:T(8,128)(2,1)S(1)} collective-permute-done((bf16[2,128,128]{2,1,0:T(8,128)(2,1)S(1)}, bf16[2,128,128]{2,1,0:T(8,128)(2,1)S(1)}, u32[]{:S(2)}, u32[]{:S(2)}) %collective-permute-start.5) | collective-permute-done | bytes 65568 | tf_op jit(solution)/shard_map/ppermute | solution.py:178
  44.2 0.6 %copy-done.6 = bf16[2,128,128]{2,1,0:T(8,128)(2,1)} copy-done((bf16[2,128,128]{2,1,0:T(8,128)(2,1)}, bf16[2,128,128]{2,1,0:T(8,128)(2,1)S(1)}, u32[]{:S(2)}) %copy-start.6) | copy-done | bytes 65560
  44.8 0.2 copy-done.2
  45.0 4.4 %shard_map.55 = bf16[10,2,128,128]{3,2,1,0:T(8,128)(2,1)} custom-call(s32[2]{0:T(128)} %pad_add_fusion.ids, f32[10,128]{1,0:T(8,128)} %q_ref.1, bf16[10,3,128,128]{3,2,1,0:T(8,128)(2,1)} %pad_maximum_fusion.jac_ref, bf16[8,3,128,128]{3,2,1,0:T(8,128)(2,1)} %pad_maximum_fusion.2.recv_ref, bf16[10,2,128,128]{3,2,1,0:T(8,128)(2,1)} %mid_ref.1, ...), custom_call_target="tpu_custom_call" | custom-call | tf_op jit(solution)/shard_map/pallas_call | solution.py:183
  (37 shorter events, 0.9 us)
Async XLA Ops:
  0.9 23.2 %collective-permute-start.4 = (bf16[2,128,128]{2,1,0:T(8,128)(2,1)S(1)}, bf16[2,128,128]{2,1,0:T(8,128)(2,1)S(1)}, u32[]{:S(2)}, u32[]{:S(2)}) collective-permute-start(bf16[2,128,128]{2,1,0:T(8,128)(2,1)S(1)} %get-tuple-element.47), channel_id=1, source_target_pairs={{8,0},{16,8},{24,16},{32,24},{40,32},{48,40},{56,48},{64,56},{72,6... | collective-permute-start | bytes 196616 | tf_op jit(solution)/shard_map/ppermute | solution.py:147
  4.3 23.3 %collective-permute-start.3 = (bf16[2,128,128]{2,1,0:T(8,128)(2,1)S(1)}, bf16[2,128,128]{2,1,0:T(8,128)(2,1)S(1)}, u32[]{:S(2)}, u32[]{:S(2)}) collective-permute-start(bf16[2,128,128]{2,1,0:T(8,128)(2,1)S(1)} %get-tuple-element.48), channel_id=1, source_target_pairs={{0,8},{8,16},{16,24},{24,32},{32,40},{40,48},{48,56},{56,64},{64,7... | collective-permute-start | bytes 196616 | tf_op jit(solution)/shard_map/ppermute | solution.py:146
  6.2 0.7 %copy-start.8 = (s32[10]{0:T(128)S(1)}, s32[10]{0:T(128)}, u32[]{:S(2)}) copy-start(s32[10]{0:T(128)} %param.12) | copy-start | bytes 124
  6.2 0.7 %copy-start.7 = (s32[10,3]{0,1:T(4,128)S(1)}, s32[10,3]{0,1:T(4,128)}, u32[]{:S(2)}) copy-start(s32[10,3]{0,1:T(4,128)} %param.11) | copy-start | bytes 364
  8.6 2.4 %copy-start = (bf16[10,2,128,128]{3,2,1,0:T(8,128)(2,1)S(1)}, bf16[10,2,128,128]{3,2,1,0:T(8,128)(2,1)}, u32[]{:S(2)}) copy-start(bf16[10,2,128,128]{3,2,1,0:T(8,128)(2,1)} %mid_ref.1) | copy-start | bytes 1966084
  8.7 21.3 %collective-permute-start = (bf16[25,128,128]{2,1,0:T(8,128)(2,1)S(1)}, bf16[25,128,128]{2,1,0:T(8,128)(2,1)S(1)}, u32[]{:S(2)}, u32[]{:S(2)}) collective-permute-start(bf16[25,128,128]{2,1,0:T(8,128)(2,1)S(1)} %pad_maximum_fusion.1), channel_id=1, source_target_pairs={{0,8},{8,16},{16,24},{24,32},{32,40},{40,48},{48,56},{56,64},{64,7... | collective-permute-start | bytes 2457608 | tf_op jit(solution)/shard_map/ppermute | solution.py:167
  10.9 10.9 %copy-start.1 = (bf16[10,3,128,128]{3,2,1,0:T(8,128)(2,1)S(1)}, bf16[10,3,128,128]{3,2,1,0:T(8,128)(2,1)}, u32[]{:S(2)}) copy-start(bf16[10,3,128,128]{3,2,1,0:T(8,128)(2,1)} %param.10) | copy-start | bytes 2949124
  12.3 31.9 %collective-permute-start.2 = (bf16[19,128,128]{2,1,0:T(8,128)(2,1)}, bf16[19,128,128]{2,1,0:T(8,128)(2,1)S(1)}, u32[]{:S(2)}, u32[]{:S(2)}) collective-permute-start(bf16[19,128,128]{2,1,0:T(8,128)(2,1)} %get-tuple-element.49), channel_id=1, source_target_pairs={{1,0},{2,1},{3,2},{4,3},{5,4},{6,5},{7,6},{9,8},{10,9},{11,10},{12... | collective-permute-start | bytes 1867784 | tf_op jit(solution)/shard_map/ppermute | solution.py:145
  15.0 29.1 %collective-permute-start.1 = (bf16[19,128,128]{2,1,0:T(8,128)(2,1)}, bf16[19,128,128]{2,1,0:T(8,128)(2,1)}, u32[]{:S(2)}, u32[]{:S(2)}) collective-permute-start(bf16[19,128,128]{2,1,0:T(8,128)(2,1)} %get-tuple-element.50), channel_id=1, source_target_pairs={{0,1},{1,2},{2,3},{3,4},{4,5},{5,6},{6,7},{8,9},{9,10},{10,11},{11... | collective-permute-start | bytes 1867784 | tf_op jit(solution)/shard_map/ppermute | solution.py:144
  24.1 6.3 %copy-start.3 = (bf16[2,128,128]{2,1,0:T(8,128)(2,1)}, bf16[2,128,128]{2,1,0:T(8,128)(2,1)S(1)}, u32[]{:S(2)}) copy-start(bf16[2,128,128]{2,1,0:T(8,128)(2,1)S(1)} %collective-permute-done.4.down_ref) | copy-start | bytes 196612
  24.1 12.9 %collective-permute-start.6 = (bf16[2,128,128]{2,1,0:T(8,128)(2,1)S(1)}, bf16[2,128,128]{2,1,0:T(8,128)(2,1)S(1)}, u32[]{:S(2)}, u32[]{:S(2)}) collective-permute-start(bf16[2,128,128]{2,1,0:T(8,128)(2,1)S(1)} %collective-permute-done.4.down_ref), channel_id=1, source_target_pairs={{0,1},{1,2},{2,3},{3,4},{4,5},{5,6},{6,7},{8,9},{9,10},{10,11},{11... | collective-permute-start | bytes 196616 | tf_op jit(solution)/shard_map/ppermute | solution.py:177
  27.6 2.8 %copy-start.4 = (bf16[2,128,128]{2,1,0:T(8,128)(2,1)}, bf16[2,128,128]{2,1,0:T(8,128)(2,1)S(1)}, u32[]{:S(2)}) copy-start(bf16[2,128,128]{2,1,0:T(8,128)(2,1)S(1)} %collective-permute-done.3.up_ref) | copy-start | bytes 196612
  27.6 16.5 %collective-permute-start.5 = (bf16[2,128,128]{2,1,0:T(8,128)(2,1)S(1)}, bf16[2,128,128]{2,1,0:T(8,128)(2,1)S(1)}, u32[]{:S(2)}, u32[]{:S(2)}) collective-permute-start(bf16[2,128,128]{2,1,0:T(8,128)(2,1)S(1)} %collective-permute-done.3.up_ref), channel_id=1, source_target_pairs={{1,0},{2,1},{3,2},{4,3},{5,4},{6,5},{7,6},{9,8},{10,9},{11,10},{12... | collective-permute-start | bytes 196616 | tf_op jit(solution)/shard_map/ppermute | solution.py:178
  37.0 7.1 %copy-start.5 = (bf16[2,128,128]{2,1,0:T(8,128)(2,1)}, bf16[2,128,128]{2,1,0:T(8,128)(2,1)S(1)}, u32[]{:S(2)}) copy-start(bf16[2,128,128]{2,1,0:T(8,128)(2,1)S(1)} %collective-permute-done.6.down_left_ref) | copy-start | bytes 196612
  44.2 0.6 %copy-start.6 = (bf16[2,128,128]{2,1,0:T(8,128)(2,1)}, bf16[2,128,128]{2,1,0:T(8,128)(2,1)S(1)}, u32[]{:S(2)}) copy-start(bf16[2,128,128]{2,1,0:T(8,128)(2,1)S(1)} %collective-permute-done.5.up_right_ref) | copy-start | bytes 196612
  44.2 0.8 %copy-start.2 = (bf16[19,128,128]{2,1,0:T(8,128)(2,1)}, bf16[19,128,128]{2,1,0:T(8,128)(2,1)S(1)}, u32[]{:S(2)}) copy-start(bf16[19,128,128]{2,1,0:T(8,128)(2,1)S(1)} %collective-permute-done.2.right_ref) | copy-start | bytes 1867780

commit v19 on v14

--- a/solution.py
+++ b/solution.py
@@ -76,19 +76,14 @@
 
         def body(masked):
             for row in range(tile_rows):
-                lhs = jnp.concatenate([jac_ref[row, f] for f in range(3)], axis=1)
-                rhs = jnp.concatenate(
-                    [
-                        jnp.concatenate(
-                            [prior_tile(row + f, u - f + 2, masked) for u in range(extended)], axis=1
-                        )
-                        for f in range(3)
-                    ],
-                    axis=0,
-                )
-                spread_ref[row] = jnp.dot(lhs, rhs, preferred_element_type=jnp.float32).astype(
-                    jnp.bfloat16
-                )
+                acc = None
+                for f in range(3):
+                    slab = jnp.concatenate(
+                        [prior_tile(row + f, u - f + 2, masked) for u in range(extended)], axis=1
+                    )
+                    term = jnp.dot(jac_ref[row, f], slab, preferred_element_type=jnp.float32)
+                    acc = term if acc is None else acc + term
+                spread_ref[row] = acc.astype(jnp.bfloat16)
             for position in range(window):
                 members = [
                     (position - k, k) for k in range(band_local) if 0 <= position - k < tile_rows

time: 49.2 us -> 49.5 us (level)
  the two profiles are of different devices: /device:TPU:414 before, /device:TPU:478 now
where the time goes in v19:
time: 49.5 us; the launch traced here: 49.1 us
  starting transfers between devices  16.9 us (34%)
  waiting for transfers between devices  16.7 us (34%)
  local copies, waits for them, and re-layouts  6.49 us (13%)
  Pallas kernels  4.72 us (10%)
  other arithmetic  4.05 us (8%)
    ppermute x1, waiting for transfers between devices, shards(): lax.ppermute(p_band[-1], 'row', [(a, a + 1) for a in range(row_count - 1)])  14.3 us
    ppermute x1, starting transfers between devices, shards(): lax.ppermute(p_band, 'col', [(b + 1, b) for b in range(col_count - 1)])  5.43 us
    pallas_call x1, Pallas kernels, shards(): pl.pallas_call(band_kernel(tile_rows, band_local, half_band, grid_tiles,...  4.72 us
    ppermute x1, starting transfers between devices, shards(): lax.ppermute(p_band[0], 'row', [(a + 1, a) for a in range(row_count - 1)])  3.16 us
    unnamed x20, local copies, waits for them, and re-layouts  2.78 us
    ppermute x1, waiting for transfers between devices, shards(): lax.ppermute(down, 'col', [(b, b + 1) for b in range(col_count - 1)])  2.46 us
    ppermute x1, starting transfers between devices, shards(): lax.ppermute(p_band[-1], 'row', [(a, a + 1) for a in range(row_count - 1)])  2.41 us
    another operation x2, other arithmetic, assemble(): return jnp.stack(pieces, axis=1)  2.05 us
  transfers between devices with their start and end apart: 7, of which 2 were waited for; matrix products, arithmetic and copies ran while one was open for 16% of the time, Pallas kernels for 0%

profile of v19, /device:TPU:478, one launch (start us, length us, event | category | flops | bytes accessed | tf_op | source)
XLA Modules:
  0.0 49.1 jit_solution(9089581571087820375)
XLA Ops:
  0.0 1.3 %collective-permute-start.1 = (bf16[10,2,128,128]{3,2,1,0:T(8,128)(2,1)}, bf16[10,2,128,128]{3,2,1,0:T(8,128)(2,1)S(1)}, u32[]{:S(2)}, u32[]{:S(2)}) collective-permute-start(bf16[10,2,128,128]{3,2,1,0:T(8,128)(2,1)} %mid_ref.1), channel_id=1, source_target_pairs={{0,1},{1,2},{2,3},{3,4},{4,5},{5,6},{6,7},{8,9},{9,10},{10,11},{11... | collective-permute-start | bytes 1966088 | tf_op jit(solution)/shard_map/ppermute | solution.py:138
  1.3 5.4 %collective-permute-start.2 = (bf16[10,2,128,128]{3,2,1,0:T(8,128)(2,1)}, bf16[10,2,128,128]{3,2,1,0:T(8,128)(2,1)}, u32[]{:S(2)}, u32[]{:S(2)}) collective-permute-start(bf16[10,2,128,128]{3,2,1,0:T(8,128)(2,1)} %mid_ref.1), channel_id=1, source_target_pairs={{1,0},{2,1},{3,2},{4,3},{5,4},{6,5},{7,6},{9,8},{10,9},{11,10},{12... | collective-permute-start | bytes 1966088 | tf_op jit(solution)/shard_map/ppermute | solution.py:139
  6.7 0.7 %copy-done.6 = s32[10,3]{0,1:T(4,128)S(1)} copy-done((s32[10,3]{0,1:T(4,128)S(1)}, s32[10,3]{0,1:T(4,128)}, u32[]{:S(2)}) %copy-start.6) | copy-done | bytes 144
  7.7 0.7 %copy-done.9 = s32[10]{0:T(128)S(1)} copy-done((s32[10]{0:T(128)S(1)}, s32[10]{0:T(128)}, u32[]{:S(2)}) %copy-start.9) | copy-done | bytes 64
  8.4 1.2 %constant_dynamic-slice_fusion = bf16[8,3,128,128]{3,2,1,0:T(8,128)(2,1)S(1)} fusion(bf16[10,3,128,128]{3,2,1,0:T(8,128)(2,1)} %param.10, s32[]{:T(128)S(6)} %select_n.90), kind=kLoop, calls=%fused_computation.81 | loop fusion | bytes 1572868 | tf_op jit(solution)/shard_map/dynamic_slice | solution.py:151
  9.8 2.1 %collective-permute-start = (bf16[25,128,128]{2,1,0:T(8,128)(2,1)S(1)}, bf16[25,128,128]{2,1,0:T(8,128)(2,1)S(1)}, u32[]{:S(2)}, u32[]{:S(2)}) collective-permute-start(bf16[25,128,128]{2,1,0:T(8,128)(2,1)S(1)} %pad_maximum_fusion.1), channel_id=1, source_target_pairs={{0,8},{8,16},{16,24},{24,32},{32,40},{40,48},{48,56},{56,64},{64,7... | collective-permute-start | bytes 2457608 | tf_op jit(solution)/shard_map/ppermute | solution.py:161
  11.9 0.9 %slice_bitcast_fusion = (bf16[2,128,128]{2,1,0:T(8,128)(2,1)S(1)}, bf16[2,128,128]{2,1,0:T(8,128)(2,1)S(1)}) fusion(bf16[10,2,128,128]{3,2,1,0:T(8,128)(2,1)} %mid_ref.1), kind=kLoop, calls=%fused_computation.39 | loop fusion | bytes 262144 | tf_op jit(solution)/shard_map/squeeze | solution.py:141
  12.8 2.4 %collective-permute-start.3 = (bf16[2,128,128]{2,1,0:T(8,128)(2,1)S(1)}, bf16[2,128,128]{2,1,0:T(8,128)(2,1)S(1)}, u32[]{:S(2)}, u32[]{:S(2)}) collective-permute-start(bf16[2,128,128]{2,1,0:T(8,128)(2,1)S(1)} %get-tuple-element.48), channel_id=1, source_target_pairs={{0,8},{8,16},{16,24},{24,32},{32,40},{40,48},{48,56},{56,64},{64,7... | collective-permute-start | bytes 196616 | tf_op jit(solution)/shard_map/ppermute | solution.py:140
  15.2 3.2 %collective-permute-start.4 = (bf16[2,128,128]{2,1,0:T(8,128)(2,1)S(1)}, bf16[2,128,128]{2,1,0:T(8,128)(2,1)S(1)}, u32[]{:S(2)}, u32[]{:S(2)}) collective-permute-start(bf16[2,128,128]{2,1,0:T(8,128)(2,1)S(1)} %get-tuple-element.47), channel_id=1, source_target_pairs={{8,0},{16,8},{24,16},{32,24},{40,32},{48,40},{56,48},{64,56},{72,6... | collective-permute-start | bytes 196616 | tf_op jit(solution)/shard_map/ppermute | solution.py:141
  18.4 0.5 %slice_bitcast_fusion.11 = (pred[10]{0:T(512)(128)(4,1)S(1)}, pred[10]{0:T(512)(128)(4,1)}, pred[10]{0:T(512)(128)(4,1)}) fusion(pred[10,3]{0,1:T(4,128)(4,1)S(1)} %get-tuple-element.49), kind=kLoop, calls=%fused_computation.73 | loop fusion | bytes 60 | tf_op jit(solution)/shard_map/jit(_where)/broadcast_in_dim | solution.py:17
  19.0 0.5 %copy-done.7 = pred[10]{0:T(512)(128)(4,1)S(1)} copy-done((pred[10]{0:T(512)(128)(4,1)S(1)}, pred[10]{0:T(512)(128)(4,1)}, u32[]{:S(2)}) %copy-start.7) | copy-done | bytes 34
  19.5 0.5 %fusion.2 = (bf16[10,1,128,128]{3,2,1,0:T(8,128)(2,1)S(1)}, bf16[10,1,128,128]{3,2,1,0:T(8,128)(2,1)S(1)}, bf16[10,1,128,128]{3,2,1,0:T(8,128)(2,1)S(1)}) fusion(pred[10]{0:T(512)(128)(4,1)S(1)} %copy-done.7, pred[10]{0:T(512)(128)(4,1)S(1)} %copy-done.8, pred[10]{0:T(512)(128)(4,1)S(1)} %get-tuple-element.55, bf16[10,3,128,128]{3,2,1,0:T(8,128)(2,1)S(1)} %copy-done, ...), kind=kLoop, calls=%fused_computation.23 | loop fusion | flops 3440640 | bytes 1966170 | tf_op jit(solution)/shard_map/convert_element_type | solution.py:18
  20.1 1.1 %pad_maximum_fusion.jac_ref = bf16[10,3,128,128]{3,2,1,0:T(8,128)(2,1)} fusion(bf16[10,1,128,128]{3,2,1,0:T(8,128)(2,1)S(1)} %get-tuple-element.42, bf16[10,1,128,128]{3,2,1,0:T(8,128)(2,1)S(1)} %get-tuple-element.43, bf16[10,1,128,128]{3,2,1,0:T(8,128)(2,1)S(1)} %get-tuple-element.41), kind=kLoop, calls=%fused_computation | loop fusion | flops 983040 | bytes 1966080 | tf_op jit(solution)/shard_map/stack | solution.py:19
  21.1 0.6 %pad_add_fusion.ids = s32[2]{0:T(128)} fusion(s32[1]{0:T(128)} %bitcast.1, s32[1]{0:T(128)} %bitcast), kind=kLoop, calls=%fused_computation.79 | loop fusion | flops 2 | bytes 16 | tf_op jit(solution)/shard_map/stack | solution.py:174
  21.8 14.3 %collective-permute-done.3.up_ref = bf16[2,128,128]{2,1,0:T(8,128)(2,1)S(1)} collective-permute-done((bf16[2,128,128]{2,1,0:T(8,128)(2,1)S(1)}, bf16[2,128,128]{2,1,0:T(8,128)(2,1)S(1)}, u32[]{:S(2)}, u32[]{:S(2)}) %collective-permute-start.3) | collective-permute-done | bytes 65568 | tf_op jit(solution)/shard_map/ppermute | solution.py:140
  36.1 1.3 %collective-permute-start.5 = (bf16[2,128,128]{2,1,0:T(8,128)(2,1)S(1)}, bf16[2,128,128]{2,1,0:T(8,128)(2,1)S(1)}, u32[]{:S(2)}, u32[]{:S(2)}) collective-permute-start(bf16[2,128,128]{2,1,0:T(8,128)(2,1)S(1)} %collective-permute-done.3.up_ref), channel_id=1, source_target_pairs={{1,0},{2,1},{3,2},{4,3},{5,4},{6,5},{7,6},{9,8},{10,9},{11,10},{12... | collective-permute-start | bytes 196616 | tf_op jit(solution)/shard_map/ppermute | solution.py:172
  37.4 1.3 %collective-permute-start.6 = (bf16[2,128,128]{2,1,0:T(8,128)(2,1)S(1)}, bf16[2,128,128]{2,1,0:T(8,128)(2,1)S(1)}, u32[]{:S(2)}, u32[]{:S(2)}) collective-permute-start(bf16[2,128,128]{2,1,0:T(8,128)(2,1)S(1)} %collective-permute-done.4.down_ref), channel_id=1, source_target_pairs={{0,1},{1,2},{2,3},{3,4},{4,5},{5,6},{6,7},{8,9},{9,10},{10,11},{11... | collective-permute-start | bytes 196616 | tf_op jit(solution)/shard_map/ppermute | solution.py:171
  39.3 0.3 slice_reduce_fusion.2
  39.6 0.5 fusion.11
  40.1 1.0 %pad_maximum_fusion.2.recv_ref = bf16[8,3,128,128]{3,2,1,0:T(8,128)(2,1)} fusion(bf16[8,1,128,128]{3,2,1,0:T(8,128)(2,1)S(1)} %get-tuple-element.45, bf16[8,1,128,128]{3,2,1,0:T(8,128)(2,1)S(1)} %get-tuple-element.46, bf16[8,1,128,128]{3,2,1,0:T(8,128)(2,1)S(1)} %get-tuple-element.44), kind=kLoop, calls=%fused_computation.11 | loop fusion | flops 786432 | bytes 1572864 | tf_op jit(solution)/shard_map/stack | solution.py:19
  41.1 2.5 %collective-permute-done.6.down_left_ref = bf16[2,128,128]{2,1,0:T(8,128)(2,1)S(1)} collective-permute-done((bf16[2,128,128]{2,1,0:T(8,128)(2,1)S(1)}, bf16[2,128,128]{2,1,0:T(8,128)(2,1)S(1)}, u32[]{:S(2)}, u32[]{:S(2)}) %collective-permute-start.6) | collective-permute-done | bytes 65568 | tf_op jit(solution)/shard_map/ppermute | solution.py:171
  43.6 0.6 %copy-done.5 = bf16[2,128,128]{2,1,0:T(8,128)(2,1)} copy-done((bf16[2,128,128]{2,1,0:T(8,128)(2,1)}, bf16[2,128,128]{2,1,0:T(8,128)(2,1)S(1)}, u32[]{:S(2)}) %copy-start.5) | copy-done | bytes 65560
  44.2 0.2 copy-done.1
  44.4 4.7 %shard_map.55 = bf16[10,2,128,128]{3,2,1,0:T(8,128)(2,1)} custom-call(s32[2]{0:T(128)} %pad_add_fusion.ids, f32[10,128]{1,0:T(8,128)} %q_ref.1, bf16[10,3,128,128]{3,2,1,0:T(8,128)(2,1)} %pad_maximum_fusion.jac_ref, bf16[8,3,128,128]{3,2,1,0:T(8,128)(2,1)} %pad_maximum_fusion.2.recv_ref, bf16[10,2,128,128]{3,2,1,0:T(8,128)(2,1)} %mid_ref.1, ...), custom_call_target="tpu_custom_call" | custom-call | tf_op jit(solution)/shard_map/pallas_call | solution.py:177
  (38 shorter events, 1.3 us)
Async XLA Ops:
  0.0 43.5 %collective-permute-start.1 = (bf16[10,2,128,128]{3,2,1,0:T(8,128)(2,1)}, bf16[10,2,128,128]{3,2,1,0:T(8,128)(2,1)S(1)}, u32[]{:S(2)}, u32[]{:S(2)}) collective-permute-start(bf16[10,2,128,128]{3,2,1,0:T(8,128)(2,1)} %mid_ref.1), channel_id=1, source_target_pairs={{0,1},{1,2},{2,3},{3,4},{4,5},{5,6},{6,7},{8,9},{9,10},{10,11},{11... | collective-permute-start | bytes 1966088 | tf_op jit(solution)/shard_map/ppermute | solution.py:138
  1.3 42.3 %collective-permute-start.2 = (bf16[10,2,128,128]{3,2,1,0:T(8,128)(2,1)}, bf16[10,2,128,128]{3,2,1,0:T(8,128)(2,1)}, u32[]{:S(2)}, u32[]{:S(2)}) collective-permute-start(bf16[10,2,128,128]{3,2,1,0:T(8,128)(2,1)} %mid_ref.1), channel_id=1, source_target_pairs={{1,0},{2,1},{3,2},{4,3},{5,4},{6,5},{7,6},{9,8},{10,9},{11,10},{12... | collective-permute-start | bytes 1966088 | tf_op jit(solution)/shard_map/ppermute | solution.py:139
  6.7 0.7 %copy-start.6 = (s32[10,3]{0,1:T(4,128)S(1)}, s32[10,3]{0,1:T(4,128)}, u32[]{:S(2)}) copy-start(s32[10,3]{0,1:T(4,128)} %param.11) | copy-start | bytes 364
  7.7 0.7 %copy-start.9 = (s32[10]{0:T(128)S(1)}, s32[10]{0:T(128)}, u32[]{:S(2)}) copy-start(s32[10]{0:T(128)} %param.12) | copy-start | bytes 124
  9.6 9.4 %copy-start = (bf16[10,3,128,128]{3,2,1,0:T(8,128)(2,1)S(1)}, bf16[10,3,128,128]{3,2,1,0:T(8,128)(2,1)}, u32[]{:S(2)}) copy-start(bf16[10,3,128,128]{3,2,1,0:T(8,128)(2,1)} %param.10) | copy-start | bytes 2949124
  9.8 28.8 %collective-permute-start = (bf16[25,128,128]{2,1,0:T(8,128)(2,1)S(1)}, bf16[25,128,128]{2,1,0:T(8,128)(2,1)S(1)}, u32[]{:S(2)}, u32[]{:S(2)}) collective-permute-start(bf16[25,128,128]{2,1,0:T(8,128)(2,1)S(1)} %pad_maximum_fusion.1), channel_id=1, source_target_pairs={{0,8},{8,16},{16,24},{24,32},{32,40},{40,48},{48,56},{56,64},{64,7... | collective-permute-start | bytes 2457608 | tf_op jit(solution)/shard_map/ppermute | solution.py:161
  12.8 23.3 %collective-permute-start.3 = (bf16[2,128,128]{2,1,0:T(8,128)(2,1)S(1)}, bf16[2,128,128]{2,1,0:T(8,128)(2,1)S(1)}, u32[]{:S(2)}, u32[]{:S(2)}) collective-permute-start(bf16[2,128,128]{2,1,0:T(8,128)(2,1)S(1)} %get-tuple-element.48), channel_id=1, source_target_pairs={{0,8},{8,16},{16,24},{24,32},{32,40},{40,48},{48,56},{56,64},{64,7... | collective-permute-start | bytes 196616 | tf_op jit(solution)/shard_map/ppermute | solution.py:140
  15.2 22.2 %collective-permute-start.4 = (bf16[2,128,128]{2,1,0:T(8,128)(2,1)S(1)}, bf16[2,128,128]{2,1,0:T(8,128)(2,1)S(1)}, u32[]{:S(2)}, u32[]{:S(2)}) collective-permute-start(bf16[2,128,128]{2,1,0:T(8,128)(2,1)S(1)} %get-tuple-element.47), channel_id=1, source_target_pairs={{8,0},{16,8},{24,16},{32,24},{40,32},{48,40},{56,48},{64,56},{72,6... | collective-permute-start | bytes 196616 | tf_op jit(solution)/shard_map/ppermute | solution.py:141
  18.9 0.6 %copy-start.7 = (pred[10]{0:T(512)(128)(4,1)S(1)}, pred[10]{0:T(512)(128)(4,1)}, u32[]{:S(2)}) copy-start(pred[10]{0:T(512)(128)(4,1)} %get-tuple-element.56) | copy-start | bytes 34
  18.9 0.6 %copy-start.8 = (pred[10]{0:T(512)(128)(4,1)S(1)}, pred[10]{0:T(512)(128)(4,1)}, u32[]{:S(2)}) copy-start(pred[10]{0:T(512)(128)(4,1)} %get-tuple-element.57) | copy-start | bytes 34
  36.1 3.1 %copy-start.2 = (bf16[2,128,128]{2,1,0:T(8,128)(2,1)}, bf16[2,128,128]{2,1,0:T(8,128)(2,1)S(1)}, u32[]{:S(2)}) copy-start(bf16[2,128,128]{2,1,0:T(8,128)(2,1)S(1)} %collective-permute-done.3.up_ref) | copy-start | bytes 196612
  36.1 5.0 %collective-permute-start.5 = (bf16[2,128,128]{2,1,0:T(8,128)(2,1)S(1)}, bf16[2,128,128]{2,1,0:T(8,128)(2,1)S(1)}, u32[]{:S(2)}, u32[]{:S(2)}) collective-permute-start(bf16[2,128,128]{2,1,0:T(8,128)(2,1)S(1)} %collective-permute-done.3.up_ref), channel_id=1, source_target_pairs={{1,0},{2,1},{3,2},{4,3},{5,4},{6,5},{7,6},{9,8},{10,9},{11,10},{12... | collective-permute-start | bytes 196616 | tf_op jit(solution)/shard_map/ppermute | solution.py:172
  37.4 1.8 %copy-start.3 = (bf16[2,128,128]{2,1,0:T(8,128)(2,1)}, bf16[2,128,128]{2,1,0:T(8,128)(2,1)S(1)}, u32[]{:S(2)}) copy-start(bf16[2,128,128]{2,1,0:T(8,128)(2,1)S(1)} %collective-permute-done.4.down_ref) | copy-start | bytes 196612
  37.4 6.2 %collective-permute-start.6 = (bf16[2,128,128]{2,1,0:T(8,128)(2,1)S(1)}, bf16[2,128,128]{2,1,0:T(8,128)(2,1)S(1)}, u32[]{:S(2)}, u32[]{:S(2)}) collective-permute-start(bf16[2,128,128]{2,1,0:T(8,128)(2,1)S(1)} %collective-permute-done.4.down_ref), channel_id=1, source_target_pairs={{0,1},{1,2},{2,3},{3,4},{4,5},{5,6},{6,7},{8,9},{9,10},{10,11},{11... | collective-permute-start | bytes 196616 | tf_op jit(solution)/shard_map/ppermute | solution.py:171
  41.1 2.5 %copy-start.4 = (bf16[2,128,128]{2,1,0:T(8,128)(2,1)}, bf16[2,128,128]{2,1,0:T(8,128)(2,1)S(1)}, u32[]{:S(2)}) copy-start(bf16[2,128,128]{2,1,0:T(8,128)(2,1)S(1)} %collective-permute-done.5.up_right_ref) | copy-start | bytes 196612
  43.5 0.6 %copy-start.5 = (bf16[2,128,128]{2,1,0:T(8,128)(2,1)}, bf16[2,128,128]{2,1,0:T(8,128)(2,1)S(1)}, u32[]{:S(2)}) copy-start(bf16[2,128,128]{2,1,0:T(8,128)(2,1)S(1)} %collective-permute-done.6.down_left_ref) | copy-start | bytes 196612
  43.5 0.9 %copy-start.1 = (bf16[10,2,128,128]{3,2,1,0:T(8,128)(2,1)}, bf16[10,2,128,128]{3,2,1,0:T(8,128)(2,1)S(1)}, u32[]{:S(2)}) copy-start(bf16[10,2,128,128]{3,2,1,0:T(8,128)(2,1)S(1)} %collective-permute-done.1.left_ref) | copy-start | bytes 1966084

commit v20 on v14

--- a/solution.py
+++ b/solution.py
@@ -32,6 +32,14 @@
         low_offset = col_id * band_local - half_band
         size = jac_ref.shape[-1]
 
+        def received_tile(row, g):
+            total = jnp.zeros((size, size), jnp.float32)
+            for m in range(3):
+                pick = (ids[2 + row * 3 + m] == g - 1) & (m < ids[2 + sent_rows * 3 + row])
+                block = recv_ref[row * 3 + m].astype(jnp.float32)
+                total = total + jnp.where(pick, block, 0.0)
+            return total.astype(win_ref.dtype)
+
         for col_value in range(col_count):
             offset = col_value * band_local - half_band
 
@@ -40,12 +48,12 @@
                 for position in range(window):
                     at = offset + position
                     for g in range(3):
-                        if at < 0:
-                            win_ref[position, g] = recv_ref[sent_rows + at, g]
-                        elif at < tile_rows:
+                        if 0 <= at < tile_rows:
                             win_ref[position, g] = jac_ref[at, g]
                         else:
-                            win_ref[position, g] = recv_ref[at - tile_rows, g]
+                            win_ref[position, g] = received_tile(
+                                sent_rows + at if at < 0 else at - tile_rows, g
+                            )
 
         def prior_tile(ext_row, ext_slot, masked):
             if ext_slot < 2:
@@ -167,16 +175,18 @@
 
     jacobian = assemble(blocks, block_offsets, block_live)
     received_meta = received_all[sent_rows * 3].astype(jnp.float32)
-    received = assemble(
-        received_all[: sent_rows * 3].reshape((sent_rows, 3, tile_size, tile_size)),
-        jnp.round(received_meta[0, : sent_rows * 3]).astype(jnp.int32).reshape(sent_rows, 3),
-        jnp.round(received_meta[1, :sent_rows]).astype(jnp.int32),
-    )
+    received_ints = jnp.round(received_meta[0:2]).astype(jnp.int32)
 
     down_left = lax.ppermute(down, "col", [(b, b + 1) for b in range(col_count - 1)])
     up_right = lax.ppermute(up, "col", [(b + 1, b) for b in range(col_count - 1)])
 
-    ids = jnp.stack([row_id, col_id]).astype(jnp.int32)
+    ids = jnp.concatenate(
+        [
+            jnp.stack([row_id, col_id]).astype(jnp.int32),
+            received_ints[0, : sent_rows * 3],
+            received_ints[1, :sent_rows],
+        ]
+    )
     vmem = pl.BlockSpec(memory_space=pltpu.MemorySpace.VMEM)
     smem = pl.BlockSpec(memory_space=pltpu.MemorySpace.SMEM)
     return pl.pallas_call(
@@ -188,7 +198,7 @@
             pltpu.VMEM((tile_rows + band_local - 1, 3, tile_size, tile_size), p_band.dtype),
             pltpu.VMEM((tile_rows, tile_size, (band_local + 2) * tile_size), p_band.dtype),
         ],
-    )(ids, q_var, jacobian, received, p_band, left, right, up, down, up_right, down_left)
+    )(ids, q_var, jacobian, received_all, p_band, left, right, up, down, up_right, down_left)
 
 
 def solution(mesh):

time: 49.2 us -> 49.5 us (level)
  the two profiles are of different devices: /device:TPU:414 before, /device:TPU:286 now
where the time goes in v20:
time: 49.5 us; the launch traced here: 49.1 us
  waiting for transfers between devices  20.1 us (41%)
  starting transfers between devices  16.9 us (34%)
  Pallas kernels  4.67 us (9%)
  local copies, waits for them, and re-layouts  4.61 us (9%)
  other arithmetic  2.56 us (5%)
    ppermute x1, waiting for transfers between devices, shards(): lax.ppermute(p_band[-1], 'row', [(a, a + 1) for a in range(row_count - 1)])  16 us
    ppermute x1, starting transfers between devices, shards(): lax.ppermute(p_band, 'col', [(b + 1, b) for b in range(col_count - 1)])  5.4 us
    pallas_call x1, Pallas kernels, shards(): pl.pallas_call(band_kernel(tile_rows, band_local, half_band, grid_tiles,...  4.67 us
    ppermute x1, waiting for transfers between devices, shards(): lax.ppermute(down, 'col', [(b, b + 1) for b in range(col_count - 1)])  4.09 us
    ppermute x1, starting transfers between devices, shards(): lax.ppermute(p_band[0], 'row', [(a + 1, a) for a in range(row_count - 1)])  3.16 us
    ppermute x1, starting transfers between devices, shards(): lax.ppermute(p_band[-1], 'row', [(a, a + 1) for a in range(row_count - 1)])  2.41 us
    unnamed x18, local copies, waits for them, and re-layouts  2.17 us
    ppermute x1, starting transfers between devices, shards(): received_all = lax.ppermute(sent, ('row', 'col'), pairs)  2.05 us
  transfers between devices with their start and end apart: 7, of which 2 were waited for; matrix products, arithmetic and copies ran while one was open for 10% of the time, Pallas kernels for 0%

profile of v20, /device:TPU:286, one launch (start us, length us, event | category | flops | bytes accessed | tf_op | source)
XLA Modules:
  0.0 49.1 jit_solution(9009706482697510269)
XLA Ops:
  0.0 1.3 %collective-permute-start.1 = (bf16[10,2,128,128]{3,2,1,0:T(8,128)(2,1)}, bf16[10,2,128,128]{3,2,1,0:T(8,128)(2,1)S(1)}, u32[]{:S(2)}, u32[]{:S(2)}) collective-permute-start(bf16[10,2,128,128]{3,2,1,0:T(8,128)(2,1)} %mid_ref.1), channel_id=1, source_target_pairs={{0,1},{1,2},{2,3},{3,4},{4,5},{5,6},{6,7},{8,9},{9,10},{10,11},{11... | collective-permute-start | bytes 1966088 | tf_op jit(solution)/shard_map/ppermute | solution.py:151
  1.3 5.4 %collective-permute-start.2 = (bf16[10,2,128,128]{3,2,1,0:T(8,128)(2,1)}, bf16[10,2,128,128]{3,2,1,0:T(8,128)(2,1)}, u32[]{:S(2)}, u32[]{:S(2)}) collective-permute-start(bf16[10,2,128,128]{3,2,1,0:T(8,128)(2,1)} %mid_ref.1), channel_id=1, source_target_pairs={{1,0},{2,1},{3,2},{4,3},{5,4},{6,5},{7,6},{9,8},{10,9},{11,10},{12... | collective-permute-start | bytes 1966088 | tf_op jit(solution)/shard_map/ppermute | solution.py:152
  6.7 0.7 %copy-done.7 = s32[10,3]{0,1:T(4,128)S(1)} copy-done((s32[10,3]{0,1:T(4,128)S(1)}, s32[10,3]{0,1:T(4,128)}, u32[]{:S(2)}) %copy-start.7) | copy-done | bytes 144
  7.5 0.1 copy.7
  7.5 0.1 convert_element_type.59
  7.6 0.7 %copy-done.8 = s32[10]{0:T(128)S(1)} copy-done((s32[10]{0:T(128)S(1)}, s32[10]{0:T(128)}, u32[]{:S(2)}) %copy-start.8) | copy-done | bytes 64
  8.3 0.1 convert_bitcast_fusion.1
  8.4 1.2 %constant_dynamic-slice_fusion = bf16[8,3,128,128]{3,2,1,0:T(8,128)(2,1)S(1)} fusion(bf16[10,3,128,128]{3,2,1,0:T(8,128)(2,1)} %param.10, s32[]{:T(128)S(6)} %select_n.44), kind=kLoop, calls=%fused_computation.42 | loop fusion | bytes 1572868 | tf_op jit(solution)/shard_map/dynamic_slice | solution.py:164
  9.6 0.2 scatter.9
  9.7 0.1 pad_maximum_fusion.1
  9.8 2.1 %collective-permute-start = (bf16[25,128,128]{2,1,0:T(8,128)(2,1)S(1)}, bf16[25,128,128]{2,1,0:T(8,128)(2,1)S(1)}, u32[]{:S(2)}, u32[]{:S(2)}) collective-permute-start(bf16[25,128,128]{2,1,0:T(8,128)(2,1)S(1)} %pad_maximum_fusion.1), channel_id=1, source_target_pairs={{0,8},{8,16},{16,24},{24,32},{32,40},{40,48},{48,56},{56,64},{64,7... | collective-permute-start | bytes 2457608 | tf_op jit(solution)/shard_map/ppermute | solution.py:174
  11.9 0.9 %slice_bitcast_fusion = (bf16[2,128,128]{2,1,0:T(8,128)(2,1)S(1)}, bf16[2,128,128]{2,1,0:T(8,128)(2,1)S(1)}) fusion(bf16[10,2,128,128]{3,2,1,0:T(8,128)(2,1)} %mid_ref.1), kind=kLoop, calls=%fused_computation.20 | loop fusion | bytes 262144 | tf_op jit(solution)/shard_map/squeeze | solution.py:154
  12.8 2.4 %collective-permute-start.3 = (bf16[2,128,128]{2,1,0:T(8,128)(2,1)S(1)}, bf16[2,128,128]{2,1,0:T(8,128)(2,1)S(1)}, u32[]{:S(2)}, u32[]{:S(2)}) collective-permute-start(bf16[2,128,128]{2,1,0:T(8,128)(2,1)S(1)} %get-tuple-element.33), channel_id=1, source_target_pairs={{0,8},{8,16},{16,24},{24,32},{32,40},{40,48},{48,56},{56,64},{64,7... | collective-permute-start | bytes 196616 | tf_op jit(solution)/shard_map/ppermute | solution.py:153
  15.2 3.2 %collective-permute-start.4 = (bf16[2,128,128]{2,1,0:T(8,128)(2,1)S(1)}, bf16[2,128,128]{2,1,0:T(8,128)(2,1)S(1)}, u32[]{:S(2)}, u32[]{:S(2)}) collective-permute-start(bf16[2,128,128]{2,1,0:T(8,128)(2,1)S(1)} %get-tuple-element.32), channel_id=1, source_target_pairs={{8,0},{16,8},{24,16},{32,24},{40,32},{48,40},{56,48},{64,56},{72,6... | collective-permute-start | bytes 196616 | tf_op jit(solution)/shard_map/ppermute | solution.py:154
  18.4 0.5 %fusion.2 = (bf16[10,1,128,128]{3,2,1,0:T(8,128)(2,1)S(1)}, bf16[10,1,128,128]{3,2,1,0:T(8,128)(2,1)S(1)}, bf16[10,1,128,128]{3,2,1,0:T(8,128)(2,1)S(1)}) fusion(pred[10]{0:T(512)(128)(4,1)S(1)} %get-tuple-element.38, pred[10]{0:T(512)(128)(4,1)S(1)} %get-tuple-element.39, pred[10]{0:T(512)(128)(4,1)S(1)} %get-tuple-element.37, ...), kind=kLoop, calls=%fused_computation.13 | loop fusion | flops 3440640 | bytes 1966170 | tf_op jit(solution)/shard_map/convert_element_type | solution.py:18
  19.0 1.1 %pad_maximum_fusion.jac_ref = bf16[10,3,128,128]{3,2,1,0:T(8,128)(2,1)} fusion(bf16[10,1,128,128]{3,2,1,0:T(8,128)(2,1)S(1)} %get-tuple-element.31, bf16[10,1,128,128]{3,2,1,0:T(8,128)(2,1)S(1)} %get-tuple-element.30, bf16[10,1,128,128]{3,2,1,0:T(8,128)(2,1)S(1)} %get-tuple-element.29), kind=kLoop, calls=%fused_computation | loop fusion | flops 983040 | bytes 1966080 | tf_op jit(solution)/shard_map/stack | solution.py:19
  20.0 16.0 %collective-permute-done.3.up_ref = bf16[2,128,128]{2,1,0:T(8,128)(2,1)S(1)} collective-permute-done((bf16[2,128,128]{2,1,0:T(8,128)(2,1)S(1)}, bf16[2,128,128]{2,1,0:T(8,128)(2,1)S(1)}, u32[]{:S(2)}, u32[]{:S(2)}) %collective-permute-start.3) | collective-permute-done | bytes 65568 | tf_op jit(solution)/shard_map/ppermute | solution.py:153
  36.1 1.3 %collective-permute-start.5 = (bf16[2,128,128]{2,1,0:T(8,128)(2,1)S(1)}, bf16[2,128,128]{2,1,0:T(8,128)(2,1)S(1)}, u32[]{:S(2)}, u32[]{:S(2)}) collective-permute-start(bf16[2,128,128]{2,1,0:T(8,128)(2,1)S(1)} %collective-permute-done.3.up_ref), channel_id=1, source_target_pairs={{1,0},{2,1},{3,2},{4,3},{5,4},{6,5},{7,6},{9,8},{10,9},{11,10},{12... | collective-permute-start | bytes 196616 | tf_op jit(solution)/shard_map/ppermute | solution.py:181
  37.4 1.3 %collective-permute-start.6 = (bf16[2,128,128]{2,1,0:T(8,128)(2,1)S(1)}, bf16[2,128,128]{2,1,0:T(8,128)(2,1)S(1)}, u32[]{:S(2)}, u32[]{:S(2)}) collective-permute-start(bf16[2,128,128]{2,1,0:T(8,128)(2,1)S(1)} %collective-permute-done.4.down_ref), channel_id=1, source_target_pairs={{0,1},{1,2},{2,3},{3,4},{4,5},{5,6},{6,7},{8,9},{9,10},{10,11},{11... | collective-permute-start | bytes 196616 | tf_op jit(solution)/shard_map/ppermute | solution.py:180
  38.7 0.7 %pad_add_fusion.ids = s32[34]{0:T(128)} fusion(s32[8]{0:T(128)S(1)} %slice_bitcast_fusion.11, s32[24]{0:T(128)S(1)} %slice_bitcast_fusion.12, s32[1]{0:T(128)} %bitcast.1, s32[1]{0:T(128)} %bitcast), kind=kLoop, calls=%fused_computation.38 | loop fusion | flops 102 | bytes 272 | tf_op jit(solution)/shard_map/concatenate | solution.py:183
  39.4 4.1 %collective-permute-done.6.down_left_ref = bf16[2,128,128]{2,1,0:T(8,128)(2,1)S(1)} collective-permute-done((bf16[2,128,128]{2,1,0:T(8,128)(2,1)S(1)}, bf16[2,128,128]{2,1,0:T(8,128)(2,1)S(1)}, u32[]{:S(2)}, u32[]{:S(2)}) %collective-permute-start.6) | collective-permute-done | bytes 65568 | tf_op jit(solution)/shard_map/ppermute | solution.py:180
  43.6 0.6 %copy-done.6 = bf16[2,128,128]{2,1,0:T(8,128)(2,1)} copy-done((bf16[2,128,128]{2,1,0:T(8,128)(2,1)}, bf16[2,128,128]{2,1,0:T(8,128)(2,1)S(1)}, u32[]{:S(2)}) %copy-start.6) | copy-done | bytes 65560
  44.2 0.2 copy-done.2
  44.4 4.7 %shard_map.55 = bf16[10,2,128,128]{3,2,1,0:T(8,128)(2,1)} custom-call(s32[34]{0:T(128)} %pad_add_fusion.ids, f32[10,128]{1,0:T(8,128)} %q_ref.1, bf16[10,3,128,128]{3,2,1,0:T(8,128)(2,1)} %pad_maximum_fusion.jac_ref, bf16[25,128,128]{2,1,0:T(8,128)(2,1)} %copy-done.1, bf16[10,2,128,128]{3,2,1,0:T(8,128)(2,1)} %mid_ref.1, ...), custom_call_target="tpu_custom_call" | custom-call | tf_op jit(solution)/shard_map/pallas_call | solution.py:192
  (27 shorter events, 0.2 us)
Async XLA Ops:
  0.0 43.5 %collective-permute-start.1 = (bf16[10,2,128,128]{3,2,1,0:T(8,128)(2,1)}, bf16[10,2,128,128]{3,2,1,0:T(8,128)(2,1)S(1)}, u32[]{:S(2)}, u32[]{:S(2)}) collective-permute-start(bf16[10,2,128,128]{3,2,1,0:T(8,128)(2,1)} %mid_ref.1), channel_id=1, source_target_pairs={{0,1},{1,2},{2,3},{3,4},{4,5},{5,6},{6,7},{8,9},{9,10},{10,11},{11... | collective-permute-start | bytes 1966088 | tf_op jit(solution)/shard_map/ppermute | solution.py:151
  1.3 42.3 %collective-permute-start.2 = (bf16[10,2,128,128]{3,2,1,0:T(8,128)(2,1)}, bf16[10,2,128,128]{3,2,1,0:T(8,128)(2,1)}, u32[]{:S(2)}, u32[]{:S(2)}) collective-permute-start(bf16[10,2,128,128]{3,2,1,0:T(8,128)(2,1)} %mid_ref.1), channel_id=1, source_target_pairs={{1,0},{2,1},{3,2},{4,3},{5,4},{6,5},{7,6},{9,8},{10,9},{11,10},{12... | collective-permute-start | bytes 1966088 | tf_op jit(solution)/shard_map/ppermute | solution.py:152
  6.7 0.7 %copy-start.7 = (s32[10,3]{0,1:T(4,128)S(1)}, s32[10,3]{0,1:T(4,128)}, u32[]{:S(2)}) copy-start(s32[10,3]{0,1:T(4,128)} %param.11) | copy-start | bytes 364
  7.6 0.7 %copy-start.8 = (s32[10]{0:T(128)S(1)}, s32[10]{0:T(128)}, u32[]{:S(2)}) copy-start(s32[10]{0:T(128)} %param.12) | copy-start | bytes 124
  9.6 8.8 %copy-start = (bf16[10,3,128,128]{3,2,1,0:T(8,128)(2,1)S(1)}, bf16[10,3,128,128]{3,2,1,0:T(8,128)(2,1)}, u32[]{:S(2)}) copy-start(bf16[10,3,128,128]{3,2,1,0:T(8,128)(2,1)} %param.10) | copy-start | bytes 2949124
  9.8 28.9 %collective-permute-start = (bf16[25,128,128]{2,1,0:T(8,128)(2,1)S(1)}, bf16[25,128,128]{2,1,0:T(8,128)(2,1)S(1)}, u32[]{:S(2)}, u32[]{:S(2)}) collective-permute-start(bf16[25,128,128]{2,1,0:T(8,128)(2,1)S(1)} %pad_maximum_fusion.1), channel_id=1, source_target_pairs={{0,8},{8,16},{16,24},{24,32},{32,40},{40,48},{48,56},{56,64},{64,7... | collective-permute-start | bytes 2457608 | tf_op jit(solution)/shard_map/ppermute | solution.py:174
  12.8 23.3 %collective-permute-start.3 = (bf16[2,128,128]{2,1,0:T(8,128)(2,1)S(1)}, bf16[2,128,128]{2,1,0:T(8,128)(2,1)S(1)}, u32[]{:S(2)}, u32[]{:S(2)}) collective-permute-start(bf16[2,128,128]{2,1,0:T(8,128)(2,1)S(1)} %get-tuple-element.33), channel_id=1, source_target_pairs={{0,8},{8,16},{16,24},{24,32},{32,40},{40,48},{48,56},{56,64},{64,7... | collective-permute-start | bytes 196616 | tf_op jit(solution)/shard_map/ppermute | solution.py:153
  15.2 22.2 %collective-permute-start.4 = (bf16[2,128,128]{2,1,0:T(8,128)(2,1)S(1)}, bf16[2,128,128]{2,1,0:T(8,128)(2,1)S(1)}, u32[]{:S(2)}, u32[]{:S(2)}) collective-permute-start(bf16[2,128,128]{2,1,0:T(8,128)(2,1)S(1)} %get-tuple-element.32), channel_id=1, source_target_pairs={{8,0},{16,8},{24,16},{32,24},{40,32},{48,40},{56,48},{64,56},{72,6... | collective-permute-start | bytes 196616 | tf_op jit(solution)/shard_map/ppermute | solution.py:154
  36.1 7.5 %copy-start.3 = (bf16[2,128,128]{2,1,0:T(8,128)(2,1)}, bf16[2,128,128]{2,1,0:T(8,128)(2,1)S(1)}, u32[]{:S(2)}) copy-start(bf16[2,128,128]{2,1,0:T(8,128)(2,1)S(1)} %collective-permute-done.3.up_ref) | copy-start | bytes 196612
  36.1 3.4 %collective-permute-start.5 = (bf16[2,128,128]{2,1,0:T(8,128)(2,1)S(1)}, bf16[2,128,128]{2,1,0:T(8,128)(2,1)S(1)}, u32[]{:S(2)}, u32[]{:S(2)}) collective-permute-start(bf16[2,128,128]{2,1,0:T(8,128)(2,1)S(1)} %collective-permute-done.3.up_ref), channel_id=1, source_target_pairs={{1,0},{2,1},{3,2},{4,3},{5,4},{6,5},{7,6},{9,8},{10,9},{11,10},{12... | collective-permute-start | bytes 196616 | tf_op jit(solution)/shard_map/ppermute | solution.py:181
  37.4 6.2 %copy-start.4 = (bf16[2,128,128]{2,1,0:T(8,128)(2,1)}, bf16[2,128,128]{2,1,0:T(8,128)(2,1)S(1)}, u32[]{:S(2)}) copy-start(bf16[2,128,128]{2,1,0:T(8,128)(2,1)S(1)} %collective-permute-done.4.down_ref) | copy-start | bytes 196612
  37.4 6.2 %collective-permute-start.6 = (bf16[2,128,128]{2,1,0:T(8,128)(2,1)S(1)}, bf16[2,128,128]{2,1,0:T(8,128)(2,1)S(1)}, u32[]{:S(2)}, u32[]{:S(2)}) collective-permute-start(bf16[2,128,128]{2,1,0:T(8,128)(2,1)S(1)} %collective-permute-done.4.down_ref), channel_id=1, source_target_pairs={{0,1},{1,2},{2,3},{3,4},{4,5},{5,6},{6,7},{8,9},{9,10},{10,11},{11... | collective-permute-start | bytes 196616 | tf_op jit(solution)/shard_map/ppermute | solution.py:180
  38.7 4.9 %copy-start.1 = (bf16[25,128,128]{2,1,0:T(8,128)(2,1)}, bf16[25,128,128]{2,1,0:T(8,128)(2,1)S(1)}, u32[]{:S(2)}) copy-start(bf16[25,128,128]{2,1,0:T(8,128)(2,1)S(1)} %collective-permute-done.recv_ref) | copy-start | bytes 2457604
  39.4 4.1 %copy-start.5 = (bf16[2,128,128]{2,1,0:T(8,128)(2,1)}, bf16[2,128,128]{2,1,0:T(8,128)(2,1)S(1)}, u32[]{:S(2)}) copy-start(bf16[2,128,128]{2,1,0:T(8,128)(2,1)S(1)} %collective-permute-done.5.up_right_ref) | copy-start | bytes 196612
  43.5 0.6 %copy-start.6 = (bf16[2,128,128]{2,1,0:T(8,128)(2,1)}, bf16[2,128,128]{2,1,0:T(8,128)(2,1)S(1)}, u32[]{:S(2)}) copy-start(bf16[2,128,128]{2,1,0:T(8,128)(2,1)S(1)} %collective-permute-done.6.down_left_ref) | copy-start | bytes 196612
  43.5 0.9 %copy-start.2 = (bf16[10,2,128,128]{3,2,1,0:T(8,128)(2,1)}, bf16[10,2,128,128]{3,2,1,0:T(8,128)(2,1)S(1)}, u32[]{:S(2)}) copy-start(bf16[10,2,128,128]{3,2,1,0:T(8,128)(2,1)S(1)} %collective-permute-done.1.left_ref) | copy-start | bytes 1966084
